TPU v7x, 32 devices: a whole 2x2x4 slice. The times are simulated.
32 devices in a mesh: parts: 2 (over x), wide: 16 (over z, y, core).
Axes of the slice: x: 2, y: 2, z: 4, core: 2. Of those that a mesh axis runs over, the one named last changes fastest.
Arguments:
- frames: float32 [65536, 80], P(('parts', 'wide')), parts along dimension 0, may hold values from -6 to 6
- seg_start: int32 [2048], P(('parts', 'wide')), parts along dimension 0, may hold values from 1 to 1983
- seg_dest: int32 [2048], P(('parts', 'wide')), parts along dimension 0, may hold values from -1 to 15, as said below
- rec_id: int32 [2048], P(('parts', 'wide')), parts along dimension 0, may hold values from 0 to 63
- conv_weight: float32 [240, 1024], replicated, may hold values from -0.375 to 0.375
- conv_bias: float32 [1024], replicated, may hold values from -0.5 to 0.5
- proj_weight: float32 [2048, 192], replicated, may hold values from -0.125 to 0.125
- smooth_kernel: float32 [3, 3], replicated, may hold values from 0.2 to 1
Outputs:
- smoothed: float32 [1024, 512], P(('parts', 'wide')), parts along dimension 0
There are 2 independent parts, one for each index of `parts`. A program takes and returns all parts, laid end to end along the dimension named above; an argument that names none is the same for every part. Nothing has to cross between parts.
Inputs may be any that keep to these rules, and one draw needn't show every extreme that they name: `seg_dest`: -1 marks an unused slot; on each device the used slots come first; at most 4 segments of one device go to one device, and some device reaches this; every device is assigned exactly 32 segments.
All inputs are finite; a program needn't handle non-finite values.
Results may differ from a plain program's by a relative error of at most 0.001.
Values may be sent and summed in bfloat16 or wider, within the bound.
No kernel may reach another device: no remote copies, remote signals or barrier semaphores. Data moves between devices by JAX's collectives and lax.ppermute only.
A program may use at most 64 MiB of HBM per device.

v0:
```python
import math

import jax
import jax.numpy as jnp
from jax import lax
from jax.sharding import PartitionSpec as P

FEAT = 80
CH = 1024
EMB = 192
SEGLEN = 64
SEG_DEV = 32


PRECISE = lax.Precision.HIGHEST
AFF_SCALE = 8.0


def pool_segments(windows, conv_weight, conv_bias, proj_weight):
    seg_total = windows.shape[0]
    block_size = math.gcd(seg_total, 16)
    grouped = windows.reshape(seg_total // block_size, block_size, SEGLEN + 2, FEAT)

    def one_block(win_block):
        stacked = jnp.concatenate(
            [win_block[:, 0:SEGLEN], win_block[:, 1 : SEGLEN + 1], win_block[:, 2 : SEGLEN + 2]],
            axis=2,
        )
        preact = jnp.dot(
            stacked.reshape(block_size * SEGLEN, 3 * FEAT),
            conv_weight,
            precision=PRECISE,
            preferred_element_type=jnp.float32,
        )
        activated = jax.nn.relu(preact + conv_bias).reshape(block_size, SEGLEN, CH)
        frame_mean = jnp.mean(activated, axis=1)
        deviation = activated - frame_mean[:, None, :]
        frame_std = jnp.sqrt(jnp.mean(deviation * deviation, axis=1) + 1e-05)
        return jnp.concatenate([frame_mean, frame_std], axis=1)

    pooled = lax.map(one_block, grouped).reshape(seg_total, 2 * CH)
    return jnp.dot(pooled, proj_weight, precision=PRECISE, preferred_element_type=jnp.float32)


def smooth_rows(padded_rows, smooth_kernel):
    padded = jnp.pad(padded_rows, ((0, 0), (1, 1)))
    height = padded.shape[0] - 2
    col_count = padded.shape[1] - 2
    result = jnp.zeros((height, col_count), padded.dtype)
    for row_off in range(3):
        for col_off in range(3):
            result = (
                result
                + smooth_kernel[row_off, col_off]
                * padded[row_off : row_off + height, col_off : col_off + col_count]
            )
    return result


def compact(arrived_rec):
    present = arrived_rec >= 0
    position = jnp.cumsum(present.astype(jnp.int32)) - 1
    selected = present[None, :] & (
        position[None, :] == jnp.arange(SEG_DEV, dtype=jnp.int32)[:, None]
    )
    seg_rec = jnp.sum(jnp.where(selected, arrived_rec[None, :], 0), axis=1).astype(jnp.int32)
    return (selected.astype(jnp.float32), seg_rec)


def score_panel(unit, seg_rec, panel_unit, panel_rec):
    scores = AFF_SCALE * jnp.dot(unit, panel_unit.T, preferred_element_type=jnp.float32)
    return jnp.where(seg_rec[:, None] == panel_rec[None, :], 0.0, scores)


def per_device(
    frames, seg_start, seg_dest, rec_id, conv_weight, conv_bias, proj_weight, smooth_kernel
):
    group_size = lax.axis_size("wide")
    slot_count = seg_dest.shape[0]
    pair_cap = -(-slot_count // group_size)
    matches = (seg_dest[None, :] == jnp.arange(group_size, dtype=jnp.int32)[:, None]).astype(
        jnp.int32
    )
    order_pos = jnp.sum(jnp.cumsum(matches, axis=1) * matches, axis=0) - 1
    target = jnp.where(seg_dest >= 0, seg_dest * pair_cap + order_pos, -1)
    table = target[None, :] == jnp.arange(group_size * pair_cap, dtype=jnp.int32)[:, None]
    router = table.astype(jnp.float32)
    send_rec = (jnp.sum(jnp.where(table, rec_id[None, :] + 1, 0), axis=1) - 1).reshape(
        group_size, pair_cap
    )

    def cut_one(offset):
        return lax.dynamic_slice_in_dim(frames, offset - 1, SEGLEN + 2, 0)

    windows = jax.vmap(cut_one)(seg_start)
    embedded = pool_segments(windows, conv_weight, conv_bias, proj_weight)
    outgoing = jnp.dot(router, embedded, precision=PRECISE).reshape(group_size, pair_cap, EMB)
    arrived, arrived_rec = (
        lax.all_to_all(outgoing, "wide", split_axis=0, concat_axis=0, tiled=True),
        lax.all_to_all(send_rec, "wide", split_axis=0, concat_axis=0, tiled=True),
    )
    selector, seg_rec = compact(arrived_rec.reshape(group_size * pair_cap))
    seg_rows = jnp.dot(selector, arrived.reshape(group_size * pair_cap, EMB), precision=PRECISE)
    mean_sum = lax.psum(jnp.sum(seg_rows, axis=0), "wide")
    centred = seg_rows - mean_sum / (SEG_DEV * group_size)
    unit = (centred / jnp.sqrt(jnp.sum(centred * centred, axis=1, keepdims=True) + 1e-06)).astype(
        jnp.bfloat16
    )
    total_rows = SEG_DEV * group_size
    all_rec = jnp.zeros((total_rows,), jnp.int32)
    kept_rec = all_rec
    panel_unit = lax.all_gather(unit, "wide", axis=0, tiled=True)
    panel_rec = lax.all_gather(seg_rec, "wide", axis=0, tiled=True)
    scores = score_panel(unit, seg_rec, panel_unit, panel_rec)
    affinity = scores
    kept_rec = lax.dynamic_update_slice_in_dim(kept_rec, panel_rec, jnp.int32(0), 0)
    folded = (affinity, panel_unit, kept_rec)
    affinity, all_unit, all_rec = folded
    my_index = lax.axis_index("wide")
    above = my_index * SEG_DEV - 1
    below = my_index * SEG_DEV + SEG_DEV
    above_safe = jnp.clip(above, 0, total_rows - 1)
    below_safe = jnp.clip(below, 0, total_rows - 1)
    edge_unit = jnp.concatenate(
        [
            lax.dynamic_slice_in_dim(all_unit, above_safe, 1, 0),
            lax.dynamic_slice_in_dim(all_unit, below_safe, 1, 0),
        ],
        axis=0,
    )
    edge_rec = jnp.concatenate(
        [
            lax.dynamic_slice_in_dim(all_rec, above_safe, 1, 0),
            lax.dynamic_slice_in_dim(all_rec, below_safe, 1, 0),
        ],
        axis=0,
    )
    edge_rows = score_panel(edge_unit, edge_rec, all_unit, all_rec)
    inside = jnp.stack([above >= 0, below < total_rows])
    edge_rows = jnp.where(inside[:, None], edge_rows, 0.0)
    padded = jnp.concatenate([edge_rows[0:1], affinity, edge_rows[1:2]], axis=0)
    return smooth_rows(padded, smooth_kernel)


def solution(mesh):
    in_specs = (
        P(("parts", "wide"), None),
        P(("parts", "wide")),
        P(("parts", "wide")),
        P(("parts", "wide")),
        P(),
        P(),
        P(),
        P(),
    )
    out_specs = P(("parts", "wide"), None)
    return jax.shard_map(
        per_device, mesh=mesh, in_specs=in_specs, out_specs=out_specs, check_vma=False
    )
```

profile of v0, /device:TPU:0, one launch (start us, length us, event | category | flops | bytes accessed | tf_op | source)
XLA Modules:
  0.0 301.8 jit_solution(8323069585257110534)
XLA Ops:
  3.2 7.4 %all-to-all-start = ((s32[16,1,4]{2,1,0:T(1,128)}), s32[16,1,4]{2,1,0:T(1,128)S(1)}, u32[]{:S(2)}, u32[]{:S(2)}) async-start(s32[16,1,4]{2,1,0:T(1,128)} %bitcast.7), calls=%async_computation | async-start | bytes 16384 | tf_op jit(solution)/shard_map/all_to_all | solution.py:100
  11.3 178.8 %while.12 = (s32[]{:T(128)}, f32[2048,80]{0,1:T(8,128)}, s32[64,2]{0,1:T(2,128)S(1)}, f32[64,66,80]{1,2,0:T(8,128)}, s32[]{:T(128)}) while((s32[]{:T(128)}, f32[2048,80]{0,1:T(8,128)}, s32[64,2]{0,1:T(2,128)S(1)}, f32[64,66,80]{1,2,0:T(8,128)}, s32[]{:T(128)}) %tuple.54), condition=%wide.while_cond, body=%wide.while_body.sunk | while | flops 2 | bytes 82533 | solution.py:93
  11.9 2.2 bitcast_dynamic-update-slice_fusion.2
  14.7 2.2 bitcast_dynamic-update-slice_fusion.2
  17.5 2.2 bitcast_dynamic-update-slice_fusion.2
  25.9 2.2 bitcast_dynamic-update-slice_fusion.2
  28.7 2.2 bitcast_dynamic-update-slice_fusion.2
  34.3 2.2 bitcast_dynamic-update-slice_fusion.2
  37.1 2.2 bitcast_dynamic-update-slice_fusion.2
  39.8 2.2 bitcast_dynamic-update-slice_fusion.2
  45.3 2.2 bitcast_dynamic-update-slice_fusion.2
  48.1 2.2 bitcast_dynamic-update-slice_fusion.2
  50.9 2.2 bitcast_dynamic-update-slice_fusion.2
  53.7 2.2 bitcast_dynamic-update-slice_fusion.2
  56.5 2.2 bitcast_dynamic-update-slice_fusion.2
  59.3 2.2 bitcast_dynamic-update-slice_fusion.2
  62.1 2.2 bitcast_dynamic-update-slice_fusion.2
  67.7 2.2 bitcast_dynamic-update-slice_fusion.2
  70.5 2.2 bitcast_dynamic-update-slice_fusion.2
  73.3 2.2 bitcast_dynamic-update-slice_fusion.2
  76.1 2.2 bitcast_dynamic-update-slice_fusion.2
  78.9 2.2 bitcast_dynamic-update-slice_fusion.2
  84.5 2.2 bitcast_dynamic-update-slice_fusion.2
  87.3 2.2 bitcast_dynamic-update-slice_fusion.2
  92.9 2.2 bitcast_dynamic-update-slice_fusion.2
  95.7 2.2 bitcast_dynamic-update-slice_fusion.2
  98.5 2.2 bitcast_dynamic-update-slice_fusion.2
  104.0 2.2 bitcast_dynamic-update-slice_fusion.2
  106.8 2.2 bitcast_dynamic-update-slice_fusion.2
  112.4 2.2 bitcast_dynamic-update-slice_fusion.2
  115.2 2.2 bitcast_dynamic-update-slice_fusion.2
  120.8 2.2 bitcast_dynamic-update-slice_fusion.2
  123.6 2.2 bitcast_dynamic-update-slice_fusion.2
  126.4 2.2 bitcast_dynamic-update-slice_fusion.2
  129.2 2.2 bitcast_dynamic-update-slice_fusion.2
  132.0 2.2 bitcast_dynamic-update-slice_fusion.2
  134.8 2.2 bitcast_dynamic-update-slice_fusion.2
  137.6 2.2 bitcast_dynamic-update-slice_fusion.2
  143.2 2.2 bitcast_dynamic-update-slice_fusion.2
  146.0 2.2 bitcast_dynamic-update-slice_fusion.2
  148.8 2.2 bitcast_dynamic-update-slice_fusion.2
  151.6 2.2 bitcast_dynamic-update-slice_fusion.2
  154.4 2.2 bitcast_dynamic-update-slice_fusion.2
  157.2 2.2 bitcast_dynamic-update-slice_fusion.2
  160.0 2.2 bitcast_dynamic-update-slice_fusion.2
  162.8 2.2 bitcast_dynamic-update-slice_fusion.2
  165.6 2.2 bitcast_dynamic-update-slice_fusion.2
  168.4 2.2 bitcast_dynamic-update-slice_fusion.2
  171.2 2.2 bitcast_dynamic-update-slice_fusion.2
  176.8 2.2 bitcast_dynamic-update-slice_fusion.2
  179.6 2.2 bitcast_dynamic-update-slice_fusion.2
  182.4 2.2 bitcast_dynamic-update-slice_fusion.2
  185.2 2.2 bitcast_dynamic-update-slice_fusion.2
  190.2 3.3 %copy.18 = f32[4,16,66,80]{3,2,1,0:T(8,128)} copy(f32[4,16,66,80]{2,3,1,0:T(8,128)} %bitcast.62) | data formatting | bytes 2703360 | tf_op jit(solution)/shard_map/while | solution.py:41
  193.5 26.8 %while.11 = (s32[]{:T(128)}, f32[4,16,2048]{2,1,0:T(8,128)S(1)}, f32[4,16,66,80]{3,2,1,0:T(8,128)}, f32[240,1024]{1,0:T(8,128)S(1)}, f32[1024]{0:T(1024)S(1)}, /*index=5*/s32[]{:T(128)}) while((s32[]{:T(128)}, f32[4,16,2048]{2,1,0:T(8,128)S(1)}, f32[4,16,66,80]{3,2,1,0:T(8,128)}, f32[240,1024]{1,0:T(8,128)S(1)}, f32[1024]{0:T(1024)S(1)}, ...), condition=%wide.region_8.9_spmd, body=%wide.region_5.8_spmd.sunk | while | flops 3028828160 | bytes 15691861 | solution.py:41
  195.2 4.0 %bitcast_reduce_fusion.2 = (f32[16,1024]{1,0:T(8,128)S(1)}, f32[1024,1024]{1,0:T(8,128)S(1)}) fusion(f32[1024]{0:T(1024)S(1)} %get-tuple-element.202, f32[1024,240]{1,0:T(8,128)S(1)} %bitcast.61, f32[240,1024]{1,0:T(8,128)S(1)} %get-tuple-element.201), kind=kOutput, calls=%fused_computation.1.clone.1 | convolution fusion | flops 3023028224 | bytes 6230016 | tf_op jit(solution)/shard_map/while/body/eval_jaxpr/dot_general | solution.py:29
  201.9 4.0 %bitcast_reduce_fusion.2 = (f32[16,1024]{1,0:T(8,128)S(1)}, f32[1024,1024]{1,0:T(8,128)S(1)}) fusion(f32[1024]{0:T(1024)S(1)} %get-tuple-element.202, f32[1024,240]{1,0:T(8,128)S(1)} %bitcast.61, f32[240,1024]{1,0:T(8,128)S(1)} %get-tuple-element.201), kind=kOutput, calls=%fused_computation.1.clone.1 | convolution fusion | flops 3023028224 | bytes 6230016 | tf_op jit(solution)/shard_map/while/body/eval_jaxpr/dot_general | solution.py:29
  208.6 4.0 %bitcast_reduce_fusion.2 = (f32[16,1024]{1,0:T(8,128)S(1)}, f32[1024,1024]{1,0:T(8,128)S(1)}) fusion(f32[1024]{0:T(1024)S(1)} %get-tuple-element.202, f32[1024,240]{1,0:T(8,128)S(1)} %bitcast.61, f32[240,1024]{1,0:T(8,128)S(1)} %get-tuple-element.201), kind=kOutput, calls=%fused_computation.1.clone.1 | convolution fusion | flops 3023028224 | bytes 6230016 | tf_op jit(solution)/shard_map/while/body/eval_jaxpr/dot_general | solution.py:29
  215.3 4.0 %bitcast_reduce_fusion.2 = (f32[16,1024]{1,0:T(8,128)S(1)}, f32[1024,1024]{1,0:T(8,128)S(1)}) fusion(f32[1024]{0:T(1024)S(1)} %get-tuple-element.202, f32[1024,240]{1,0:T(8,128)S(1)} %bitcast.61, f32[240,1024]{1,0:T(8,128)S(1)} %get-tuple-element.201), kind=kOutput, calls=%fused_computation.1.clone.1 | convolution fusion | flops 3023028224 | bytes 6230016 | tf_op jit(solution)/shard_map/while/body/eval_jaxpr/dot_general | solution.py:29
  224.8 5.8 %all-to-all-start.1 = ((f32[16,4,192]{2,1,0:T(4,128)}), f32[16,4,192]{2,1,0:T(4,128)S(1)}, u32[]{:S(2)}, u32[]{:S(2)}) async-start(f32[16,4,192]{2,1,0:T(4,128)} %reshape.108), calls=%async_computation.1 | async-start | bytes 131072 | tf_op jit(solution)/shard_map/all_to_all | solution.py:99
  232.7 12.4 %all-reduce.2 = s32[512]{0:T(512)S(1)} all-reduce(s32[512]{0:T(512)S(1)} %dynamic-update-slice.2), channel_id=1, replica_groups=mesh['parts'=2,'wide'=16] {'wide'}, use_global_device_ids=true, to_apply=%add.2 | all-reduce | flops 512 | bytes 4096
  247.3 29.5 %psum.7 = f32[192]{0:T(256)S(1)} all-reduce(f32[192]{0:T(256)S(1)} %get-tuple-element.101), channel_id=1, replica_groups=mesh['parts'=2,'wide'=16] {'wide'}, use_global_device_ids=true, to_apply=%region_10.11 | all-reduce | flops 192 | bytes 1536 | tf_op jit(solution)/shard_map/psum | solution.py:104
  277.0 17.9 %all_gather.7 = bf16[512,192]{1,0:T(8,128)(2,1)S(1)} all-gather(bf16[32,192]{1,0:T(8,128)(2,1)S(1)} %divide_convert_fusion), channel_id=1, replica_groups=mesh['parts'=2,'wide'=16] {'wide'}, dimensions={0}, use_global_device_ids=true | all-gather | bytes 208896 | tf_op jit(solution)/shard_map/all_gather | solution.py:112
  295.5 6.3 %fusion.7 = f32[32,512]{1,0:T(8,128)} fusion(f32[34,514]{1,0:T(8,128)S(1)} %select_maximum_fusion, f32[1,512]{1,0:T(1,128)S(1)} %get-tuple-element.89, f32[32,512]{1,0:T(8,128)S(1)} %fusion.3, f32[1,512]{1,0:T(1,128)S(1)} %get-tuple-element.88, f32[]{:T(128)} %bitcast.19, f32[]{:T(128)} %bitcast.18, f32[]{:T(128)} %bitcast.17, f32[]{:T(128)} %bitcast.16, ...), kind=kLoop, calls=%fused_computation.24 | loop fusion | flops 311296 | bytes 528420 | tf_op jit(solution)/shard_map/add | solution.py:53
  (221 shorter events, 89.5 us)
Async XLA Ops:
  0.0 220.3 %copy-start = (f32[2048,192]{0,1:T(8,128)S(1)}, f32[2048,192]{0,1:T(8,128)}, u32[]{:S(2)}) copy-start(f32[2048,192]{0,1:T(8,128)} %param.16) | copy-start | bytes 4718596
  0.0 193.4 %copy-start.1 = (f32[240,1024]{1,0:T(8,128)S(1)}, f32[240,1024]{1,0:T(8,128)}, u32[]{:S(2)}) copy-start(f32[240,1024]{1,0:T(8,128)} %param.14) | copy-start | bytes 2949124
  0.0 193.4 %copy-start.2 = (f32[1024]{0:T(1024)S(1)}, f32[1024]{0:T(1024)}, u32[]{:S(2)}) copy-start(f32[1024]{0:T(1024)} %param.15) | copy-start | bytes 12292
  3.2 221.6 %all-to-all-start = ((s32[16,1,4]{2,1,0:T(1,128)}), s32[16,1,4]{2,1,0:T(1,128)S(1)}, u32[]{:S(2)}, u32[]{:S(2)}) async-start(s32[16,1,4]{2,1,0:T(1,128)} %bitcast.7), calls=%async_computation | async-start | bytes 16384 | tf_op jit(solution)/shard_map/all_to_all | solution.py:100
  193.4 29.3 %copy-start.3 = (f32[3,3]{1,0:T(4,128)S(1)}, f32[3,3]{1,0:T(4,128)}, u32[]{:S(2)}) copy-start(f32[3,3]{1,0:T(4,128)} %param.17) | copy-start | bytes 112
  193.4 30.1 %copy-start.4 = (u32[32]{0:T(128)S(1)}, u32[32]{0:T(128)}, u32[]{:S(2)}) copy-start(u32[32]{0:T(128)} %constant.91) | copy-start | bytes 388
  224.8 22.3 %all-to-all-start.1 = ((f32[16,4,192]{2,1,0:T(4,128)}), f32[16,4,192]{2,1,0:T(4,128)S(1)}, u32[]{:S(2)}, u32[]{:S(2)}) async-start(f32[16,4,192]{2,1,0:T(4,128)} %reshape.108), calls=%async_computation.1 | async-start | bytes 131072 | tf_op jit(solution)/shard_map/all_to_all | solution.py:99
where the time goes:
time: 306 us; the launch traced here: 302 us
  local copies, waits for them, and re-layouts  191 us (62%)
  blocking collectives  59.8 us (20%)
  matrix products  18.5 us (6%)
  other arithmetic  17.7 us (6%)
  starting transfers between devices  13.2 us (4%)
    gather x192, local copies, waits for them, and re-layouts  179 us
    psum x1, blocking collectives, per_device(): mean_sum = lax.psum(jnp.sum(seg_rows, axis=0), 'wide')  29.5 us
    all_gather x1, blocking collectives, per_device(): panel_unit = lax.all_gather(unit, 'wide', axis=0, tiled=True)  17.9 us
    dot_general x4, matrix products, one_block(): jnp.dot(stacked.reshape(block_size * SEGLEN, 3 * FEAT), conv_weight, prec...  16.2 us
    unnamed x1, blocking collectives  12.4 us
    all_to_all x1, starting transfers between devices, per_device(): lax.all_to_all(send_rec, 'wide', split_axis=0, concat_axis=0, tiled=True)  7.39 us
    add x1, other arithmetic, smooth_rows(): result + smooth_kernel[row_off, col_off] * padded[row_off:row_off + heigh...  6.29 us
  transfers between devices with their start and end apart: 2, of which 0 were waited for; matrix products, arithmetic and copies ran while one was open for 72% of the time, Pallas kernels for 0%

commit v1 on v0

v1 whole, which is shorter than its diff:
```python
import functools

import jax
import jax.numpy as jnp
from jax import lax
from jax.experimental import pallas as pl
from jax.experimental.pallas import tpu as pltpu
from jax.sharding import PartitionSpec as P

FEAT = 80
CH = 1024
EMB = 192
SEGLEN = 64
SEG_DEV = 32


PRECISE = lax.Precision.HIGHEST
AFF_SCALE = 8.0
SEG_BLOCK = 8
WIN = SEGLEN + 8


def _pool_kernel(starts_ref, x3_hbm, w_ref, b_ref, out_ref, buf, sem):
    step = pl.program_id(0)
    steps = pl.num_programs(0)
    block = buf.shape[1]
    rows = x3_hbm.shape[0]

    def aligned_start(blk, j):
        start = starts_ref[blk * block + j]
        return jnp.minimum((start // 8) * 8, rows - WIN)

    def window_copy(blk, slot, j):
        base = pl.multiple_of(aligned_start(blk, j), 8)
        return pltpu.make_async_copy(
            x3_hbm.at[pl.ds(base, WIN)], buf.at[slot, j], sem.at[slot, j]
        )

    @pl.when(step == 0)
    def _():
        for j in range(block):
            window_copy(0, 0, j).start()

    slot = step % 2

    @pl.when(step + 1 < steps)
    def _():
        for j in range(block):
            window_copy(step + 1, 1 - slot, j).start()

    for j in range(block):
        window_copy(step, slot, j).wait()

    stacked = buf[slot].reshape(block * WIN, 3 * FEAT)
    preact = jnp.dot(stacked, w_ref[...], precision=PRECISE, preferred_element_type=jnp.float32)
    activated = jnp.maximum(preact + b_ref[...], 0.0)
    frame_idx = lax.broadcasted_iota(jnp.int32, (WIN, CH), 0)
    means = []
    stds = []
    for j in range(block):
        shift = starts_ref[step * block + j] - aligned_start(step, j)
        inside = (frame_idx >= shift) & (frame_idx < shift + SEGLEN)
        seg_act = activated[j * WIN : (j + 1) * WIN]
        frame_mean = jnp.sum(jnp.where(inside, seg_act, 0.0), axis=0, keepdims=True) / SEGLEN
        deviation = jnp.where(inside, seg_act - frame_mean, 0.0)
        frame_var = jnp.sum(deviation * deviation, axis=0, keepdims=True) / SEGLEN
        means.append(frame_mean)
        stds.append(jnp.sqrt(frame_var + 1e-05))
    out_ref[:, :CH] = jnp.concatenate(means, axis=0)
    out_ref[:, CH:] = jnp.concatenate(stds, axis=0)


def pool_slots(frames, seg_start, conv_weight, conv_bias):
    rows = frames.shape[0]
    slots = seg_start.shape[0]
    zero = jnp.zeros((1, FEAT), frames.dtype)
    x3 = jnp.concatenate(
        [
            jnp.concatenate([zero, frames[:-1]], axis=0),
            frames,
            jnp.concatenate([frames[1:], zero], axis=0),
        ],
        axis=1,
    )
    starts = jnp.clip(seg_start, 0, rows - SEGLEN).astype(jnp.int32)
    block = SEG_BLOCK if slots % SEG_BLOCK == 0 else 1
    grid_spec = pltpu.PrefetchScalarGridSpec(
        num_scalar_prefetch=1,
        grid=(slots // block,),
        in_specs=[
            pl.BlockSpec(memory_space=pl.ANY),
            pl.BlockSpec((3 * FEAT, CH), lambda i, s: (0, 0)),
            pl.BlockSpec((1, CH), lambda i, s: (0, 0)),
        ],
        out_specs=pl.BlockSpec((block, 2 * CH), lambda i, s: (i, 0)),
        scratch_shapes=[
            pltpu.VMEM((2, block, WIN, 3 * FEAT), jnp.float32),
            pltpu.SemaphoreType.DMA((2, block)),
        ],
    )
    return pl.pallas_call(
        _pool_kernel,
        out_shape=jax.ShapeDtypeStruct((slots, 2 * CH), jnp.float32),
        grid_spec=grid_spec,
        compiler_params=pltpu.CompilerParams(dimension_semantics=("arbitrary",)),
        cost_estimate=pl.CostEstimate(
            flops=2 * slots * WIN * 3 * FEAT * CH * 6,
            transcendentals=slots * CH,
            bytes_accessed=slots * WIN * 3 * FEAT * 4 + 3 * FEAT * CH * 4 + slots * 2 * CH * 4,
        ),
    )(starts, x3, conv_weight, conv_bias.reshape(1, CH))


def smooth_rows(padded_rows, smooth_kernel):
    padded = jnp.pad(padded_rows, ((0, 0), (1, 1)))
    height = padded.shape[0] - 2
    col_count = padded.shape[1] - 2
    result = jnp.zeros((height, col_count), padded.dtype)
    for row_off in range(3):
        for col_off in range(3):
            result = (
                result
                + smooth_kernel[row_off, col_off]
                * padded[row_off : row_off + height, col_off : col_off + col_count]
            )
    return result


def per_device(
    frames, seg_start, seg_dest, rec_id, conv_weight, conv_bias, proj_weight, smooth_kernel
):
    group_size = lax.axis_size("wide")
    total_rows = SEG_DEV * group_size
    pooled = pool_slots(frames, seg_start, conv_weight, conv_bias)
    embedded = jnp.dot(pooled, proj_weight, precision=PRECISE, preferred_element_type=jnp.float32)
    packed = jnp.concatenate(
        [
            embedded,
            seg_dest.astype(jnp.float32)[:, None],
            rec_id.astype(jnp.float32)[:, None],
        ],
        axis=1,
    )
    every = lax.all_gather(packed, "wide", axis=0, tiled=True)
    all_emb = every[:, :EMB]
    all_dest = every[:, EMB].astype(jnp.int32)
    all_rec = every[:, EMB + 1].astype(jnp.int32)
    slot_total = all_dest.shape[0]
    used = all_dest >= 0

    mean_sum = jnp.sum(jnp.where(used[:, None], all_emb, 0.0), axis=0)
    centred = all_emb - mean_sum / total_rows
    unit = (centred / jnp.sqrt(jnp.sum(centred * centred, axis=1, keepdims=True) + 1e-06)).astype(
        jnp.bfloat16
    )

    slot_ids = jnp.arange(slot_total, dtype=jnp.int32)
    earlier = (slot_ids[None, :] < slot_ids[:, None]) & (all_dest[None, :] == all_dest[:, None])
    rank = jnp.sum(earlier.astype(jnp.int32), axis=1)
    position = jnp.where(used, all_dest * SEG_DEV + rank, -1)
    picks = position[None, :] == jnp.arange(total_rows, dtype=jnp.int32)[:, None]
    slot_of_pos = jnp.sum(jnp.where(picks, slot_ids[None, :], 0), axis=1)

    col_unit = jnp.take(unit, slot_of_pos, axis=0)
    col_rec = jnp.take(all_rec, slot_of_pos, axis=0)
    zero_unit = jnp.zeros((1, EMB), jnp.bfloat16)
    pad_unit = jnp.concatenate([zero_unit, col_unit, zero_unit], axis=0)
    pad_rec = jnp.concatenate([jnp.full((1,), -1, jnp.int32), col_rec, jnp.full((1,), -1, jnp.int32)])
    my_index = lax.axis_index("wide")
    row_unit = lax.dynamic_slice_in_dim(pad_unit, my_index * SEG_DEV, SEG_DEV + 2, 0)
    row_rec = lax.dynamic_slice_in_dim(pad_rec, my_index * SEG_DEV, SEG_DEV + 2, 0)
    scores = AFF_SCALE * jnp.dot(row_unit, col_unit.T, preferred_element_type=jnp.float32)
    affinity = jnp.where(row_rec[:, None] == col_rec[None, :], 0.0, scores)
    return smooth_rows(affinity, smooth_kernel)


def solution(mesh):
    in_specs = (
        P(("parts", "wide"), None),
        P(("parts", "wide")),
        P(("parts", "wide")),
        P(("parts", "wide")),
        P(),
        P(),
        P(),
        P(),
    )
    out_specs = P(("parts", "wide"), None)
    return jax.shard_map(
        per_device, mesh=mesh, in_specs=in_specs, out_specs=out_specs, check_vma=False
    )
```

time: 306 us -> 74.9 us (0.24); the launches traced: 302 us -> 74.5 us
  local copies, waits for them, and re-layouts: 191 us -> 6.89 us
  blocking collectives: 59.8 us -> 26.3 us
  Pallas kernels: 0 us -> 26.4 us
  matrix products: 18.5 us -> 2.87 us
  starting transfers between devices: 13.2 us -> 0 us
  other arithmetic: 17.7 us -> 11.9 us
    gather x192 -> x2, local copies, waits for them, and re-layouts: 179 us -> 4.24 us  [the longest x1 2.29 us: per_device(): col_rec = jnp.take(all_rec, slot_of_pos, axis=0)]
    psum x1 -> x0, blocking collectives: 29.5 us -> none  [per_device(): mean_sum = lax.psum(jnp.sum(seg_rows, axis=0), 'wide')]
    pallas_call x0 -> x1, Pallas kernels: none -> 26.4 us  [pool_slots(): pl.pallas_call(_pool_kernel, out_shape=jax.ShapeDtypeStruct((slots, 2 * C...]
    dot_general x9 -> x2, matrix products: 18.5 us -> 2.87 us  [the longest x1 2.68 us: per_device(): jnp.dot(pooled, proj_weight, precision=PRECISE, preferred_element_type=jn...]
    all_to_all x2 -> x0, starting transfers between devices: 13.2 us -> none  [the longest x1 7.39 us: per_device(): lax.all_to_all(send_rec, 'wide', split_axis=0, concat_axis=0, tiled=True)]
    unnamed x1 -> x0, blocking collectives: 12.4 us -> none
    all_gather x1, blocking collectives: 17.9 us -> 26.3 us  [per_device(): every = lax.all_gather(packed, 'wide', axis=0, tiled=True)]
    squeeze x4 -> x0, local copies, waits for them, and re-layouts: 4.43 us -> none  [pool_segments(): pooled = lax.map(one_block, grouped).reshape(seg_total, 2 * CH)]
  transfers between devices with their start and end apart: 2 -> 0, of which waited for: 0 -> 0; matrix products, arithmetic and copies ran while one was open for 72% -> 0% of each run, Pallas kernels for 0% -> 0%
where the time goes in v1:
time: 74.9 us; the launch traced here: 74.5 us
  Pallas kernels  26.4 us (35%)
  blocking collectives  26.3 us (35%)
  other arithmetic  11.9 us (16%)
  local copies, waits for them, and re-layouts  6.89 us (9%)
  matrix products  2.87 us (4%)
    pallas_call x1, Pallas kernels, pool_slots(): pl.pallas_call(_pool_kernel, out_shape=jax.ShapeDtypeStruct((slots, 2 * C...  26.4 us
    all_gather x1, blocking collectives, per_device(): every = lax.all_gather(packed, 'wide', axis=0, tiled=True)  26.3 us
    add x1, other arithmetic, smooth_rows(): result + smooth_kernel[row_off, col_off] * padded[row_off:row_off + heigh...  6.34 us
    dot_general x1, matrix products, per_device(): jnp.dot(pooled, proj_weight, precision=PRECISE, preferred_element_type=jn...  2.68 us
    gather x1, local copies, waits for them, and re-layouts, per_device(): col_rec = jnp.take(all_rec, slot_of_pos, axis=0)  2.29 us
    concatenate x1, other arithmetic, pool_slots(): jnp.concatenate([jnp.concatenate([zero, frames[:-1]], axis=0), frames, jn...  2.25 us
    gather x1, local copies, waits for them, and re-layouts, per_device(): col_unit = jnp.take(unit, slot_of_pos, axis=0)  1.95 us
    unnamed x11, local copies, waits for them, and re-layouts  1.56 us

profile of v1, /device:TPU:0, one launch (start us, length us, event | category | flops | bytes accessed | tf_op | source)
XLA Modules:
  0.0 74.5 jit_solution(12509579627006208096)
XLA Ops:
  0.0 0.0 copy-start
  0.0 1.5 %copy.19 = f32[2048,80]{1,0:T(8,128)S(1)} copy(f32[2048,80]{0,1:T(8,128)} %param.8) | data formatting | bytes 1310720 | tf_op args[0]
  1.5 0.1 fusion.24
  1.7 0.0 copy-start.2
  1.7 2.2 %select_maximum_fusion.x3_hbm = f32[2048,240]{1,0:T(8,128)} fusion(f32[2047,80]{1,0:T(8,128)S(1)} %get-tuple-element.10, f32[2047,80]{1,0:T(8,128)S(1)} %get-tuple-element.9, f32[2048,80]{1,0:T(8,128)S(1)} %copy.19), kind=kLoop, calls=%fused_computation.5 | loop fusion | flops 2949120 | bytes 3931520 | tf_op jit(solution)/shard_map/concatenate | solution.py:77
  4.0 0.0 copy-done.2
  4.0 0.5 broadcast_clamp_fusion.starts_ref
  4.5 26.4 %shard_map.82 = f32[64,2048]{1,0:T(8,128)} custom-call(s32[64]{0:T(128)} %broadcast_clamp_fusion.starts_ref, f32[2048,240]{1,0:T(8,128)} %select_maximum_fusion.x3_hbm, f32[240,1024]{1,0:T(8,128)} %w_ref.1, f32[1,1024]{1,0:T(1,128)} %bitcast.21), custom_call_target="tpu_custom_call" | custom-call | flops 13589544960 | bytes 5931008 | tf_op jit(solution)/shard_map/pallas_call | solution.py:101
  30.9 0.0 copy-done
  30.9 0.0 copy-start.3
  30.9 0.0 copy-start.4
  31.0 2.7 %fusion.26 = f32[64,192]{1,0:T(8,128)S(1)} fusion(f32[64,2048]{1,0:T(8,128)} %shard_map.82, f32[2048,192]{0,1:T(8,128)S(1)} %copy-done), kind=kOutput, calls=%fused_computation.68 | convolution fusion | flops 301989888 | bytes 2146304 | tf_op jit(solution)/shard_map/dot_general | solution.py:135
  33.6 0.0 copy-done.3
  33.7 0.1 copy.22
  33.7 0.0 copy-done.4
  33.8 0.1 copy.23
  33.9 0.1 pad_maximum_fusion
  33.9 26.3 %all_gather.3 = f32[1024,194]{1,0:T(8,128)S(1)} all-gather(f32[64,194]{1,0:T(8,128)S(1)} %pad_maximum_fusion), channel_id=1, replica_groups=mesh['parts'=2,'wide'=16] {'wide'}, dimensions={0}, use_global_device_ids=true | all-gather | bytes 844288 | tf_op jit(solution)/shard_map/all_gather | solution.py:144
  60.2 0.4 compare_reduce_fusion
  60.6 0.2 select_reduce_fusion.1
  60.8 0.2 multiply_reduce_fusion
  61.0 0.2 divide_convert_fusion
  61.3 0.6 fusion.2
  61.9 0.5 convert_reduce_fusion
  62.4 0.3 select_reduce_fusion
  62.7 0.0 copy-start.1
  62.8 2.0 %gather_fusion.1 = bf16[512,192]{1,0:T(8,128)(2,1)S(1)} fusion(bf16[1024,192]{1,0:T(8,128)(2,1)S(1)} %divide_convert_fusion, s32[1024]{0:T(1024)S(1)} %pad_clamp_fusion), kind=kCustom, calls=%fused_computation.1 | custom fusion | bytes 395264 | tf_op jit(solution)/shard_map/jit(_take)/gather | solution.py:164
  64.7 2.3 %gather_fusion = s32[512]{0:T(512)S(1)} fusion(s32[1024]{0:T(1024)S(1)} %get-tuple-element.5, s32[1024]{0:T(1024)S(1)} %pad_clamp_fusion), kind=kCustom, calls=%fused_computation | custom fusion | bytes 6144 | tf_op jit(solution)/shard_map/jit(_take)/gather | solution.py:165
  67.0 0.1 broadcast_select_fusion
  67.2 0.1 pad_add_fusion
  67.2 0.1 dynamic_slice.6
  67.3 0.2 fusion.1
  67.5 0.0 copy-done.1
  67.5 0.7 fusion.25
  68.2 6.3 %fusion.12 = f32[32,512]{1,0:T(8,128)} fusion(f32[34,512]{1,0:T(8,128)S(1)} %fusion.1, f32[]{:T(128)} %bitcast.13, f32[]{:T(128)} %bitcast.12, f32[]{:T(128)} %bitcast.11, f32[]{:T(128)} %bitcast.10, f32[]{:T(128)} %bitcast.9, f32[]{:T(128)} %bitcast.8, f32[]{:T(128)} %bitcast.7, f32[]{:T(128)} %bitcast.6, f32[]{:T(128)} %bitcast), kind=kLoop, calls=%fused_computation.40 | loop fusion | flops 278528 | bytes 344100 | tf_op jit(solution)/shard_map/add | solution.py:122
  (9 shorter events, 0.1 us)
Async XLA Ops:
  0.0 30.9 %copy-start = (f32[2048,192]{0,1:T(8,128)S(1)}, f32[2048,192]{0,1:T(8,128)}, u32[]{:S(2)}) copy-start(f32[2048,192]{0,1:T(8,128)} %param.14) | copy-start | bytes 4718596
  1.7 2.3 %copy-start.2 = (s32[64]{0:T(128)S(1)}, s32[64]{0:T(128)}, u32[]{:S(2)}) copy-start(s32[64]{0:T(128)} %param.9) | copy-start | bytes 772
  30.9 2.7 %copy-start.3 = (s32[64]{0:T(128)S(1)}, s32[64]{0:T(128)}, u32[]{:S(2)}) copy-start(s32[64]{0:T(128)} %param.10) | copy-start | bytes 772
  30.9 2.8 %copy-start.4 = (s32[64]{0:T(128)S(1)}, s32[64]{0:T(128)}, u32[]{:S(2)}) copy-start(s32[64]{0:T(128)} %param.11) | copy-start | bytes 772
  62.7 4.8 %copy-start.1 = (f32[3,3]{1,0:T(4,128)S(1)}, f32[3,3]{1,0:T(4,128)}, u32[]{:S(2)}) copy-start(f32[3,3]{1,0:T(4,128)} %param.15) | copy-start | bytes 112

commit v2 on v1

--- a/solution.py
+++ b/solution.py
@@ -126,6 +126,24 @@
     return result
 
 
+def gather_wide(x, group_size):
+    my_index = lax.axis_index("wide")
+    if group_size & (group_size - 1):
+        every = lax.all_gather(x, "wide", axis=0, tiled=False)
+        source = jnp.arange(group_size, dtype=jnp.int32)
+        return every, source
+    pattern = [0]
+    buf = x[None]
+    dist = group_size // 2
+    while dist >= 1:
+        perm = [(i, i ^ dist) for i in range(group_size)]
+        buf = jnp.concatenate([buf, lax.ppermute(buf, "wide", perm)], axis=0)
+        pattern = pattern + [p ^ dist for p in pattern]
+        dist //= 2
+    source = jnp.asarray(pattern, dtype=jnp.int32) ^ my_index
+    return buf, source
+
+
 def per_device(
     frames, seg_start, seg_dest, rec_id, conv_weight, conv_bias, proj_weight, smooth_kernel
 ):
@@ -141,7 +159,12 @@
         ],
         axis=1,
     )
-    every = lax.all_gather(packed, "wide", axis=0, tiled=True)
+    blocks, source = gather_wide(packed, group_size)
+    per_block = packed.shape[0]
+    every = blocks.reshape(group_size * per_block, packed.shape[1])
+    slot_ids = (
+        source[:, None] * per_block + jnp.arange(per_block, dtype=jnp.int32)[None, :]
+    ).reshape(-1)
     all_emb = every[:, :EMB]
     all_dest = every[:, EMB].astype(jnp.int32)
     all_rec = every[:, EMB + 1].astype(jnp.int32)
@@ -154,12 +177,12 @@
         jnp.bfloat16
     )
 
-    slot_ids = jnp.arange(slot_total, dtype=jnp.int32)
     earlier = (slot_ids[None, :] < slot_ids[:, None]) & (all_dest[None, :] == all_dest[:, None])
     rank = jnp.sum(earlier.astype(jnp.int32), axis=1)
     position = jnp.where(used, all_dest * SEG_DEV + rank, -1)
     picks = position[None, :] == jnp.arange(total_rows, dtype=jnp.int32)[:, None]
-    slot_of_pos = jnp.sum(jnp.where(picks, slot_ids[None, :], 0), axis=1)
+    row_ids = jnp.arange(slot_total, dtype=jnp.int32)
+    slot_of_pos = jnp.sum(jnp.where(picks, row_ids[None, :], 0), axis=1)
 
     col_unit = jnp.take(unit, slot_of_pos, axis=0)
     col_rec = jnp.take(all_rec, slot_of_pos, axis=0)

time: 74.9 us -> 74.9 us (level)
  blocking collectives: 26.3 us -> 0 us
  waiting for transfers between devices: 0 us -> 14.1 us
  starting transfers between devices: 0 us -> 6.53 us
  other arithmetic: 11.9 us -> 15 us
  local copies, waits for them, and re-layouts: 6.89 us -> 9.37 us
    all_gather x1 -> x0, blocking collectives: 26.3 us -> none  [per_device(): every = lax.all_gather(packed, 'wide', axis=0, tiled=True)]
    ppermute x0 -> x4, waiting for transfers between devices: none -> 14.1 us  [gather_wide(): buf = jnp.concatenate([buf, lax.ppermute(buf, 'wide', perm)], axis=0)]
    ppermute x0 -> x4, starting transfers between devices: none -> 6.53 us  [gather_wide(): buf = jnp.concatenate([buf, lax.ppermute(buf, 'wide', perm)], axis=0)]
    concatenate x1, other arithmetic: 2.25 us -> 3.77 us  [pool_slots(): jnp.concatenate([jnp.concatenate([zero, frames[:-1]], axis=0), frames, jn...]
    slice x1, local copies, waits for them, and re-layouts: 0.15 us -> 1.42 us  [pool_slots(): frames[:-1]]
    concatenate x0 -> x1, local copies, waits for them, and re-layouts: none -> 1.08 us  [gather_wide(): buf = jnp.concatenate([buf, lax.ppermute(buf, 'wide', perm)], axis=0)]
    concatenate x1 -> x3, other arithmetic: 0.08 us -> 0.87 us  [gather_wide(): buf = jnp.concatenate([buf, lax.ppermute(buf, 'wide', perm)], axis=0)]
    unnamed x11 -> x16, local copies, waits for them, and re-layouts: 1.56 us -> 1.61 us
  transfers between devices with their start and end apart: 0 -> 4, of which waited for: 0 -> 4; matrix products, arithmetic and copies ran while one was open for 0% -> 1% of each run, Pallas kernels for 0% -> 0%
where the time goes in v2:
time: 74.9 us; the launch traced here: 74.5 us
  Pallas kernels  26.4 us (35%)
  other arithmetic  15 us (20%)
  waiting for transfers between devices  14.1 us (19%)
  local copies, waits for them, and re-layouts  9.37 us (13%)
  starting transfers between devices  6.53 us (9%)
  matrix products  2.87 us (4%)
    pallas_call x1, Pallas kernels, pool_slots(): pl.pallas_call(_pool_kernel, out_shape=jax.ShapeDtypeStruct((slots, 2 * C...  26.4 us
    ppermute x4, waiting for transfers between devices, gather_wide(): buf = jnp.concatenate([buf, lax.ppermute(buf, 'wide', perm)], axis=0)  14.1 us
    ppermute x4, starting transfers between devices, gather_wide(): buf = jnp.concatenate([buf, lax.ppermute(buf, 'wide', perm)], axis=0)  6.53 us
    add x1, other arithmetic, smooth_rows(): result + smooth_kernel[row_off, col_off] * padded[row_off:row_off + heigh...  6.43 us
    concatenate x1, other arithmetic, pool_slots(): jnp.concatenate([jnp.concatenate([zero, frames[:-1]], axis=0), frames, jn...  3.77 us
    dot_general x1, matrix products, per_device(): jnp.dot(pooled, proj_weight, precision=PRECISE, preferred_element_type=jn...  2.68 us
    gather x1, local copies, waits for them, and re-layouts, per_device(): col_rec = jnp.take(all_rec, slot_of_pos, axis=0)  2.29 us
    gather x1, local copies, waits for them, and re-layouts, per_device(): col_unit = jnp.take(unit, slot_of_pos, axis=0)  1.95 us
  transfers between devices with their start and end apart: 4, of which 4 were waited for; matrix products, arithmetic and copies ran while one was open for 1% of the time, Pallas kernels for 0%

profile of v2, /device:TPU:0, one launch (start us, length us, event | category | flops | bytes accessed | tf_op | source)
XLA Modules:
  0.0 74.5 jit_solution(14841803054313765285)
XLA Ops:
  0.0 0.0 copy-start
  0.0 1.5 %copy.20 = f32[2048,80]{1,0:T(8,128)S(1)} copy(f32[2048,80]{0,1:T(8,128)} %param.9) | data formatting | bytes 1310720 | tf_op args[0]
  1.5 0.0 copy-start.2
  1.6 0.0 copy-start.3
  1.6 0.0 copy-start.4
  1.6 1.4 %fusion.23 = (f32[2047,80]{1,0:T(8,128)}, f32[2047,80]{1,0:T(8,128)}) fusion(f32[2048,80]{1,0:T(8,128)S(1)} %copy.20), kind=kLoop, calls=%fused_computation.74 | loop fusion | bytes 2620160 | tf_op jit(solution)/shard_map/slice | solution.py:79
  3.0 0.0 copy-done.2
  3.0 0.5 broadcast_clamp_fusion.starts_ref
  3.5 0.0 copy-done.3
  3.5 0.1 copy.23
  3.6 0.0 copy-done.4
  3.6 0.1 copy.24
  3.7 3.8 %select_maximum_fusion.x3_hbm = f32[2048,240]{1,0:T(8,128)} fusion(f32[2047,80]{1,0:T(8,128)} %get-tuple-element.12, f32[2047,80]{1,0:T(8,128)} %get-tuple-element.11, f32[2048,80]{1,0:T(8,128)S(1)} %copy.20), kind=kLoop, calls=%fused_computation.3 | loop fusion | flops 2949120 | bytes 3931520 | tf_op jit(solution)/shard_map/concatenate | solution.py:77
  7.5 26.4 %shard_map.91 = f32[64,2048]{1,0:T(8,128)} custom-call(s32[64]{0:T(128)} %broadcast_clamp_fusion.starts_ref, f32[2048,240]{1,0:T(8,128)} %select_maximum_fusion.x3_hbm, f32[240,1024]{1,0:T(8,128)} %w_ref.1, f32[1,1024]{1,0:T(1,128)} %bitcast.30), custom_call_target="tpu_custom_call" | custom-call | flops 13589544960 | bytes 5931008 | tf_op jit(solution)/shard_map/pallas_call | solution.py:101
  33.9 0.0 copy-done
  34.0 0.0 copy-start.5
  34.0 0.0 copy-start.1
  34.0 2.7 %fusion.25 = f32[64,192]{1,0:T(8,128)S(1)} fusion(f32[64,2048]{1,0:T(8,128)} %shard_map.91, f32[2048,192]{0,1:T(8,128)S(1)} %copy-done), kind=kOutput, calls=%fused_computation.76 | convolution fusion | flops 301989888 | bytes 2146304 | tf_op jit(solution)/shard_map/dot_general | solution.py:153
  36.7 0.1 constant_dynamic-update-slice_fusion.4
  36.8 4.1 %collective-permute-start = (f32[1,64,194]{2,1,0:T(8,128)S(1)}, f32[1,64,194]{2,1,0:T(8,128)S(1)}, u32[]{:S(2)}, u32[]{:S(2)}) collective-permute-start(f32[1,64,194]{2,1,0:T(8,128)S(1)} %get-tuple-element.10), channel_id=1, source_target_pairs={{0,8},{1,9},{2,10},{3,11},{4,12},{5,13},{6,14},{7,15},{8,0},{9,1},... | collective-permute-start | bytes 149000 | tf_op jit(solution)/shard_map/ppermute | solution.py:140
  40.9 3.6 %collective-permute-done = f32[1,64,194]{2,1,0:T(8,128)S(1)} collective-permute-done((f32[1,64,194]{2,1,0:T(8,128)S(1)}, f32[1,64,194]{2,1,0:T(8,128)S(1)}, u32[]{:S(2)}, u32[]{:S(2)}) %collective-permute-start) | collective-permute-done | bytes 49696 | tf_op jit(solution)/shard_map/ppermute | solution.py:140
  44.5 0.6 collective-permute-start.1
  45.2 0.0 copy-done.5
  45.2 4.4 %collective-permute-done.1 = f32[2,64,194]{2,1,0:T(8,128)S(1)} collective-permute-done((f32[2,64,194]{2,1,0:T(8,128)S(1)}, f32[2,64,194]{2,1,0:T(8,128)S(1)}, u32[]{:S(2)}, u32[]{:S(2)}) %collective-permute-start.1) | collective-permute-done | bytes 99360 | tf_op jit(solution)/shard_map/ppermute | solution.py:140
  49.6 1.8 %collective-permute-start.2 = (f32[4,64,194]{2,1,0:T(8,128)S(1)}, f32[4,64,194]{2,1,0:T(8,128)S(1)}, u32[]{:S(2)}, u32[]{:S(2)}) collective-permute-start(f32[4,64,194]{2,1,0:T(8,128)S(1)} %pad_maximum_fusion.1), channel_id=1, source_target_pairs={{0,2},{1,3},{2,0},{3,1},{4,6},{5,7},{6,4},{7,5},{8,10},{9,11},{10,... | collective-permute-start | bytes 595976 | tf_op jit(solution)/shard_map/ppermute | solution.py:140
  51.4 0.1 iota_add_fusion
  51.4 4.6 %collective-permute-done.2 = f32[4,64,194]{2,1,0:T(8,128)S(1)} collective-permute-done((f32[4,64,194]{2,1,0:T(8,128)S(1)}, f32[4,64,194]{2,1,0:T(8,128)S(1)}, u32[]{:S(2)}, u32[]{:S(2)}) %collective-permute-start.2) | collective-permute-done | bytes 198688 | tf_op jit(solution)/shard_map/ppermute | solution.py:140
  56.0 0.8 %pad_maximum_fusion = f32[8,64,194]{2,1,0:T(8,128)} fusion(f32[4,64,194]{2,1,0:T(8,128)S(1)} %collective-permute-done.2, f32[2,64,194]{2,1,0:T(8,128)S(1)} %collective-permute-done.1, f32[1,64,194]{2,1,0:T(8,128)S(1)} %collective-permute-done, f32[1,64,194]{2,1,0:T(8,128)S(1)} %get-tuple-element.10), kind=kLoop, calls=%fused_computation.18 | loop fusion | flops 297984 | bytes 794624 | tf_op jit(solution)/shard_map/concatenate | solution.py:140
  56.9 0.0 collective-permute-start.3
  56.9 0.0 copy-done.1
  56.9 0.7 fusion.24
  57.5 0.1 add.108
  57.7 1.5 %collective-permute-done.3 = f32[8,64,194]{2,1,0:T(8,128)} collective-permute-done((f32[8,64,194]{2,1,0:T(8,128)}, f32[8,64,194]{2,1,0:T(8,128)}, u32[]{:S(2)}, u32[]{:S(2)}) %collective-permute-start.3) | collective-permute-done | bytes 397344 | tf_op jit(solution)/shard_map/ppermute | solution.py:140
  59.1 1.1 %constant_dynamic-update-slice_fusion = f32[16,64,194]{2,1,0:T(8,128)S(1)} fusion(f32[16,64,194]{2,1,0:T(8,128)S(1)} %constant_dynamic-update-slice_fusion.1, f32[8,64,194]{2,1,0:T(8,128)} %collective-permute-done.3), kind=kLoop, calls=%fused_computation.54 | loop fusion | bytes 921600 | tf_op jit(solution)/shard_map/concatenate | solution.py:140
  60.2 0.6 fusion.1
  60.8 0.4 compare_reduce_fusion
  61.2 1.0 %convert_reduce_fusion = s32[1024]{0:T(1024)S(1)} fusion(s32[1024]{0:T(1024)S(1)} %get-tuple-element.6, s32[1024]{0:T(1024)S(1)} %add.108), kind=kLoop, calls=%fused_computation.2 | loop fusion | flops 5241856 | bytes 12288 | tf_op jit(solution)/shard_map/reduce_sum | solution.py:181
  62.3 0.3 select_reduce_fusion
  62.6 2.3 %gather_fusion = s32[512]{0:T(512)S(1)} fusion(s32[1024]{0:T(1024)S(1)} %get-tuple-element.5, s32[1024]{0:T(1024)S(1)} %pad_clamp_fusion), kind=kCustom, calls=%fused_computation | custom fusion | bytes 6144 | tf_op jit(solution)/shard_map/jit(_take)/gather | solution.py:188
  64.9 0.2 select_reduce_fusion.1
  65.1 0.2 multiply_reduce_fusion
  65.4 0.2 divide_convert_fusion
  65.6 2.0 %gather_fusion.1 = bf16[512,192]{1,0:T(8,128)(2,1)S(1)} fusion(bf16[1024,192]{1,0:T(8,128)(2,1)S(1)} %divide_convert_fusion, s32[1024]{0:T(1024)S(1)} %pad_clamp_fusion), kind=kCustom, calls=%fused_computation.1 | custom fusion | bytes 395264 | tf_op jit(solution)/shard_map/jit(_take)/gather | solution.py:187
  67.5 0.1 broadcast_select_fusion
  67.7 0.1 pad_add_fusion
  67.8 0.1 dynamic_slice.6
  67.8 0.2 fusion
  68.0 6.4 %fusion.11 = f32[32,512]{1,0:T(8,128)} fusion(f32[34,512]{1,0:T(8,128)S(1)} %fusion, f32[]{:T(128)} %bitcast.15, f32[]{:T(128)} %bitcast.14, f32[]{:T(128)} %bitcast.13, f32[]{:T(128)} %bitcast.12, f32[]{:T(128)} %bitcast.11, f32[]{:T(128)} %bitcast.10, f32[]{:T(128)} %bitcast.9, f32[]{:T(128)} %bitcast.8, f32[]{:T(128)} %bitcast), kind=kLoop, calls=%fused_computation.41 | loop fusion | flops 278528 | bytes 344100 | tf_op jit(solution)/shard_map/add | solution.py:122
  (15 shorter events, 0.1 us)
Async XLA Ops:
  0.0 34.0 %copy-start = (f32[2048,192]{0,1:T(8,128)S(1)}, f32[2048,192]{0,1:T(8,128)}, u32[]{:S(2)}) copy-start(f32[2048,192]{0,1:T(8,128)} %param.15) | copy-start | bytes 4718596
  1.5 1.5 %copy-start.2 = (s32[64]{0:T(128)S(1)}, s32[64]{0:T(128)}, u32[]{:S(2)}) copy-start(s32[64]{0:T(128)} %param.10) | copy-start | bytes 772
  1.6 2.0 %copy-start.3 = (s32[64]{0:T(128)S(1)}, s32[64]{0:T(128)}, u32[]{:S(2)}) copy-start(s32[64]{0:T(128)} %param.11) | copy-start | bytes 772
  1.6 2.1 %copy-start.4 = (s32[64]{0:T(128)S(1)}, s32[64]{0:T(128)}, u32[]{:S(2)}) copy-start(s32[64]{0:T(128)} %param.12) | copy-start | bytes 772
  34.0 11.2 %copy-start.5 = (s32[16]{0:T(128)S(1)}, s32[16]{0:T(128)}, u32[]{:S(2)}) copy-start(s32[16]{0:T(128)} %constant.63.clone) | copy-start | bytes 196
  34.0 22.9 %copy-start.1 = (f32[3,3]{1,0:T(4,128)S(1)}, f32[3,3]{1,0:T(4,128)}, u32[]{:S(2)}) copy-start(f32[3,3]{1,0:T(4,128)} %param.16) | copy-start | bytes 112
  36.8 7.7 %collective-permute-start = (f32[1,64,194]{2,1,0:T(8,128)S(1)}, f32[1,64,194]{2,1,0:T(8,128)S(1)}, u32[]{:S(2)}, u32[]{:S(2)}) collective-permute-start(f32[1,64,194]{2,1,0:T(8,128)S(1)} %get-tuple-element.10), channel_id=1, source_target_pairs={{0,8},{1,9},{2,10},{3,11},{4,12},{5,13},{6,14},{7,15},{8,0},{9,1},... | collective-permute-start | bytes 149000 | tf_op jit(solution)/shard_map/ppermute | solution.py:140
  44.5 5.0 %collective-permute-start.1 = (f32[2,64,194]{2,1,0:T(8,128)S(1)}, f32[2,64,194]{2,1,0:T(8,128)S(1)}, u32[]{:S(2)}, u32[]{:S(2)}) collective-permute-start(f32[2,64,194]{2,1,0:T(8,128)S(1)} %pad_maximum_fusion.2), channel_id=1, source_target_pairs={{0,4},{1,5},{2,6},{3,7},{4,0},{5,1},{6,2},{7,3},{8,12},{9,13},{10,... | collective-permute-start | bytes 297992 | tf_op jit(solution)/shard_map/ppermute | solution.py:140
  49.6 6.4 %collective-permute-start.2 = (f32[4,64,194]{2,1,0:T(8,128)S(1)}, f32[4,64,194]{2,1,0:T(8,128)S(1)}, u32[]{:S(2)}, u32[]{:S(2)}) collective-permute-start(f32[4,64,194]{2,1,0:T(8,128)S(1)} %pad_maximum_fusion.1), channel_id=1, source_target_pairs={{0,2},{1,3},{2,0},{3,1},{4,6},{5,7},{6,4},{7,5},{8,10},{9,11},{10,... | collective-permute-start | bytes 595976 | tf_op jit(solution)/shard_map/ppermute | solution.py:140
  56.9 2.3 %collective-permute-start.3 = (f32[8,64,194]{2,1,0:T(8,128)}, f32[8,64,194]{2,1,0:T(8,128)}, u32[]{:S(2)}, u32[]{:S(2)}) collective-permute-start(f32[8,64,194]{2,1,0:T(8,128)} %pad_maximum_fusion), channel_id=1, source_target_pairs={{0,1},{1,0},{2,3},{3,2},{4,5},{5,4},{6,7},{7,6},{8,9},{9,8},{10,11... | collective-permute-start | bytes 1191944 | tf_op jit(solution)/shard_map/ppermute | solution.py:140

commit v3 on v1

--- a/solution.py
+++ b/solution.py
@@ -126,6 +126,13 @@
     return result
 
 
+def gather_wide(x, group_size):
+    spread = jnp.broadcast_to(x[None], (group_size,) + x.shape)
+    every = lax.all_to_all(spread, "wide", 0, 0, tiled=True)
+    source = jnp.arange(group_size, dtype=jnp.int32)
+    return every, source
+
+
 def per_device(
     frames, seg_start, seg_dest, rec_id, conv_weight, conv_bias, proj_weight, smooth_kernel
 ):
@@ -141,7 +148,12 @@
         ],
         axis=1,
     )
-    every = lax.all_gather(packed, "wide", axis=0, tiled=True)
+    blocks, source = gather_wide(packed, group_size)
+    per_block = packed.shape[0]
+    every = blocks.reshape(group_size * per_block, packed.shape[1])
+    slot_ids = (
+        source[:, None] * per_block + jnp.arange(per_block, dtype=jnp.int32)[None, :]
+    ).reshape(-1)
     all_emb = every[:, :EMB]
     all_dest = every[:, EMB].astype(jnp.int32)
     all_rec = every[:, EMB + 1].astype(jnp.int32)
@@ -154,12 +166,12 @@
         jnp.bfloat16
     )
 
-    slot_ids = jnp.arange(slot_total, dtype=jnp.int32)
     earlier = (slot_ids[None, :] < slot_ids[:, None]) & (all_dest[None, :] == all_dest[:, None])
     rank = jnp.sum(earlier.astype(jnp.int32), axis=1)
     position = jnp.where(used, all_dest * SEG_DEV + rank, -1)
     picks = position[None, :] == jnp.arange(total_rows, dtype=jnp.int32)[:, None]
-    slot_of_pos = jnp.sum(jnp.where(picks, slot_ids[None, :], 0), axis=1)
+    row_ids = jnp.arange(slot_total, dtype=jnp.int32)
+    slot_of_pos = jnp.sum(jnp.where(picks, row_ids[None, :], 0), axis=1)
 
     col_unit = jnp.take(unit, slot_of_pos, axis=0)
     col_rec = jnp.take(all_rec, slot_of_pos, axis=0)

time: 74.9 us -> 84 us (1.12); the launches traced: 74.5 us -> 82.4 us
  blocking collectives: 26.3 us -> 0 us
  waiting for transfers between devices: 0 us -> 22.1 us
  starting transfers between devices: 0 us -> 7.38 us
  local copies, waits for them, and re-layouts: 6.89 us -> 9.34 us
  other arithmetic: 11.9 us -> 14.1 us
    all_gather x1 -> x0, blocking collectives: 26.3 us -> none  [per_device(): every = lax.all_gather(packed, 'wide', axis=0, tiled=True)]
    all_to_all x0 -> x1, waiting for transfers between devices: none -> 22.1 us  [gather_wide(): every = lax.all_to_all(spread, 'wide', 0, 0, tiled=True)]
    all_to_all x0 -> x1, starting transfers between devices: none -> 7.38 us  [gather_wide(): every = lax.all_to_all(spread, 'wide', 0, 0, tiled=True)]
    concatenate x1, other arithmetic: 2.25 us -> 3.77 us  [pool_slots(): jnp.concatenate([jnp.concatenate([zero, frames[:-1]], axis=0), frames, jn...]
    slice x1, local copies, waits for them, and re-layouts: 0.15 us -> 1.42 us  [pool_slots(): frames[:-1]]
    broadcast_in_dim x0 -> x1, local copies, waits for them, and re-layouts: none -> 1.1 us  [gather_wide(): spread = jnp.broadcast_to(x[None], (group_size,) + x.shape)]
  transfers between devices with their start and end apart: 0 -> 1, of which waited for: 0 -> 1; matrix products, arithmetic and copies ran while one was open for 0% -> 1% of each run, Pallas kernels for 0% -> 0%
where the time goes in v3:
time: 84 us; the launch traced here: 82.4 us
  Pallas kernels  26.4 us (31%)
  waiting for transfers between devices  22.1 us (26%)
  other arithmetic  14.1 us (17%)
  local copies, waits for them, and re-layouts  9.34 us (11%)
  starting transfers between devices  7.38 us (9%)
  matrix products  2.86 us (3%)
    pallas_call x1, Pallas kernels, pool_slots(): pl.pallas_call(_pool_kernel, out_shape=jax.ShapeDtypeStruct((slots, 2 * C...  26.4 us
    all_to_all x1, waiting for transfers between devices, gather_wide(): every = lax.all_to_all(spread, 'wide', 0, 0, tiled=True)  22.1 us
    all_to_all x1, starting transfers between devices, gather_wide(): every = lax.all_to_all(spread, 'wide', 0, 0, tiled=True)  7.38 us
    add x1, other arithmetic, smooth_rows(): result + smooth_kernel[row_off, col_off] * padded[row_off:row_off + heigh...  6.43 us
    concatenate x1, other arithmetic, pool_slots(): jnp.concatenate([jnp.concatenate([zero, frames[:-1]], axis=0), frames, jn...  3.77 us
    dot_general x1, matrix products, per_device(): jnp.dot(pooled, proj_weight, precision=PRECISE, preferred_element_type=jn...  2.67 us
    gather x1, local copies, waits for them, and re-layouts, per_device(): col_rec = jnp.take(all_rec, slot_of_pos, axis=0)  2.29 us
    gather x1, local copies, waits for them, and re-layouts, per_device(): col_unit = jnp.take(unit, slot_of_pos, axis=0)  1.95 us
  transfers between devices with their start and end apart: 1, of which 1 were waited for; matrix products, arithmetic and copies ran while one was open for 1% of the time, Pallas kernels for 0%

profile of v3, /device:TPU:0, one launch (start us, length us, event | category | flops | bytes accessed | tf_op | source)
XLA Modules:
  0.0 82.4 jit_solution(18121261524496424626)
XLA Ops:
  0.0 0.0 copy-start
  0.0 1.5 %copy.19 = f32[2048,80]{1,0:T(8,128)S(1)} copy(f32[2048,80]{0,1:T(8,128)} %param.8) | data formatting | bytes 1310720 | tf_op args[0]
  1.5 0.0 copy-start.2
  1.6 0.0 copy-start.3
  1.6 0.0 copy-start.4
  1.6 1.4 %fusion.23 = (f32[2047,80]{1,0:T(8,128)}, f32[2047,80]{1,0:T(8,128)}) fusion(f32[2048,80]{1,0:T(8,128)S(1)} %copy.19), kind=kLoop, calls=%fused_computation.66 | loop fusion | bytes 2620160 | tf_op jit(solution)/shard_map/slice | solution.py:79
  3.0 0.0 copy-done.2
  3.0 0.5 broadcast_clamp_fusion.starts_ref
  3.5 0.0 copy-done.3
  3.5 0.1 copy.22
  3.6 0.0 copy-done.4
  3.6 0.1 copy.23
  3.7 3.8 %select_maximum_fusion.x3_hbm = f32[2048,240]{1,0:T(8,128)} fusion(f32[2047,80]{1,0:T(8,128)} %get-tuple-element.10, f32[2047,80]{1,0:T(8,128)} %get-tuple-element.9, f32[2048,80]{1,0:T(8,128)S(1)} %copy.19), kind=kLoop, calls=%fused_computation.3 | loop fusion | flops 2949120 | bytes 3931520 | tf_op jit(solution)/shard_map/concatenate | solution.py:77
  7.5 26.4 %shard_map.82 = f32[64,2048]{1,0:T(8,128)} custom-call(s32[64]{0:T(128)} %broadcast_clamp_fusion.starts_ref, f32[2048,240]{1,0:T(8,128)} %select_maximum_fusion.x3_hbm, f32[240,1024]{1,0:T(8,128)} %w_ref.1, f32[1,1024]{1,0:T(1,128)} %bitcast.27), custom_call_target="tpu_custom_call" | custom-call | flops 13589544960 | bytes 5931008 | tf_op jit(solution)/shard_map/pallas_call | solution.py:101
  33.9 0.0 copy-done
  34.0 2.7 %fusion.25 = f32[64,192]{1,0:T(8,128)S(1)} fusion(f32[64,2048]{1,0:T(8,128)} %shard_map.82, f32[2048,192]{0,1:T(8,128)S(1)} %copy-done), kind=kOutput, calls=%fused_computation.68 | convolution fusion | flops 301989888 | bytes 2146304 | tf_op jit(solution)/shard_map/dot_general | solution.py:142
  36.6 0.0 copy-start.1
  36.6 0.1 pad_maximum_fusion
  36.7 1.1 %broadcast_in_dim.80 = f32[16,64,194]{2,1,0:T(8,128)} broadcast(f32[64,194]{1,0:T(8,128)S(1)} %pad_maximum_fusion), dimensions={1,2} | broadcast | bytes 844288 | tf_op jit(solution)/shard_map/broadcast_in_dim | solution.py:130
  37.8 7.4 %all-to-all-start = ((f32[16,64,194]{2,1,0:T(8,128)}), f32[16,64,194]{2,1,0:T(8,128)S(1)}, u32[]{:S(2)}, u32[]{:S(2)}) async-start(f32[16,64,194]{2,1,0:T(8,128)} %broadcast_in_dim.80), calls=%async_computation | async-start | bytes 2097152 | tf_op jit(solution)/shard_map/all_to_all | solution.py:131
  45.2 0.1 iota_add_fusion
  45.3 0.1 add.108
  45.4 0.0 copy-done.1
  45.4 0.7 fusion.24
  46.0 22.1 %all-to-all-done = f32[16,64,194]{2,1,0:T(8,128)S(1)} async-done(((f32[16,64,194]{2,1,0:T(8,128)}), f32[16,64,194]{2,1,0:T(8,128)S(1)}, u32[]{:S(2)}, u32[]{:S(2)}) %all-to-all-start) | async-done | bytes 794656 | tf_op jit(solution)/shard_map/all_to_all | solution.py:131
  68.2 0.4 compare_reduce_fusion
  68.5 0.6 fusion.1
  69.2 0.2 select_reduce_fusion.1
  69.4 0.2 multiply_reduce_fusion
  69.6 0.2 divide_convert_fusion
  69.8 1.0 %convert_reduce_fusion = s32[1024]{0:T(1024)S(1)} fusion(s32[1024]{0:T(1024)S(1)} %get-tuple-element.6, s32[1024]{0:T(1024)S(1)} %add.108), kind=kLoop, calls=%fused_computation.2 | loop fusion | flops 5241856 | bytes 12288 | tf_op jit(solution)/shard_map/reduce_sum | solution.py:170
  70.9 0.3 select_reduce_fusion
  71.2 2.0 %gather_fusion.1 = bf16[512,192]{1,0:T(8,128)(2,1)S(1)} fusion(bf16[1024,192]{1,0:T(8,128)(2,1)S(1)} %divide_convert_fusion, s32[1024]{0:T(1024)S(1)} %pad_clamp_fusion), kind=kCustom, calls=%fused_computation.1 | custom fusion | bytes 395264 | tf_op jit(solution)/shard_map/jit(_take)/gather | solution.py:176
  73.2 2.3 %gather_fusion = s32[512]{0:T(512)S(1)} fusion(s32[1024]{0:T(1024)S(1)} %get-tuple-element.5, s32[1024]{0:T(1024)S(1)} %pad_clamp_fusion), kind=kCustom, calls=%fused_computation | custom fusion | bytes 6144 | tf_op jit(solution)/shard_map/jit(_take)/gather | solution.py:177
  75.5 0.1 broadcast_select_fusion
  75.6 0.1 pad_add_fusion
  75.7 0.1 dynamic_slice.6
  75.8 0.2 fusion
  76.0 6.4 %fusion.11 = f32[32,512]{1,0:T(8,128)} fusion(f32[34,512]{1,0:T(8,128)S(1)} %fusion, f32[]{:T(128)} %bitcast.14, f32[]{:T(128)} %bitcast.13, f32[]{:T(128)} %bitcast.12, f32[]{:T(128)} %bitcast.11, f32[]{:T(128)} %bitcast.10, f32[]{:T(128)} %bitcast.9, f32[]{:T(128)} %bitcast.8, f32[]{:T(128)} %bitcast.7, f32[]{:T(128)} %bitcast), kind=kLoop, calls=%fused_computation.38 | loop fusion | flops 278528 | bytes 344100 | tf_op jit(solution)/shard_map/add | solution.py:122
  (10 shorter events, 0.1 us)
Async XLA Ops:
  0.0 34.0 %copy-start = (f32[2048,192]{0,1:T(8,128)S(1)}, f32[2048,192]{0,1:T(8,128)}, u32[]{:S(2)}) copy-start(f32[2048,192]{0,1:T(8,128)} %param.14) | copy-start | bytes 4718596
  1.5 1.5 %copy-start.2 = (s32[64]{0:T(128)S(1)}, s32[64]{0:T(128)}, u32[]{:S(2)}) copy-start(s32[64]{0:T(128)} %param.9) | copy-start | bytes 772
  1.6 2.0 %copy-start.3 = (s32[64]{0:T(128)S(1)}, s32[64]{0:T(128)}, u32[]{:S(2)}) copy-start(s32[64]{0:T(128)} %param.10) | copy-start | bytes 772
  1.6 2.1 %copy-start.4 = (s32[64]{0:T(128)S(1)}, s32[64]{0:T(128)}, u32[]{:S(2)}) copy-start(s32[64]{0:T(128)} %param.11) | copy-start | bytes 772
  36.6 8.7 %copy-start.1 = (f32[3,3]{1,0:T(4,128)S(1)}, f32[3,3]{1,0:T(4,128)}, u32[]{:S(2)}) copy-start(f32[3,3]{1,0:T(4,128)} %param.15) | copy-start | bytes 112
  37.8 30.3 %all-to-all-start = ((f32[16,64,194]{2,1,0:T(8,128)}), f32[16,64,194]{2,1,0:T(8,128)S(1)}, u32[]{:S(2)}, u32[]{:S(2)}) async-start(f32[16,64,194]{2,1,0:T(8,128)} %broadcast_in_dim.80), calls=%async_computation | async-start | bytes 2097152 | tf_op jit(solution)/shard_map/all_to_all | solution.py:131

commit v4 on v3

--- a/solution.py
+++ b/solution.py
@@ -127,10 +127,22 @@
 
 
 def gather_wide(x, group_size):
-    spread = jnp.broadcast_to(x[None], (group_size,) + x.shape)
-    every = lax.all_to_all(spread, "wide", 0, 0, tiled=True)
-    source = jnp.arange(group_size, dtype=jnp.int32)
-    return every, source
+    my_index = lax.axis_index("wide")
+    if group_size % 2 or group_size & (group_size - 1):
+        every = lax.all_gather(x, "wide", axis=0, tiled=False)
+        return every, jnp.arange(group_size, dtype=jnp.int32)
+    pattern = [0]
+    blocks = [x]
+    for flip in range(2, group_size, 2):
+        perm = [(i, i ^ flip) for i in range(group_size)]
+        blocks.append(lax.ppermute(x, "wide", perm))
+        pattern.append(flip)
+    buf = jnp.stack(blocks, axis=0)
+    perm = [(i, i ^ 1) for i in range(group_size)]
+    buf = jnp.concatenate([buf, lax.ppermute(buf, "wide", perm)], axis=0)
+    pattern = pattern + [p ^ 1 for p in pattern]
+    source = jnp.asarray(pattern, dtype=jnp.int32) ^ my_index
+    return buf, source
 
 
 def per_device(

time: 84 us -> 74 us (0.88); the launches traced: 82.4 us -> 73.6 us
  waiting for transfers between devices: 22.1 us -> 8.24 us
  starting transfers between devices: 7.38 us -> 12.7 us
    all_to_all x1 -> x0, waiting for transfers between devices: 22.1 us -> none  [gather_wide(): every = lax.all_to_all(spread, 'wide', 0, 0, tiled=True)]
    ppermute x0 -> x8, starting transfers between devices: none -> 12.7 us  [the longest x7 12.7 us: gather_wide(): blocks.append(lax.ppermute(x, 'wide', perm))]
    ppermute x0 -> x8, waiting for transfers between devices: none -> 8.24 us  [the longest x7 6.94 us: gather_wide(): blocks.append(lax.ppermute(x, 'wide', perm))]
    all_to_all x1 -> x0, starting transfers between devices: 7.38 us -> none  [gather_wide(): every = lax.all_to_all(spread, 'wide', 0, 0, tiled=True)]
    broadcast_in_dim x1 -> x0, local copies, waits for them, and re-layouts: 1.1 us -> none  [gather_wide(): spread = jnp.broadcast_to(x[None], (group_size,) + x.shape)]
    unnamed x11 -> x22, local copies, waits for them, and re-layouts: 1.56 us -> 2.43 us
  transfers between devices with their start and end apart: 1 -> 8, of which waited for: 1 -> 3; matrix products, arithmetic and copies ran while one was open for 1% -> 1% of each run, Pallas kernels for 0% -> 0%
where the time goes in v4:
time: 74 us; the launch traced here: 73.6 us
  Pallas kernels  26.4 us (36%)
  other arithmetic  14 us (19%)
  starting transfers between devices  12.7 us (17%)
  local copies, waits for them, and re-layouts  9.16 us (12%)
  waiting for transfers between devices  8.24 us (11%)
  matrix products  2.87 us (4%)
    pallas_call x1, Pallas kernels, pool_slots(): pl.pallas_call(_pool_kernel, out_shape=jax.ShapeDtypeStruct((slots, 2 * C...  26.4 us
    ppermute x7, starting transfers between devices, gather_wide(): blocks.append(lax.ppermute(x, 'wide', perm))  12.7 us
    ppermute x7, waiting for transfers between devices, gather_wide(): blocks.append(lax.ppermute(x, 'wide', perm))  6.94 us
    add x1, other arithmetic, smooth_rows(): result + smooth_kernel[row_off, col_off] * padded[row_off:row_off + heigh...  6.28 us
    concatenate x1, other arithmetic, pool_slots(): jnp.concatenate([jnp.concatenate([zero, frames[:-1]], axis=0), frames, jn...  3.77 us
    dot_general x1, matrix products, per_device(): jnp.dot(pooled, proj_weight, precision=PRECISE, preferred_element_type=jn...  2.68 us
    unnamed x22, local copies, waits for them, and re-layouts  2.43 us
    gather x1, local copies, waits for them, and re-layouts, per_device(): col_rec = jnp.take(all_rec, slot_of_pos, axis=0)  2.29 us
  transfers between devices with their start and end apart: 8, of which 3 were waited for; matrix products, arithmetic and copies ran while one was open for 1% of the time, Pallas kernels for 0%

profile of v4, /device:TPU:0, one launch (start us, length us, event | category | flops | bytes accessed | tf_op | source)
XLA Modules:
  0.0 73.6 jit_solution(9019544931364807471)
XLA Ops:
  0.0 0.0 copy-start
  0.0 1.5 %copy.20 = f32[2048,80]{1,0:T(8,128)S(1)} copy(f32[2048,80]{0,1:T(8,128)} %param.9) | data formatting | bytes 1310720 | tf_op args[0]
  1.5 0.0 copy-start.3
  1.6 0.0 copy-start.4
  1.6 0.0 copy-start.5
  1.6 1.4 %fusion.23 = (f32[2047,80]{1,0:T(8,128)}, f32[2047,80]{1,0:T(8,128)}) fusion(f32[2048,80]{1,0:T(8,128)S(1)} %copy.20), kind=kLoop, calls=%fused_computation.83 | loop fusion | bytes 2620160 | tf_op jit(solution)/shard_map/slice | solution.py:79
  3.0 0.0 copy-done.3
  3.0 0.5 broadcast_clamp_fusion.starts_ref
  3.5 0.0 copy-done.4
  3.5 0.1 copy.23
  3.6 0.0 copy-done.5
  3.6 0.1 copy.24
  3.7 3.8 %select_maximum_fusion.x3_hbm = f32[2048,240]{1,0:T(8,128)} fusion(f32[2047,80]{1,0:T(8,128)} %get-tuple-element.12, f32[2047,80]{1,0:T(8,128)} %get-tuple-element.11, f32[2048,80]{1,0:T(8,128)S(1)} %copy.20), kind=kLoop, calls=%fused_computation.3 | loop fusion | flops 2949120 | bytes 3931520 | tf_op jit(solution)/shard_map/concatenate | solution.py:77
  7.5 26.4 %shard_map.91 = f32[64,2048]{1,0:T(8,128)} custom-call(s32[64]{0:T(128)} %broadcast_clamp_fusion.starts_ref, f32[2048,240]{1,0:T(8,128)} %select_maximum_fusion.x3_hbm, f32[240,1024]{1,0:T(8,128)} %w_ref.1, f32[1,1024]{1,0:T(1,128)} %bitcast.51), custom_call_target="tpu_custom_call" | custom-call | flops 13589544960 | bytes 5931008 | tf_op jit(solution)/shard_map/pallas_call | solution.py:101
  34.0 0.0 copy-done
  34.0 0.0 copy-start.6
  34.0 0.0 copy-start.1
  34.0 2.7 %fusion.25 = f32[64,192]{1,0:T(8,128)S(1)} fusion(f32[64,2048]{1,0:T(8,128)} %shard_map.91, f32[2048,192]{0,1:T(8,128)S(1)} %copy-done), kind=kOutput, calls=%fused_computation.85 | convolution fusion | flops 301989888 | bytes 2146304 | tf_op jit(solution)/shard_map/dot_general | solution.py:154
  36.7 0.1 bitcast_dynamic-update-slice_fusion.15
  36.8 3.0 %collective-permute-start = (f32[64,194]{1,0:T(8,128)S(1)}, f32[64,194]{1,0:T(8,128)S(1)}, u32[]{:S(2)}, u32[]{:S(2)}) collective-permute-start(f32[64,194]{1,0:T(8,128)S(1)} %get-tuple-element.10), channel_id=1, source_target_pairs={{0,2},{1,3},{2,0},{3,1},{4,6},{5,7},{6,4},{7,5},{8,10},{9,11},{10,... | collective-permute-start | bytes 149000 | tf_op jit(solution)/shard_map/ppermute | solution.py:138
  39.8 1.6 %collective-permute-start.1 = (f32[64,194]{1,0:T(8,128)S(1)}, f32[64,194]{1,0:T(8,128)S(1)}, u32[]{:S(2)}, u32[]{:S(2)}) collective-permute-start(f32[64,194]{1,0:T(8,128)S(1)} %get-tuple-element.10), channel_id=1, source_target_pairs={{0,4},{1,5},{2,6},{3,7},{4,0},{5,1},{6,2},{7,3},{8,12},{9,13},{10,... | collective-permute-start | bytes 149000 | tf_op jit(solution)/shard_map/ppermute | solution.py:138
  41.4 0.0 collective-permute-start.2
  41.4 3.0 %collective-permute-start.3 = (f32[64,194]{1,0:T(8,128)S(1)}, f32[64,194]{1,0:T(8,128)S(1)}, u32[]{:S(2)}, u32[]{:S(2)}) collective-permute-start(f32[64,194]{1,0:T(8,128)S(1)} %get-tuple-element.10), channel_id=1, source_target_pairs={{0,8},{1,9},{2,10},{3,11},{4,12},{5,13},{6,14},{7,15},{8,0},{9,1},... | collective-permute-start | bytes 149000 | tf_op jit(solution)/shard_map/ppermute | solution.py:138
  44.4 1.3 %collective-permute-start.4 = (f32[64,194]{1,0:T(8,128)S(1)}, f32[64,194]{1,0:T(8,128)S(1)}, u32[]{:S(2)}, u32[]{:S(2)}) collective-permute-start(f32[64,194]{1,0:T(8,128)S(1)} %get-tuple-element.10), channel_id=1, source_target_pairs={{0,10},{1,11},{2,8},{3,9},{4,14},{5,15},{6,12},{7,13},{8,2},{9,3},... | collective-permute-start | bytes 149000 | tf_op jit(solution)/shard_map/ppermute | solution.py:138
  45.7 0.0 collective-permute-done
  45.7 3.7 %collective-permute-start.5 = (f32[64,194]{1,0:T(8,128)S(1)}, f32[64,194]{1,0:T(8,128)S(1)}, u32[]{:S(2)}, u32[]{:S(2)}) collective-permute-start(f32[64,194]{1,0:T(8,128)S(1)} %get-tuple-element.10), channel_id=1, source_target_pairs={{0,12},{1,13},{2,14},{3,15},{4,8},{5,9},{6,10},{7,11},{8,4},{9,5},... | collective-permute-start | bytes 149000 | tf_op jit(solution)/shard_map/ppermute | solution.py:138
  49.4 0.0 collective-permute-done.1
  49.4 0.1 collective-permute-start.6
  49.5 0.0 collective-permute-done.2
  49.6 0.0 collective-permute-done.3
  49.6 5.0 %collective-permute-done.4 = f32[64,194]{1,0:T(8,128)S(1)} collective-permute-done((f32[64,194]{1,0:T(8,128)S(1)}, f32[64,194]{1,0:T(8,128)S(1)}, u32[]{:S(2)}, u32[]{:S(2)}) %collective-permute-start.4) | collective-permute-done | bytes 49696 | tf_op jit(solution)/shard_map/ppermute | solution.py:138
  54.6 0.0 collective-permute-done.5
  54.6 1.9 %collective-permute-done.6 = f32[64,194]{1,0:T(8,128)S(1)} collective-permute-done((f32[64,194]{1,0:T(8,128)S(1)}, f32[64,194]{1,0:T(8,128)S(1)}, u32[]{:S(2)}, u32[]{:S(2)}) %collective-permute-start.6) | collective-permute-done | bytes 49696 | tf_op jit(solution)/shard_map/ppermute | solution.py:138
  56.6 0.0 copy-start.2
  56.6 0.8 %copy-done.2 = f32[8,64,194]{2,1,0:T(8,128)} copy-done((f32[8,64,194]{2,1,0:T(8,128)}, f32[8,64,194]{2,1,0:T(8,128)S(1)}, u32[]{:S(2)}) %copy-start.2) | copy-done | bytes 397336
  57.4 0.0 collective-permute-start.7
  57.4 0.0 copy-done.6
  57.4 0.1 iota_add_fusion
  57.4 0.1 add.108
  57.5 0.0 copy-done.1
  57.5 0.7 fusion.24
  58.2 1.3 %collective-permute-done.7 = f32[8,64,194]{2,1,0:T(8,128)S(1)} collective-permute-done((f32[8,64,194]{2,1,0:T(8,128)}, f32[8,64,194]{2,1,0:T(8,128)S(1)}, u32[]{:S(2)}, u32[]{:S(2)}) %collective-permute-start.7) | collective-permute-done | bytes 397344 | tf_op jit(solution)/shard_map/ppermute | solution.py:142
  59.5 0.6 fusion.1
  60.2 0.4 compare_reduce_fusion
  60.5 1.0 %convert_reduce_fusion = s32[1024]{0:T(1024)S(1)} fusion(s32[1024]{0:T(1024)S(1)} %get-tuple-element.6, s32[1024]{0:T(1024)S(1)} %add.108), kind=kLoop, calls=%fused_computation.2 | loop fusion | flops 5241856 | bytes 12288 | tf_op jit(solution)/shard_map/reduce_sum | solution.py:182
  61.6 0.3 select_reduce_fusion
  61.9 2.3 %gather_fusion = s32[512]{0:T(512)S(1)} fusion(s32[1024]{0:T(1024)S(1)} %get-tuple-element.5, s32[1024]{0:T(1024)S(1)} %pad_clamp_fusion), kind=kCustom, calls=%fused_computation | custom fusion | bytes 6144 | tf_op jit(solution)/shard_map/jit(_take)/gather | solution.py:189
  64.2 0.2 select_reduce_fusion.1
  64.5 0.2 multiply_reduce_fusion
  64.7 0.2 divide_convert_fusion
  64.9 2.0 %gather_fusion.1 = bf16[512,192]{1,0:T(8,128)(2,1)S(1)} fusion(bf16[1024,192]{1,0:T(8,128)(2,1)S(1)} %divide_convert_fusion, s32[1024]{0:T(1024)S(1)} %pad_clamp_fusion), kind=kCustom, calls=%fused_computation.1 | custom fusion | bytes 395264 | tf_op jit(solution)/shard_map/jit(_take)/gather | solution.py:188
  66.9 0.1 broadcast_select_fusion
  67.0 0.1 pad_add_fusion
  67.1 0.1 dynamic_slice.6
  67.2 0.2 fusion
  67.4 6.3 %fusion.11 = f32[32,512]{1,0:T(8,128)} fusion(f32[34,512]{1,0:T(8,128)S(1)} %fusion, f32[]{:T(128)} %bitcast.22, f32[]{:T(128)} %bitcast.21, f32[]{:T(128)} %bitcast.20, f32[]{:T(128)} %bitcast.19, f32[]{:T(128)} %bitcast.18, f32[]{:T(128)} %bitcast.17, f32[]{:T(128)} %bitcast.16, f32[]{:T(128)} %bitcast.15, f32[]{:T(128)} %bitcast), kind=kLoop, calls=%fused_computation.38 | loop fusion | flops 278528 | bytes 344100 | tf_op jit(solution)/shard_map/add | solution.py:122
  (19 shorter events, 0.2 us)
Async XLA Ops:
  0.0 34.0 %copy-start = (f32[2048,192]{0,1:T(8,128)S(1)}, f32[2048,192]{0,1:T(8,128)}, u32[]{:S(2)}) copy-start(f32[2048,192]{0,1:T(8,128)} %param.15) | copy-start | bytes 4718596
  1.5 1.5 %copy-start.3 = (s32[64]{0:T(128)S(1)}, s32[64]{0:T(128)}, u32[]{:S(2)}) copy-start(s32[64]{0:T(128)} %param.10) | copy-start | bytes 772
  1.6 2.0 %copy-start.4 = (s32[64]{0:T(128)S(1)}, s32[64]{0:T(128)}, u32[]{:S(2)}) copy-start(s32[64]{0:T(128)} %param.11) | copy-start | bytes 772
  1.6 2.1 %copy-start.5 = (s32[64]{0:T(128)S(1)}, s32[64]{0:T(128)}, u32[]{:S(2)}) copy-start(s32[64]{0:T(128)} %param.12) | copy-start | bytes 772
  34.0 23.4 %copy-start.6 = (s32[16]{0:T(128)S(1)}, s32[16]{0:T(128)}, u32[]{:S(2)}) copy-start(s32[16]{0:T(128)} %constant.63.clone) | copy-start | bytes 196
  34.0 23.5 %copy-start.1 = (f32[3,3]{1,0:T(4,128)S(1)}, f32[3,3]{1,0:T(4,128)}, u32[]{:S(2)}) copy-start(f32[3,3]{1,0:T(4,128)} %param.16) | copy-start | bytes 112
  36.8 8.9 %collective-permute-start = (f32[64,194]{1,0:T(8,128)S(1)}, f32[64,194]{1,0:T(8,128)S(1)}, u32[]{:S(2)}, u32[]{:S(2)}) collective-permute-start(f32[64,194]{1,0:T(8,128)S(1)} %get-tuple-element.10), channel_id=1, source_target_pairs={{0,2},{1,3},{2,0},{3,1},{4,6},{5,7},{6,4},{7,5},{8,10},{9,11},{10,... | collective-permute-start | bytes 149000 | tf_op jit(solution)/shard_map/ppermute | solution.py:138
  39.8 9.6 %collective-permute-start.1 = (f32[64,194]{1,0:T(8,128)S(1)}, f32[64,194]{1,0:T(8,128)S(1)}, u32[]{:S(2)}, u32[]{:S(2)}) collective-permute-start(f32[64,194]{1,0:T(8,128)S(1)} %get-tuple-element.10), channel_id=1, source_target_pairs={{0,4},{1,5},{2,6},{3,7},{4,0},{5,1},{6,2},{7,3},{8,12},{9,13},{10,... | collective-permute-start | bytes 149000 | tf_op jit(solution)/shard_map/ppermute | solution.py:138
  41.4 8.1 %collective-permute-start.2 = (f32[64,194]{1,0:T(8,128)S(1)}, f32[64,194]{1,0:T(8,128)S(1)}, u32[]{:S(2)}, u32[]{:S(2)}) collective-permute-start(f32[64,194]{1,0:T(8,128)S(1)} %get-tuple-element.10), channel_id=1, source_target_pairs={{0,6},{1,7},{2,4},{3,5},{4,2},{5,3},{6,0},{7,1},{8,14},{9,15},{10,... | collective-permute-start | bytes 149000 | tf_op jit(solution)/shard_map/ppermute | solution.py:138
  41.4 8.1 %collective-permute-start.3 = (f32[64,194]{1,0:T(8,128)S(1)}, f32[64,194]{1,0:T(8,128)S(1)}, u32[]{:S(2)}, u32[]{:S(2)}) collective-permute-start(f32[64,194]{1,0:T(8,128)S(1)} %get-tuple-element.10), channel_id=1, source_target_pairs={{0,8},{1,9},{2,10},{3,11},{4,12},{5,13},{6,14},{7,15},{8,0},{9,1},... | collective-permute-start | bytes 149000 | tf_op jit(solution)/shard_map/ppermute | solution.py:138
  44.4 10.2 %collective-permute-start.4 = (f32[64,194]{1,0:T(8,128)S(1)}, f32[64,194]{1,0:T(8,128)S(1)}, u32[]{:S(2)}, u32[]{:S(2)}) collective-permute-start(f32[64,194]{1,0:T(8,128)S(1)} %get-tuple-element.10), channel_id=1, source_target_pairs={{0,10},{1,11},{2,8},{3,9},{4,14},{5,15},{6,12},{7,13},{8,2},{9,3},... | collective-permute-start | bytes 149000 | tf_op jit(solution)/shard_map/ppermute | solution.py:138
  45.7 8.9 %collective-permute-start.5 = (f32[64,194]{1,0:T(8,128)S(1)}, f32[64,194]{1,0:T(8,128)S(1)}, u32[]{:S(2)}, u32[]{:S(2)}) collective-permute-start(f32[64,194]{1,0:T(8,128)S(1)} %get-tuple-element.10), channel_id=1, source_target_pairs={{0,12},{1,13},{2,14},{3,15},{4,8},{5,9},{6,10},{7,11},{8,4},{9,5},... | collective-permute-start | bytes 149000 | tf_op jit(solution)/shard_map/ppermute | solution.py:138
  49.4 7.1 %collective-permute-start.6 = (f32[64,194]{1,0:T(8,128)S(1)}, f32[64,194]{1,0:T(8,128)S(1)}, u32[]{:S(2)}, u32[]{:S(2)}) collective-permute-start(f32[64,194]{1,0:T(8,128)S(1)} %get-tuple-element.10), channel_id=1, source_target_pairs={{0,14},{1,15},{2,12},{3,13},{4,10},{5,11},{6,8},{7,9},{8,6},{9,7},... | collective-permute-start | bytes 149000 | tf_op jit(solution)/shard_map/ppermute | solution.py:138
  56.6 0.8 %copy-start.2 = (f32[8,64,194]{2,1,0:T(8,128)}, f32[8,64,194]{2,1,0:T(8,128)S(1)}, u32[]{:S(2)}) copy-start(f32[8,64,194]{2,1,0:T(8,128)S(1)} %get-tuple-element.13) | copy-start | bytes 1191940
  57.4 2.1 %collective-permute-start.7 = (f32[8,64,194]{2,1,0:T(8,128)}, f32[8,64,194]{2,1,0:T(8,128)S(1)}, u32[]{:S(2)}, u32[]{:S(2)}) collective-permute-start(f32[8,64,194]{2,1,0:T(8,128)} %copy-done.2), channel_id=1, source_target_pairs={{0,1},{1,0},{2,3},{3,2},{4,5},{5,4},{6,7},{7,6},{8,9},{9,8},{10,11... | collective-permute-start | bytes 1191944 | tf_op jit(solution)/shard_map/ppermute | solution.py:142

commit v5 on v4

--- a/solution.py
+++ b/solution.py
@@ -18,97 +18,80 @@
 AFF_SCALE = 8.0
 SEG_BLOCK = 8
 WIN = SEGLEN + 8
+CONV_ROWS = 256
 
 
-def _pool_kernel(starts_ref, x3_hbm, w_ref, b_ref, out_ref, buf, sem):
-    step = pl.program_id(0)
-    steps = pl.num_programs(0)
-    block = buf.shape[1]
-    rows = x3_hbm.shape[0]
+def _pool_kernel(starts_ref, frames_ref, w_ref, b_ref, out_ref, x3_ref, act_ref):
+    rows = frames_ref.shape[0]
+    slots = out_ref.shape[0]
+    frames = frames_ref[...]
+    x3_ref[...] = jnp.concatenate(
+        [pltpu.roll(frames, 1, 0), frames, pltpu.roll(frames, rows - 1, 0)], axis=1
+    )
+    chunk = CONV_ROWS if rows % CONV_ROWS == 0 else rows
 
-    def aligned_start(blk, j):
-        start = starts_ref[blk * block + j]
-        return jnp.minimum((start // 8) * 8, rows - WIN)
+    def conv_chunk(c, carry):
+        base = pl.multiple_of(c * chunk, chunk)
+        preact = jnp.dot(
+            x3_ref[pl.ds(base, chunk), :],
+            w_ref[...],
+            precision=PRECISE,
+            preferred_element_type=jnp.float32,
+        )
+        act_ref[pl.ds(base, chunk), :] = jnp.maximum(preact + b_ref[...], 0.0)
+        return carry
 
-    def window_copy(blk, slot, j):
-        base = pl.multiple_of(aligned_start(blk, j), 8)
-        return pltpu.make_async_copy(
-            x3_hbm.at[pl.ds(base, WIN)], buf.at[slot, j], sem.at[slot, j]
-        )
+    lax.fori_loop(0, rows // chunk, conv_chunk, 0)
+    frame_idx = lax.broadcasted_iota(jnp.int32, (WIN, CH), 0)
 
-    @pl.when(step == 0)
-    def _():
-        for j in range(block):
-            window_copy(0, 0, j).start()
+    def stats_block(blk, carry):
+        means = []
+        stds = []
+        for j in range(SEG_BLOCK):
+            start = starts_ref[blk * SEG_BLOCK + j]
+            base = jnp.minimum((start // 8) * 8, rows - WIN)
+            shift = start - base
+            inside = (frame_idx >= shift) & (frame_idx < shift + SEGLEN)
+            seg_act = act_ref[pl.ds(pl.multiple_of(base, 8), WIN), :]
+            frame_mean = jnp.sum(jnp.where(inside, seg_act, 0.0), axis=0, keepdims=True) / SEGLEN
+            deviation = jnp.where(inside, seg_act - frame_mean, 0.0)
+            frame_var = jnp.sum(deviation * deviation, axis=0, keepdims=True) / SEGLEN
+            means.append(frame_mean)
+            stds.append(jnp.sqrt(frame_var + 1e-05))
+        row0 = pl.multiple_of(blk * SEG_BLOCK, SEG_BLOCK)
+        out_ref[pl.ds(row0, SEG_BLOCK), :CH] = jnp.concatenate(means, axis=0)
+        out_ref[pl.ds(row0, SEG_BLOCK), CH:] = jnp.concatenate(stds, axis=0)
+        return carry
 
-    slot = step % 2
-
-    @pl.when(step + 1 < steps)
-    def _():
-        for j in range(block):
-            window_copy(step + 1, 1 - slot, j).start()
-
-    for j in range(block):
-        window_copy(step, slot, j).wait()
-
-    stacked = buf[slot].reshape(block * WIN, 3 * FEAT)
-    preact = jnp.dot(stacked, w_ref[...], precision=PRECISE, preferred_element_type=jnp.float32)
-    activated = jnp.maximum(preact + b_ref[...], 0.0)
-    frame_idx = lax.broadcasted_iota(jnp.int32, (WIN, CH), 0)
-    means = []
-    stds = []
-    for j in range(block):
-        shift = starts_ref[step * block + j] - aligned_start(step, j)
-        inside = (frame_idx >= shift) & (frame_idx < shift + SEGLEN)
-        seg_act = activated[j * WIN : (j + 1) * WIN]
-        frame_mean = jnp.sum(jnp.where(inside, seg_act, 0.0), axis=0, keepdims=True) / SEGLEN
-        deviation = jnp.where(inside, seg_act - frame_mean, 0.0)
-        frame_var = jnp.sum(deviation * deviation, axis=0, keepdims=True) / SEGLEN
-        means.append(frame_mean)
-        stds.append(jnp.sqrt(frame_var + 1e-05))
-    out_ref[:, :CH] = jnp.concatenate(means, axis=0)
-    out_ref[:, CH:] = jnp.concatenate(stds, axis=0)
+    lax.fori_loop(0, slots // SEG_BLOCK, stats_block, 0)
 
 
 def pool_slots(frames, seg_start, conv_weight, conv_bias):
     rows = frames.shape[0]
     slots = seg_start.shape[0]
-    zero = jnp.zeros((1, FEAT), frames.dtype)
-    x3 = jnp.concatenate(
-        [
-            jnp.concatenate([zero, frames[:-1]], axis=0),
-            frames,
-            jnp.concatenate([frames[1:], zero], axis=0),
-        ],
-        axis=1,
-    )
     starts = jnp.clip(seg_start, 0, rows - SEGLEN).astype(jnp.int32)
-    block = SEG_BLOCK if slots % SEG_BLOCK == 0 else 1
-    grid_spec = pltpu.PrefetchScalarGridSpec(
-        num_scalar_prefetch=1,
-        grid=(slots // block,),
-        in_specs=[
-            pl.BlockSpec(memory_space=pl.ANY),
-            pl.BlockSpec((3 * FEAT, CH), lambda i, s: (0, 0)),
-            pl.BlockSpec((1, CH), lambda i, s: (0, 0)),
-        ],
-        out_specs=pl.BlockSpec((block, 2 * CH), lambda i, s: (i, 0)),
-        scratch_shapes=[
-            pltpu.VMEM((2, block, WIN, 3 * FEAT), jnp.float32),
-            pltpu.SemaphoreType.DMA((2, block)),
-        ],
-    )
+    vmem = pltpu.MemorySpace.VMEM
     return pl.pallas_call(
         _pool_kernel,
         out_shape=jax.ShapeDtypeStruct((slots, 2 * CH), jnp.float32),
-        grid_spec=grid_spec,
-        compiler_params=pltpu.CompilerParams(dimension_semantics=("arbitrary",)),
+        in_specs=[
+            pl.BlockSpec(memory_space=pltpu.MemorySpace.SMEM),
+            pl.BlockSpec(memory_space=vmem),
+            pl.BlockSpec(memory_space=vmem),
+            pl.BlockSpec(memory_space=vmem),
+        ],
+        out_specs=pl.BlockSpec(memory_space=vmem),
+        scratch_shapes=[
+            pltpu.VMEM((rows, 3 * FEAT), jnp.float32),
+            pltpu.VMEM((rows, CH), jnp.float32),
+        ],
+        compiler_params=pltpu.CompilerParams(vmem_limit_bytes=48 * 1024 * 1024),
         cost_estimate=pl.CostEstimate(
-            flops=2 * slots * WIN * 3 * FEAT * CH * 6,
+            flops=2 * rows * 3 * FEAT * CH * 6 + 8 * slots * WIN * CH,
             transcendentals=slots * CH,
-            bytes_accessed=slots * WIN * 3 * FEAT * 4 + 3 * FEAT * CH * 4 + slots * 2 * CH * 4,
+            bytes_accessed=rows * FEAT * 4 + 3 * FEAT * CH * 4 + slots * 2 * CH * 4,
         ),
-    )(starts, x3, conv_weight, conv_bias.reshape(1, CH))
+    )(starts, frames, conv_weight, conv_bias.reshape(1, CH))
 
 
 def smooth_rows(padded_rows, smooth_kernel):

time: 74 us -> 58.8 us (0.79)
  Pallas kernels: 26.4 us -> 16.9 us
  other arithmetic: 14 us -> 9.75 us
  matrix products: 2.87 us -> 1.82 us
    pallas_call x1, Pallas kernels: 26.4 us -> 16.9 us  [pool_slots(): pl.pallas_call(_pool_kernel, out_shape=jax.ShapeDtypeStruct((slots, 2 * C...]
    concatenate x1 -> x0, other arithmetic: 3.77 us -> none  [pool_slots(): jnp.concatenate([jnp.concatenate([zero, frames[:-1]], axis=0), frames, jn...]
    slice x1 -> x0, local copies, waits for them, and re-layouts: 1.43 us -> none  [pool_slots(): frames[:-1]]
    unnamed x22 -> x26, local copies, waits for them, and re-layouts: 2.43 us -> 3.61 us
    dot_general x1, matrix products: 2.68 us -> 1.63 us  [per_device(): jnp.dot(pooled, proj_weight, precision=PRECISE, preferred_element_type=jn...]
  transfers between devices with their start and end apart: 8 -> 8, of which waited for: 3 -> 3; matrix products, arithmetic and copies ran while one was open for 1% -> 2% of each run, Pallas kernels for 0% -> 0%
where the time goes in v5:
time: 58.8 us; the launch traced here: 58.5 us
  Pallas kernels  16.9 us (29%)
  starting transfers between devices  12.6 us (21%)
  other arithmetic  9.75 us (17%)
  local copies, waits for them, and re-layouts  8.93 us (15%)
  waiting for transfers between devices  8.23 us (14%)
  matrix products  1.82 us (3%)
    pallas_call x1, Pallas kernels, pool_slots(): pl.pallas_call(_pool_kernel, out_shape=jax.ShapeDtypeStruct((slots, 2 * C...  16.9 us
    ppermute x7, starting transfers between devices, gather_wide(): blocks.append(lax.ppermute(x, 'wide', perm))  12.6 us
    ppermute x7, waiting for transfers between devices, gather_wide(): blocks.append(lax.ppermute(x, 'wide', perm))  6.94 us
    add x1, other arithmetic, smooth_rows(): result + smooth_kernel[row_off, col_off] * padded[row_off:row_off + heigh...  6.34 us
    unnamed x26, local copies, waits for them, and re-layouts  3.61 us
    gather x1, local copies, waits for them, and re-layouts, per_device(): col_rec = jnp.take(all_rec, slot_of_pos, axis=0)  2.29 us
    gather x1, local copies, waits for them, and re-layouts, per_device(): col_unit = jnp.take(unit, slot_of_pos, axis=0)  1.95 us
    dot_general x1, matrix products, per_device(): jnp.dot(pooled, proj_weight, precision=PRECISE, preferred_element_type=jn...  1.63 us
  transfers between devices with their start and end apart: 8, of which 3 were waited for; matrix products, arithmetic and copies ran while one was open for 2% of the time, Pallas kernels for 0%

profile of v5, /device:TPU:0, one launch (start us, length us, event | category | flops | bytes accessed | tf_op | source)
XLA Modules:
  0.0 58.5 jit_solution(814226708988533808)
XLA Ops:
  0.0 0.0 copy-start
  0.0 0.0 copy-start.5
  0.0 0.0 copy-start.6
  0.0 0.0 copy-start.7
  0.0 0.0 copy-start.2
  0.0 1.5 %copy.16.frames_ref = f32[2048,80]{1,0:T(8,128)S(1)} copy(f32[2048,80]{0,1:T(8,128)} %param.9) | data formatting | bytes 1310720 | tf_op args[0]
  1.6 0.0 copy-done.5
  1.6 0.0 copy-done.6
  1.6 0.1 copy.17
  1.7 0.0 copy-done.7
  1.7 0.1 copy.18
  1.8 0.0 copy-done.2
  1.8 0.0 copy-start.1
  1.8 1.2 %copy-done.1 = f32[240,1024]{1,0:T(8,128)S(1)} copy-done((f32[240,1024]{1,0:T(8,128)S(1)}, f32[240,1024]{1,0:T(8,128)}, u32[]{:S(2)}) %copy-start.1) | copy-done | bytes 983064
  3.0 16.9 %shard_map.91 = f32[64,2048]{1,0:T(8,128)S(1)} custom-call(s32[64]{0:T(128)S(1)} %broadcast_clamp_fusion.starts_ref, f32[2048,80]{1,0:T(8,128)S(1)} %copy.16.frames_ref, f32[240,1024]{1,0:T(8,128)S(1)} %copy-done.1, f32[1,1024]{1,0:T(1,128)S(1)} %bitcast.44), custom_call_target="tpu_custom_call" | custom-call | flops 6077546496 | bytes 2162688 | tf_op jit(solution)/shard_map/pallas_call | solution.py:74
  19.9 0.0 copy-done
  19.9 0.0 copy-start.8
  19.9 0.0 copy-start.3
  19.9 1.6 %fusion.24 = f32[64,192]{1,0:T(8,128)S(1)} fusion(f32[64,2048]{1,0:T(8,128)S(1)} %shard_map.91, f32[2048,192]{0,1:T(8,128)S(1)} %copy-done), kind=kOutput, calls=%fused_computation.80 | convolution fusion | flops 301989888 | bytes 2146304 | tf_op jit(solution)/shard_map/dot_general | solution.py:137
  21.5 0.1 bitcast_dynamic-update-slice_fusion.15
  21.6 3.0 %collective-permute-start = (f32[64,194]{1,0:T(8,128)S(1)}, f32[64,194]{1,0:T(8,128)S(1)}, u32[]{:S(2)}, u32[]{:S(2)}) collective-permute-start(f32[64,194]{1,0:T(8,128)S(1)} %get-tuple-element.10), channel_id=1, source_target_pairs={{0,2},{1,3},{2,0},{3,1},{4,6},{5,7},{6,4},{7,5},{8,10},{9,11},{10,... | collective-permute-start | bytes 149000 | tf_op jit(solution)/shard_map/ppermute | solution.py:121
  24.7 1.6 %collective-permute-start.1 = (f32[64,194]{1,0:T(8,128)S(1)}, f32[64,194]{1,0:T(8,128)S(1)}, u32[]{:S(2)}, u32[]{:S(2)}) collective-permute-start(f32[64,194]{1,0:T(8,128)S(1)} %get-tuple-element.10), channel_id=1, source_target_pairs={{0,4},{1,5},{2,6},{3,7},{4,0},{5,1},{6,2},{7,3},{8,12},{9,13},{10,... | collective-permute-start | bytes 149000 | tf_op jit(solution)/shard_map/ppermute | solution.py:121
  26.3 0.0 collective-permute-start.2
  26.3 3.0 %collective-permute-start.3 = (f32[64,194]{1,0:T(8,128)S(1)}, f32[64,194]{1,0:T(8,128)S(1)}, u32[]{:S(2)}, u32[]{:S(2)}) collective-permute-start(f32[64,194]{1,0:T(8,128)S(1)} %get-tuple-element.10), channel_id=1, source_target_pairs={{0,8},{1,9},{2,10},{3,11},{4,12},{5,13},{6,14},{7,15},{8,0},{9,1},... | collective-permute-start | bytes 149000 | tf_op jit(solution)/shard_map/ppermute | solution.py:121
  29.2 1.3 %collective-permute-start.4 = (f32[64,194]{1,0:T(8,128)S(1)}, f32[64,194]{1,0:T(8,128)S(1)}, u32[]{:S(2)}, u32[]{:S(2)}) collective-permute-start(f32[64,194]{1,0:T(8,128)S(1)} %get-tuple-element.10), channel_id=1, source_target_pairs={{0,10},{1,11},{2,8},{3,9},{4,14},{5,15},{6,12},{7,13},{8,2},{9,3},... | collective-permute-start | bytes 149000 | tf_op jit(solution)/shard_map/ppermute | solution.py:121
  30.5 0.0 collective-permute-done
  30.5 3.7 %collective-permute-start.5 = (f32[64,194]{1,0:T(8,128)S(1)}, f32[64,194]{1,0:T(8,128)S(1)}, u32[]{:S(2)}, u32[]{:S(2)}) collective-permute-start(f32[64,194]{1,0:T(8,128)S(1)} %get-tuple-element.10), channel_id=1, source_target_pairs={{0,12},{1,13},{2,14},{3,15},{4,8},{5,9},{6,10},{7,11},{8,4},{9,5},... | collective-permute-start | bytes 149000 | tf_op jit(solution)/shard_map/ppermute | solution.py:121
  34.2 0.0 collective-permute-done.1
  34.2 0.1 collective-permute-start.6
  34.3 0.0 collective-permute-done.2
  34.4 0.0 collective-permute-done.3
  34.4 5.1 %collective-permute-done.4 = f32[64,194]{1,0:T(8,128)S(1)} collective-permute-done((f32[64,194]{1,0:T(8,128)S(1)}, f32[64,194]{1,0:T(8,128)S(1)}, u32[]{:S(2)}, u32[]{:S(2)}) %collective-permute-start.4) | collective-permute-done | bytes 49696 | tf_op jit(solution)/shard_map/ppermute | solution.py:121
  39.5 0.0 collective-permute-done.5
  39.5 1.9 %collective-permute-done.6 = f32[64,194]{1,0:T(8,128)S(1)} collective-permute-done((f32[64,194]{1,0:T(8,128)S(1)}, f32[64,194]{1,0:T(8,128)S(1)}, u32[]{:S(2)}, u32[]{:S(2)}) %collective-permute-start.6) | collective-permute-done | bytes 49696 | tf_op jit(solution)/shard_map/ppermute | solution.py:121
  41.4 0.0 copy-start.4
  41.4 0.8 %copy-done.4 = f32[8,64,194]{2,1,0:T(8,128)} copy-done((f32[8,64,194]{2,1,0:T(8,128)}, f32[8,64,194]{2,1,0:T(8,128)S(1)}, u32[]{:S(2)}) %copy-start.4) | copy-done | bytes 397336
  42.2 0.0 collective-permute-start.7
  42.2 0.0 copy-done.8
  42.2 0.1 iota_add_fusion
  42.3 0.1 add.104
  42.3 0.0 copy-done.3
  42.3 0.7 %fusion.23 = (f32[1,1]{1,0:T(1,128)}, f32[1,1]{1,0:T(1,128)}, f32[1,1]{1,0:T(1,128)}, f32[1,1]{1,0:T(1,128)}, f32[1,1]{1,0:T(1,128)}, /*index=5*/f32[1,1]{1,0:T(...) fusion(f32[3,3]{1,0:T(4,128)S(1)} %copy-done.3), kind=kLoop, calls=%fused_computation.79 | loop fusion | bytes 72 | tf_op jit(solution)/shard_map/slice | solution.py:106
  43.0 1.3 %collective-permute-done.7 = f32[8,64,194]{2,1,0:T(8,128)S(1)} collective-permute-done((f32[8,64,194]{2,1,0:T(8,128)}, f32[8,64,194]{2,1,0:T(8,128)S(1)}, u32[]{:S(2)}, u32[]{:S(2)}) %collective-permute-start.7) | collective-permute-done | bytes 397344 | tf_op jit(solution)/shard_map/ppermute | solution.py:125
  44.3 0.6 %fusion.1 = (s32[1024]{0:T(1024)S(1)}, s32[1024]{0:T(1024)S(1)}) fusion(f32[1024,194]{1,0:T(8,128)S(1)} %bitcast.45), kind=kLoop, calls=%fused_computation.12 | loop fusion | flops 2048 | bytes 16384 | tf_op jit(solution)/shard_map/convert_element_type | solution.py:154
  45.0 0.4 compare_reduce_fusion
  45.4 1.0 %convert_reduce_fusion = s32[1024]{0:T(1024)S(1)} fusion(s32[1024]{0:T(1024)S(1)} %get-tuple-element.6, s32[1024]{0:T(1024)S(1)} %add.104), kind=kLoop, calls=%fused_computation.2 | loop fusion | flops 5241856 | bytes 12288 | tf_op jit(solution)/shard_map/reduce_sum | solution.py:165
  46.4 0.3 select_reduce_fusion
  46.7 2.3 %gather_fusion = s32[512]{0:T(512)S(1)} fusion(s32[1024]{0:T(1024)S(1)} %get-tuple-element.5, s32[1024]{0:T(1024)S(1)} %pad_clamp_fusion), kind=kCustom, calls=%fused_computation | custom fusion | bytes 6144 | tf_op jit(solution)/shard_map/jit(_take)/gather | solution.py:172
  49.0 0.2 select_reduce_fusion.1
  49.3 0.2 multiply_reduce_fusion
  49.5 0.2 divide_convert_fusion
  49.7 2.0 %gather_fusion.1 = bf16[512,192]{1,0:T(8,128)(2,1)S(1)} fusion(bf16[1024,192]{1,0:T(8,128)(2,1)S(1)} %divide_convert_fusion, s32[1024]{0:T(1024)S(1)} %pad_clamp_fusion), kind=kCustom, calls=%fused_computation.1 | custom fusion | bytes 395264 | tf_op jit(solution)/shard_map/jit(_take)/gather | solution.py:171
  51.7 0.1 broadcast_select_fusion
  51.8 0.1 pad_add_fusion
  51.9 0.1 dynamic_slice.6
  52.0 0.2 fusion
  52.2 6.3 %fusion.11 = f32[32,512]{1,0:T(8,128)} fusion(f32[34,512]{1,0:T(8,128)S(1)} %fusion, f32[]{:T(128)} %bitcast.22, f32[]{:T(128)} %bitcast.21, f32[]{:T(128)} %bitcast.20, f32[]{:T(128)} %bitcast.19, f32[]{:T(128)} %bitcast.18, f32[]{:T(128)} %bitcast.17, f32[]{:T(128)} %bitcast.16, f32[]{:T(128)} %bitcast.15, f32[]{:T(128)} %bitcast), kind=kLoop, calls=%fused_computation.34 | loop fusion | flops 278528 | bytes 344100 | tf_op jit(solution)/shard_map/add | solution.py:105
  (20 shorter events, 0.2 us)
Async XLA Ops:
  0.0 19.9 %copy-start = (f32[2048,192]{0,1:T(8,128)S(1)}, f32[2048,192]{0,1:T(8,128)}, u32[]{:S(2)}) copy-start(f32[2048,192]{0,1:T(8,128)} %param.15) | copy-start | bytes 4718596
  0.0 1.6 %copy-start.5 = (s32[64]{0:T(128)S(1)}, s32[64]{0:T(128)}, u32[]{:S(2)}) copy-start(s32[64]{0:T(128)} %param.10) | copy-start | bytes 772
  0.0 1.6 %copy-start.6 = (s32[64]{0:T(128)S(1)}, s32[64]{0:T(128)}, u32[]{:S(2)}) copy-start(s32[64]{0:T(128)} %param.11) | copy-start | bytes 772
  0.0 1.7 %copy-start.7 = (s32[64]{0:T(128)S(1)}, s32[64]{0:T(128)}, u32[]{:S(2)}) copy-start(s32[64]{0:T(128)} %param.12) | copy-start | bytes 772
  0.0 1.8 %copy-start.2 = (f32[1024]{0:T(1024)S(1)}, f32[1024]{0:T(1024)}, u32[]{:S(2)}) copy-start(f32[1024]{0:T(1024)} %param.14) | copy-start | bytes 12292
  1.8 1.2 %copy-start.1 = (f32[240,1024]{1,0:T(8,128)S(1)}, f32[240,1024]{1,0:T(8,128)}, u32[]{:S(2)}) copy-start(f32[240,1024]{1,0:T(8,128)} %w_ref.1) | copy-start | bytes 2949124
  19.9 22.3 %copy-start.8 = (s32[16]{0:T(128)S(1)}, s32[16]{0:T(128)}, u32[]{:S(2)}) copy-start(s32[16]{0:T(128)} %constant.62.clone) | copy-start | bytes 196
  19.9 22.4 %copy-start.3 = (f32[3,3]{1,0:T(4,128)S(1)}, f32[3,3]{1,0:T(4,128)}, u32[]{:S(2)}) copy-start(f32[3,3]{1,0:T(4,128)} %param.16) | copy-start | bytes 112
  21.6 8.9 %collective-permute-start = (f32[64,194]{1,0:T(8,128)S(1)}, f32[64,194]{1,0:T(8,128)S(1)}, u32[]{:S(2)}, u32[]{:S(2)}) collective-permute-start(f32[64,194]{1,0:T(8,128)S(1)} %get-tuple-element.10), channel_id=1, source_target_pairs={{0,2},{1,3},{2,0},{3,1},{4,6},{5,7},{6,4},{7,5},{8,10},{9,11},{10,... | collective-permute-start | bytes 149000 | tf_op jit(solution)/shard_map/ppermute | solution.py:121
  24.7 9.5 %collective-permute-start.1 = (f32[64,194]{1,0:T(8,128)S(1)}, f32[64,194]{1,0:T(8,128)S(1)}, u32[]{:S(2)}, u32[]{:S(2)}) collective-permute-start(f32[64,194]{1,0:T(8,128)S(1)} %get-tuple-element.10), channel_id=1, source_target_pairs={{0,4},{1,5},{2,6},{3,7},{4,0},{5,1},{6,2},{7,3},{8,12},{9,13},{10,... | collective-permute-start | bytes 149000 | tf_op jit(solution)/shard_map/ppermute | solution.py:121
  26.3 8.1 %collective-permute-start.2 = (f32[64,194]{1,0:T(8,128)S(1)}, f32[64,194]{1,0:T(8,128)S(1)}, u32[]{:S(2)}, u32[]{:S(2)}) collective-permute-start(f32[64,194]{1,0:T(8,128)S(1)} %get-tuple-element.10), channel_id=1, source_target_pairs={{0,6},{1,7},{2,4},{3,5},{4,2},{5,3},{6,0},{7,1},{8,14},{9,15},{10,... | collective-permute-start | bytes 149000 | tf_op jit(solution)/shard_map/ppermute | solution.py:121
  26.3 8.1 %collective-permute-start.3 = (f32[64,194]{1,0:T(8,128)S(1)}, f32[64,194]{1,0:T(8,128)S(1)}, u32[]{:S(2)}, u32[]{:S(2)}) collective-permute-start(f32[64,194]{1,0:T(8,128)S(1)} %get-tuple-element.10), channel_id=1, source_target_pairs={{0,8},{1,9},{2,10},{3,11},{4,12},{5,13},{6,14},{7,15},{8,0},{9,1},... | collective-permute-start | bytes 149000 | tf_op jit(solution)/shard_map/ppermute | solution.py:121
  29.2 10.2 %collective-permute-start.4 = (f32[64,194]{1,0:T(8,128)S(1)}, f32[64,194]{1,0:T(8,128)S(1)}, u32[]{:S(2)}, u32[]{:S(2)}) collective-permute-start(f32[64,194]{1,0:T(8,128)S(1)} %get-tuple-element.10), channel_id=1, source_target_pairs={{0,10},{1,11},{2,8},{3,9},{4,14},{5,15},{6,12},{7,13},{8,2},{9,3},... | collective-permute-start | bytes 149000 | tf_op jit(solution)/shard_map/ppermute | solution.py:121
  30.5 8.9 %collective-permute-start.5 = (f32[64,194]{1,0:T(8,128)S(1)}, f32[64,194]{1,0:T(8,128)S(1)}, u32[]{:S(2)}, u32[]{:S(2)}) collective-permute-start(f32[64,194]{1,0:T(8,128)S(1)} %get-tuple-element.10), channel_id=1, source_target_pairs={{0,12},{1,13},{2,14},{3,15},{4,8},{5,9},{6,10},{7,11},{8,4},{9,5},... | collective-permute-start | bytes 149000 | tf_op jit(solution)/shard_map/ppermute | solution.py:121
  34.2 7.1 %collective-permute-start.6 = (f32[64,194]{1,0:T(8,128)S(1)}, f32[64,194]{1,0:T(8,128)S(1)}, u32[]{:S(2)}, u32[]{:S(2)}) collective-permute-start(f32[64,194]{1,0:T(8,128)S(1)} %get-tuple-element.10), channel_id=1, source_target_pairs={{0,14},{1,15},{2,12},{3,13},{4,10},{5,11},{6,8},{7,9},{8,6},{9,7},... | collective-permute-start | bytes 149000 | tf_op jit(solution)/shard_map/ppermute | solution.py:121
  41.4 0.8 %copy-start.4 = (f32[8,64,194]{2,1,0:T(8,128)}, f32[8,64,194]{2,1,0:T(8,128)S(1)}, u32[]{:S(2)}) copy-start(f32[8,64,194]{2,1,0:T(8,128)S(1)} %get-tuple-element.11) | copy-start | bytes 1191940
  42.2 2.1 %collective-permute-start.7 = (f32[8,64,194]{2,1,0:T(8,128)}, f32[8,64,194]{2,1,0:T(8,128)S(1)}, u32[]{:S(2)}, u32[]{:S(2)}) collective-permute-start(f32[8,64,194]{2,1,0:T(8,128)} %copy-done.4), channel_id=1, source_target_pairs={{0,1},{1,0},{2,3},{3,2},{4,5},{5,4},{6,7},{7,6},{8,9},{9,8},{10,11... | collective-permute-start | bytes 1191944 | tf_op jit(solution)/shard_map/ppermute | solution.py:125

commit v6 on v5

--- a/solution.py
+++ b/solution.py
@@ -19,6 +19,7 @@
 SEG_BLOCK = 8
 WIN = SEGLEN + 8
 CONV_ROWS = 256
+ONE_HOT_LIMIT = 1 << 20
 
 
 def _pool_kernel(starts_ref, frames_ref, w_ref, b_ref, out_ref, x3_ref, act_ref):
@@ -94,19 +95,46 @@
     )(starts, frames, conv_weight, conv_bias.reshape(1, CH))
 
 
-def smooth_rows(padded_rows, smooth_kernel):
-    padded = jnp.pad(padded_rows, ((0, 0), (1, 1)))
-    height = padded.shape[0] - 2
-    col_count = padded.shape[1] - 2
-    result = jnp.zeros((height, col_count), padded.dtype)
+def _affinity_kernel(k_ref, row_unit_ref, col_unit_ref, row_rec_ref, col_rec_ref, out_ref, pad_ref):
+    height, width = out_ref.shape
+    scores = lax.dot_general(
+        row_unit_ref[...],
+        col_unit_ref[...],
+        (((1,), (1,)), ((), ())),
+        preferred_element_type=jnp.float32,
+    )
+    affinity = jnp.where(row_rec_ref[...] == col_rec_ref[...], 0.0, AFF_SCALE * scores)
+    pad_ref[...] = jnp.zeros(pad_ref.shape, jnp.float32)
+    pad_ref[0 : height + 2, 1 : width + 1] = affinity
+    result = jnp.zeros((height, width), jnp.float32)
     for row_off in range(3):
         for col_off in range(3):
-            result = (
-                result
-                + smooth_kernel[row_off, col_off]
-                * padded[row_off : row_off + height, col_off : col_off + col_count]
-            )
-    return result
+            result = result + k_ref[row_off, col_off] * pad_ref[
+                row_off : row_off + height, col_off : col_off + width
+            ]
+    out_ref[...] = result
+
+
+def smooth_affinity(row_unit, col_unit, row_rec, col_rec, smooth_kernel):
+    height = row_unit.shape[0] - 2
+    width = col_unit.shape[0]
+    vmem = pltpu.MemorySpace.VMEM
+    return pl.pallas_call(
+        _affinity_kernel,
+        out_shape=jax.ShapeDtypeStruct((height, width), jnp.float32),
+        in_specs=[pl.BlockSpec(memory_space=pltpu.MemorySpace.SMEM)]
+        + [pl.BlockSpec(memory_space=vmem)] * 4,
+        out_specs=pl.BlockSpec(memory_space=vmem),
+        scratch_shapes=[
+            pltpu.VMEM((-(-(height + 2) // 8) * 8, -(-(width + 2) // 128) * 128), jnp.float32)
+        ],
+        compiler_params=pltpu.CompilerParams(vmem_limit_bytes=48 * 1024 * 1024),
+        cost_estimate=pl.CostEstimate(
+            flops=2 * (height + 2) * width * EMB + 20 * height * width,
+            transcendentals=0,
+            bytes_accessed=(width + height + 2) * EMB * 2 + height * width * 4,
+        ),
+    )(smooth_kernel, row_unit, col_unit, row_rec.reshape(-1, 1), col_rec.reshape(1, -1))
 
 
 def gather_wide(x, group_size):
@@ -168,17 +196,24 @@
     row_ids = jnp.arange(slot_total, dtype=jnp.int32)
     slot_of_pos = jnp.sum(jnp.where(picks, row_ids[None, :], 0), axis=1)
 
-    col_unit = jnp.take(unit, slot_of_pos, axis=0)
-    col_rec = jnp.take(all_rec, slot_of_pos, axis=0)
+    if total_rows * slot_total <= ONE_HOT_LIMIT:
+        rec_hi = (all_rec // 16).astype(jnp.bfloat16)[:, None]
+        rec_lo = (all_rec % 16).astype(jnp.bfloat16)[:, None]
+        unit_ext = jnp.concatenate([unit, rec_hi, rec_lo], axis=1)
+        selector = picks.astype(jnp.bfloat16)
+        col_ext = jnp.dot(selector, unit_ext, preferred_element_type=jnp.float32)
+        col_unit = col_ext[:, :EMB].astype(jnp.bfloat16)
+        col_rec = (col_ext[:, EMB] * 16 + col_ext[:, EMB + 1]).astype(jnp.int32)
+    else:
+        col_unit = jnp.take(unit, slot_of_pos, axis=0)
+        col_rec = jnp.take(all_rec, slot_of_pos, axis=0)
     zero_unit = jnp.zeros((1, EMB), jnp.bfloat16)
     pad_unit = jnp.concatenate([zero_unit, col_unit, zero_unit], axis=0)
     pad_rec = jnp.concatenate([jnp.full((1,), -1, jnp.int32), col_rec, jnp.full((1,), -1, jnp.int32)])
     my_index = lax.axis_index("wide")
     row_unit = lax.dynamic_slice_in_dim(pad_unit, my_index * SEG_DEV, SEG_DEV + 2, 0)
     row_rec = lax.dynamic_slice_in_dim(pad_rec, my_index * SEG_DEV, SEG_DEV + 2, 0)
-    scores = AFF_SCALE * jnp.dot(row_unit, col_unit.T, preferred_element_type=jnp.float32)
-    affinity = jnp.where(row_rec[:, None] == col_rec[None, :], 0.0, scores)
-    return smooth_rows(affinity, smooth_kernel)
+    return smooth_affinity(row_unit, col_unit, row_rec, col_rec, smooth_kernel)
 
 
 def solution(mesh):

time: 58.8 us -> 55.2 us (0.939)
  other arithmetic: 9.75 us -> 3.53 us
  waiting for transfers between devices: 8.23 us -> 5.85 us
  local copies, waits for them, and re-layouts: 8.93 us -> 10.8 us
  matrix products: 1.82 us -> 3.54 us
  Pallas kernels: 16.9 us -> 18.6 us
    add x1 -> x0, other arithmetic: 6.34 us -> none  [smooth_rows(): result + smooth_kernel[row_off, col_off] * padded[row_off:row_off + heigh...]
    unnamed x26 -> x27, local copies, waits for them, and re-layouts: 3.61 us -> 8.12 us
    gather x2 -> x0, local copies, waits for them, and re-layouts: 4.24 us -> none  [the longest x1 2.29 us: per_device(): col_rec = jnp.take(all_rec, slot_of_pos, axis=0)]
    ppermute x7, waiting for transfers between devices: 6.94 us -> 3.88 us  [gather_wide(): blocks.append(lax.ppermute(x, 'wide', perm))]
    dot_general x1, matrix products: 0.19 us -> 1.9 us  [per_device(): col_ext = jnp.dot(selector, unit_ext, preferred_element_type=jnp.float32)]
    pallas_call x0 -> x1, Pallas kernels: none -> 1.65 us  [smooth_affinity(): pl.pallas_call(_affinity_kernel, out_shape=jax.ShapeDtypeStruct((height,...]
    convert_element_type x1, other arithmetic: 0.22 us -> 1.01 us  [per_device(): (centred / jnp.sqrt(jnp.sum(centred * centred, axis=1, keepdims=True) + 1...]
    ppermute x1, waiting for transfers between devices: 1.29 us -> 1.96 us  [gather_wide(): buf = jnp.concatenate([buf, lax.ppermute(buf, 'wide', perm)], axis=0)]
  transfers between devices with their start and end apart: 8 -> 8, of which waited for: 3 -> 3; matrix products, arithmetic and copies ran while one was open for 2% -> 7% of each run, Pallas kernels for 0% -> 0%
where the time goes in v6:
time: 55.2 us; the launch traced here: 55 us
  Pallas kernels  18.6 us (34%)
  starting transfers between devices  12.5 us (23%)
  local copies, waits for them, and re-layouts  10.8 us (20%)
  waiting for transfers between devices  5.85 us (11%)
  matrix products  3.54 us (6%)
  other arithmetic  3.53 us (6%)
    pallas_call x1, Pallas kernels, pool_slots(): pl.pallas_call(_pool_kernel, out_shape=jax.ShapeDtypeStruct((slots, 2 * C...  16.9 us
    ppermute x7, starting transfers between devices, gather_wide(): blocks.append(lax.ppermute(x, 'wide', perm))  12.5 us
    unnamed x27, local copies, waits for them, and re-layouts  8.12 us
    ppermute x7, waiting for transfers between devices, gather_wide(): blocks.append(lax.ppermute(x, 'wide', perm))  3.88 us
    ppermute x1, waiting for transfers between devices, gather_wide(): buf = jnp.concatenate([buf, lax.ppermute(buf, 'wide', perm)], axis=0)  1.96 us
    dot_general x1, matrix products, per_device(): col_ext = jnp.dot(selector, unit_ext, preferred_element_type=jnp.float32)  1.9 us
    pallas_call x1, Pallas kernels, smooth_affinity(): pl.pallas_call(_affinity_kernel, out_shape=jax.ShapeDtypeStruct((height,...  1.65 us
    dot_general x1, matrix products, per_device(): jnp.dot(pooled, proj_weight, precision=PRECISE, preferred_element_type=jn...  1.64 us
  transfers between devices with their start and end apart: 8, of which 3 were waited for; matrix products, arithmetic and copies ran while one was open for 7% of the time, Pallas kernels for 0%

profile of v6, /device:TPU:0, one launch (start us, length us, event | category | flops | bytes accessed | tf_op | source)
XLA Modules:
  0.0 55.0 jit_solution(9718590526283056228)
XLA Ops:
  0.0 0.0 copy-start
  0.0 0.0 copy-start.4
  0.0 0.0 copy-start.5
  0.0 0.0 copy-start.6
  0.0 0.0 copy-start.3
  0.0 1.5 %copy.33.frames_ref = f32[2048,80]{1,0:T(8,128)S(1)} copy(f32[2048,80]{0,1:T(8,128)} %param.9) | data formatting | bytes 1310720 | tf_op args[0]
  1.6 0.0 copy-done.4
  1.6 0.0 copy-done.5
  1.6 0.1 copy.34
  1.7 0.0 copy-done.6
  1.7 0.1 copy.35
  1.8 0.0 copy-done.3
  1.8 0.0 copy-start.2
  1.8 1.2 %copy-done.2 = f32[240,1024]{1,0:T(8,128)S(1)} copy-done((f32[240,1024]{1,0:T(8,128)S(1)}, f32[240,1024]{1,0:T(8,128)}, u32[]{:S(2)}) %copy-start.2) | copy-done | bytes 983064
  3.0 16.9 %shard_map.91 = f32[64,2048]{1,0:T(8,128)S(1)} custom-call(s32[64]{0:T(128)S(1)} %broadcast_clamp_fusion.starts_ref, f32[2048,80]{1,0:T(8,128)S(1)} %copy.33.frames_ref, f32[240,1024]{1,0:T(8,128)S(1)} %copy-done.2, f32[1,1024]{1,0:T(1,128)S(1)} %bitcast.38), custom_call_target="tpu_custom_call" | custom-call | flops 6077546496 | bytes 2162688 | tf_op jit(solution)/shard_map/pallas_call | solution.py:75
  19.9 0.0 copy-done
  19.9 0.0 copy-start.7
  20.0 1.6 %fusion.14 = f32[64,192]{1,0:T(8,128)S(1)} fusion(f32[64,2048]{1,0:T(8,128)S(1)} %shard_map.91, f32[2048,192]{0,1:T(8,128)S(1)} %copy-done), kind=kOutput, calls=%fused_computation.60 | convolution fusion | flops 301989888 | bytes 2146304 | tf_op jit(solution)/shard_map/dot_general | solution.py:165
  21.6 0.7 %bitcast_dynamic-update-slice_fusion.15 = (f32[8,64,194]{2,1,0:T(8,128)}, f32[64,194]{1,0:T(8,128)S(1)}) fusion(f32[64,1]{1,0:T(8,128)S(1)} %copy.35, f32[64,1]{1,0:T(8,128)S(1)} %copy.34, f32[64,192]{1,0:T(8,128)S(1)} %fusion.14), kind=kLoop, calls=%fused_computation.33 | loop fusion | flops 24831 | bytes 164864
  22.3 3.0 %collective-permute-start = (f32[64,194]{1,0:T(8,128)S(1)}, f32[64,194]{1,0:T(8,128)S(1)}, u32[]{:S(2)}, u32[]{:S(2)}) collective-permute-start(f32[64,194]{1,0:T(8,128)S(1)} %get-tuple-element.8), channel_id=1, source_target_pairs={{0,2},{1,3},{2,0},{3,1},{4,6},{5,7},{6,4},{7,5},{8,10},{9,11},{10,... | collective-permute-start | bytes 149000 | tf_op jit(solution)/shard_map/ppermute | solution.py:149
  25.3 1.6 %collective-permute-start.1 = (f32[64,194]{1,0:T(8,128)S(1)}, f32[64,194]{1,0:T(8,128)S(1)}, u32[]{:S(2)}, u32[]{:S(2)}) collective-permute-start(f32[64,194]{1,0:T(8,128)S(1)} %get-tuple-element.8), channel_id=1, source_target_pairs={{0,4},{1,5},{2,6},{3,7},{4,0},{5,1},{6,2},{7,3},{8,12},{9,13},{10,... | collective-permute-start | bytes 149000 | tf_op jit(solution)/shard_map/ppermute | solution.py:149
  26.9 0.0 collective-permute-start.2
  26.9 3.0 %collective-permute-start.3 = (f32[64,194]{1,0:T(8,128)S(1)}, f32[64,194]{1,0:T(8,128)S(1)}, u32[]{:S(2)}, u32[]{:S(2)}) collective-permute-start(f32[64,194]{1,0:T(8,128)S(1)} %get-tuple-element.8), channel_id=1, source_target_pairs={{0,8},{1,9},{2,10},{3,11},{4,12},{5,13},{6,14},{7,15},{8,0},{9,1},... | collective-permute-start | bytes 149000 | tf_op jit(solution)/shard_map/ppermute | solution.py:149
  29.8 1.3 %collective-permute-start.4 = (f32[64,194]{1,0:T(8,128)S(1)}, f32[64,194]{1,0:T(8,128)S(1)}, u32[]{:S(2)}, u32[]{:S(2)}) collective-permute-start(f32[64,194]{1,0:T(8,128)S(1)} %get-tuple-element.8), channel_id=1, source_target_pairs={{0,10},{1,11},{2,8},{3,9},{4,14},{5,15},{6,12},{7,13},{8,2},{9,3},... | collective-permute-start | bytes 149000 | tf_op jit(solution)/shard_map/ppermute | solution.py:149
  31.1 0.0 collective-permute-done
  31.1 3.7 %collective-permute-start.5 = (f32[64,194]{1,0:T(8,128)S(1)}, f32[64,194]{1,0:T(8,128)S(1)}, u32[]{:S(2)}, u32[]{:S(2)}) collective-permute-start(f32[64,194]{1,0:T(8,128)S(1)} %get-tuple-element.8), channel_id=1, source_target_pairs={{0,12},{1,13},{2,14},{3,15},{4,8},{5,9},{6,10},{7,11},{8,4},{9,5},... | collective-permute-start | bytes 149000 | tf_op jit(solution)/shard_map/ppermute | solution.py:149
  34.8 0.6 %bitcast_dynamic-update-slice_fusion.13 = (f32[8,64,194]{2,1,0:T(8,128)}, f32[16,64,194]{2,1,0:T(8,128)S(1)}) fusion(f32[8,64,194]{2,1,0:T(8,128)} %get-tuple-element.7, f32[64,194]{1,0:T(8,128)S(1)} %collective-permute-done, f32[16,64,194]{2,1,0:T(8,128)S(1)} %bitcast_dynamic-update-slice_fusion.14), kind=kLoop, calls=%fused_computation.31 | loop fusion | bytes 196608
  35.5 0.0 collective-permute-done.1
  35.5 0.0 collective-permute-start.6
  35.5 0.6 %bitcast_dynamic-update-slice_fusion.11 = (f32[8,64,194]{2,1,0:T(8,128)}, f32[16,64,194]{2,1,0:T(8,128)S(1)}) fusion(f32[8,64,194]{2,1,0:T(8,128)} %get-tuple-element.23, f32[64,194]{1,0:T(8,128)S(1)} %collective-permute-done.1, f32[16,64,194]{2,1,0:T(8,128)S(1)} %get-tuple-element.24), kind=kLoop, calls=%fused_computation.29 | loop fusion | bytes 196608
  36.1 0.0 collective-permute-done.2
  36.1 0.6 %bitcast_dynamic-update-slice_fusion.9 = (f32[8,64,194]{2,1,0:T(8,128)}, f32[16,64,194]{2,1,0:T(8,128)S(1)}) fusion(f32[8,64,194]{2,1,0:T(8,128)} %get-tuple-element.21, f32[64,194]{1,0:T(8,128)S(1)} %collective-permute-done.2, f32[16,64,194]{2,1,0:T(8,128)S(1)} %get-tuple-element.22), kind=kLoop, calls=%fused_computation.27 | loop fusion | bytes 196608
  36.7 0.0 collective-permute-done.3
  36.7 0.6 %bitcast_dynamic-update-slice_fusion.7 = (f32[8,64,194]{2,1,0:T(8,128)}, f32[16,64,194]{2,1,0:T(8,128)S(1)}) fusion(f32[8,64,194]{2,1,0:T(8,128)} %get-tuple-element.19, f32[64,194]{1,0:T(8,128)S(1)} %collective-permute-done.3, f32[16,64,194]{2,1,0:T(8,128)S(1)} %get-tuple-element.20), kind=kLoop, calls=%fused_computation.25 | loop fusion | bytes 196608
  37.4 2.7 %collective-permute-done.4 = f32[64,194]{1,0:T(8,128)S(1)} collective-permute-done((f32[64,194]{1,0:T(8,128)S(1)}, f32[64,194]{1,0:T(8,128)S(1)}, u32[]{:S(2)}, u32[]{:S(2)}) %collective-permute-start.4) | collective-permute-done | bytes 49696 | tf_op jit(solution)/shard_map/ppermute | solution.py:149
  40.0 0.6 %bitcast_dynamic-update-slice_fusion.5 = (f32[8,64,194]{2,1,0:T(8,128)}, f32[16,64,194]{2,1,0:T(8,128)S(1)}) fusion(f32[8,64,194]{2,1,0:T(8,128)} %get-tuple-element.17, f32[64,194]{1,0:T(8,128)S(1)} %collective-permute-done.4, f32[16,64,194]{2,1,0:T(8,128)S(1)} %get-tuple-element.18), kind=kLoop, calls=%fused_computation.23 | loop fusion | bytes 196608
  40.7 0.0 collective-permute-done.5
  40.7 0.6 %bitcast_dynamic-update-slice_fusion.3 = (f32[8,64,194]{2,1,0:T(8,128)}, f32[16,64,194]{2,1,0:T(8,128)S(1)}) fusion(f32[8,64,194]{2,1,0:T(8,128)} %get-tuple-element.15, f32[64,194]{1,0:T(8,128)S(1)} %collective-permute-done.5, f32[16,64,194]{2,1,0:T(8,128)S(1)} %get-tuple-element.16), kind=kLoop, calls=%fused_computation.21 | loop fusion | bytes 196608
  41.3 1.2 %collective-permute-done.6 = f32[64,194]{1,0:T(8,128)S(1)} collective-permute-done((f32[64,194]{1,0:T(8,128)S(1)}, f32[64,194]{1,0:T(8,128)S(1)}, u32[]{:S(2)}, u32[]{:S(2)}) %collective-permute-start.6) | collective-permute-done | bytes 49696 | tf_op jit(solution)/shard_map/ppermute | solution.py:149
  42.5 0.6 %bitcast_dynamic-update-slice_fusion.1 = (f32[8,64,194]{2,1,0:T(8,128)}, f32[16,64,194]{2,1,0:T(8,128)S(1)}) fusion(f32[8,64,194]{2,1,0:T(8,128)} %get-tuple-element.13, f32[64,194]{1,0:T(8,128)S(1)} %collective-permute-done.6, f32[16,64,194]{2,1,0:T(8,128)S(1)} %get-tuple-element.14), kind=kLoop, calls=%fused_computation.19 | loop fusion | bytes 196608 | tf_op jit(solution)/shard_map/stack | solution.py:151
  43.2 0.0 collective-permute-start.7
  43.2 0.0 copy-done.7
  43.2 0.1 iota_add_fusion
  43.2 0.1 add.70
  43.3 2.0 %collective-permute-done.7 = f32[8,64,194]{2,1,0:T(8,128)S(1)} collective-permute-done((f32[8,64,194]{2,1,0:T(8,128)}, f32[8,64,194]{2,1,0:T(8,128)S(1)}, u32[]{:S(2)}, u32[]{:S(2)}) %collective-permute-start.7) | collective-permute-done | bytes 397344 | tf_op jit(solution)/shard_map/ppermute | solution.py:153
  45.3 1.1 %fusion.13 = (f32[1024,1]{1,0:T(8,128)S(1)}, f32[1024,1]{1,0:T(8,128)}) fusion(f32[1024,194]{1,0:T(8,128)S(1)} %bitcast.39), kind=kLoop, calls=%fused_computation.59 | loop fusion | bytes 16384 | tf_op jit(solution)/shard_map/slice | solution.py:182
  46.4 1.2 %copy.42 = f32[1024,1]{0,1:T(1,128)S(1)} copy(f32[1024,1]{1,0:T(8,128)} %get-tuple-element.10) | data formatting | bytes 8192
  47.7 0.2 select_reduce_fusion
  47.9 0.2 multiply_reduce_fusion
  48.2 1.0 %divide_convert_fusion = bf16[1024,192]{1,0:T(8,128)(2,1)} fusion(f32[1024,194]{1,0:T(8,128)S(1)} %bitcast.42, f32[1024]{0:T(1024)S(1)} %add_sqrt_fusion, f32[192]{0:T(256)S(1)} %broadcast_multiply_fusion), kind=kLoop, calls=%fused_computation.3 | loop fusion | flops 589824 | bytes 1184512 | tf_op jit(solution)/shard_map/convert_element_type | solution.py:188
  49.2 0.2 copy.43
  49.4 0.2 copy.39
  49.6 0.2 copy.38
  49.8 1.0 %convert_reduce_fusion = s32[1024]{0:T(1024)S(1)} fusion(s32[1024]{0:T(1024)S(1)} %bitcast.43, s32[1024]{0:T(1024)S(1)} %add.70), kind=kLoop, calls=%fused_computation | loop fusion | flops 5241856 | bytes 12288 | tf_op jit(solution)/shard_map/reduce_sum | solution.py:193
  50.9 0.0 copy-start.1
  50.9 1.9 %fusion = f32[512,194]{0,1:T(8,128)S(1)} fusion(s32[1024]{0:T(1024)S(1)} %add_select_fusion, bf16[1024,1]{1,0:T(8,128)(2,1)S(1)} %copy.39, bf16[1024,1]{1,0:T(8,128)(2,1)S(1)} %copy.38, bf16[1024,192]{1,0:T(8,128)(2,1)} %divide_convert_fusion), kind=kOutput, calls=%fused_computation.2 | convolution fusion | flops 205139968 | bytes 798720 | tf_op jit(solution)/shard_map/dot_general | solution.py:204
  52.9 0.1 copy.44.col_unit_ref
  53.0 0.1 pad_add_fusion
  53.1 0.1 dynamic-slice_bitcast_fusion
  53.2 0.1 copy.41.row_rec_ref
  53.3 0.0 copy-done.1
  53.3 1.6 %shard_map.92 = f32[32,512]{1,0:T(8,128)} custom-call(f32[3,3]{1,0:T(4,128)S(1)} %copy-done.1, bf16[34,192]{1,0:T(8,128)(2,1)S(1)} %fusion.8.row_unit_ref, bf16[512,192]{1,0:T(8,128)(2,1)S(1)} %copy.44.col_unit_ref, s32[34,1]{1,0:T(8,128)S(1)} %copy.41.row_rec_ref, s32[1,512]{1,0:T(1,128)S(1)} %fusion.17.col_rec_ref), custom_call_target="tpu_custom_call" | custom-call | flops 7012352 | bytes 275200 | tf_op jit(solution)/shard_map/pallas_call | solution.py:122
  (18 shorter events, 0.3 us)
Async XLA Ops:
  0.0 19.9 %copy-start = (f32[2048,192]{0,1:T(8,128)S(1)}, f32[2048,192]{0,1:T(8,128)}, u32[]{:S(2)}) copy-start(f32[2048,192]{0,1:T(8,128)} %param.15) | copy-start | bytes 4718596
  0.0 1.6 %copy-start.4 = (s32[64]{0:T(128)S(1)}, s32[64]{0:T(128)}, u32[]{:S(2)}) copy-start(s32[64]{0:T(128)} %param.10) | copy-start | bytes 772
  0.0 1.6 %copy-start.5 = (s32[64]{0:T(128)S(1)}, s32[64]{0:T(128)}, u32[]{:S(2)}) copy-start(s32[64]{0:T(128)} %param.11) | copy-start | bytes 772
  0.0 1.7 %copy-start.6 = (s32[64]{0:T(128)S(1)}, s32[64]{0:T(128)}, u32[]{:S(2)}) copy-start(s32[64]{0:T(128)} %param.12) | copy-start | bytes 772
  0.0 1.8 %copy-start.3 = (f32[1024]{0:T(1024)S(1)}, f32[1024]{0:T(1024)}, u32[]{:S(2)}) copy-start(f32[1024]{0:T(1024)} %param.14) | copy-start | bytes 12292
  1.8 1.2 %copy-start.2 = (f32[240,1024]{1,0:T(8,128)S(1)}, f32[240,1024]{1,0:T(8,128)}, u32[]{:S(2)}) copy-start(f32[240,1024]{1,0:T(8,128)} %w_ref.1) | copy-start | bytes 2949124
  19.9 23.2 %copy-start.7 = (s32[16]{0:T(128)S(1)}, s32[16]{0:T(128)}, u32[]{:S(2)}) copy-start(s32[16]{0:T(128)} %constant.59.clone) | copy-start | bytes 196
  22.3 8.8 %collective-permute-start = (f32[64,194]{1,0:T(8,128)S(1)}, f32[64,194]{1,0:T(8,128)S(1)}, u32[]{:S(2)}, u32[]{:S(2)}) collective-permute-start(f32[64,194]{1,0:T(8,128)S(1)} %get-tuple-element.8), channel_id=1, source_target_pairs={{0,2},{1,3},{2,0},{3,1},{4,6},{5,7},{6,4},{7,5},{8,10},{9,11},{10,... | collective-permute-start | bytes 149000 | tf_op jit(solution)/shard_map/ppermute | solution.py:149
  25.3 10.2 %collective-permute-start.1 = (f32[64,194]{1,0:T(8,128)S(1)}, f32[64,194]{1,0:T(8,128)S(1)}, u32[]{:S(2)}, u32[]{:S(2)}) collective-permute-start(f32[64,194]{1,0:T(8,128)S(1)} %get-tuple-element.8), channel_id=1, source_target_pairs={{0,4},{1,5},{2,6},{3,7},{4,0},{5,1},{6,2},{7,3},{8,12},{9,13},{10,... | collective-permute-start | bytes 149000 | tf_op jit(solution)/shard_map/ppermute | solution.py:149
  26.9 9.2 %collective-permute-start.2 = (f32[64,194]{1,0:T(8,128)S(1)}, f32[64,194]{1,0:T(8,128)S(1)}, u32[]{:S(2)}, u32[]{:S(2)}) collective-permute-start(f32[64,194]{1,0:T(8,128)S(1)} %get-tuple-element.8), channel_id=1, source_target_pairs={{0,6},{1,7},{2,4},{3,5},{4,2},{5,3},{6,0},{7,1},{8,14},{9,15},{10,... | collective-permute-start | bytes 149000 | tf_op jit(solution)/shard_map/ppermute | solution.py:149
  26.9 9.9 %collective-permute-start.3 = (f32[64,194]{1,0:T(8,128)S(1)}, f32[64,194]{1,0:T(8,128)S(1)}, u32[]{:S(2)}, u32[]{:S(2)}) collective-permute-start(f32[64,194]{1,0:T(8,128)S(1)} %get-tuple-element.8), channel_id=1, source_target_pairs={{0,8},{1,9},{2,10},{3,11},{4,12},{5,13},{6,14},{7,15},{8,0},{9,1},... | collective-permute-start | bytes 149000 | tf_op jit(solution)/shard_map/ppermute | solution.py:149
  29.8 10.2 %collective-permute-start.4 = (f32[64,194]{1,0:T(8,128)S(1)}, f32[64,194]{1,0:T(8,128)S(1)}, u32[]{:S(2)}, u32[]{:S(2)}) collective-permute-start(f32[64,194]{1,0:T(8,128)S(1)} %get-tuple-element.8), channel_id=1, source_target_pairs={{0,10},{1,11},{2,8},{3,9},{4,14},{5,15},{6,12},{7,13},{8,2},{9,3},... | collective-permute-start | bytes 149000 | tf_op jit(solution)/shard_map/ppermute | solution.py:149
  31.1 9.5 %collective-permute-start.5 = (f32[64,194]{1,0:T(8,128)S(1)}, f32[64,194]{1,0:T(8,128)S(1)}, u32[]{:S(2)}, u32[]{:S(2)}) collective-permute-start(f32[64,194]{1,0:T(8,128)S(1)} %get-tuple-element.8), channel_id=1, source_target_pairs={{0,12},{1,13},{2,14},{3,15},{4,8},{5,9},{6,10},{7,11},{8,4},{9,5},... | collective-permute-start | bytes 149000 | tf_op jit(solution)/shard_map/ppermute | solution.py:149
  35.5 7.1 %collective-permute-start.6 = (f32[64,194]{1,0:T(8,128)S(1)}, f32[64,194]{1,0:T(8,128)S(1)}, u32[]{:S(2)}, u32[]{:S(2)}) collective-permute-start(f32[64,194]{1,0:T(8,128)S(1)} %get-tuple-element.8), channel_id=1, source_target_pairs={{0,14},{1,15},{2,12},{3,13},{4,10},{5,11},{6,8},{7,9},{8,6},{9,7},... | collective-permute-start | bytes 149000 | tf_op jit(solution)/shard_map/ppermute | solution.py:149
  43.2 2.1 %collective-permute-start.7 = (f32[8,64,194]{2,1,0:T(8,128)}, f32[8,64,194]{2,1,0:T(8,128)S(1)}, u32[]{:S(2)}, u32[]{:S(2)}) collective-permute-start(f32[8,64,194]{2,1,0:T(8,128)} %get-tuple-element.11), channel_id=1, source_target_pairs={{0,1},{1,0},{2,3},{3,2},{4,5},{5,4},{6,7},{7,6},{8,9},{9,8},{10,11... | collective-permute-start | bytes 1191944 | tf_op jit(solution)/shard_map/ppermute | solution.py:153
  50.9 2.4 %copy-start.1 = (f32[3,3]{1,0:T(4,128)S(1)}, f32[3,3]{1,0:T(4,128)}, u32[]{:S(2)}) copy-start(f32[3,3]{1,0:T(4,128)} %k_ref.1) | copy-start | bytes 112

commit v7 on v6

--- a/solution.py
+++ b/solution.py
@@ -43,7 +43,7 @@
         return carry
 
     lax.fori_loop(0, rows // chunk, conv_chunk, 0)
-    frame_idx = lax.broadcasted_iota(jnp.int32, (WIN, CH), 0)
+    frame_idx = lax.broadcasted_iota(jnp.int32, (WIN, 1), 0)
 
     def stats_block(blk, carry):
         means = []

time: 55.2 us -> 55.5 us (level)
  no operation moved by 1% of the time
where the time goes in v7:
time: 55.5 us; the launch traced here: 55.3 us
  Pallas kernels  18.8 us (34%)
  starting transfers between devices  12.5 us (23%)
  local copies, waits for them, and re-layouts  10.8 us (19%)
  waiting for transfers between devices  5.85 us (11%)
  matrix products  3.54 us (6%)
  other arithmetic  3.53 us (6%)
    pallas_call x1, Pallas kernels, pool_slots(): pl.pallas_call(_pool_kernel, out_shape=jax.ShapeDtypeStruct((slots, 2 * C...  17.2 us
    ppermute x7, starting transfers between devices, gather_wide(): blocks.append(lax.ppermute(x, 'wide', perm))  12.5 us
    unnamed x27, local copies, waits for them, and re-layouts  8.12 us
    ppermute x7, waiting for transfers between devices, gather_wide(): blocks.append(lax.ppermute(x, 'wide', perm))  3.88 us
    ppermute x1, waiting for transfers between devices, gather_wide(): buf = jnp.concatenate([buf, lax.ppermute(buf, 'wide', perm)], axis=0)  1.96 us
    dot_general x1, matrix products, per_device(): col_ext = jnp.dot(selector, unit_ext, preferred_element_type=jnp.float32)  1.9 us
    pallas_call x1, Pallas kernels, smooth_affinity(): pl.pallas_call(_affinity_kernel, out_shape=jax.ShapeDtypeStruct((height,...  1.65 us
    dot_general x1, matrix products, per_device(): jnp.dot(pooled, proj_weight, precision=PRECISE, preferred_element_type=jn...  1.64 us
  transfers between devices with their start and end apart: 8, of which 3 were waited for; matrix products, arithmetic and copies ran while one was open for 7% of the time, Pallas kernels for 0%

profile of v7, /device:TPU:0, one launch (start us, length us, event | category | flops | bytes accessed | tf_op | source)
XLA Modules:
  0.0 55.3 jit_solution(6865077599262373323)
XLA Ops:
  0.0 0.0 copy-start
  0.0 0.0 copy-start.4
  0.0 0.0 copy-start.5
  0.0 0.0 copy-start.6
  0.0 0.0 copy-start.3
  0.0 1.5 %copy.33.frames_ref = f32[2048,80]{1,0:T(8,128)S(1)} copy(f32[2048,80]{0,1:T(8,128)} %param.9) | data formatting | bytes 1310720 | tf_op args[0]
  1.6 0.0 copy-done.4
  1.6 0.0 copy-done.5
  1.6 0.1 copy.34
  1.7 0.0 copy-done.6
  1.7 0.1 copy.35
  1.8 0.0 copy-done.3
  1.8 0.0 copy-start.2
  1.8 1.2 %copy-done.2 = f32[240,1024]{1,0:T(8,128)S(1)} copy-done((f32[240,1024]{1,0:T(8,128)S(1)}, f32[240,1024]{1,0:T(8,128)}, u32[]{:S(2)}) %copy-start.2) | copy-done | bytes 983064
  3.0 17.2 %shard_map.91 = f32[64,2048]{1,0:T(8,128)S(1)} custom-call(s32[64]{0:T(128)S(1)} %broadcast_clamp_fusion.starts_ref, f32[2048,80]{1,0:T(8,128)S(1)} %copy.33.frames_ref, f32[240,1024]{1,0:T(8,128)S(1)} %copy-done.2, f32[1,1024]{1,0:T(1,128)S(1)} %bitcast.38), custom_call_target="tpu_custom_call" | custom-call | flops 6077546496 | bytes 2162688 | tf_op jit(solution)/shard_map/pallas_call | solution.py:75
  20.2 0.0 copy-done
  20.2 0.0 copy-start.7
  20.2 1.6 %fusion.14 = f32[64,192]{1,0:T(8,128)S(1)} fusion(f32[64,2048]{1,0:T(8,128)S(1)} %shard_map.91, f32[2048,192]{0,1:T(8,128)S(1)} %copy-done), kind=kOutput, calls=%fused_computation.60 | convolution fusion | flops 301989888 | bytes 2146304 | tf_op jit(solution)/shard_map/dot_general | solution.py:165
  21.9 0.7 %bitcast_dynamic-update-slice_fusion.15 = (f32[8,64,194]{2,1,0:T(8,128)}, f32[64,194]{1,0:T(8,128)S(1)}) fusion(f32[64,1]{1,0:T(8,128)S(1)} %copy.35, f32[64,1]{1,0:T(8,128)S(1)} %copy.34, f32[64,192]{1,0:T(8,128)S(1)} %fusion.14), kind=kLoop, calls=%fused_computation.33 | loop fusion | flops 24831 | bytes 164864
  22.6 3.0 %collective-permute-start = (f32[64,194]{1,0:T(8,128)S(1)}, f32[64,194]{1,0:T(8,128)S(1)}, u32[]{:S(2)}, u32[]{:S(2)}) collective-permute-start(f32[64,194]{1,0:T(8,128)S(1)} %get-tuple-element.8), channel_id=1, source_target_pairs={{0,2},{1,3},{2,0},{3,1},{4,6},{5,7},{6,4},{7,5},{8,10},{9,11},{10,... | collective-permute-start | bytes 149000 | tf_op jit(solution)/shard_map/ppermute | solution.py:149
  25.6 1.6 %collective-permute-start.1 = (f32[64,194]{1,0:T(8,128)S(1)}, f32[64,194]{1,0:T(8,128)S(1)}, u32[]{:S(2)}, u32[]{:S(2)}) collective-permute-start(f32[64,194]{1,0:T(8,128)S(1)} %get-tuple-element.8), channel_id=1, source_target_pairs={{0,4},{1,5},{2,6},{3,7},{4,0},{5,1},{6,2},{7,3},{8,12},{9,13},{10,... | collective-permute-start | bytes 149000 | tf_op jit(solution)/shard_map/ppermute | solution.py:149
  27.1 0.0 collective-permute-start.2
  27.1 3.0 %collective-permute-start.3 = (f32[64,194]{1,0:T(8,128)S(1)}, f32[64,194]{1,0:T(8,128)S(1)}, u32[]{:S(2)}, u32[]{:S(2)}) collective-permute-start(f32[64,194]{1,0:T(8,128)S(1)} %get-tuple-element.8), channel_id=1, source_target_pairs={{0,8},{1,9},{2,10},{3,11},{4,12},{5,13},{6,14},{7,15},{8,0},{9,1},... | collective-permute-start | bytes 149000 | tf_op jit(solution)/shard_map/ppermute | solution.py:149
  30.1 1.3 %collective-permute-start.4 = (f32[64,194]{1,0:T(8,128)S(1)}, f32[64,194]{1,0:T(8,128)S(1)}, u32[]{:S(2)}, u32[]{:S(2)}) collective-permute-start(f32[64,194]{1,0:T(8,128)S(1)} %get-tuple-element.8), channel_id=1, source_target_pairs={{0,10},{1,11},{2,8},{3,9},{4,14},{5,15},{6,12},{7,13},{8,2},{9,3},... | collective-permute-start | bytes 149000 | tf_op jit(solution)/shard_map/ppermute | solution.py:149
  31.4 0.0 collective-permute-done
  31.4 3.7 %collective-permute-start.5 = (f32[64,194]{1,0:T(8,128)S(1)}, f32[64,194]{1,0:T(8,128)S(1)}, u32[]{:S(2)}, u32[]{:S(2)}) collective-permute-start(f32[64,194]{1,0:T(8,128)S(1)} %get-tuple-element.8), channel_id=1, source_target_pairs={{0,12},{1,13},{2,14},{3,15},{4,8},{5,9},{6,10},{7,11},{8,4},{9,5},... | collective-permute-start | bytes 149000 | tf_op jit(solution)/shard_map/ppermute | solution.py:149
  35.1 0.6 %bitcast_dynamic-update-slice_fusion.13 = (f32[8,64,194]{2,1,0:T(8,128)}, f32[16,64,194]{2,1,0:T(8,128)S(1)}) fusion(f32[8,64,194]{2,1,0:T(8,128)} %get-tuple-element.7, f32[64,194]{1,0:T(8,128)S(1)} %collective-permute-done, f32[16,64,194]{2,1,0:T(8,128)S(1)} %bitcast_dynamic-update-slice_fusion.14), kind=kLoop, calls=%fused_computation.31 | loop fusion | bytes 196608
  35.7 0.0 collective-permute-done.1
  35.7 0.0 collective-permute-start.6
  35.7 0.6 %bitcast_dynamic-update-slice_fusion.11 = (f32[8,64,194]{2,1,0:T(8,128)}, f32[16,64,194]{2,1,0:T(8,128)S(1)}) fusion(f32[8,64,194]{2,1,0:T(8,128)} %get-tuple-element.23, f32[64,194]{1,0:T(8,128)S(1)} %collective-permute-done.1, f32[16,64,194]{2,1,0:T(8,128)S(1)} %get-tuple-element.24), kind=kLoop, calls=%fused_computation.29 | loop fusion | bytes 196608
  36.4 0.0 collective-permute-done.2
  36.4 0.6 %bitcast_dynamic-update-slice_fusion.9 = (f32[8,64,194]{2,1,0:T(8,128)}, f32[16,64,194]{2,1,0:T(8,128)S(1)}) fusion(f32[8,64,194]{2,1,0:T(8,128)} %get-tuple-element.21, f32[64,194]{1,0:T(8,128)S(1)} %collective-permute-done.2, f32[16,64,194]{2,1,0:T(8,128)S(1)} %get-tuple-element.22), kind=kLoop, calls=%fused_computation.27 | loop fusion | bytes 196608
  37.0 0.0 collective-permute-done.3
  37.0 0.6 %bitcast_dynamic-update-slice_fusion.7 = (f32[8,64,194]{2,1,0:T(8,128)}, f32[16,64,194]{2,1,0:T(8,128)S(1)}) fusion(f32[8,64,194]{2,1,0:T(8,128)} %get-tuple-element.19, f32[64,194]{1,0:T(8,128)S(1)} %collective-permute-done.3, f32[16,64,194]{2,1,0:T(8,128)S(1)} %get-tuple-element.20), kind=kLoop, calls=%fused_computation.25 | loop fusion | bytes 196608
  37.7 2.7 %collective-permute-done.4 = f32[64,194]{1,0:T(8,128)S(1)} collective-permute-done((f32[64,194]{1,0:T(8,128)S(1)}, f32[64,194]{1,0:T(8,128)S(1)}, u32[]{:S(2)}, u32[]{:S(2)}) %collective-permute-start.4) | collective-permute-done | bytes 49696 | tf_op jit(solution)/shard_map/ppermute | solution.py:149
  40.3 0.6 %bitcast_dynamic-update-slice_fusion.5 = (f32[8,64,194]{2,1,0:T(8,128)}, f32[16,64,194]{2,1,0:T(8,128)S(1)}) fusion(f32[8,64,194]{2,1,0:T(8,128)} %get-tuple-element.17, f32[64,194]{1,0:T(8,128)S(1)} %collective-permute-done.4, f32[16,64,194]{2,1,0:T(8,128)S(1)} %get-tuple-element.18), kind=kLoop, calls=%fused_computation.23 | loop fusion | bytes 196608
  41.0 0.0 collective-permute-done.5
  41.0 0.6 %bitcast_dynamic-update-slice_fusion.3 = (f32[8,64,194]{2,1,0:T(8,128)}, f32[16,64,194]{2,1,0:T(8,128)S(1)}) fusion(f32[8,64,194]{2,1,0:T(8,128)} %get-tuple-element.15, f32[64,194]{1,0:T(8,128)S(1)} %collective-permute-done.5, f32[16,64,194]{2,1,0:T(8,128)S(1)} %get-tuple-element.16), kind=kLoop, calls=%fused_computation.21 | loop fusion | bytes 196608
  41.6 1.2 %collective-permute-done.6 = f32[64,194]{1,0:T(8,128)S(1)} collective-permute-done((f32[64,194]{1,0:T(8,128)S(1)}, f32[64,194]{1,0:T(8,128)S(1)}, u32[]{:S(2)}, u32[]{:S(2)}) %collective-permute-start.6) | collective-permute-done | bytes 49696 | tf_op jit(solution)/shard_map/ppermute | solution.py:149
  42.8 0.6 %bitcast_dynamic-update-slice_fusion.1 = (f32[8,64,194]{2,1,0:T(8,128)}, f32[16,64,194]{2,1,0:T(8,128)S(1)}) fusion(f32[8,64,194]{2,1,0:T(8,128)} %get-tuple-element.13, f32[64,194]{1,0:T(8,128)S(1)} %collective-permute-done.6, f32[16,64,194]{2,1,0:T(8,128)S(1)} %get-tuple-element.14), kind=kLoop, calls=%fused_computation.19 | loop fusion | bytes 196608 | tf_op jit(solution)/shard_map/stack | solution.py:151
  43.4 0.0 collective-permute-start.7
  43.4 0.0 copy-done.7
  43.4 0.1 iota_add_fusion
  43.5 0.1 add.70
  43.6 2.0 %collective-permute-done.7 = f32[8,64,194]{2,1,0:T(8,128)S(1)} collective-permute-done((f32[8,64,194]{2,1,0:T(8,128)}, f32[8,64,194]{2,1,0:T(8,128)S(1)}, u32[]{:S(2)}, u32[]{:S(2)}) %collective-permute-start.7) | collective-permute-done | bytes 397344 | tf_op jit(solution)/shard_map/ppermute | solution.py:153
  45.6 1.1 %fusion.13 = (f32[1024,1]{1,0:T(8,128)S(1)}, f32[1024,1]{1,0:T(8,128)}) fusion(f32[1024,194]{1,0:T(8,128)S(1)} %bitcast.39), kind=kLoop, calls=%fused_computation.59 | loop fusion | bytes 16384 | tf_op jit(solution)/shard_map/slice | solution.py:182
  46.7 1.2 %copy.42 = f32[1024,1]{0,1:T(1,128)S(1)} copy(f32[1024,1]{1,0:T(8,128)} %get-tuple-element.10) | data formatting | bytes 8192
  48.0 0.2 select_reduce_fusion
  48.2 0.2 multiply_reduce_fusion
  48.4 1.0 %divide_convert_fusion = bf16[1024,192]{1,0:T(8,128)(2,1)} fusion(f32[1024,194]{1,0:T(8,128)S(1)} %bitcast.42, f32[1024]{0:T(1024)S(1)} %add_sqrt_fusion, f32[192]{0:T(256)S(1)} %broadcast_multiply_fusion), kind=kLoop, calls=%fused_computation.3 | loop fusion | flops 589824 | bytes 1184512 | tf_op jit(solution)/shard_map/convert_element_type | solution.py:188
  49.5 0.2 copy.43
  49.7 0.2 copy.39
  49.9 0.2 copy.38
  50.1 1.0 %convert_reduce_fusion = s32[1024]{0:T(1024)S(1)} fusion(s32[1024]{0:T(1024)S(1)} %bitcast.43, s32[1024]{0:T(1024)S(1)} %add.70), kind=kLoop, calls=%fused_computation | loop fusion | flops 5241856 | bytes 12288 | tf_op jit(solution)/shard_map/reduce_sum | solution.py:193
  51.2 0.0 copy-start.1
  51.2 1.9 %fusion = f32[512,194]{0,1:T(8,128)S(1)} fusion(s32[1024]{0:T(1024)S(1)} %add_select_fusion, bf16[1024,1]{1,0:T(8,128)(2,1)S(1)} %copy.39, bf16[1024,1]{1,0:T(8,128)(2,1)S(1)} %copy.38, bf16[1024,192]{1,0:T(8,128)(2,1)} %divide_convert_fusion), kind=kOutput, calls=%fused_computation.2 | convolution fusion | flops 205139968 | bytes 798720 | tf_op jit(solution)/shard_map/dot_general | solution.py:204
  53.2 0.1 copy.44.col_unit_ref
  53.3 0.1 pad_add_fusion
  53.4 0.1 dynamic-slice_bitcast_fusion
  53.5 0.1 copy.41.row_rec_ref
  53.6 0.0 copy-done.1
  53.6 1.6 %shard_map.92 = f32[32,512]{1,0:T(8,128)} custom-call(f32[3,3]{1,0:T(4,128)S(1)} %copy-done.1, bf16[34,192]{1,0:T(8,128)(2,1)S(1)} %fusion.8.row_unit_ref, bf16[512,192]{1,0:T(8,128)(2,1)S(1)} %copy.44.col_unit_ref, s32[34,1]{1,0:T(8,128)S(1)} %copy.41.row_rec_ref, s32[1,512]{1,0:T(1,128)S(1)} %fusion.17.col_rec_ref), custom_call_target="tpu_custom_call" | custom-call | flops 7012352 | bytes 275200 | tf_op jit(solution)/shard_map/pallas_call | solution.py:122
  (18 shorter events, 0.3 us)
Async XLA Ops:
  0.0 20.2 %copy-start = (f32[2048,192]{0,1:T(8,128)S(1)}, f32[2048,192]{0,1:T(8,128)}, u32[]{:S(2)}) copy-start(f32[2048,192]{0,1:T(8,128)} %param.15) | copy-start | bytes 4718596
  0.0 1.6 %copy-start.4 = (s32[64]{0:T(128)S(1)}, s32[64]{0:T(128)}, u32[]{:S(2)}) copy-start(s32[64]{0:T(128)} %param.10) | copy-start | bytes 772
  0.0 1.6 %copy-start.5 = (s32[64]{0:T(128)S(1)}, s32[64]{0:T(128)}, u32[]{:S(2)}) copy-start(s32[64]{0:T(128)} %param.11) | copy-start | bytes 772
  0.0 1.7 %copy-start.6 = (s32[64]{0:T(128)S(1)}, s32[64]{0:T(128)}, u32[]{:S(2)}) copy-start(s32[64]{0:T(128)} %param.12) | copy-start | bytes 772
  0.0 1.8 %copy-start.3 = (f32[1024]{0:T(1024)S(1)}, f32[1024]{0:T(1024)}, u32[]{:S(2)}) copy-start(f32[1024]{0:T(1024)} %param.14) | copy-start | bytes 12292
  1.8 1.2 %copy-start.2 = (f32[240,1024]{1,0:T(8,128)S(1)}, f32[240,1024]{1,0:T(8,128)}, u32[]{:S(2)}) copy-start(f32[240,1024]{1,0:T(8,128)} %w_ref.1) | copy-start | bytes 2949124
  20.2 23.2 %copy-start.7 = (s32[16]{0:T(128)S(1)}, s32[16]{0:T(128)}, u32[]{:S(2)}) copy-start(s32[16]{0:T(128)} %constant.59.clone) | copy-start | bytes 196
  22.6 8.8 %collective-permute-start = (f32[64,194]{1,0:T(8,128)S(1)}, f32[64,194]{1,0:T(8,128)S(1)}, u32[]{:S(2)}, u32[]{:S(2)}) collective-permute-start(f32[64,194]{1,0:T(8,128)S(1)} %get-tuple-element.8), channel_id=1, source_target_pairs={{0,2},{1,3},{2,0},{3,1},{4,6},{5,7},{6,4},{7,5},{8,10},{9,11},{10,... | collective-permute-start | bytes 149000 | tf_op jit(solution)/shard_map/ppermute | solution.py:149
  25.6 10.2 %collective-permute-start.1 = (f32[64,194]{1,0:T(8,128)S(1)}, f32[64,194]{1,0:T(8,128)S(1)}, u32[]{:S(2)}, u32[]{:S(2)}) collective-permute-start(f32[64,194]{1,0:T(8,128)S(1)} %get-tuple-element.8), channel_id=1, source_target_pairs={{0,4},{1,5},{2,6},{3,7},{4,0},{5,1},{6,2},{7,3},{8,12},{9,13},{10,... | collective-permute-start | bytes 149000 | tf_op jit(solution)/shard_map/ppermute | solution.py:149
  27.1 9.2 %collective-permute-start.2 = (f32[64,194]{1,0:T(8,128)S(1)}, f32[64,194]{1,0:T(8,128)S(1)}, u32[]{:S(2)}, u32[]{:S(2)}) collective-permute-start(f32[64,194]{1,0:T(8,128)S(1)} %get-tuple-element.8), channel_id=1, source_target_pairs={{0,6},{1,7},{2,4},{3,5},{4,2},{5,3},{6,0},{7,1},{8,14},{9,15},{10,... | collective-permute-start | bytes 149000 | tf_op jit(solution)/shard_map/ppermute | solution.py:149
  27.1 9.9 %collective-permute-start.3 = (f32[64,194]{1,0:T(8,128)S(1)}, f32[64,194]{1,0:T(8,128)S(1)}, u32[]{:S(2)}, u32[]{:S(2)}) collective-permute-start(f32[64,194]{1,0:T(8,128)S(1)} %get-tuple-element.8), channel_id=1, source_target_pairs={{0,8},{1,9},{2,10},{3,11},{4,12},{5,13},{6,14},{7,15},{8,0},{9,1},... | collective-permute-start | bytes 149000 | tf_op jit(solution)/shard_map/ppermute | solution.py:149
  30.1 10.2 %collective-permute-start.4 = (f32[64,194]{1,0:T(8,128)S(1)}, f32[64,194]{1,0:T(8,128)S(1)}, u32[]{:S(2)}, u32[]{:S(2)}) collective-permute-start(f32[64,194]{1,0:T(8,128)S(1)} %get-tuple-element.8), channel_id=1, source_target_pairs={{0,10},{1,11},{2,8},{3,9},{4,14},{5,15},{6,12},{7,13},{8,2},{9,3},... | collective-permute-start | bytes 149000 | tf_op jit(solution)/shard_map/ppermute | solution.py:149
  31.4 9.5 %collective-permute-start.5 = (f32[64,194]{1,0:T(8,128)S(1)}, f32[64,194]{1,0:T(8,128)S(1)}, u32[]{:S(2)}, u32[]{:S(2)}) collective-permute-start(f32[64,194]{1,0:T(8,128)S(1)} %get-tuple-element.8), channel_id=1, source_target_pairs={{0,12},{1,13},{2,14},{3,15},{4,8},{5,9},{6,10},{7,11},{8,4},{9,5},... | collective-permute-start | bytes 149000 | tf_op jit(solution)/shard_map/ppermute | solution.py:149
  35.7 7.1 %collective-permute-start.6 = (f32[64,194]{1,0:T(8,128)S(1)}, f32[64,194]{1,0:T(8,128)S(1)}, u32[]{:S(2)}, u32[]{:S(2)}) collective-permute-start(f32[64,194]{1,0:T(8,128)S(1)} %get-tuple-element.8), channel_id=1, source_target_pairs={{0,14},{1,15},{2,12},{3,13},{4,10},{5,11},{6,8},{7,9},{8,6},{9,7},... | collective-permute-start | bytes 149000 | tf_op jit(solution)/shard_map/ppermute | solution.py:149
  43.4 2.1 %collective-permute-start.7 = (f32[8,64,194]{2,1,0:T(8,128)}, f32[8,64,194]{2,1,0:T(8,128)S(1)}, u32[]{:S(2)}, u32[]{:S(2)}) collective-permute-start(f32[8,64,194]{2,1,0:T(8,128)} %get-tuple-element.11), channel_id=1, source_target_pairs={{0,1},{1,0},{2,3},{3,2},{4,5},{5,4},{6,7},{7,6},{8,9},{9,8},{10,11... | collective-permute-start | bytes 1191944 | tf_op jit(solution)/shard_map/ppermute | solution.py:153
  51.2 2.4 %copy-start.1 = (f32[3,3]{1,0:T(4,128)S(1)}, f32[3,3]{1,0:T(4,128)}, u32[]{:S(2)}) copy-start(f32[3,3]{1,0:T(4,128)} %k_ref.1) | copy-start | bytes 112

commit v8 on v6

--- a/solution.py
+++ b/solution.py
@@ -22,23 +22,26 @@
 ONE_HOT_LIMIT = 1 << 20
 
 
-def _pool_kernel(starts_ref, frames_ref, w_ref, b_ref, out_ref, x3_ref, act_ref):
+def _pool_kernel(starts_ref, frames_ref, w_hi_ref, w_lo_ref, b_ref, out_ref, hi_ref, lo_ref, act_ref):
     rows = frames_ref.shape[0]
     slots = out_ref.shape[0]
     frames = frames_ref[...]
-    x3_ref[...] = jnp.concatenate(
+    x3 = jnp.concatenate(
         [pltpu.roll(frames, 1, 0), frames, pltpu.roll(frames, rows - 1, 0)], axis=1
     )
+    x3_hi = x3.astype(jnp.bfloat16)
+    hi_ref[...] = x3_hi
+    lo_ref[...] = (x3 - x3_hi.astype(jnp.float32)).astype(jnp.bfloat16)
     chunk = CONV_ROWS if rows % CONV_ROWS == 0 else rows
 
     def conv_chunk(c, carry):
         base = pl.multiple_of(c * chunk, chunk)
-        preact = jnp.dot(
-            x3_ref[pl.ds(base, chunk), :],
-            w_ref[...],
-            precision=PRECISE,
-            preferred_element_type=jnp.float32,
-        )
+        x_hi = hi_ref[pl.ds(base, chunk), :]
+        x_lo = lo_ref[pl.ds(base, chunk), :]
+        w_hi = w_hi_ref[...]
+        preact = jnp.dot(x_hi, w_hi, preferred_element_type=jnp.float32)
+        preact = preact + jnp.dot(x_hi, w_lo_ref[...], preferred_element_type=jnp.float32)
+        preact = preact + jnp.dot(x_lo, w_hi, preferred_element_type=jnp.float32)
         act_ref[pl.ds(base, chunk), :] = jnp.maximum(preact + b_ref[...], 0.0)
         return carry
 
@@ -72,6 +75,8 @@
     slots = seg_start.shape[0]
     starts = jnp.clip(seg_start, 0, rows - SEGLEN).astype(jnp.int32)
     vmem = pltpu.MemorySpace.VMEM
+    w_hi = conv_weight.astype(jnp.bfloat16)
+    w_lo = (conv_weight - w_hi.astype(jnp.float32)).astype(jnp.bfloat16)
     return pl.pallas_call(
         _pool_kernel,
         out_shape=jax.ShapeDtypeStruct((slots, 2 * CH), jnp.float32),
@@ -80,19 +85,21 @@
             pl.BlockSpec(memory_space=vmem),
             pl.BlockSpec(memory_space=vmem),
             pl.BlockSpec(memory_space=vmem),
+            pl.BlockSpec(memory_space=vmem),
         ],
         out_specs=pl.BlockSpec(memory_space=vmem),
         scratch_shapes=[
-            pltpu.VMEM((rows, 3 * FEAT), jnp.float32),
+            pltpu.VMEM((rows, 3 * FEAT), jnp.bfloat16),
+            pltpu.VMEM((rows, 3 * FEAT), jnp.bfloat16),
             pltpu.VMEM((rows, CH), jnp.float32),
         ],
         compiler_params=pltpu.CompilerParams(vmem_limit_bytes=48 * 1024 * 1024),
         cost_estimate=pl.CostEstimate(
-            flops=2 * rows * 3 * FEAT * CH * 6 + 8 * slots * WIN * CH,
+            flops=2 * rows * 3 * FEAT * CH * 3 + 8 * slots * WIN * CH,
             transcendentals=slots * CH,
             bytes_accessed=rows * FEAT * 4 + 3 * FEAT * CH * 4 + slots * 2 * CH * 4,
         ),
-    )(starts, frames, conv_weight, conv_bias.reshape(1, CH))
+    )(starts, frames, w_hi, w_lo, conv_bias.reshape(1, CH))
 
 
 def _affinity_kernel(k_ref, row_unit_ref, col_unit_ref, row_rec_ref, col_rec_ref, out_ref, pad_ref):

time: 55.2 us -> 54 us (0.978)
  Pallas kernels: 18.6 us -> 15 us
  other arithmetic: 3.53 us -> 6.15 us
    pallas_call x1, Pallas kernels: 16.9 us -> 13.3 us  [pool_slots(): pl.pallas_call(_pool_kernel, out_shape=jax.ShapeDtypeStruct((slots, 2 * C...]
    convert_element_type x0 -> x1, other arithmetic: none -> 2.63 us  [pool_slots(): w_lo = (conv_weight - w_hi.astype(jnp.float32)).astype(jnp.bfloat16)]
where the time goes in v8:
time: 54 us; the launch traced here: 53.7 us
  Pallas kernels  15 us (28%)
  starting transfers between devices  12.5 us (23%)
  local copies, waits for them, and re-layouts  10.4 us (19%)
  other arithmetic  6.15 us (11%)
  waiting for transfers between devices  5.89 us (11%)
  matrix products  3.54 us (7%)
    pallas_call x1, Pallas kernels, pool_slots(): pl.pallas_call(_pool_kernel, out_shape=jax.ShapeDtypeStruct((slots, 2 * C...  13.3 us
    ppermute x7, starting transfers between devices, gather_wide(): blocks.append(lax.ppermute(x, 'wide', perm))  12.5 us
    unnamed x27, local copies, waits for them, and re-layouts  7.79 us
    ppermute x7, waiting for transfers between devices, gather_wide(): blocks.append(lax.ppermute(x, 'wide', perm))  3.92 us
    convert_element_type x1, other arithmetic, pool_slots(): w_lo = (conv_weight - w_hi.astype(jnp.float32)).astype(jnp.bfloat16)  2.63 us
    ppermute x1, waiting for transfers between devices, gather_wide(): buf = jnp.concatenate([buf, lax.ppermute(buf, 'wide', perm)], axis=0)  1.96 us
    dot_general x1, matrix products, per_device(): col_ext = jnp.dot(selector, unit_ext, preferred_element_type=jnp.float32)  1.9 us
    pallas_call x1, Pallas kernels, smooth_affinity(): pl.pallas_call(_affinity_kernel, out_shape=jax.ShapeDtypeStruct((height,...  1.65 us
  transfers between devices with their start and end apart: 8, of which 3 were waited for; matrix products, arithmetic and copies ran while one was open for 7% of the time, Pallas kernels for 0%

profile of v8, /device:TPU:0, one launch (start us, length us, event | category | flops | bytes accessed | tf_op | source)
XLA Modules:
  0.0 53.7 jit_solution(8096076978521319748)
XLA Ops:
  0.0 0.0 copy-start
  0.0 0.0 copy-start.4
  0.0 0.0 copy-start.5
  0.0 0.0 copy-start.6
  0.0 0.0 copy-start.3
  0.0 2.6 %subtract_convert_fusion = (bf16[240,1024]{1,0:T(8,128)(2,1)S(1)}, bf16[240,1024]{1,0:T(8,128)(2,1)}) fusion(f32[240,1024]{1,0:T(8,128)} %param.13), kind=kLoop, calls=%fused_computation.8 | loop fusion | flops 983040 | bytes 1966080 | tf_op jit(solution)/shard_map/convert_element_type | solution.py:79
  2.6 1.4 %copy.33.frames_ref = f32[2048,80]{1,0:T(8,128)S(1)} copy(f32[2048,80]{0,1:T(8,128)} %param.9) | data formatting | bytes 1310720 | tf_op args[0]
  4.1 0.0 copy-done.4
  4.1 0.0 copy-done.5
  4.1 0.1 copy.34
  4.2 0.0 copy-done.6
  4.2 0.1 copy.35
  4.3 0.0 copy-done.3
  4.3 0.0 copy-start.1
  4.3 1.0 %copy-done.1 = bf16[240,1024]{1,0:T(8,128)(2,1)S(1)} copy-done((bf16[240,1024]{1,0:T(8,128)(2,1)S(1)}, bf16[240,1024]{1,0:T(8,128)(2,1)}, u32[]{:S(2)}) %copy-start.1) | copy-done | bytes 491544
  5.4 13.3 %shard_map.91 = f32[64,2048]{1,0:T(8,128)S(1)} custom-call(s32[64]{0:T(128)S(1)} %broadcast_clamp_fusion.starts_ref, f32[2048,80]{1,0:T(8,128)S(1)} %copy.33.frames_ref, bf16[240,1024]{1,0:T(8,128)(2,1)S(1)} %copy-done.1, bf16[240,1024]{1,0:T(8,128)(2,1)S(1)} %get-tuple-element.9.w_lo_ref, f32[1,1024]{1,0:T(1,128)S(1)} %bitcast.38), custom_call_target="tpu_custom_call" | custom-call | flops 3057647616 | bytes 2162688 | tf_op jit(solution)/shard_map/pallas_call | solution.py:80
  18.7 0.0 copy-done
  18.7 0.0 copy-start.7
  18.7 1.6 %fusion.14 = f32[64,192]{1,0:T(8,128)S(1)} fusion(f32[64,2048]{1,0:T(8,128)S(1)} %shard_map.91, f32[2048,192]{0,1:T(8,128)S(1)} %copy-done), kind=kOutput, calls=%fused_computation.61 | convolution fusion | flops 301989888 | bytes 2146304 | tf_op jit(solution)/shard_map/dot_general | solution.py:172
  20.3 0.7 %bitcast_dynamic-update-slice_fusion.15 = (f32[8,64,194]{2,1,0:T(8,128)}, f32[64,194]{1,0:T(8,128)S(1)}) fusion(f32[64,1]{1,0:T(8,128)S(1)} %copy.35, f32[64,1]{1,0:T(8,128)S(1)} %copy.34, f32[64,192]{1,0:T(8,128)S(1)} %fusion.14), kind=kLoop, calls=%fused_computation.34 | loop fusion | flops 24831 | bytes 164864
  21.1 3.0 %collective-permute-start = (f32[64,194]{1,0:T(8,128)S(1)}, f32[64,194]{1,0:T(8,128)S(1)}, u32[]{:S(2)}, u32[]{:S(2)}) collective-permute-start(f32[64,194]{1,0:T(8,128)S(1)} %get-tuple-element.8), channel_id=1, source_target_pairs={{0,2},{1,3},{2,0},{3,1},{4,6},{5,7},{6,4},{7,5},{8,10},{9,11},{10,... | collective-permute-start | bytes 149000 | tf_op jit(solution)/shard_map/ppermute | solution.py:156
  24.0 1.6 %collective-permute-start.1 = (f32[64,194]{1,0:T(8,128)S(1)}, f32[64,194]{1,0:T(8,128)S(1)}, u32[]{:S(2)}, u32[]{:S(2)}) collective-permute-start(f32[64,194]{1,0:T(8,128)S(1)} %get-tuple-element.8), channel_id=1, source_target_pairs={{0,4},{1,5},{2,6},{3,7},{4,0},{5,1},{6,2},{7,3},{8,12},{9,13},{10,... | collective-permute-start | bytes 149000 | tf_op jit(solution)/shard_map/ppermute | solution.py:156
  25.6 0.0 collective-permute-start.2
  25.6 3.0 %collective-permute-start.3 = (f32[64,194]{1,0:T(8,128)S(1)}, f32[64,194]{1,0:T(8,128)S(1)}, u32[]{:S(2)}, u32[]{:S(2)}) collective-permute-start(f32[64,194]{1,0:T(8,128)S(1)} %get-tuple-element.8), channel_id=1, source_target_pairs={{0,8},{1,9},{2,10},{3,11},{4,12},{5,13},{6,14},{7,15},{8,0},{9,1},... | collective-permute-start | bytes 149000 | tf_op jit(solution)/shard_map/ppermute | solution.py:156
  28.6 1.3 %collective-permute-start.4 = (f32[64,194]{1,0:T(8,128)S(1)}, f32[64,194]{1,0:T(8,128)S(1)}, u32[]{:S(2)}, u32[]{:S(2)}) collective-permute-start(f32[64,194]{1,0:T(8,128)S(1)} %get-tuple-element.8), channel_id=1, source_target_pairs={{0,10},{1,11},{2,8},{3,9},{4,14},{5,15},{6,12},{7,13},{8,2},{9,3},... | collective-permute-start | bytes 149000 | tf_op jit(solution)/shard_map/ppermute | solution.py:156
  29.9 0.0 collective-permute-done
  29.9 3.7 %collective-permute-start.5 = (f32[64,194]{1,0:T(8,128)S(1)}, f32[64,194]{1,0:T(8,128)S(1)}, u32[]{:S(2)}, u32[]{:S(2)}) collective-permute-start(f32[64,194]{1,0:T(8,128)S(1)} %get-tuple-element.8), channel_id=1, source_target_pairs={{0,12},{1,13},{2,14},{3,15},{4,8},{5,9},{6,10},{7,11},{8,4},{9,5},... | collective-permute-start | bytes 149000 | tf_op jit(solution)/shard_map/ppermute | solution.py:156
  33.6 0.6 %bitcast_dynamic-update-slice_fusion.13 = (f32[8,64,194]{2,1,0:T(8,128)}, f32[16,64,194]{2,1,0:T(8,128)S(1)}) fusion(f32[8,64,194]{2,1,0:T(8,128)} %get-tuple-element.7, f32[64,194]{1,0:T(8,128)S(1)} %collective-permute-done, f32[16,64,194]{2,1,0:T(8,128)S(1)} %bitcast_dynamic-update-slice_fusion.14), kind=kLoop, calls=%fused_computation.32 | loop fusion | bytes 196608
  34.2 0.0 collective-permute-done.1
  34.2 0.0 collective-permute-start.6
  34.2 0.6 %bitcast_dynamic-update-slice_fusion.11 = (f32[8,64,194]{2,1,0:T(8,128)}, f32[16,64,194]{2,1,0:T(8,128)S(1)}) fusion(f32[8,64,194]{2,1,0:T(8,128)} %get-tuple-element.25, f32[64,194]{1,0:T(8,128)S(1)} %collective-permute-done.1, f32[16,64,194]{2,1,0:T(8,128)S(1)} %get-tuple-element.26), kind=kLoop, calls=%fused_computation.30 | loop fusion | bytes 196608
  34.8 0.0 collective-permute-done.2
  34.8 0.6 %bitcast_dynamic-update-slice_fusion.9 = (f32[8,64,194]{2,1,0:T(8,128)}, f32[16,64,194]{2,1,0:T(8,128)S(1)}) fusion(f32[8,64,194]{2,1,0:T(8,128)} %get-tuple-element.23, f32[64,194]{1,0:T(8,128)S(1)} %collective-permute-done.2, f32[16,64,194]{2,1,0:T(8,128)S(1)} %get-tuple-element.24), kind=kLoop, calls=%fused_computation.28 | loop fusion | bytes 196608
  35.5 0.0 collective-permute-done.3
  35.5 0.6 %bitcast_dynamic-update-slice_fusion.7 = (f32[8,64,194]{2,1,0:T(8,128)}, f32[16,64,194]{2,1,0:T(8,128)S(1)}) fusion(f32[8,64,194]{2,1,0:T(8,128)} %get-tuple-element.21, f32[64,194]{1,0:T(8,128)S(1)} %collective-permute-done.3, f32[16,64,194]{2,1,0:T(8,128)S(1)} %get-tuple-element.22), kind=kLoop, calls=%fused_computation.26 | loop fusion | bytes 196608
  36.1 2.7 %collective-permute-done.4 = f32[64,194]{1,0:T(8,128)S(1)} collective-permute-done((f32[64,194]{1,0:T(8,128)S(1)}, f32[64,194]{1,0:T(8,128)S(1)}, u32[]{:S(2)}, u32[]{:S(2)}) %collective-permute-start.4) | collective-permute-done | bytes 49696 | tf_op jit(solution)/shard_map/ppermute | solution.py:156
  38.8 0.6 %bitcast_dynamic-update-slice_fusion.5 = (f32[8,64,194]{2,1,0:T(8,128)}, f32[16,64,194]{2,1,0:T(8,128)S(1)}) fusion(f32[8,64,194]{2,1,0:T(8,128)} %get-tuple-element.19, f32[64,194]{1,0:T(8,128)S(1)} %collective-permute-done.4, f32[16,64,194]{2,1,0:T(8,128)S(1)} %get-tuple-element.20), kind=kLoop, calls=%fused_computation.24 | loop fusion | bytes 196608
  39.4 0.0 collective-permute-done.5
  39.4 0.6 %bitcast_dynamic-update-slice_fusion.3 = (f32[8,64,194]{2,1,0:T(8,128)}, f32[16,64,194]{2,1,0:T(8,128)S(1)}) fusion(f32[8,64,194]{2,1,0:T(8,128)} %get-tuple-element.17, f32[64,194]{1,0:T(8,128)S(1)} %collective-permute-done.5, f32[16,64,194]{2,1,0:T(8,128)S(1)} %get-tuple-element.18), kind=kLoop, calls=%fused_computation.22 | loop fusion | bytes 196608
  40.1 1.2 %collective-permute-done.6 = f32[64,194]{1,0:T(8,128)S(1)} collective-permute-done((f32[64,194]{1,0:T(8,128)S(1)}, f32[64,194]{1,0:T(8,128)S(1)}, u32[]{:S(2)}, u32[]{:S(2)}) %collective-permute-start.6) | collective-permute-done | bytes 49696 | tf_op jit(solution)/shard_map/ppermute | solution.py:156
  41.3 0.6 %bitcast_dynamic-update-slice_fusion.1 = (f32[8,64,194]{2,1,0:T(8,128)}, f32[16,64,194]{2,1,0:T(8,128)S(1)}) fusion(f32[8,64,194]{2,1,0:T(8,128)} %get-tuple-element.15, f32[64,194]{1,0:T(8,128)S(1)} %collective-permute-done.6, f32[16,64,194]{2,1,0:T(8,128)S(1)} %get-tuple-element.16), kind=kLoop, calls=%fused_computation.20 | loop fusion | bytes 196608 | tf_op jit(solution)/shard_map/stack | solution.py:158
  41.9 0.0 collective-permute-start.7
  41.9 0.0 copy-done.7
  41.9 0.1 iota_add_fusion
  42.0 0.1 add.70
  42.0 2.0 %collective-permute-done.7 = f32[8,64,194]{2,1,0:T(8,128)S(1)} collective-permute-done((f32[8,64,194]{2,1,0:T(8,128)}, f32[8,64,194]{2,1,0:T(8,128)S(1)}, u32[]{:S(2)}, u32[]{:S(2)}) %collective-permute-start.7) | collective-permute-done | bytes 397344 | tf_op jit(solution)/shard_map/ppermute | solution.py:160
  44.1 1.1 %fusion.13 = (f32[1024,1]{1,0:T(8,128)S(1)}, f32[1024,1]{1,0:T(8,128)}) fusion(f32[1024,194]{1,0:T(8,128)S(1)} %bitcast.39), kind=kLoop, calls=%fused_computation.60 | loop fusion | bytes 16384 | tf_op jit(solution)/shard_map/slice | solution.py:189
  45.2 1.2 %copy.42 = f32[1024,1]{0,1:T(1,128)S(1)} copy(f32[1024,1]{1,0:T(8,128)} %get-tuple-element.12) | data formatting | bytes 8192
  46.4 0.2 select_reduce_fusion
  46.7 0.2 multiply_reduce_fusion
  46.9 1.0 %divide_convert_fusion = bf16[1024,192]{1,0:T(8,128)(2,1)} fusion(f32[1024,194]{1,0:T(8,128)S(1)} %bitcast.42, f32[1024]{0:T(1024)S(1)} %add_sqrt_fusion, f32[192]{0:T(256)S(1)} %broadcast_multiply_fusion), kind=kLoop, calls=%fused_computation.3 | loop fusion | flops 589824 | bytes 1184512 | tf_op jit(solution)/shard_map/convert_element_type | solution.py:195
  47.9 0.2 copy.43
  48.2 0.2 copy.39
  48.4 0.2 copy.38
  48.6 1.0 %convert_reduce_fusion = s32[1024]{0:T(1024)S(1)} fusion(s32[1024]{0:T(1024)S(1)} %bitcast.43, s32[1024]{0:T(1024)S(1)} %add.70), kind=kLoop, calls=%fused_computation | loop fusion | flops 5241856 | bytes 12288 | tf_op jit(solution)/shard_map/reduce_sum | solution.py:200
  49.6 0.0 copy-start.2
  49.6 1.9 %fusion = f32[512,194]{0,1:T(8,128)S(1)} fusion(s32[1024]{0:T(1024)S(1)} %add_select_fusion, bf16[1024,1]{1,0:T(8,128)(2,1)S(1)} %copy.39, bf16[1024,1]{1,0:T(8,128)(2,1)S(1)} %copy.38, bf16[1024,192]{1,0:T(8,128)(2,1)} %divide_convert_fusion), kind=kOutput, calls=%fused_computation.2 | convolution fusion | flops 205139968 | bytes 798720 | tf_op jit(solution)/shard_map/dot_general | solution.py:211
  51.6 0.1 copy.44.col_unit_ref
  51.8 0.1 pad_add_fusion
  51.8 0.1 dynamic-slice_bitcast_fusion
  51.9 0.1 copy.41.row_rec_ref
  52.1 0.0 copy-done.2
  52.1 1.6 %shard_map.92 = f32[32,512]{1,0:T(8,128)} custom-call(f32[3,3]{1,0:T(4,128)S(1)} %copy-done.2, bf16[34,192]{1,0:T(8,128)(2,1)S(1)} %fusion.8.row_unit_ref, bf16[512,192]{1,0:T(8,128)(2,1)S(1)} %copy.44.col_unit_ref, s32[34,1]{1,0:T(8,128)S(1)} %copy.41.row_rec_ref, s32[1,512]{1,0:T(1,128)S(1)} %fusion.17.col_rec_ref), custom_call_target="tpu_custom_call" | custom-call | flops 7012352 | bytes 275200 | tf_op jit(solution)/shard_map/pallas_call | solution.py:129
  (18 shorter events, 0.3 us)
Async XLA Ops:
  0.0 18.7 %copy-start = (f32[2048,192]{0,1:T(8,128)S(1)}, f32[2048,192]{0,1:T(8,128)}, u32[]{:S(2)}) copy-start(f32[2048,192]{0,1:T(8,128)} %param.15) | copy-start | bytes 4718596
  0.0 4.1 %copy-start.4 = (s32[64]{0:T(128)S(1)}, s32[64]{0:T(128)}, u32[]{:S(2)}) copy-start(s32[64]{0:T(128)} %param.10) | copy-start | bytes 772
  0.0 4.1 %copy-start.5 = (s32[64]{0:T(128)S(1)}, s32[64]{0:T(128)}, u32[]{:S(2)}) copy-start(s32[64]{0:T(128)} %param.11) | copy-start | bytes 772
  0.0 4.2 %copy-start.6 = (s32[64]{0:T(128)S(1)}, s32[64]{0:T(128)}, u32[]{:S(2)}) copy-start(s32[64]{0:T(128)} %param.12) | copy-start | bytes 772
  0.0 4.3 %copy-start.3 = (f32[1024]{0:T(1024)S(1)}, f32[1024]{0:T(1024)}, u32[]{:S(2)}) copy-start(f32[1024]{0:T(1024)} %param.14) | copy-start | bytes 12292
  4.3 1.0 %copy-start.1 = (bf16[240,1024]{1,0:T(8,128)(2,1)S(1)}, bf16[240,1024]{1,0:T(8,128)(2,1)}, u32[]{:S(2)}) copy-start(bf16[240,1024]{1,0:T(8,128)(2,1)} %get-tuple-element.10.w_hi_ref) | copy-start | bytes 1474564
  18.7 23.2 %copy-start.7 = (s32[16]{0:T(128)S(1)}, s32[16]{0:T(128)}, u32[]{:S(2)}) copy-start(s32[16]{0:T(128)} %constant.59.clone) | copy-start | bytes 196
  21.1 8.8 %collective-permute-start = (f32[64,194]{1,0:T(8,128)S(1)}, f32[64,194]{1,0:T(8,128)S(1)}, u32[]{:S(2)}, u32[]{:S(2)}) collective-permute-start(f32[64,194]{1,0:T(8,128)S(1)} %get-tuple-element.8), channel_id=1, source_target_pairs={{0,2},{1,3},{2,0},{3,1},{4,6},{5,7},{6,4},{7,5},{8,10},{9,11},{10,... | collective-permute-start | bytes 149000 | tf_op jit(solution)/shard_map/ppermute | solution.py:156
  24.0 10.2 %collective-permute-start.1 = (f32[64,194]{1,0:T(8,128)S(1)}, f32[64,194]{1,0:T(8,128)S(1)}, u32[]{:S(2)}, u32[]{:S(2)}) collective-permute-start(f32[64,194]{1,0:T(8,128)S(1)} %get-tuple-element.8), channel_id=1, source_target_pairs={{0,4},{1,5},{2,6},{3,7},{4,0},{5,1},{6,2},{7,3},{8,12},{9,13},{10,... | collective-permute-start | bytes 149000 | tf_op jit(solution)/shard_map/ppermute | solution.py:156
  25.6 9.2 %collective-permute-start.2 = (f32[64,194]{1,0:T(8,128)S(1)}, f32[64,194]{1,0:T(8,128)S(1)}, u32[]{:S(2)}, u32[]{:S(2)}) collective-permute-start(f32[64,194]{1,0:T(8,128)S(1)} %get-tuple-element.8), channel_id=1, source_target_pairs={{0,6},{1,7},{2,4},{3,5},{4,2},{5,3},{6,0},{7,1},{8,14},{9,15},{10,... | collective-permute-start | bytes 149000 | tf_op jit(solution)/shard_map/ppermute | solution.py:156
  25.6 9.8 %collective-permute-start.3 = (f32[64,194]{1,0:T(8,128)S(1)}, f32[64,194]{1,0:T(8,128)S(1)}, u32[]{:S(2)}, u32[]{:S(2)}) collective-permute-start(f32[64,194]{1,0:T(8,128)S(1)} %get-tuple-element.8), channel_id=1, source_target_pairs={{0,8},{1,9},{2,10},{3,11},{4,12},{5,13},{6,14},{7,15},{8,0},{9,1},... | collective-permute-start | bytes 149000 | tf_op jit(solution)/shard_map/ppermute | solution.py:156
  28.6 10.2 %collective-permute-start.4 = (f32[64,194]{1,0:T(8,128)S(1)}, f32[64,194]{1,0:T(8,128)S(1)}, u32[]{:S(2)}, u32[]{:S(2)}) collective-permute-start(f32[64,194]{1,0:T(8,128)S(1)} %get-tuple-element.8), channel_id=1, source_target_pairs={{0,10},{1,11},{2,8},{3,9},{4,14},{5,15},{6,12},{7,13},{8,2},{9,3},... | collective-permute-start | bytes 149000 | tf_op jit(solution)/shard_map/ppermute | solution.py:156
  29.9 9.5 %collective-permute-start.5 = (f32[64,194]{1,0:T(8,128)S(1)}, f32[64,194]{1,0:T(8,128)S(1)}, u32[]{:S(2)}, u32[]{:S(2)}) collective-permute-start(f32[64,194]{1,0:T(8,128)S(1)} %get-tuple-element.8), channel_id=1, source_target_pairs={{0,12},{1,13},{2,14},{3,15},{4,8},{5,9},{6,10},{7,11},{8,4},{9,5},... | collective-permute-start | bytes 149000 | tf_op jit(solution)/shard_map/ppermute | solution.py:156
  34.2 7.1 %collective-permute-start.6 = (f32[64,194]{1,0:T(8,128)S(1)}, f32[64,194]{1,0:T(8,128)S(1)}, u32[]{:S(2)}, u32[]{:S(2)}) collective-permute-start(f32[64,194]{1,0:T(8,128)S(1)} %get-tuple-element.8), channel_id=1, source_target_pairs={{0,14},{1,15},{2,12},{3,13},{4,10},{5,11},{6,8},{7,9},{8,6},{9,7},... | collective-permute-start | bytes 149000 | tf_op jit(solution)/shard_map/ppermute | solution.py:156
  41.9 2.1 %collective-permute-start.7 = (f32[8,64,194]{2,1,0:T(8,128)}, f32[8,64,194]{2,1,0:T(8,128)S(1)}, u32[]{:S(2)}, u32[]{:S(2)}) collective-permute-start(f32[8,64,194]{2,1,0:T(8,128)} %get-tuple-element.13), channel_id=1, source_target_pairs={{0,1},{1,0},{2,3},{3,2},{4,5},{5,4},{6,7},{7,6},{8,9},{9,8},{10,11... | collective-permute-start | bytes 1191944 | tf_op jit(solution)/shard_map/ppermute | solution.py:160
  49.6 2.4 %copy-start.2 = (f32[3,3]{1,0:T(4,128)S(1)}, f32[3,3]{1,0:T(4,128)}, u32[]{:S(2)}) copy-start(f32[3,3]{1,0:T(4,128)} %k_ref.1) | copy-start | bytes 112

commit v9 on v6

--- a/solution.py
+++ b/solution.py
@@ -138,22 +138,10 @@
 
 
 def gather_wide(x, group_size):
-    my_index = lax.axis_index("wide")
-    if group_size % 2 or group_size & (group_size - 1):
-        every = lax.all_gather(x, "wide", axis=0, tiled=False)
-        return every, jnp.arange(group_size, dtype=jnp.int32)
-    pattern = [0]
-    blocks = [x]
-    for flip in range(2, group_size, 2):
-        perm = [(i, i ^ flip) for i in range(group_size)]
-        blocks.append(lax.ppermute(x, "wide", perm))
-        pattern.append(flip)
-    buf = jnp.stack(blocks, axis=0)
-    perm = [(i, i ^ 1) for i in range(group_size)]
-    buf = jnp.concatenate([buf, lax.ppermute(buf, "wide", perm)], axis=0)
-    pattern = pattern + [p ^ 1 for p in pattern]
-    source = jnp.asarray(pattern, dtype=jnp.int32) ^ my_index
-    return buf, source
+    lanes = -(-x.shape[1] // 256) * 256
+    wide = jnp.pad(x, ((0, 0), (0, lanes - x.shape[1])))
+    every = lax.all_gather(wide, "wide", axis=0, tiled=False)
+    return every[:, :, : x.shape[1]], jnp.arange(group_size, dtype=jnp.int32)
 
 
 def per_device(

time: 55.2 us -> 87.1 us (1.58)
  waiting for transfers between devices: 5.85 us -> 40.7 us
  between operations: 0.24 us -> 13.6 us
  starting transfers between devices: 12.5 us -> 0.01 us
  local copies, waits for them, and re-layouts: 10.8 us -> 3.24 us
  other arithmetic: 3.53 us -> 8.31 us
  matrix products: 3.54 us -> 2.49 us
    all_gather x0 -> x1, waiting for transfers between devices: none -> 40.6 us  [gather_wide(): every = lax.all_gather(wide, 'wide', axis=0, tiled=False)]
    ppermute x8 -> x0, starting transfers between devices: 12.5 us -> none  [the longest x7 12.5 us: gather_wide(): blocks.append(lax.ppermute(x, 'wide', perm))]
    ppermute x8 -> x0, waiting for transfers between devices: 5.85 us -> none  [the longest x7 3.88 us: gather_wide(): blocks.append(lax.ppermute(x, 'wide', perm))]
    unnamed x27 -> x12, local copies, waits for them, and re-layouts: 8.12 us -> 2.76 us
    convert_element_type x1, other arithmetic: 0.04 us -> 1.61 us  [per_device(): rec_hi = (all_rec // 16).astype(jnp.bfloat16)[:, None]]
    ge x1, other arithmetic: 0.04 us -> 1.41 us  [per_device(): used = all_dest >= 0]
    slice x1 -> x0, local copies, waits for them, and re-layouts: 1.11 us -> none  [per_device(): all_rec = every[:, EMB + 1].astype(jnp.int32)]
    dot_general x1, matrix products: 1.9 us -> 0.85 us  [per_device(): col_ext = jnp.dot(selector, unit_ext, preferred_element_type=jnp.float32)]
  transfers between devices with their start and end apart: 8 -> 1, of which waited for: 3 -> 1; matrix products, arithmetic and copies ran while one was open for 7% -> 0% of each run, Pallas kernels for 0% -> 0%
where the time goes in v9:
time: 87.1 us; the launch traced here: 86.8 us
  waiting for transfers between devices  40.7 us (47%)
  Pallas kernels  18.6 us (21%)
  between operations  13.6 us (16%)
  other arithmetic  8.31 us (10%)
  local copies, waits for them, and re-layouts  3.24 us (4%)
  matrix products  2.49 us (3%)
    all_gather x1, waiting for transfers between devices, gather_wide(): every = lax.all_gather(wide, 'wide', axis=0, tiled=False)  40.6 us
    pallas_call x1, Pallas kernels, pool_slots(): pl.pallas_call(_pool_kernel, out_shape=jax.ShapeDtypeStruct((slots, 2 * C...  16.9 us
    unnamed x12, local copies, waits for them, and re-layouts  2.76 us
  transfers between devices with their start and end apart: 1, of which 1 were waited for; matrix products, arithmetic and copies ran while one was open for 0% of the time, Pallas kernels for 0%

profile of v9, /device:TPU:0, one launch (start us, length us, event | category | flops | bytes accessed | tf_op | source)
XLA Modules:
  0.0 86.8 jit_solution(7881268422093656943)
XLA Ops:
  6.5 0.0 copy-start
  6.5 0.0 copy-start.3
  6.5 0.0 all-gather.3.cloned.1.call-start
  6.5 0.8 convert_bitcast_fusion
  7.3 0.1 copy.32
  7.4 0.7 convert_bitcast_fusion.1
  8.1 0.1 copy.31
  8.2 0.7 broadcast_clamp_fusion.starts_ref
  8.8 1.4 %copy.30.frames_ref = f32[2048,80]{1,0:T(8,128)S(1)} copy(f32[2048,80]{0,1:T(8,128)} %param.8) | data formatting | bytes 1310720 | tf_op args[0]
  10.3 0.0 copy-done.3
  10.3 0.0 copy-start.2
  10.3 1.2 %copy-done.2 = f32[240,1024]{1,0:T(8,128)S(1)} copy-done((f32[240,1024]{1,0:T(8,128)S(1)}, f32[240,1024]{1,0:T(8,128)}, u32[]{:S(2)}) %copy-start.2) | copy-done | bytes 983064
  11.5 16.9 %shard_map.82 = f32[64,2048]{1,0:T(8,128)S(1)} custom-call(s32[64]{0:T(128)S(1)} %broadcast_clamp_fusion.starts_ref, f32[2048,80]{1,0:T(8,128)S(1)} %copy.30.frames_ref, f32[240,1024]{1,0:T(8,128)S(1)} %copy-done.2, f32[1,1024]{1,0:T(1,128)S(1)} %bitcast.15), custom_call_target="tpu_custom_call" | custom-call | flops 6077546496 | bytes 2162688 | tf_op jit(solution)/shard_map/pallas_call | solution.py:75
  28.4 0.0 copy-done
  28.4 1.6 %fusion.18 = f32[64,192]{1,0:T(8,128)S(1)} fusion(f32[64,2048]{1,0:T(8,128)S(1)} %shard_map.82, f32[2048,192]{0,1:T(8,128)S(1)} %copy-done), kind=kOutput, calls=%fused_computation.51 | convolution fusion | flops 301989888 | bytes 2146304 | tf_op jit(solution)/shard_map/dot_general | solution.py:153
  30.0 0.7 select_maximum_fusion
  30.8 0.0 all-gather.3.cloned.1.call-update
  30.8 0.1 iota_add_fusion
  30.9 0.1 add.72
  31.0 40.6 %all-gather.3.cloned.1.call-done = f32[1024,256]{1,0:T(8,128)} async-done(((f32[64,256]{1,0:T(8,128)}), f32[1024,256]{1,0:T(8,128)}) %all-gather.3.cloned.1.call-update) | async-done | bytes 1048592 | tf_op jit(solution)/shard_map/all_gather | solution.py:143
  71.6 0.0 copy-start.4
  71.6 1.6 %fusion.2 = (bf16[1024,1]{1,0:T(8,128)(2,1)S(1)}, pred[1024,1]{1,0:T(8,128)(4,1)S(1)}) fusion(f32[1024,194]{1,0:T(8,128)} %bitcast.16), kind=kLoop, calls=%fused_computation.13 | loop fusion | flops 17408 | bytes 7168 | tf_op jit(solution)/shard_map/convert_element_type | solution.py:188
  73.2 1.4 %compare_reduce_fusion = pred[1024]{0:T(1024)(128)(4,1)S(1)} fusion(f32[1024,194]{1,0:T(8,128)} %bitcast.17), kind=kLoop, calls=%fused_computation.24 | loop fusion | flops 2048 | bytes 5120 | tf_op jit(solution)/shard_map/ge | solution.py:172
  74.6 0.0 copy-done.4
  74.6 0.5 fusion.3
  75.2 1.0 %convert_reduce_fusion = s32[1024]{0:T(1024)S(1)} fusion(s32[1024]{0:T(1024)S(1)} %get-tuple-element.8, s32[1024]{0:T(1024)S(1)} %add.72), kind=kLoop, calls=%fused_computation | loop fusion | flops 5241856 | bytes 12288 | tf_op jit(solution)/shard_map/reduce_sum | solution.py:181
  76.2 0.2 select_reduce_fusion
  76.5 0.2 multiply_reduce_fusion
  76.7 0.2 divide_convert_fusion
  76.9 0.0 copy-start.1
  76.9 0.9 fusion
  77.9 0.1 copy.35.col_unit_ref
  78.0 0.1 pad_add_fusion
  78.1 0.1 dynamic-slice_bitcast_fusion
  78.2 0.1 copy.34.row_rec_ref
  78.3 0.0 copy-done.1
  78.3 1.6 %shard_map.83 = f32[32,512]{1,0:T(8,128)} custom-call(f32[3,3]{1,0:T(4,128)S(1)} %copy-done.1, bf16[34,192]{1,0:T(8,128)(2,1)S(1)} %fusion.14.row_unit_ref, bf16[512,192]{1,0:T(8,128)(2,1)S(1)} %copy.35.col_unit_ref, s32[34,1]{1,0:T(8,128)S(1)} %copy.34.row_rec_ref, s32[1,512]{1,0:T(1,128)S(1)} %fusion.21.col_rec_ref), custom_call_target="tpu_custom_call" | custom-call | flops 7012352 | bytes 275200 | tf_op jit(solution)/shard_map/pallas_call | solution.py:122
  (9 shorter events, 0.1 us)
Async XLA Ops:
  6.5 21.9 %copy-start = (f32[2048,192]{0,1:T(8,128)S(1)}, f32[2048,192]{0,1:T(8,128)}, u32[]{:S(2)}) copy-start(f32[2048,192]{0,1:T(8,128)} %param.14) | copy-start | bytes 4718596
  6.5 3.7 %copy-start.3 = (f32[1024]{0:T(1024)S(1)}, f32[1024]{0:T(1024)}, u32[]{:S(2)}) copy-start(f32[1024]{0:T(1024)} %param.13) | copy-start | bytes 12292
  6.5 65.0 %all-gather.3.cloned.1.call-start = ((), (), s32[]{:S(2)}) async-start(), calls=%async_computation | async-start | bytes 1114112 | tf_op jit(solution)/shard_map/all_gather | solution.py:143
  10.3 1.2 %copy-start.2 = (f32[240,1024]{1,0:T(8,128)S(1)}, f32[240,1024]{1,0:T(8,128)}, u32[]{:S(2)}) copy-start(f32[240,1024]{1,0:T(8,128)} %w_ref.1) | copy-start | bytes 2949124
  71.6 3.0 %copy-start.4 = (f32[1024,256]{1,0:T(8,128)S(1)}, f32[1024,256]{1,0:T(8,128)}, u32[]{:S(2)}) copy-start(f32[1024,256]{1,0:T(8,128)} %all-gather.3.cloned.1.call-done) | copy-start | bytes 3145732
  76.9 1.4 %copy-start.1 = (f32[3,3]{1,0:T(4,128)S(1)}, f32[3,3]{1,0:T(4,128)}, u32[]{:S(2)}) copy-start(f32[3,3]{1,0:T(4,128)} %k_ref.1) | copy-start | bytes 112
Sparse Core Ops, SparseCore 0:
  30.9 40.6 all-gather.2

commit v10 on v6

--- a/solution.py
+++ b/solution.py
@@ -22,14 +22,22 @@
 ONE_HOT_LIMIT = 1 << 20
 
 
-def _pool_kernel(starts_ref, frames_ref, w_ref, b_ref, out_ref, x3_ref, act_ref):
+def _pool_kernel(
+    starts_ref, frames_hbm, w_hbm, b_ref, out_ref, frames_ref, w_ref, x3_ref, act_ref, sem
+):
     rows = frames_ref.shape[0]
     slots = out_ref.shape[0]
+    frames_copy = pltpu.make_async_copy(frames_hbm, frames_ref, sem.at[0])
+    w_copy = pltpu.make_async_copy(w_hbm, w_ref, sem.at[1])
+    frames_copy.start()
+    w_copy.start()
+    frames_copy.wait()
     frames = frames_ref[...]
     x3_ref[...] = jnp.concatenate(
         [pltpu.roll(frames, 1, 0), frames, pltpu.roll(frames, rows - 1, 0)], axis=1
     )
     chunk = CONV_ROWS if rows % CONV_ROWS == 0 else rows
+    w_copy.wait()
 
     def conv_chunk(c, carry):
         base = pl.multiple_of(c * chunk, chunk)
@@ -77,14 +85,17 @@
         out_shape=jax.ShapeDtypeStruct((slots, 2 * CH), jnp.float32),
         in_specs=[
             pl.BlockSpec(memory_space=pltpu.MemorySpace.SMEM),
-            pl.BlockSpec(memory_space=vmem),
-            pl.BlockSpec(memory_space=vmem),
+            pl.BlockSpec(memory_space=pl.ANY),
+            pl.BlockSpec(memory_space=pl.ANY),
             pl.BlockSpec(memory_space=vmem),
         ],
         out_specs=pl.BlockSpec(memory_space=vmem),
         scratch_shapes=[
+            pltpu.VMEM((rows, FEAT), jnp.float32),
+            pltpu.VMEM((3 * FEAT, CH), jnp.float32),
             pltpu.VMEM((rows, 3 * FEAT), jnp.float32),
             pltpu.VMEM((rows, CH), jnp.float32),
+            pltpu.SemaphoreType.DMA((2,)),
         ],
         compiler_params=pltpu.CompilerParams(vmem_limit_bytes=48 * 1024 * 1024),
         cost_estimate=pl.CostEstimate(
@@ -163,23 +174,25 @@
     total_rows = SEG_DEV * group_size
     pooled = pool_slots(frames, seg_start, conv_weight, conv_bias)
     embedded = jnp.dot(pooled, proj_weight, precision=PRECISE, preferred_element_type=jnp.float32)
-    packed = jnp.concatenate(
-        [
-            embedded,
-            seg_dest.astype(jnp.float32)[:, None],
-            rec_id.astype(jnp.float32)[:, None],
-        ],
-        axis=1,
-    )
+    slots = embedded.shape[0]
+    meta = jnp.concatenate(
+        [seg_dest.astype(jnp.float32), rec_id.astype(jnp.float32)]
+    )
+    if meta.shape[0] <= EMB:
+        meta_rows = jnp.zeros((8, EMB), jnp.float32).at[0, : meta.shape[0]].set(meta)
+    else:
+        meta_rows = jnp.zeros((-(-meta.shape[0] // EMB) // 8 * 8 + 8, EMB), jnp.float32)
+        meta_rows = meta_rows.reshape(-1).at[: meta.shape[0]].set(meta).reshape(-1, EMB)
+    packed = jnp.concatenate([embedded, meta_rows], axis=0)
     blocks, source = gather_wide(packed, group_size)
-    per_block = packed.shape[0]
-    every = blocks.reshape(group_size * per_block, packed.shape[1])
+    per_block = slots
+    all_emb = blocks[:, :slots, :].reshape(group_size * slots, EMB)
+    meta_all = blocks[:, slots:, :].reshape(group_size, -1)[:, : 2 * slots]
+    all_dest = meta_all[:, :slots].reshape(-1).astype(jnp.int32)
+    all_rec = meta_all[:, slots:].reshape(-1).astype(jnp.int32)
     slot_ids = (
         source[:, None] * per_block + jnp.arange(per_block, dtype=jnp.int32)[None, :]
     ).reshape(-1)
-    all_emb = every[:, :EMB]
-    all_dest = every[:, EMB].astype(jnp.int32)
-    all_rec = every[:, EMB + 1].astype(jnp.int32)
     slot_total = all_dest.shape[0]
     used = all_dest >= 0
 

time: 55.2 us -> 53.6 us (0.971)
  local copies, waits for them, and re-layouts: 10.8 us -> 8.55 us
  other arithmetic: 3.53 us -> 4.81 us
  matrix products: 3.54 us -> 2.49 us
    unnamed x27 -> x28, local copies, waits for them, and re-layouts: 8.12 us -> 6.87 us
    convert_element_type x1, other arithmetic: 0.04 us -> 1.24 us  [per_device(): rec_hi = (all_rec // 16).astype(jnp.bfloat16)[:, None]]
    slice x1, local copies, waits for them, and re-layouts: 1.11 us -> 0.01 us  [per_device(): meta_all = blocks[:, slots:, :].reshape(group_size, -1)[:, :2 * slots]]
    dot_general x1, matrix products: 1.9 us -> 0.85 us  [per_device(): col_ext = jnp.dot(selector, unit_ext, preferred_element_type=jnp.float32)]
    reduce_sum x1, other arithmetic: 0.21 us -> 1.09 us  [per_device(): jnp.sum(centred * centred, axis=1, keepdims=True) + 1e-06]
    convert_element_type x1, other arithmetic: 1.01 us -> 0.21 us  [per_device(): (centred / jnp.sqrt(jnp.sum(centred * centred, axis=1, keepdims=True) + 1...]
  transfers between devices with their start and end apart: 8 -> 8, of which waited for: 3 -> 3; matrix products, arithmetic and copies ran while one was open for 7% -> 9% of each run, Pallas kernels for 0% -> 0%
where the time goes in v10:
time: 53.6 us; the launch traced here: 53.4 us
  Pallas kernels  18.8 us (35%)
  starting transfers between devices  12.5 us (23%)
  local copies, waits for them, and re-layouts  8.55 us (16%)
  waiting for transfers between devices  6.02 us (11%)
  other arithmetic  4.81 us (9%)
  matrix products  2.49 us (5%)
    pallas_call x1, Pallas kernels, pool_slots(): pl.pallas_call(_pool_kernel, out_shape=jax.ShapeDtypeStruct((slots, 2 * C...  17.2 us
    ppermute x7, starting transfers between devices, gather_wide(): blocks.append(lax.ppermute(x, 'wide', perm))  12.5 us
    unnamed x28, local copies, waits for them, and re-layouts  6.87 us
    ppermute x7, waiting for transfers between devices, gather_wide(): blocks.append(lax.ppermute(x, 'wide', perm))  3.96 us
    ppermute x1, waiting for transfers between devices, gather_wide(): buf = jnp.concatenate([buf, lax.ppermute(buf, 'wide', perm)], axis=0)  2.06 us
    pallas_call x1, Pallas kernels, smooth_affinity(): pl.pallas_call(_affinity_kernel, out_shape=jax.ShapeDtypeStruct((height,...  1.65 us
    dot_general x1, matrix products, per_device(): jnp.dot(pooled, proj_weight, precision=PRECISE, preferred_element_type=jn...  1.64 us
    convert_element_type x1, other arithmetic, per_device(): rec_hi = (all_rec // 16).astype(jnp.bfloat16)[:, None]  1.24 us
  transfers between devices with their start and end apart: 8, of which 3 were waited for; matrix products, arithmetic and copies ran while one was open for 9% of the time, Pallas kernels for 0%

profile of v10, /device:TPU:0, one launch (start us, length us, event | category | flops | bytes accessed | tf_op | source)
XLA Modules:
  0.0 53.4 jit_solution(7339002249574025340)
XLA Ops:
  0.0 0.0 copy-start
  0.0 0.0 copy-start.6
  0.0 0.0 copy-start.7
  0.0 0.0 copy-start.8
  0.0 0.0 copy-start.3
  0.0 1.5 %copy.24.frames_hbm = f32[2048,80]{1,0:T(8,128)S(1)} copy(f32[2048,80]{0,1:T(8,128)} %param.11) | data formatting | bytes 1310720 | tf_op args[0]
  1.6 0.0 copy-done.6
  1.6 0.0 copy-done.7
  1.6 0.0 copy-done.8
  1.6 0.0 copy-done.3
  1.6 0.0 copy-start.2
  1.6 1.2 %copy-done.2 = f32[240,1024]{1,0:T(8,128)S(1)} copy-done((f32[240,1024]{1,0:T(8,128)S(1)}, f32[240,1024]{1,0:T(8,128)}, u32[]{:S(2)}) %copy-start.2) | copy-done | bytes 983064
  2.8 17.2 %shard_map.91 = f32[64,2048]{1,0:T(8,128)S(1)} custom-call(s32[64]{0:T(128)S(1)} %broadcast_clamp_fusion.starts_ref, f32[2048,80]{1,0:T(8,128)S(1)} %copy.24.frames_hbm, f32[240,1024]{1,0:T(8,128)S(1)} %copy-done.2, f32[1,1024]{1,0:T(1,128)S(1)} %bitcast.40), custom_call_target="tpu_custom_call" | custom-call | flops 6077546496 | bytes 2162688 | tf_op jit(solution)/shard_map/pallas_call | solution.py:83
  20.0 0.0 copy-done
  20.0 1.6 %fusion.17 = f32[64,192]{1,0:T(8,128)S(1)} fusion(f32[64,2048]{1,0:T(8,128)S(1)} %shard_map.91, f32[2048,192]{0,1:T(8,128)S(1)} %copy-done), kind=kOutput, calls=%fused_computation.65 | convolution fusion | flops 301989888 | bytes 2146304 | tf_op jit(solution)/shard_map/dot_general | solution.py:176
  21.7 0.0 copy-start.9
  21.7 0.1 maximum_bitcast_fusion
  21.8 3.0 %collective-permute-start = (f32[72,192]{1,0:T(8,128)S(1)}, f32[72,192]{1,0:T(8,128)S(1)}, u32[]{:S(2)}, u32[]{:S(2)}) collective-permute-start(f32[72,192]{1,0:T(8,128)S(1)} %select_maximum_fusion), channel_id=1, source_target_pairs={{0,2},{1,3},{2,0},{3,1},{4,6},{5,7},{6,4},{7,5},{8,10},{9,11},{10,... | collective-permute-start | bytes 165896 | tf_op jit(solution)/shard_map/ppermute | solution.py:160
  24.8 1.6 %collective-permute-start.1 = (f32[72,192]{1,0:T(8,128)S(1)}, f32[72,192]{1,0:T(8,128)S(1)}, u32[]{:S(2)}, u32[]{:S(2)}) collective-permute-start(f32[72,192]{1,0:T(8,128)S(1)} %select_maximum_fusion), channel_id=1, source_target_pairs={{0,4},{1,5},{2,6},{3,7},{4,0},{5,1},{6,2},{7,3},{8,12},{9,13},{10,... | collective-permute-start | bytes 165896 | tf_op jit(solution)/shard_map/ppermute | solution.py:160
  26.4 0.0 collective-permute-start.2
  26.4 3.0 %collective-permute-start.3 = (f32[72,192]{1,0:T(8,128)S(1)}, f32[72,192]{1,0:T(8,128)S(1)}, u32[]{:S(2)}, u32[]{:S(2)}) collective-permute-start(f32[72,192]{1,0:T(8,128)S(1)} %select_maximum_fusion), channel_id=1, source_target_pairs={{0,8},{1,9},{2,10},{3,11},{4,12},{5,13},{6,14},{7,15},{8,0},{9,1},... | collective-permute-start | bytes 165896 | tf_op jit(solution)/shard_map/ppermute | solution.py:160
  29.4 1.3 %collective-permute-start.4 = (f32[72,192]{1,0:T(8,128)S(1)}, f32[72,192]{1,0:T(8,128)S(1)}, u32[]{:S(2)}, u32[]{:S(2)}) collective-permute-start(f32[72,192]{1,0:T(8,128)S(1)} %select_maximum_fusion), channel_id=1, source_target_pairs={{0,10},{1,11},{2,8},{3,9},{4,14},{5,15},{6,12},{7,13},{8,2},{9,3},... | collective-permute-start | bytes 165896 | tf_op jit(solution)/shard_map/ppermute | solution.py:160
  30.6 0.6 %bitcast_dynamic-update-slice_fusion.15 = (f32[8,72,192]{2,1,0:T(8,128)}, f32[16,72,192]{2,1,0:T(8,128)S(1)}) fusion(f32[1,128]{1,0:T(1,128)S(1)} %maximum_bitcast_fusion, f32[64,192]{1,0:T(8,128)S(1)} %fusion.17), kind=kLoop, calls=%fused_computation.45 | loop fusion | flops 41470 | bytes 197120
  31.3 0.0 collective-permute-done
  31.3 3.6 %collective-permute-start.5 = (f32[72,192]{1,0:T(8,128)S(1)}, f32[72,192]{1,0:T(8,128)S(1)}, u32[]{:S(2)}, u32[]{:S(2)}) collective-permute-start(f32[72,192]{1,0:T(8,128)S(1)} %select_maximum_fusion), channel_id=1, source_target_pairs={{0,12},{1,13},{2,14},{3,15},{4,8},{5,9},{6,10},{7,11},{8,4},{9,5},... | collective-permute-start | bytes 165896 | tf_op jit(solution)/shard_map/ppermute | solution.py:160
  34.9 0.6 %bitcast_dynamic-update-slice_fusion.13 = (f32[8,72,192]{2,1,0:T(8,128)}, f32[16,72,192]{2,1,0:T(8,128)S(1)}) fusion(f32[8,72,192]{2,1,0:T(8,128)} %get-tuple-element.37, f32[72,192]{1,0:T(8,128)S(1)} %collective-permute-done, f32[16,72,192]{2,1,0:T(8,128)S(1)} %get-tuple-element.38), kind=kLoop, calls=%fused_computation.43 | loop fusion | bytes 221184
  35.5 0.0 collective-permute-done.1
  35.5 0.0 collective-permute-start.6
  35.5 0.6 %bitcast_dynamic-update-slice_fusion.11 = (f32[8,72,192]{2,1,0:T(8,128)}, f32[16,72,192]{2,1,0:T(8,128)S(1)}) fusion(f32[8,72,192]{2,1,0:T(8,128)} %get-tuple-element.35, f32[72,192]{1,0:T(8,128)S(1)} %collective-permute-done.1, f32[16,72,192]{2,1,0:T(8,128)S(1)} %get-tuple-element.36), kind=kLoop, calls=%fused_computation.41 | loop fusion | bytes 221184
  36.2 0.0 collective-permute-done.2
  36.2 0.6 %bitcast_dynamic-update-slice_fusion.9 = (f32[8,72,192]{2,1,0:T(8,128)}, f32[16,72,192]{2,1,0:T(8,128)S(1)}) fusion(f32[8,72,192]{2,1,0:T(8,128)} %get-tuple-element.33, f32[72,192]{1,0:T(8,128)S(1)} %collective-permute-done.2, f32[16,72,192]{2,1,0:T(8,128)S(1)} %get-tuple-element.34), kind=kLoop, calls=%fused_computation.39 | loop fusion | bytes 221184
  36.8 0.0 collective-permute-done.3
  36.8 0.6 %bitcast_dynamic-update-slice_fusion.7 = (f32[8,72,192]{2,1,0:T(8,128)}, f32[16,72,192]{2,1,0:T(8,128)S(1)}) fusion(f32[8,72,192]{2,1,0:T(8,128)} %get-tuple-element.31, f32[72,192]{1,0:T(8,128)S(1)} %collective-permute-done.3, f32[16,72,192]{2,1,0:T(8,128)S(1)} %get-tuple-element.32), kind=kLoop, calls=%fused_computation.37 | loop fusion | bytes 221184
  37.4 3.2 %collective-permute-done.4 = f32[72,192]{1,0:T(8,128)S(1)} collective-permute-done((f32[72,192]{1,0:T(8,128)S(1)}, f32[72,192]{1,0:T(8,128)S(1)}, u32[]{:S(2)}, u32[]{:S(2)}) %collective-permute-start.4) | collective-permute-done | bytes 55328 | tf_op jit(solution)/shard_map/ppermute | solution.py:160
  40.6 0.6 %bitcast_dynamic-update-slice_fusion.5 = (f32[8,72,192]{2,1,0:T(8,128)}, f32[16,72,192]{2,1,0:T(8,128)S(1)}) fusion(f32[8,72,192]{2,1,0:T(8,128)} %get-tuple-element.29, f32[72,192]{1,0:T(8,128)S(1)} %collective-permute-done.4, f32[16,72,192]{2,1,0:T(8,128)S(1)} %get-tuple-element.30), kind=kLoop, calls=%fused_computation.35 | loop fusion | bytes 221184
  41.2 0.0 collective-permute-done.5
  41.3 0.6 %bitcast_dynamic-update-slice_fusion.3 = (f32[8,72,192]{2,1,0:T(8,128)}, f32[16,72,192]{2,1,0:T(8,128)S(1)}) fusion(f32[8,72,192]{2,1,0:T(8,128)} %get-tuple-element.27, f32[72,192]{1,0:T(8,128)S(1)} %collective-permute-done.5, f32[16,72,192]{2,1,0:T(8,128)S(1)} %get-tuple-element.28), kind=kLoop, calls=%fused_computation.33 | loop fusion | bytes 221184
  41.9 0.8 %collective-permute-done.6 = f32[72,192]{1,0:T(8,128)S(1)} collective-permute-done((f32[72,192]{1,0:T(8,128)S(1)}, f32[72,192]{1,0:T(8,128)S(1)}, u32[]{:S(2)}, u32[]{:S(2)}) %collective-permute-start.6) | collective-permute-done | bytes 55328 | tf_op jit(solution)/shard_map/ppermute | solution.py:160
  42.7 0.6 %bitcast_dynamic-update-slice_fusion.1 = (f32[8,72,192]{2,1,0:T(8,128)}, f32[16,72,192]{2,1,0:T(8,128)S(1)}) fusion(f32[8,72,192]{2,1,0:T(8,128)} %get-tuple-element.25, f32[72,192]{1,0:T(8,128)S(1)} %collective-permute-done.6, f32[16,72,192]{2,1,0:T(8,128)S(1)} %get-tuple-element.26), kind=kLoop, calls=%fused_computation.31 | loop fusion | bytes 221184 | tf_op jit(solution)/shard_map/stack | solution.py:162
  43.3 0.0 collective-permute-start.7
  43.3 0.0 copy-done.9
  43.3 0.1 iota_add_fusion
  43.4 0.1 add.87
  43.5 2.1 %collective-permute-done.7 = f32[8,72,192]{2,1,0:T(8,128)S(1)} collective-permute-done((f32[8,72,192]{2,1,0:T(8,128)}, f32[8,72,192]{2,1,0:T(8,128)S(1)}, u32[]{:S(2)}, u32[]{:S(2)}) %collective-permute-start.7) | collective-permute-done | bytes 442400 | tf_op jit(solution)/shard_map/ppermute | solution.py:164
  45.6 0.1 reshape.241
  45.7 0.1 slice_convert_fusion.1
  45.8 0.2 select_reduce_fusion
  46.0 1.1 %multiply_reduce_fusion = (f32[16,64]{1,0:T(8,128)S(1)}, f32[16,64,192]{2,1,0:T(8,128)}) fusion(f32[192]{0:T(256)S(1)} %broadcast_multiply_fusion, f32[16,72,192]{2,1,0:T(8,128)S(1)} %constant_dynamic-update-slice_fusion), kind=kLoop, calls=%fused_computation.6 | loop fusion | flops 588800 | bytes 1577728 | tf_op jit(solution)/shard_map/reduce_sum | solution.py:201
  47.1 0.1 sqrt.12
  47.2 0.5 convert_element_type.100
  47.6 1.2 %fusion.4 = (bf16[1024,1]{1,0:T(8,128)(2,1)S(1)}, bf16[1024,1]{1,0:T(8,128)(2,1)}) fusion(s32[1024,1]{1,0:T(8,128)S(1)} %convert_element_type.100), kind=kLoop, calls=%fused_computation.14 | loop fusion | flops 21504 | bytes 8192 | tf_op jit(solution)/shard_map/convert_element_type | solution.py:213
  48.9 0.1 convert_element_type.90
  49.0 1.0 %convert_reduce_fusion = s32[1024]{0:T(1024)S(1)} fusion(s32[1024]{0:T(1024)S(1)} %convert_element_type.90, s32[1024]{0:T(1024)S(1)} %add.87), kind=kLoop, calls=%fused_computation | loop fusion | flops 5241856 | bytes 12288 | tf_op jit(solution)/shard_map/reduce_sum | solution.py:206
  50.0 0.0 copy-done.4
  50.0 0.2 fusion.2
  50.2 0.0 copy-done.5
  50.2 0.9 %fusion = f32[512,194]{0,1:T(8,128)S(1)} fusion(s32[1024]{0:T(1024)S(1)} %add_select_fusion.2, bf16[1024,1]{1,0:T(8,128)(2,1)S(1)} %copy-done.5, bf16[1024,1]{1,0:T(8,128)(2,1)S(1)} %get-tuple-element.19, bf16[1024,192]{1,0:T(8,128)(2,1)S(1)} %fusion.2), kind=kOutput, calls=%fused_computation.2 | convolution fusion | flops 205139968 | bytes 798720 | tf_op jit(solution)/shard_map/dot_general | solution.py:217
  51.1 0.0 copy-start.1
  51.2 0.1 copy.31.col_unit_ref
  51.3 0.1 pad_add_fusion
  51.4 0.1 dynamic-slice_bitcast_fusion
  51.5 0.1 copy.30.row_rec_ref
  51.6 0.2 copy-done.1
  51.8 1.6 %shard_map.92 = f32[32,512]{1,0:T(8,128)} custom-call(f32[3,3]{1,0:T(4,128)S(1)} %copy-done.1, bf16[34,192]{1,0:T(8,128)(2,1)S(1)} %fusion.14.row_unit_ref, bf16[512,192]{1,0:T(8,128)(2,1)S(1)} %copy.31.col_unit_ref, s32[34,1]{1,0:T(8,128)S(1)} %copy.30.row_rec_ref, s32[1,512]{1,0:T(1,128)S(1)} %fusion.20.col_rec_ref), custom_call_target="tpu_custom_call" | custom-call | flops 7012352 | bytes 275200 | tf_op jit(solution)/shard_map/pallas_call | solution.py:133
  (18 shorter events, 0.2 us)
Async XLA Ops:
  0.0 20.0 %copy-start = (f32[2048,192]{0,1:T(8,128)S(1)}, f32[2048,192]{0,1:T(8,128)}, u32[]{:S(2)}) copy-start(f32[2048,192]{0,1:T(8,128)} %param.17) | copy-start | bytes 4718596
  0.0 1.6 %copy-start.6 = (s32[64]{0:T(128)S(1)}, s32[64]{0:T(128)}, u32[]{:S(2)}) copy-start(s32[64]{0:T(128)} %param.12) | copy-start | bytes 772
  0.0 1.6 %copy-start.7 = (s32[64]{0:T(128)S(1)}, s32[64]{0:T(128)}, u32[]{:S(2)}) copy-start(s32[64]{0:T(128)} %param.13) | copy-start | bytes 772
  0.0 1.6 %copy-start.8 = (s32[64]{0:T(128)S(1)}, s32[64]{0:T(128)}, u32[]{:S(2)}) copy-start(s32[64]{0:T(128)} %param.14) | copy-start | bytes 772
  0.0 1.6 %copy-start.3 = (f32[1024]{0:T(1024)S(1)}, f32[1024]{0:T(1024)}, u32[]{:S(2)}) copy-start(f32[1024]{0:T(1024)} %param.16) | copy-start | bytes 12292
  1.6 1.2 %copy-start.2 = (f32[240,1024]{1,0:T(8,128)S(1)}, f32[240,1024]{1,0:T(8,128)}, u32[]{:S(2)}) copy-start(f32[240,1024]{1,0:T(8,128)} %w_hbm.1) | copy-start | bytes 2949124
  21.7 21.6 %copy-start.9 = (s32[16]{0:T(128)S(1)}, s32[16]{0:T(128)}, u32[]{:S(2)}) copy-start(s32[16]{0:T(128)} %constant.85.clone) | copy-start | bytes 196
  21.8 9.5 %collective-permute-start = (f32[72,192]{1,0:T(8,128)S(1)}, f32[72,192]{1,0:T(8,128)S(1)}, u32[]{:S(2)}, u32[]{:S(2)}) collective-permute-start(f32[72,192]{1,0:T(8,128)S(1)} %select_maximum_fusion), channel_id=1, source_target_pairs={{0,2},{1,3},{2,0},{3,1},{4,6},{5,7},{6,4},{7,5},{8,10},{9,11},{10,... | collective-permute-start | bytes 165896 | tf_op jit(solution)/shard_map/ppermute | solution.py:160
  24.8 10.7 %collective-permute-start.1 = (f32[72,192]{1,0:T(8,128)S(1)}, f32[72,192]{1,0:T(8,128)S(1)}, u32[]{:S(2)}, u32[]{:S(2)}) collective-permute-start(f32[72,192]{1,0:T(8,128)S(1)} %select_maximum_fusion), channel_id=1, source_target_pairs={{0,4},{1,5},{2,6},{3,7},{4,0},{5,1},{6,2},{7,3},{8,12},{9,13},{10,... | collective-permute-start | bytes 165896 | tf_op jit(solution)/shard_map/ppermute | solution.py:160
  26.4 9.8 %collective-permute-start.2 = (f32[72,192]{1,0:T(8,128)S(1)}, f32[72,192]{1,0:T(8,128)S(1)}, u32[]{:S(2)}, u32[]{:S(2)}) collective-permute-start(f32[72,192]{1,0:T(8,128)S(1)} %select_maximum_fusion), channel_id=1, source_target_pairs={{0,6},{1,7},{2,4},{3,5},{4,2},{5,3},{6,0},{7,1},{8,14},{9,15},{10,... | collective-permute-start | bytes 165896 | tf_op jit(solution)/shard_map/ppermute | solution.py:160
  26.4 10.4 %collective-permute-start.3 = (f32[72,192]{1,0:T(8,128)S(1)}, f32[72,192]{1,0:T(8,128)S(1)}, u32[]{:S(2)}, u32[]{:S(2)}) collective-permute-start(f32[72,192]{1,0:T(8,128)S(1)} %select_maximum_fusion), channel_id=1, source_target_pairs={{0,8},{1,9},{2,10},{3,11},{4,12},{5,13},{6,14},{7,15},{8,0},{9,1},... | collective-permute-start | bytes 165896 | tf_op jit(solution)/shard_map/ppermute | solution.py:160
  29.4 11.3 %collective-permute-start.4 = (f32[72,192]{1,0:T(8,128)S(1)}, f32[72,192]{1,0:T(8,128)S(1)}, u32[]{:S(2)}, u32[]{:S(2)}) collective-permute-start(f32[72,192]{1,0:T(8,128)S(1)} %select_maximum_fusion), channel_id=1, source_target_pairs={{0,10},{1,11},{2,8},{3,9},{4,14},{5,15},{6,12},{7,13},{8,2},{9,3},... | collective-permute-start | bytes 165896 | tf_op jit(solution)/shard_map/ppermute | solution.py:160
  31.3 10.0 %collective-permute-start.5 = (f32[72,192]{1,0:T(8,128)S(1)}, f32[72,192]{1,0:T(8,128)S(1)}, u32[]{:S(2)}, u32[]{:S(2)}) collective-permute-start(f32[72,192]{1,0:T(8,128)S(1)} %select_maximum_fusion), channel_id=1, source_target_pairs={{0,12},{1,13},{2,14},{3,15},{4,8},{5,9},{6,10},{7,11},{8,4},{9,5},... | collective-permute-start | bytes 165896 | tf_op jit(solution)/shard_map/ppermute | solution.py:160
  35.5 7.2 %collective-permute-start.6 = (f32[72,192]{1,0:T(8,128)S(1)}, f32[72,192]{1,0:T(8,128)S(1)}, u32[]{:S(2)}, u32[]{:S(2)}) collective-permute-start(f32[72,192]{1,0:T(8,128)S(1)} %select_maximum_fusion), channel_id=1, source_target_pairs={{0,14},{1,15},{2,12},{3,13},{4,10},{5,11},{6,8},{7,9},{8,6},{9,7},... | collective-permute-start | bytes 165896 | tf_op jit(solution)/shard_map/ppermute | solution.py:160
  43.3 2.2 %collective-permute-start.7 = (f32[8,72,192]{2,1,0:T(8,128)}, f32[8,72,192]{2,1,0:T(8,128)S(1)}, u32[]{:S(2)}, u32[]{:S(2)}) collective-permute-start(f32[8,72,192]{2,1,0:T(8,128)} %get-tuple-element.23), channel_id=1, source_target_pairs={{0,1},{1,0},{2,3},{3,2},{4,5},{5,4},{6,7},{7,6},{8,9},{9,8},{10,11... | collective-permute-start | bytes 1327112 | tf_op jit(solution)/shard_map/ppermute | solution.py:164
  47.1 2.9 %copy-start.4 = (f32[16,64,192]{2,1,0:T(8,128)S(1)}, f32[16,64,192]{2,1,0:T(8,128)}, u32[]{:S(2)}) copy-start(f32[16,64,192]{2,1,0:T(8,128)} %get-tuple-element.18) | copy-start | bytes 2359300
  48.9 1.3 %copy-start.5 = (bf16[1024,1]{1,0:T(8,128)(2,1)S(1)}, bf16[1024,1]{1,0:T(8,128)(2,1)}, u32[]{:S(2)}) copy-start(bf16[1024,1]{1,0:T(8,128)(2,1)} %get-tuple-element.20) | copy-start | bytes 6148
  51.1 0.7 %copy-start.1 = (f32[3,3]{1,0:T(4,128)S(1)}, f32[3,3]{1,0:T(4,128)}, u32[]{:S(2)}) copy-start(f32[3,3]{1,0:T(4,128)} %k_ref.1) | copy-start | bytes 112

commit v11 on v10

--- a/solution.py
+++ b/solution.py
@@ -20,19 +20,20 @@
 WIN = SEGLEN + 8
 CONV_ROWS = 256
 ONE_HOT_LIMIT = 1 << 20
+VMEM_ALL = 67043328
 
 
 def _pool_kernel(
     starts_ref, frames_hbm, w_hbm, b_ref, out_ref, frames_ref, w_ref, x3_ref, act_ref, sem
 ):
-    rows = frames_ref.shape[0]
+    rows = frames_ref.shape[1]
     slots = out_ref.shape[0]
     frames_copy = pltpu.make_async_copy(frames_hbm, frames_ref, sem.at[0])
     w_copy = pltpu.make_async_copy(w_hbm, w_ref, sem.at[1])
     frames_copy.start()
     w_copy.start()
     frames_copy.wait()
-    frames = frames_ref[...]
+    frames = jnp.transpose(frames_ref[...])
     x3_ref[...] = jnp.concatenate(
         [pltpu.roll(frames, 1, 0), frames, pltpu.roll(frames, rows - 1, 0)], axis=1
     )
@@ -91,19 +92,19 @@
         ],
         out_specs=pl.BlockSpec(memory_space=vmem),
         scratch_shapes=[
-            pltpu.VMEM((rows, FEAT), jnp.float32),
+            pltpu.VMEM((FEAT, rows), jnp.float32),
             pltpu.VMEM((3 * FEAT, CH), jnp.float32),
             pltpu.VMEM((rows, 3 * FEAT), jnp.float32),
             pltpu.VMEM((rows, CH), jnp.float32),
             pltpu.SemaphoreType.DMA((2,)),
         ],
-        compiler_params=pltpu.CompilerParams(vmem_limit_bytes=48 * 1024 * 1024),
+        compiler_params=pltpu.CompilerParams(vmem_limit_bytes=VMEM_ALL),
         cost_estimate=pl.CostEstimate(
             flops=2 * rows * 3 * FEAT * CH * 6 + 8 * slots * WIN * CH,
             transcendentals=slots * CH,
             bytes_accessed=rows * FEAT * 4 + 3 * FEAT * CH * 4 + slots * 2 * CH * 4,
         ),
-    )(starts, frames, conv_weight, conv_bias.reshape(1, CH))
+    )(starts, frames.T, conv_weight, conv_bias.reshape(1, CH))
 
 
 def _affinity_kernel(k_ref, row_unit_ref, col_unit_ref, row_rec_ref, col_rec_ref, out_ref, pad_ref):

time: 53.6 us -> 54.6 us (1.019)
  local copies, waits for them, and re-layouts: 8.55 us -> 1.43 us
  waiting for transfers between devices: 6.02 us -> 8.85 us
  Pallas kernels: 18.8 us -> 20.8 us
  matrix products: 2.49 us -> 4.07 us
  other arithmetic: 4.81 us -> 6.15 us
    unnamed x28 -> x15, local copies, waits for them, and re-layouts: 6.87 us -> 0.39 us
    ppermute x7, waiting for transfers between devices: 3.96 us -> 7.02 us  [gather_wide(): blocks.append(lax.ppermute(x, 'wide', perm))]
    pallas_call x1, Pallas kernels: 17.2 us -> 19.1 us  [pool_slots(): pl.pallas_call(_pool_kernel, out_shape=jax.ShapeDtypeStruct((slots, 2 * C...]
    dot_general x1, matrix products: 1.64 us -> 3.22 us  [per_device(): jnp.dot(pooled, proj_weight, precision=PRECISE, preferred_element_type=jn...]
    min x1, other arithmetic: 0.01 us -> 1.23 us  [pool_slots(): starts = jnp.clip(seg_start, 0, rows - SEGLEN).astype(jnp.int32)]
    convert_element_type x1, other arithmetic: 0.01 us -> 1.17 us  [per_device(): rec_id.astype(jnp.float32)]
    convert_element_type x1, other arithmetic: 0.01 us -> 1.14 us  [per_device(): seg_dest.astype(jnp.float32)]
    reduce_sum x1, other arithmetic: 1.09 us -> 0.23 us  [per_device(): jnp.sum(centred * centred, axis=1, keepdims=True) + 1e-06]
  transfers between devices with their start and end apart: 8 -> 8, of which waited for: 3 -> 3; matrix products, arithmetic and copies ran while one was open for 9% -> 0% of each run, Pallas kernels for 0% -> 0%
where the time goes in v11:
time: 54.6 us; the launch traced here: 54.2 us
  Pallas kernels  20.8 us (38%)
  starting transfers between devices  12.7 us (23%)
  waiting for transfers between devices  8.85 us (16%)
  other arithmetic  6.15 us (11%)
  matrix products  4.07 us (7%)
  local copies, waits for them, and re-layouts  1.43 us (3%)
    pallas_call x1, Pallas kernels, pool_slots(): pl.pallas_call(_pool_kernel, out_shape=jax.ShapeDtypeStruct((slots, 2 * C...  19.1 us
    ppermute x7, starting transfers between devices, gather_wide(): blocks.append(lax.ppermute(x, 'wide', perm))  12.6 us
    ppermute x7, waiting for transfers between devices, gather_wide(): blocks.append(lax.ppermute(x, 'wide', perm))  7.02 us
    dot_general x1, matrix products, per_device(): jnp.dot(pooled, proj_weight, precision=PRECISE, preferred_element_type=jn...  3.22 us
    ppermute x1, waiting for transfers between devices, gather_wide(): buf = jnp.concatenate([buf, lax.ppermute(buf, 'wide', perm)], axis=0)  1.82 us
    pallas_call x1, Pallas kernels, smooth_affinity(): pl.pallas_call(_affinity_kernel, out_shape=jax.ShapeDtypeStruct((height,...  1.65 us
    min x1, other arithmetic, pool_slots(): starts = jnp.clip(seg_start, 0, rows - SEGLEN).astype(jnp.int32)  1.23 us
    convert_element_type x1, other arithmetic, per_device(): rec_id.astype(jnp.float32)  1.17 us
  transfers between devices with their start and end apart: 8, of which 3 were waited for; matrix products, arithmetic and copies ran while one was open for 0% of the time, Pallas kernels for 0%

profile of v11, /device:TPU:0, one launch (start us, length us, event | category | flops | bytes accessed | tf_op | source)
XLA Modules:
  0.0 54.2 jit_solution(14163150394357252692)
XLA Ops:
  0.0 1.2 %broadcast_clamp_fusion.starts_ref = s32[64]{0:T(128)} fusion(s32[64]{0:T(128)} %param.12), kind=kLoop, calls=%fused_computation.63 | loop fusion | flops 64 | bytes 512 | tf_op jit(solution)/shard_map/jit(clip)/min | solution.py:82
  1.2 1.1 %convert_element_type.87 = f32[64]{0:T(128)} convert(s32[64]{0:T(128)} %param.13) | non-fusion elementwise | flops 64 | bytes 512 | tf_op jit(solution)/shard_map/convert_element_type | solution.py:180
  2.4 1.2 %convert_element_type.88 = f32[64]{0:T(128)} convert(s32[64]{0:T(128)} %param.14) | non-fusion elementwise | flops 64 | bytes 512 | tf_op jit(solution)/shard_map/convert_element_type | solution.py:180
  3.5 19.1 %shard_map.91 = f32[64,2048]{1,0:T(8,128)} custom-call(s32[64]{0:T(128)} %broadcast_clamp_fusion.starts_ref, f32[80,2048]{1,0:T(8,128)} %bitcast.42, f32[240,1024]{1,0:T(8,128)} %w_hbm.1, f32[1,1024]{1,0:T(1,128)} %bitcast.43), custom_call_target="tpu_custom_call" | custom-call | flops 6077546496 | bytes 2162688 | tf_op jit(solution)/shard_map/pallas_call | solution.py:84
  22.7 0.0 copy-start.2
  22.7 0.0 copy-start.3
  22.7 3.2 %fusion.17 = f32[64,192]{1,0:T(8,128)S(1)} fusion(f32[64,2048]{1,0:T(8,128)} %shard_map.91, f32[2048,192]{0,1:T(8,128)} %param.17), kind=kOutput, calls=%fused_computation.65 | convolution fusion | flops 301989888 | bytes 2146304 | tf_op jit(solution)/shard_map/dot_general | solution.py:177
  25.9 0.0 copy-done.2
  25.9 0.0 copy-done.3
  25.9 0.0 copy-start.1
  25.9 0.1 maximum_bitcast_fusion
  26.0 3.0 %collective-permute-start = (f32[72,192]{1,0:T(8,128)S(1)}, f32[72,192]{1,0:T(8,128)S(1)}, u32[]{:S(2)}, u32[]{:S(2)}) collective-permute-start(f32[72,192]{1,0:T(8,128)S(1)} %select_maximum_fusion), channel_id=1, source_target_pairs={{0,2},{1,3},{2,0},{3,1},{4,6},{5,7},{6,4},{7,5},{8,10},{9,11},{10,... | collective-permute-start | bytes 165896 | tf_op jit(solution)/shard_map/ppermute | solution.py:161
  29.0 1.6 %collective-permute-start.1 = (f32[72,192]{1,0:T(8,128)S(1)}, f32[72,192]{1,0:T(8,128)S(1)}, u32[]{:S(2)}, u32[]{:S(2)}) collective-permute-start(f32[72,192]{1,0:T(8,128)S(1)} %select_maximum_fusion), channel_id=1, source_target_pairs={{0,4},{1,5},{2,6},{3,7},{4,0},{5,1},{6,2},{7,3},{8,12},{9,13},{10,... | collective-permute-start | bytes 165896 | tf_op jit(solution)/shard_map/ppermute | solution.py:161
  30.6 0.0 collective-permute-start.2
  30.6 3.0 %collective-permute-start.3 = (f32[72,192]{1,0:T(8,128)S(1)}, f32[72,192]{1,0:T(8,128)S(1)}, u32[]{:S(2)}, u32[]{:S(2)}) collective-permute-start(f32[72,192]{1,0:T(8,128)S(1)} %select_maximum_fusion), channel_id=1, source_target_pairs={{0,8},{1,9},{2,10},{3,11},{4,12},{5,13},{6,14},{7,15},{8,0},{9,1},... | collective-permute-start | bytes 165896 | tf_op jit(solution)/shard_map/ppermute | solution.py:161
  33.6 1.3 %collective-permute-start.4 = (f32[72,192]{1,0:T(8,128)S(1)}, f32[72,192]{1,0:T(8,128)S(1)}, u32[]{:S(2)}, u32[]{:S(2)}) collective-permute-start(f32[72,192]{1,0:T(8,128)S(1)} %select_maximum_fusion), channel_id=1, source_target_pairs={{0,10},{1,11},{2,8},{3,9},{4,14},{5,15},{6,12},{7,13},{8,2},{9,3},... | collective-permute-start | bytes 165896 | tf_op jit(solution)/shard_map/ppermute | solution.py:161
  34.9 0.0 collective-permute-done
  34.9 3.7 %collective-permute-start.5 = (f32[72,192]{1,0:T(8,128)S(1)}, f32[72,192]{1,0:T(8,128)S(1)}, u32[]{:S(2)}, u32[]{:S(2)}) collective-permute-start(f32[72,192]{1,0:T(8,128)S(1)} %select_maximum_fusion), channel_id=1, source_target_pairs={{0,12},{1,13},{2,14},{3,15},{4,8},{5,9},{6,10},{7,11},{8,4},{9,5},... | collective-permute-start | bytes 165896 | tf_op jit(solution)/shard_map/ppermute | solution.py:161
  38.6 0.0 collective-permute-done.1
  38.6 0.1 collective-permute-start.6
  38.7 0.0 collective-permute-done.2
  38.7 0.0 collective-permute-done.3
  38.8 6.1 %collective-permute-done.4 = f32[72,192]{1,0:T(8,128)S(1)} collective-permute-done((f32[72,192]{1,0:T(8,128)S(1)}, f32[72,192]{1,0:T(8,128)S(1)}, u32[]{:S(2)}, u32[]{:S(2)}) %collective-permute-start.4) | collective-permute-done | bytes 55328 | tf_op jit(solution)/shard_map/ppermute | solution.py:161
  44.9 0.0 collective-permute-done.5
  44.9 0.9 %collective-permute-done.6 = f32[72,192]{1,0:T(8,128)S(1)} collective-permute-done((f32[72,192]{1,0:T(8,128)S(1)}, f32[72,192]{1,0:T(8,128)S(1)}, u32[]{:S(2)}, u32[]{:S(2)}) %collective-permute-start.6) | collective-permute-done | bytes 55328 | tf_op jit(solution)/shard_map/ppermute | solution.py:161
  45.8 0.1 collective-permute-start.7
  45.9 0.0 copy-done.1
  45.9 0.1 iota_add_fusion
  46.0 0.1 add.87
  46.1 1.8 %collective-permute-done.7 = f32[8,72,192]{2,1,0:T(8,128)S(1)} collective-permute-done((f32[8,72,192]{2,1,0:T(8,128)S(1)}, f32[8,72,192]{2,1,0:T(8,128)S(1)}, u32[]{:S(2)}, u32[]{:S(2)}) %collective-permute-start.7) | collective-permute-done | bytes 442400 | tf_op jit(solution)/shard_map/ppermute | solution.py:165
  48.0 0.1 reshape.241
  48.1 0.1 slice_convert_fusion.1
  48.2 0.2 select_reduce_fusion
  48.4 0.2 multiply_reduce_fusion
  48.7 0.1 sqrt.12
  48.7 0.5 convert_element_type.100
  49.2 0.5 fusion.4
  49.7 0.1 convert_element_type.90
  49.8 1.0 %convert_reduce_fusion = s32[1024]{0:T(1024)S(1)} fusion(s32[1024]{0:T(1024)S(1)} %convert_element_type.90, s32[1024]{0:T(1024)S(1)} %add.87), kind=kLoop, calls=%fused_computation | loop fusion | flops 5241856 | bytes 12288 | tf_op jit(solution)/shard_map/reduce_sum | solution.py:207
  50.8 0.2 fusion.2
  51.1 0.9 %fusion = f32[512,194]{0,1:T(8,128)S(1)} fusion(s32[1024]{0:T(1024)S(1)} %add_select_fusion.2, bf16[1024,1]{1,0:T(8,128)(2,1)S(1)} %get-tuple-element.20, bf16[1024,1]{1,0:T(8,128)(2,1)S(1)} %get-tuple-element.19, bf16[1024,192]{1,0:T(8,128)(2,1)S(1)} %fusion.2), kind=kOutput, calls=%fused_computation.2 | convolution fusion | flops 205139968 | bytes 798720 | tf_op jit(solution)/shard_map/dot_general | solution.py:218
  51.9 0.0 copy-start
  52.0 0.1 copy.28.col_unit_ref
  52.1 0.1 pad_add_fusion
  52.2 0.1 dynamic-slice_bitcast_fusion
  52.3 0.1 copy.27.row_rec_ref
  52.4 0.2 copy-done
  52.6 1.6 %shard_map.92 = f32[32,512]{1,0:T(8,128)} custom-call(f32[3,3]{1,0:T(4,128)S(1)} %copy-done, bf16[34,192]{1,0:T(8,128)(2,1)S(1)} %fusion.14.row_unit_ref, bf16[512,192]{1,0:T(8,128)(2,1)S(1)} %copy.28.col_unit_ref, s32[34,1]{1,0:T(8,128)S(1)} %copy.27.row_rec_ref, s32[1,512]{1,0:T(1,128)S(1)} %fusion.20.col_rec_ref), custom_call_target="tpu_custom_call" | custom-call | flops 7012352 | bytes 275200 | tf_op jit(solution)/shard_map/pallas_call | solution.py:134
  (21 shorter events, 0.3 us)
Async XLA Ops:
  22.7 3.2 %copy-start.2 = (f32[64]{0:T(128)S(1)}, f32[64]{0:T(128)}, u32[]{:S(2)}) copy-start(f32[64]{0:T(128)} %convert_element_type.87) | copy-start | bytes 772
  22.7 3.2 %copy-start.3 = (f32[64]{0:T(128)S(1)}, f32[64]{0:T(128)}, u32[]{:S(2)}) copy-start(f32[64]{0:T(128)} %convert_element_type.88) | copy-start | bytes 772
  25.9 20.0 %copy-start.1 = (s32[16]{0:T(128)S(1)}, s32[16]{0:T(128)}, u32[]{:S(2)}) copy-start(s32[16]{0:T(128)} %constant.85.clone) | copy-start | bytes 196
  26.0 8.9 %collective-permute-start = (f32[72,192]{1,0:T(8,128)S(1)}, f32[72,192]{1,0:T(8,128)S(1)}, u32[]{:S(2)}, u32[]{:S(2)}) collective-permute-start(f32[72,192]{1,0:T(8,128)S(1)} %select_maximum_fusion), channel_id=1, source_target_pairs={{0,2},{1,3},{2,0},{3,1},{4,6},{5,7},{6,4},{7,5},{8,10},{9,11},{10,... | collective-permute-start | bytes 165896 | tf_op jit(solution)/shard_map/ppermute | solution.py:161
  29.0 9.6 %collective-permute-start.1 = (f32[72,192]{1,0:T(8,128)S(1)}, f32[72,192]{1,0:T(8,128)S(1)}, u32[]{:S(2)}, u32[]{:S(2)}) collective-permute-start(f32[72,192]{1,0:T(8,128)S(1)} %select_maximum_fusion), channel_id=1, source_target_pairs={{0,4},{1,5},{2,6},{3,7},{4,0},{5,1},{6,2},{7,3},{8,12},{9,13},{10,... | collective-permute-start | bytes 165896 | tf_op jit(solution)/shard_map/ppermute | solution.py:161
  30.6 8.1 %collective-permute-start.2 = (f32[72,192]{1,0:T(8,128)S(1)}, f32[72,192]{1,0:T(8,128)S(1)}, u32[]{:S(2)}, u32[]{:S(2)}) collective-permute-start(f32[72,192]{1,0:T(8,128)S(1)} %select_maximum_fusion), channel_id=1, source_target_pairs={{0,6},{1,7},{2,4},{3,5},{4,2},{5,3},{6,0},{7,1},{8,14},{9,15},{10,... | collective-permute-start | bytes 165896 | tf_op jit(solution)/shard_map/ppermute | solution.py:161
  30.6 8.1 %collective-permute-start.3 = (f32[72,192]{1,0:T(8,128)S(1)}, f32[72,192]{1,0:T(8,128)S(1)}, u32[]{:S(2)}, u32[]{:S(2)}) collective-permute-start(f32[72,192]{1,0:T(8,128)S(1)} %select_maximum_fusion), channel_id=1, source_target_pairs={{0,8},{1,9},{2,10},{3,11},{4,12},{5,13},{6,14},{7,15},{8,0},{9,1},... | collective-permute-start | bytes 165896 | tf_op jit(solution)/shard_map/ppermute | solution.py:161
  33.6 11.3 %collective-permute-start.4 = (f32[72,192]{1,0:T(8,128)S(1)}, f32[72,192]{1,0:T(8,128)S(1)}, u32[]{:S(2)}, u32[]{:S(2)}) collective-permute-start(f32[72,192]{1,0:T(8,128)S(1)} %select_maximum_fusion), channel_id=1, source_target_pairs={{0,10},{1,11},{2,8},{3,9},{4,14},{5,15},{6,12},{7,13},{8,2},{9,3},... | collective-permute-start | bytes 165896 | tf_op jit(solution)/shard_map/ppermute | solution.py:161
  34.9 10.0 %collective-permute-start.5 = (f32[72,192]{1,0:T(8,128)S(1)}, f32[72,192]{1,0:T(8,128)S(1)}, u32[]{:S(2)}, u32[]{:S(2)}) collective-permute-start(f32[72,192]{1,0:T(8,128)S(1)} %select_maximum_fusion), channel_id=1, source_target_pairs={{0,12},{1,13},{2,14},{3,15},{4,8},{5,9},{6,10},{7,11},{8,4},{9,5},... | collective-permute-start | bytes 165896 | tf_op jit(solution)/shard_map/ppermute | solution.py:161
  38.6 7.2 %collective-permute-start.6 = (f32[72,192]{1,0:T(8,128)S(1)}, f32[72,192]{1,0:T(8,128)S(1)}, u32[]{:S(2)}, u32[]{:S(2)}) collective-permute-start(f32[72,192]{1,0:T(8,128)S(1)} %select_maximum_fusion), channel_id=1, source_target_pairs={{0,14},{1,15},{2,12},{3,13},{4,10},{5,11},{6,8},{7,9},{8,6},{9,7},... | collective-permute-start | bytes 165896 | tf_op jit(solution)/shard_map/ppermute | solution.py:161
  45.8 2.1 %collective-permute-start.7 = (f32[8,72,192]{2,1,0:T(8,128)S(1)}, f32[8,72,192]{2,1,0:T(8,128)S(1)}, u32[]{:S(2)}, u32[]{:S(2)}) collective-permute-start(f32[8,72,192]{2,1,0:T(8,128)S(1)} %get-tuple-element.23), channel_id=1, source_target_pairs={{0,1},{1,0},{2,3},{3,2},{4,5},{5,4},{6,7},{7,6},{8,9},{9,8},{10,11... | collective-permute-start | bytes 1327112 | tf_op jit(solution)/shard_map/ppermute | solution.py:165
  51.9 0.7 %copy-start = (f32[3,3]{1,0:T(4,128)S(1)}, f32[3,3]{1,0:T(4,128)}, u32[]{:S(2)}) copy-start(f32[3,3]{1,0:T(4,128)} %k_ref.1) | copy-start | bytes 112

commit v12 on v11

--- a/solution.py
+++ b/solution.py
@@ -20,7 +20,6 @@
 WIN = SEGLEN + 8
 CONV_ROWS = 256
 ONE_HOT_LIMIT = 1 << 20
-VMEM_ALL = 67043328
 
 
 def _pool_kernel(
@@ -98,7 +97,7 @@
             pltpu.VMEM((rows, CH), jnp.float32),
             pltpu.SemaphoreType.DMA((2,)),
         ],
-        compiler_params=pltpu.CompilerParams(vmem_limit_bytes=VMEM_ALL),
+        compiler_params=pltpu.CompilerParams(vmem_limit_bytes=48 * 1024 * 1024),
         cost_estimate=pl.CostEstimate(
             flops=2 * rows * 3 * FEAT * CH * 6 + 8 * slots * WIN * CH,
             transcendentals=slots * CH,

time: 54.6 us -> 56.4 us (1.033)
  local copies, waits for them, and re-layouts: 1.43 us -> 8.79 us
  waiting for transfers between devices: 8.85 us -> 6.01 us
  matrix products: 4.07 us -> 2.5 us
  Pallas kernels: 20.8 us -> 19.3 us
  other arithmetic: 6.15 us -> 6.9 us
    unnamed x15 -> x23, local copies, waits for them, and re-layouts: 0.39 us -> 7.11 us
    ppermute x7, waiting for transfers between devices: 7.02 us -> 3.95 us  [gather_wide(): blocks.append(lax.ppermute(x, 'wide', perm))]
    dot_general x1, matrix products: 3.22 us -> 1.64 us  [per_device(): jnp.dot(pooled, proj_weight, precision=PRECISE, preferred_element_type=jn...]
    pallas_call x1, Pallas kernels: 19.1 us -> 17.6 us  [pool_slots(): pl.pallas_call(_pool_kernel, out_shape=jax.ShapeDtypeStruct((slots, 2 * C...]
    reduce_sum x1, other arithmetic: 0.23 us -> 1.08 us  [per_device(): jnp.sum(centred * centred, axis=1, keepdims=True) + 1e-06]
    convert_element_type x1, other arithmetic: 0.52 us -> 1.23 us  [per_device(): rec_hi = (all_rec // 16).astype(jnp.bfloat16)[:, None]]
    unnamed x1, other arithmetic: 0.01 us -> 0.66 us
    another operation x1, local copies, waits for them, and re-layouts: 0.01 us -> 0.64 us  [gather_wide(): buf = jnp.stack(blocks, axis=0)]
  transfers between devices with their start and end apart: 8 -> 8, of which waited for: 3 -> 3; matrix products, arithmetic and copies ran while one was open for 0% -> 8% of each run, Pallas kernels for 0% -> 0%
where the time goes in v12:
time: 56.4 us; the launch traced here: 56.1 us
  Pallas kernels  19.3 us (34%)
  starting transfers between devices  12.5 us (22%)
  local copies, waits for them, and re-layouts  8.79 us (16%)
  other arithmetic  6.9 us (12%)
  waiting for transfers between devices  6.01 us (11%)
  matrix products  2.5 us (4%)
    pallas_call x1, Pallas kernels, pool_slots(): pl.pallas_call(_pool_kernel, out_shape=jax.ShapeDtypeStruct((slots, 2 * C...  17.6 us
    ppermute x7, starting transfers between devices, gather_wide(): blocks.append(lax.ppermute(x, 'wide', perm))  12.5 us
    unnamed x23, local copies, waits for them, and re-layouts  7.11 us
    ppermute x7, waiting for transfers between devices, gather_wide(): blocks.append(lax.ppermute(x, 'wide', perm))  3.95 us
    ppermute x1, waiting for transfers between devices, gather_wide(): buf = jnp.concatenate([buf, lax.ppermute(buf, 'wide', perm)], axis=0)  2.06 us
    pallas_call x1, Pallas kernels, smooth_affinity(): pl.pallas_call(_affinity_kernel, out_shape=jax.ShapeDtypeStruct((height,...  1.65 us
    dot_general x1, matrix products, per_device(): jnp.dot(pooled, proj_weight, precision=PRECISE, preferred_element_type=jn...  1.64 us
    convert_element_type x1, other arithmetic, per_device(): rec_hi = (all_rec // 16).astype(jnp.bfloat16)[:, None]  1.23 us
  transfers between devices with their start and end apart: 8, of which 3 were waited for; matrix products, arithmetic and copies ran while one was open for 8% of the time, Pallas kernels for 0%

profile of v12, /device:TPU:0, one launch (start us, length us, event | category | flops | bytes accessed | tf_op | source)
XLA Modules:
  0.0 56.1 jit_solution(6944035324446063950)
XLA Ops:
  0.0 0.0 copy-start
  0.0 0.8 %broadcast_clamp_fusion.starts_ref = s32[64]{0:T(128)S(1)} fusion(s32[64]{0:T(128)} %param.12), kind=kLoop, calls=%fused_computation.63 | loop fusion | flops 64 | bytes 512 | tf_op jit(solution)/shard_map/jit(clip)/min | solution.py:81
  0.8 0.7 %convert_element_type.87 = f32[64]{0:T(128)S(1)} convert(s32[64]{0:T(128)} %param.13) | non-fusion elementwise | flops 64 | bytes 512 | tf_op jit(solution)/shard_map/convert_element_type | solution.py:179
  1.4 0.7 %convert_element_type.88 = f32[64]{0:T(128)S(1)} convert(s32[64]{0:T(128)} %param.14) | non-fusion elementwise | flops 64 | bytes 512 | tf_op jit(solution)/shard_map/convert_element_type | solution.py:179
  2.1 0.0 copy-start.2
  2.1 1.2 %copy-done.2 = f32[240,1024]{1,0:T(8,128)S(1)} copy-done((f32[240,1024]{1,0:T(8,128)S(1)}, f32[240,1024]{1,0:T(8,128)}, u32[]{:S(2)}) %copy-start.2) | copy-done | bytes 983064
  3.3 0.0 copy-start.3
  3.3 1.1 %copy-done.3 = f32[2048,80]{0,1:T(8,128)S(1)} copy-done((f32[2048,80]{0,1:T(8,128)S(1)}, f32[2048,80]{0,1:T(8,128)}, u32[]{:S(2)}) %copy-start.3) | copy-done | bytes 655384
  4.4 0.0 copy-start.4
  4.4 0.7 %copy-done.4 = f32[1024]{0:T(1024)S(1)} copy-done((f32[1024]{0:T(1024)S(1)}, f32[1024]{0:T(1024)}, u32[]{:S(2)}) %copy-start.4) | copy-done | bytes 4120
  5.1 17.6 %shard_map.91 = f32[64,2048]{1,0:T(8,128)S(1)} custom-call(s32[64]{0:T(128)S(1)} %broadcast_clamp_fusion.starts_ref, f32[80,2048]{1,0:T(8,128)S(1)} %bitcast.41, f32[240,1024]{1,0:T(8,128)S(1)} %copy-done.2, f32[1,1024]{1,0:T(1,128)S(1)} %bitcast.42), custom_call_target="tpu_custom_call" | custom-call | flops 6077546496 | bytes 2162688 | tf_op jit(solution)/shard_map/pallas_call | solution.py:83
  22.7 0.0 copy-done
  22.7 1.6 %fusion.17 = f32[64,192]{1,0:T(8,128)S(1)} fusion(f32[64,2048]{1,0:T(8,128)S(1)} %shard_map.91, f32[2048,192]{0,1:T(8,128)S(1)} %copy-done), kind=kOutput, calls=%fused_computation.65 | convolution fusion | flops 301989888 | bytes 2146304 | tf_op jit(solution)/shard_map/dot_general | solution.py:176
  24.3 0.0 copy-start.7
  24.4 0.1 maximum_bitcast_fusion
  24.4 3.0 %collective-permute-start = (f32[72,192]{1,0:T(8,128)S(1)}, f32[72,192]{1,0:T(8,128)S(1)}, u32[]{:S(2)}, u32[]{:S(2)}) collective-permute-start(f32[72,192]{1,0:T(8,128)S(1)} %select_maximum_fusion), channel_id=1, source_target_pairs={{0,2},{1,3},{2,0},{3,1},{4,6},{5,7},{6,4},{7,5},{8,10},{9,11},{10,... | collective-permute-start | bytes 165896 | tf_op jit(solution)/shard_map/ppermute | solution.py:160
  27.5 1.6 %collective-permute-start.1 = (f32[72,192]{1,0:T(8,128)S(1)}, f32[72,192]{1,0:T(8,128)S(1)}, u32[]{:S(2)}, u32[]{:S(2)}) collective-permute-start(f32[72,192]{1,0:T(8,128)S(1)} %select_maximum_fusion), channel_id=1, source_target_pairs={{0,4},{1,5},{2,6},{3,7},{4,0},{5,1},{6,2},{7,3},{8,12},{9,13},{10,... | collective-permute-start | bytes 165896 | tf_op jit(solution)/shard_map/ppermute | solution.py:160
  29.0 0.0 collective-permute-start.2
  29.0 3.0 %collective-permute-start.3 = (f32[72,192]{1,0:T(8,128)S(1)}, f32[72,192]{1,0:T(8,128)S(1)}, u32[]{:S(2)}, u32[]{:S(2)}) collective-permute-start(f32[72,192]{1,0:T(8,128)S(1)} %select_maximum_fusion), channel_id=1, source_target_pairs={{0,8},{1,9},{2,10},{3,11},{4,12},{5,13},{6,14},{7,15},{8,0},{9,1},... | collective-permute-start | bytes 165896 | tf_op jit(solution)/shard_map/ppermute | solution.py:160
  32.0 1.3 %collective-permute-start.4 = (f32[72,192]{1,0:T(8,128)S(1)}, f32[72,192]{1,0:T(8,128)S(1)}, u32[]{:S(2)}, u32[]{:S(2)}) collective-permute-start(f32[72,192]{1,0:T(8,128)S(1)} %select_maximum_fusion), channel_id=1, source_target_pairs={{0,10},{1,11},{2,8},{3,9},{4,14},{5,15},{6,12},{7,13},{8,2},{9,3},... | collective-permute-start | bytes 165896 | tf_op jit(solution)/shard_map/ppermute | solution.py:160
  33.3 0.7 %bitcast_dynamic-update-slice_fusion.15 = (f32[8,72,192]{2,1,0:T(8,128)}, f32[16,72,192]{2,1,0:T(8,128)S(1)}) fusion(f32[1,128]{1,0:T(1,128)S(1)} %maximum_bitcast_fusion, f32[64,192]{1,0:T(8,128)S(1)} %fusion.17), kind=kLoop, calls=%fused_computation.45 | loop fusion | flops 41470 | bytes 197120
  34.0 0.0 collective-permute-done
  34.0 3.6 %collective-permute-start.5 = (f32[72,192]{1,0:T(8,128)S(1)}, f32[72,192]{1,0:T(8,128)S(1)}, u32[]{:S(2)}, u32[]{:S(2)}) collective-permute-start(f32[72,192]{1,0:T(8,128)S(1)} %select_maximum_fusion), channel_id=1, source_target_pairs={{0,12},{1,13},{2,14},{3,15},{4,8},{5,9},{6,10},{7,11},{8,4},{9,5},... | collective-permute-start | bytes 165896 | tf_op jit(solution)/shard_map/ppermute | solution.py:160
  37.6 0.6 %bitcast_dynamic-update-slice_fusion.13 = (f32[8,72,192]{2,1,0:T(8,128)}, f32[16,72,192]{2,1,0:T(8,128)S(1)}) fusion(f32[8,72,192]{2,1,0:T(8,128)} %get-tuple-element.37, f32[72,192]{1,0:T(8,128)S(1)} %collective-permute-done, f32[16,72,192]{2,1,0:T(8,128)S(1)} %get-tuple-element.38), kind=kLoop, calls=%fused_computation.43 | loop fusion | bytes 221184
  38.2 0.0 collective-permute-done.1
  38.2 0.0 collective-permute-start.6
  38.2 0.6 %bitcast_dynamic-update-slice_fusion.11 = (f32[8,72,192]{2,1,0:T(8,128)}, f32[16,72,192]{2,1,0:T(8,128)S(1)}) fusion(f32[8,72,192]{2,1,0:T(8,128)} %get-tuple-element.35, f32[72,192]{1,0:T(8,128)S(1)} %collective-permute-done.1, f32[16,72,192]{2,1,0:T(8,128)S(1)} %get-tuple-element.36), kind=kLoop, calls=%fused_computation.41 | loop fusion | bytes 221184
  38.8 0.0 collective-permute-done.2
  38.8 0.6 %bitcast_dynamic-update-slice_fusion.9 = (f32[8,72,192]{2,1,0:T(8,128)}, f32[16,72,192]{2,1,0:T(8,128)S(1)}) fusion(f32[8,72,192]{2,1,0:T(8,128)} %get-tuple-element.33, f32[72,192]{1,0:T(8,128)S(1)} %collective-permute-done.2, f32[16,72,192]{2,1,0:T(8,128)S(1)} %get-tuple-element.34), kind=kLoop, calls=%fused_computation.39 | loop fusion | bytes 221184
  39.5 0.0 collective-permute-done.3
  39.5 0.6 %bitcast_dynamic-update-slice_fusion.7 = (f32[8,72,192]{2,1,0:T(8,128)}, f32[16,72,192]{2,1,0:T(8,128)S(1)}) fusion(f32[8,72,192]{2,1,0:T(8,128)} %get-tuple-element.31, f32[72,192]{1,0:T(8,128)S(1)} %collective-permute-done.3, f32[16,72,192]{2,1,0:T(8,128)S(1)} %get-tuple-element.32), kind=kLoop, calls=%fused_computation.37 | loop fusion | bytes 221184
  40.1 3.1 %collective-permute-done.4 = f32[72,192]{1,0:T(8,128)S(1)} collective-permute-done((f32[72,192]{1,0:T(8,128)S(1)}, f32[72,192]{1,0:T(8,128)S(1)}, u32[]{:S(2)}, u32[]{:S(2)}) %collective-permute-start.4) | collective-permute-done | bytes 55328 | tf_op jit(solution)/shard_map/ppermute | solution.py:160
  43.3 0.6 %bitcast_dynamic-update-slice_fusion.5 = (f32[8,72,192]{2,1,0:T(8,128)}, f32[16,72,192]{2,1,0:T(8,128)S(1)}) fusion(f32[8,72,192]{2,1,0:T(8,128)} %get-tuple-element.29, f32[72,192]{1,0:T(8,128)S(1)} %collective-permute-done.4, f32[16,72,192]{2,1,0:T(8,128)S(1)} %get-tuple-element.30), kind=kLoop, calls=%fused_computation.35 | loop fusion | bytes 221184
  43.9 0.0 collective-permute-done.5
  43.9 0.6 %bitcast_dynamic-update-slice_fusion.3 = (f32[8,72,192]{2,1,0:T(8,128)}, f32[16,72,192]{2,1,0:T(8,128)S(1)}) fusion(f32[8,72,192]{2,1,0:T(8,128)} %get-tuple-element.27, f32[72,192]{1,0:T(8,128)S(1)} %collective-permute-done.5, f32[16,72,192]{2,1,0:T(8,128)S(1)} %get-tuple-element.28), kind=kLoop, calls=%fused_computation.33 | loop fusion | bytes 221184
  44.6 0.8 %collective-permute-done.6 = f32[72,192]{1,0:T(8,128)S(1)} collective-permute-done((f32[72,192]{1,0:T(8,128)S(1)}, f32[72,192]{1,0:T(8,128)S(1)}, u32[]{:S(2)}, u32[]{:S(2)}) %collective-permute-start.6) | collective-permute-done | bytes 55328 | tf_op jit(solution)/shard_map/ppermute | solution.py:160
  45.4 0.6 %bitcast_dynamic-update-slice_fusion.1 = (f32[8,72,192]{2,1,0:T(8,128)}, f32[16,72,192]{2,1,0:T(8,128)S(1)}) fusion(f32[8,72,192]{2,1,0:T(8,128)} %get-tuple-element.25, f32[72,192]{1,0:T(8,128)S(1)} %collective-permute-done.6, f32[16,72,192]{2,1,0:T(8,128)S(1)} %get-tuple-element.26), kind=kLoop, calls=%fused_computation.31 | loop fusion | bytes 221184 | tf_op jit(solution)/shard_map/stack | solution.py:162
  46.0 0.0 collective-permute-start.7
  46.0 0.0 copy-done.7
  46.0 0.1 iota_add_fusion
  46.1 0.1 add.87
  46.2 2.1 %collective-permute-done.7 = f32[8,72,192]{2,1,0:T(8,128)S(1)} collective-permute-done((f32[8,72,192]{2,1,0:T(8,128)}, f32[8,72,192]{2,1,0:T(8,128)S(1)}, u32[]{:S(2)}, u32[]{:S(2)}) %collective-permute-start.7) | collective-permute-done | bytes 442400 | tf_op jit(solution)/shard_map/ppermute | solution.py:164
  48.3 0.1 reshape.241
  48.4 0.1 slice_convert_fusion.1
  48.5 0.2 select_reduce_fusion
  48.7 1.1 %multiply_reduce_fusion = (f32[16,64]{1,0:T(8,128)S(1)}, f32[16,64,192]{2,1,0:T(8,128)}) fusion(f32[192]{0:T(256)S(1)} %broadcast_multiply_fusion, f32[16,72,192]{2,1,0:T(8,128)S(1)} %constant_dynamic-update-slice_fusion), kind=kLoop, calls=%fused_computation.6 | loop fusion | flops 588800 | bytes 1577728 | tf_op jit(solution)/shard_map/reduce_sum | solution.py:201
  49.8 0.0 copy-start.5
  49.8 0.1 sqrt.12
  49.9 0.5 convert_element_type.100
  50.3 1.2 %fusion.4 = (bf16[1024,1]{1,0:T(8,128)(2,1)S(1)}, bf16[1024,1]{1,0:T(8,128)(2,1)}) fusion(s32[1024,1]{1,0:T(8,128)S(1)} %convert_element_type.100), kind=kLoop, calls=%fused_computation.14 | loop fusion | flops 21504 | bytes 8192 | tf_op jit(solution)/shard_map/convert_element_type | solution.py:213
  51.6 0.0 copy-start.6
  51.6 0.1 convert_element_type.90
  51.6 1.0 %convert_reduce_fusion = s32[1024]{0:T(1024)S(1)} fusion(s32[1024]{0:T(1024)S(1)} %convert_element_type.90, s32[1024]{0:T(1024)S(1)} %add.87), kind=kLoop, calls=%fused_computation | loop fusion | flops 5241856 | bytes 12288 | tf_op jit(solution)/shard_map/reduce_sum | solution.py:206
  52.7 0.0 copy-done.5
  52.7 0.2 fusion.2
  52.9 0.0 copy-done.6
  52.9 0.9 %fusion = f32[512,194]{0,1:T(8,128)S(1)} fusion(s32[1024]{0:T(1024)S(1)} %add_select_fusion.2, bf16[1024,1]{1,0:T(8,128)(2,1)S(1)} %copy-done.6, bf16[1024,1]{1,0:T(8,128)(2,1)S(1)} %get-tuple-element.19, bf16[1024,192]{1,0:T(8,128)(2,1)S(1)} %fusion.2), kind=kOutput, calls=%fused_computation.2 | convolution fusion | flops 205139968 | bytes 798720 | tf_op jit(solution)/shard_map/dot_general | solution.py:217
  53.8 0.0 copy-start.1
  53.9 0.1 copy.28.col_unit_ref
  54.0 0.1 pad_add_fusion
  54.1 0.1 dynamic-slice_bitcast_fusion
  54.2 0.1 copy.27.row_rec_ref
  54.3 0.2 copy-done.1
  54.5 1.6 %shard_map.92 = f32[32,512]{1,0:T(8,128)} custom-call(f32[3,3]{1,0:T(4,128)S(1)} %copy-done.1, bf16[34,192]{1,0:T(8,128)(2,1)S(1)} %fusion.14.row_unit_ref, bf16[512,192]{1,0:T(8,128)(2,1)S(1)} %copy.28.col_unit_ref, s32[34,1]{1,0:T(8,128)S(1)} %copy.27.row_rec_ref, s32[1,512]{1,0:T(1,128)S(1)} %fusion.20.col_rec_ref), custom_call_target="tpu_custom_call" | custom-call | flops 7012352 | bytes 275200 | tf_op jit(solution)/shard_map/pallas_call | solution.py:133
  (13 shorter events, 0.2 us)
Async XLA Ops:
  0.0 22.7 %copy-start = (f32[2048,192]{0,1:T(8,128)S(1)}, f32[2048,192]{0,1:T(8,128)}, u32[]{:S(2)}) copy-start(f32[2048,192]{0,1:T(8,128)} %param.17) | copy-start | bytes 4718596
  2.1 1.2 %copy-start.2 = (f32[240,1024]{1,0:T(8,128)S(1)}, f32[240,1024]{1,0:T(8,128)}, u32[]{:S(2)}) copy-start(f32[240,1024]{1,0:T(8,128)} %w_hbm.1) | copy-start | bytes 2949124
  3.3 1.1 %copy-start.3 = (f32[2048,80]{0,1:T(8,128)S(1)}, f32[2048,80]{0,1:T(8,128)}, u32[]{:S(2)}) copy-start(f32[2048,80]{0,1:T(8,128)} %param.11) | copy-start | bytes 1966084
  4.4 0.7 %copy-start.4 = (f32[1024]{0:T(1024)S(1)}, f32[1024]{0:T(1024)}, u32[]{:S(2)}) copy-start(f32[1024]{0:T(1024)} %param.16) | copy-start | bytes 12292
  24.3 21.7 %copy-start.7 = (s32[16]{0:T(128)S(1)}, s32[16]{0:T(128)}, u32[]{:S(2)}) copy-start(s32[16]{0:T(128)} %constant.85.clone) | copy-start | bytes 196
  24.4 9.5 %collective-permute-start = (f32[72,192]{1,0:T(8,128)S(1)}, f32[72,192]{1,0:T(8,128)S(1)}, u32[]{:S(2)}, u32[]{:S(2)}) collective-permute-start(f32[72,192]{1,0:T(8,128)S(1)} %select_maximum_fusion), channel_id=1, source_target_pairs={{0,2},{1,3},{2,0},{3,1},{4,6},{5,7},{6,4},{7,5},{8,10},{9,11},{10,... | collective-permute-start | bytes 165896 | tf_op jit(solution)/shard_map/ppermute | solution.py:160
  27.5 10.7 %collective-permute-start.1 = (f32[72,192]{1,0:T(8,128)S(1)}, f32[72,192]{1,0:T(8,128)S(1)}, u32[]{:S(2)}, u32[]{:S(2)}) collective-permute-start(f32[72,192]{1,0:T(8,128)S(1)} %select_maximum_fusion), channel_id=1, source_target_pairs={{0,4},{1,5},{2,6},{3,7},{4,0},{5,1},{6,2},{7,3},{8,12},{9,13},{10,... | collective-permute-start | bytes 165896 | tf_op jit(solution)/shard_map/ppermute | solution.py:160
  29.0 9.8 %collective-permute-start.2 = (f32[72,192]{1,0:T(8,128)S(1)}, f32[72,192]{1,0:T(8,128)S(1)}, u32[]{:S(2)}, u32[]{:S(2)}) collective-permute-start(f32[72,192]{1,0:T(8,128)S(1)} %select_maximum_fusion), channel_id=1, source_target_pairs={{0,6},{1,7},{2,4},{3,5},{4,2},{5,3},{6,0},{7,1},{8,14},{9,15},{10,... | collective-permute-start | bytes 165896 | tf_op jit(solution)/shard_map/ppermute | solution.py:160
  29.0 10.5 %collective-permute-start.3 = (f32[72,192]{1,0:T(8,128)S(1)}, f32[72,192]{1,0:T(8,128)S(1)}, u32[]{:S(2)}, u32[]{:S(2)}) collective-permute-start(f32[72,192]{1,0:T(8,128)S(1)} %select_maximum_fusion), channel_id=1, source_target_pairs={{0,8},{1,9},{2,10},{3,11},{4,12},{5,13},{6,14},{7,15},{8,0},{9,1},... | collective-permute-start | bytes 165896 | tf_op jit(solution)/shard_map/ppermute | solution.py:160
  32.0 11.3 %collective-permute-start.4 = (f32[72,192]{1,0:T(8,128)S(1)}, f32[72,192]{1,0:T(8,128)S(1)}, u32[]{:S(2)}, u32[]{:S(2)}) collective-permute-start(f32[72,192]{1,0:T(8,128)S(1)} %select_maximum_fusion), channel_id=1, source_target_pairs={{0,10},{1,11},{2,8},{3,9},{4,14},{5,15},{6,12},{7,13},{8,2},{9,3},... | collective-permute-start | bytes 165896 | tf_op jit(solution)/shard_map/ppermute | solution.py:160
  34.0 10.0 %collective-permute-start.5 = (f32[72,192]{1,0:T(8,128)S(1)}, f32[72,192]{1,0:T(8,128)S(1)}, u32[]{:S(2)}, u32[]{:S(2)}) collective-permute-start(f32[72,192]{1,0:T(8,128)S(1)} %select_maximum_fusion), channel_id=1, source_target_pairs={{0,12},{1,13},{2,14},{3,15},{4,8},{5,9},{6,10},{7,11},{8,4},{9,5},... | collective-permute-start | bytes 165896 | tf_op jit(solution)/shard_map/ppermute | solution.py:160
  38.2 7.2 %collective-permute-start.6 = (f32[72,192]{1,0:T(8,128)S(1)}, f32[72,192]{1,0:T(8,128)S(1)}, u32[]{:S(2)}, u32[]{:S(2)}) collective-permute-start(f32[72,192]{1,0:T(8,128)S(1)} %select_maximum_fusion), channel_id=1, source_target_pairs={{0,14},{1,15},{2,12},{3,13},{4,10},{5,11},{6,8},{7,9},{8,6},{9,7},... | collective-permute-start | bytes 165896 | tf_op jit(solution)/shard_map/ppermute | solution.py:160
  46.0 2.2 %collective-permute-start.7 = (f32[8,72,192]{2,1,0:T(8,128)}, f32[8,72,192]{2,1,0:T(8,128)S(1)}, u32[]{:S(2)}, u32[]{:S(2)}) collective-permute-start(f32[8,72,192]{2,1,0:T(8,128)} %get-tuple-element.23), channel_id=1, source_target_pairs={{0,1},{1,0},{2,3},{3,2},{4,5},{5,4},{6,7},{7,6},{8,9},{9,8},{10,11... | collective-permute-start | bytes 1327112 | tf_op jit(solution)/shard_map/ppermute | solution.py:164
  49.8 2.9 %copy-start.5 = (f32[16,64,192]{2,1,0:T(8,128)S(1)}, f32[16,64,192]{2,1,0:T(8,128)}, u32[]{:S(2)}) copy-start(f32[16,64,192]{2,1,0:T(8,128)} %get-tuple-element.18) | copy-start | bytes 2359300
  51.6 1.3 %copy-start.6 = (bf16[1024,1]{1,0:T(8,128)(2,1)S(1)}, bf16[1024,1]{1,0:T(8,128)(2,1)}, u32[]{:S(2)}) copy-start(bf16[1024,1]{1,0:T(8,128)(2,1)} %get-tuple-element.20) | copy-start | bytes 6148
  53.8 0.7 %copy-start.1 = (f32[3,3]{1,0:T(4,128)S(1)}, f32[3,3]{1,0:T(4,128)}, u32[]{:S(2)}) copy-start(f32[3,3]{1,0:T(4,128)} %k_ref.1) | copy-start | bytes 112

commit v13 on v10

--- a/solution.py
+++ b/solution.py
@@ -153,17 +153,13 @@
     if group_size % 2 or group_size & (group_size - 1):
         every = lax.all_gather(x, "wide", axis=0, tiled=False)
         return every, jnp.arange(group_size, dtype=jnp.int32)
-    pattern = [0]
-    blocks = [x]
+    pair = jnp.stack([x, lax.ppermute(x, "wide", [(i, i ^ 1) for i in range(group_size)])])
+    blocks = [pair]
     for flip in range(2, group_size, 2):
         perm = [(i, i ^ flip) for i in range(group_size)]
-        blocks.append(lax.ppermute(x, "wide", perm))
-        pattern.append(flip)
-    buf = jnp.stack(blocks, axis=0)
-    perm = [(i, i ^ 1) for i in range(group_size)]
-    buf = jnp.concatenate([buf, lax.ppermute(buf, "wide", perm)], axis=0)
-    pattern = pattern + [p ^ 1 for p in pattern]
-    source = jnp.asarray(pattern, dtype=jnp.int32) ^ my_index
+        blocks.append(lax.ppermute(pair, "wide", perm))
+    buf = jnp.concatenate(blocks, axis=0)
+    source = jnp.arange(group_size, dtype=jnp.int32) ^ my_index
     return buf, source
 
 

time: 53.6 us -> 63.9 us (1.19)
  the two profiles are of different devices: /device:TPU:0 before, /device:TPU:16 now
where the time goes in v13:
time: 63.9 us; the launch traced here: 63.8 us
  waiting for transfers between devices  25.8 us (40%)
  Pallas kernels  18.8 us (29%)
  starting transfers between devices  8.02 us (13%)
  other arithmetic  4.19 us (7%)
  local copies, waits for them, and re-layouts  4.13 us (6%)
  matrix products  2.5 us (4%)
    ppermute x7, waiting for transfers between devices, gather_wide(): blocks.append(lax.ppermute(pair, 'wide', perm))  24.7 us
    pallas_call x1, Pallas kernels, pool_slots(): pl.pallas_call(_pool_kernel, out_shape=jax.ShapeDtypeStruct((slots, 2 * C...  17.2 us
    ppermute x7, starting transfers between devices, gather_wide(): blocks.append(lax.ppermute(pair, 'wide', perm))  7.95 us
    unnamed x27, local copies, waits for them, and re-layouts  3.12 us
    pallas_call x1, Pallas kernels, smooth_affinity(): pl.pallas_call(_affinity_kernel, out_shape=jax.ShapeDtypeStruct((height,...  1.65 us
    dot_general x1, matrix products, per_device(): jnp.dot(pooled, proj_weight, precision=PRECISE, preferred_element_type=jn...  1.64 us
  transfers between devices with their start and end apart: 8, of which 7 were waited for; matrix products, arithmetic and copies ran while one was open for 0% of the time, Pallas kernels for 0%

profile of v13, /device:TPU:16, one launch (start us, length us, event | category | flops | bytes accessed | tf_op | source)
XLA Modules:
  0.0 63.8 jit_solution(7605624302413859318)
XLA Ops:
  0.0 0.0 copy-start
  0.0 0.0 copy-start.6
  0.0 0.0 copy-start.7
  0.0 0.0 copy-start.8
  0.0 0.0 copy-start.3
  0.0 1.5 %copy.23.frames_hbm = f32[2048,80]{1,0:T(8,128)S(1)} copy(f32[2048,80]{0,1:T(8,128)} %param.10) | data formatting | bytes 1310720 | tf_op args[0]
  1.6 0.0 copy-done.6
  1.6 0.0 copy-done.7
  1.6 0.0 copy-done.8
  1.6 0.0 copy-done.3
  1.6 0.0 copy-start.2
  1.7 1.2 %copy-done.2 = f32[240,1024]{1,0:T(8,128)S(1)} copy-done((f32[240,1024]{1,0:T(8,128)S(1)}, f32[240,1024]{1,0:T(8,128)}, u32[]{:S(2)}) %copy-start.2) | copy-done | bytes 983064
  2.8 17.2 %shard_map.82 = f32[64,2048]{1,0:T(8,128)S(1)} custom-call(s32[64]{0:T(128)S(1)} %broadcast_clamp_fusion.starts_ref, f32[2048,80]{1,0:T(8,128)S(1)} %copy.23.frames_hbm, f32[240,1024]{1,0:T(8,128)S(1)} %copy-done.2, f32[1,1024]{1,0:T(1,128)S(1)} %bitcast.21), custom_call_target="tpu_custom_call" | custom-call | flops 6077546496 | bytes 2162688 | tf_op jit(solution)/shard_map/pallas_call | solution.py:83
  20.0 0.0 copy-done
  20.0 1.6 %fusion.18 = f32[64,192]{1,0:T(8,128)S(1)} fusion(f32[64,2048]{1,0:T(8,128)S(1)} %shard_map.82, f32[2048,192]{0,1:T(8,128)S(1)} %copy-done), kind=kOutput, calls=%fused_computation.59 | convolution fusion | flops 301989888 | bytes 2146304 | tf_op jit(solution)/shard_map/dot_general | solution.py:172
  21.7 0.1 maximum_bitcast_fusion
  21.8 0.1 collective-permute-start
  21.9 0.1 iota_add_fusion
  21.9 0.1 add.87
  22.0 1.1 %collective-permute-done = f32[72,192]{1,0:T(8,128)S(1)} collective-permute-done((f32[72,192]{1,0:T(8,128)S(1)}, f32[72,192]{1,0:T(8,128)S(1)}, u32[]{:S(2)}, u32[]{:S(2)}) %collective-permute-start) | collective-permute-done | bytes 55328 | tf_op jit(solution)/shard_map/ppermute | solution.py:156
  23.1 1.6 %collective-permute-start.1 = (f32[2,72,192]{2,1,0:T(8,128)S(1)}, f32[2,72,192]{2,1,0:T(8,128)S(1)}, u32[]{:S(2)}, u32[]{:S(2)}) collective-permute-start(f32[2,72,192]{2,1,0:T(8,128)S(1)} %pad_maximum_fusion), channel_id=1, source_target_pairs={{0,2},{1,3},{2,0},{3,1},{4,6},{5,7},{6,4},{7,5},{8,10},{9,11},{10,... | collective-permute-start | bytes 331784 | tf_op jit(solution)/shard_map/ppermute | solution.py:160
  24.7 1.6 %collective-permute-start.2 = (f32[2,72,192]{2,1,0:T(8,128)S(1)}, f32[2,72,192]{2,1,0:T(8,128)S(1)}, u32[]{:S(2)}, u32[]{:S(2)}) collective-permute-start(f32[2,72,192]{2,1,0:T(8,128)S(1)} %pad_maximum_fusion), channel_id=1, source_target_pairs={{0,4},{1,5},{2,6},{3,7},{4,0},{5,1},{6,2},{7,3},{8,12},{9,13},{10,... | collective-permute-start | bytes 331784 | tf_op jit(solution)/shard_map/ppermute | solution.py:160
  26.3 0.4 collective-permute-start.3
  26.7 0.0 collective-permute-start.4
  26.7 3.9 %collective-permute-start.5 = (f32[2,72,192]{2,1,0:T(8,128)S(1)}, f32[2,72,192]{2,1,0:T(8,128)S(1)}, u32[]{:S(2)}, u32[]{:S(2)}) collective-permute-start(f32[2,72,192]{2,1,0:T(8,128)S(1)} %pad_maximum_fusion), channel_id=1, source_target_pairs={{0,10},{1,11},{2,8},{3,9},{4,14},{5,15},{6,12},{7,13},{8,2},{9,3},... | collective-permute-start | bytes 331784 | tf_op jit(solution)/shard_map/ppermute | solution.py:160
  30.6 0.0 collective-permute-done.1
  30.6 0.5 collective-permute-start.6
  31.1 3.3 %collective-permute-done.2 = f32[2,72,192]{2,1,0:T(8,128)S(1)} collective-permute-done((f32[2,72,192]{2,1,0:T(8,128)S(1)}, f32[2,72,192]{2,1,0:T(8,128)S(1)}, u32[]{:S(2)}, u32[]{:S(2)}) %collective-permute-start.2) | collective-permute-done | bytes 110624 | tf_op jit(solution)/shard_map/ppermute | solution.py:160
  34.4 0.0 collective-permute-start.7
  34.4 2.0 %collective-permute-done.3 = f32[2,72,192]{2,1,0:T(8,128)S(1)} collective-permute-done((f32[2,72,192]{2,1,0:T(8,128)S(1)}, f32[2,72,192]{2,1,0:T(8,128)S(1)}, u32[]{:S(2)}, u32[]{:S(2)}) %collective-permute-start.3) | collective-permute-done | bytes 110624 | tf_op jit(solution)/shard_map/ppermute | solution.py:160
  36.4 1.3 %collective-permute-done.4 = f32[2,72,192]{2,1,0:T(8,128)S(1)} collective-permute-done((f32[2,72,192]{2,1,0:T(8,128)S(1)}, f32[2,72,192]{2,1,0:T(8,128)S(1)}, u32[]{:S(2)}, u32[]{:S(2)}) %collective-permute-start.4) | collective-permute-done | bytes 110624 | tf_op jit(solution)/shard_map/ppermute | solution.py:160
  37.8 9.6 %collective-permute-done.5 = f32[2,72,192]{2,1,0:T(8,128)S(1)} collective-permute-done((f32[2,72,192]{2,1,0:T(8,128)S(1)}, f32[2,72,192]{2,1,0:T(8,128)S(1)}, u32[]{:S(2)}, u32[]{:S(2)}) %collective-permute-start.5) | collective-permute-done | bytes 110624 | tf_op jit(solution)/shard_map/ppermute | solution.py:160
  47.4 6.0 %collective-permute-done.6 = f32[2,72,192]{2,1,0:T(8,128)S(1)} collective-permute-done((f32[2,72,192]{2,1,0:T(8,128)S(1)}, f32[2,72,192]{2,1,0:T(8,128)S(1)}, u32[]{:S(2)}, u32[]{:S(2)}) %collective-permute-start.6) | collective-permute-done | bytes 110624 | tf_op jit(solution)/shard_map/ppermute | solution.py:160
  53.4 2.5 %collective-permute-done.7 = f32[2,72,192]{2,1,0:T(8,128)S(1)} collective-permute-done((f32[2,72,192]{2,1,0:T(8,128)S(1)}, f32[2,72,192]{2,1,0:T(8,128)S(1)}, u32[]{:S(2)}, u32[]{:S(2)}) %collective-permute-start.7) | collective-permute-done | bytes 110624 | tf_op jit(solution)/shard_map/ppermute | solution.py:160
  55.9 0.1 reshape.245
  56.0 0.1 slice_convert_fusion.1
  56.1 0.2 select_reduce_fusion
  56.3 1.1 %multiply_reduce_fusion = (f32[16,64]{1,0:T(8,128)S(1)}, f32[16,64,192]{2,1,0:T(8,128)}) fusion(f32[192]{0:T(256)S(1)} %broadcast_multiply_fusion, f32[16,72,192]{2,1,0:T(8,128)S(1)} %constant_dynamic-update-slice_fusion), kind=kLoop, calls=%fused_computation.6 | loop fusion | flops 588800 | bytes 1577728 | tf_op jit(solution)/shard_map/reduce_sum | solution.py:197
  57.4 0.0 copy-start.4
  57.4 0.1 sqrt.12
  57.5 0.5 convert_element_type.100
  58.0 1.2 %fusion.4 = (bf16[1024,1]{1,0:T(8,128)(2,1)S(1)}, bf16[1024,1]{1,0:T(8,128)(2,1)}) fusion(s32[1024,1]{1,0:T(8,128)S(1)} %convert_element_type.100), kind=kLoop, calls=%fused_computation.14 | loop fusion | flops 21504 | bytes 8192 | tf_op jit(solution)/shard_map/convert_element_type | solution.py:209
  59.2 0.0 copy-start.5
  59.2 0.1 convert_element_type.90
  59.3 1.0 %convert_reduce_fusion = s32[1024]{0:T(1024)S(1)} fusion(s32[1024]{0:T(1024)S(1)} %convert_element_type.90, s32[1024]{0:T(1024)S(1)} %add.87), kind=kLoop, calls=%fused_computation | loop fusion | flops 5241856 | bytes 12288 | tf_op jit(solution)/shard_map/reduce_sum | solution.py:202
  60.3 0.0 copy-done.4
  60.3 0.2 fusion.2
  60.5 0.0 copy-done.5
  60.6 0.9 %fusion = f32[512,194]{0,1:T(8,128)S(1)} fusion(s32[1024]{0:T(1024)S(1)} %add_select_fusion.2, bf16[1024,1]{1,0:T(8,128)(2,1)S(1)} %copy-done.5, bf16[1024,1]{1,0:T(8,128)(2,1)S(1)} %get-tuple-element.19, bf16[1024,192]{1,0:T(8,128)(2,1)S(1)} %fusion.2), kind=kOutput, calls=%fused_computation.2 | convolution fusion | flops 205139968 | bytes 798720 | tf_op jit(solution)/shard_map/dot_general | solution.py:213
  61.4 0.0 copy-start.1
  61.5 0.1 copy.30.col_unit_ref
  61.6 0.1 pad_add_fusion
  61.7 0.1 dynamic-slice_bitcast_fusion
  61.8 0.1 copy.29.row_rec_ref
  61.9 0.2 copy-done.1
  62.1 1.6 %shard_map.83 = f32[32,512]{1,0:T(8,128)} custom-call(f32[3,3]{1,0:T(4,128)S(1)} %copy-done.1, bf16[34,192]{1,0:T(8,128)(2,1)S(1)} %fusion.14.row_unit_ref, bf16[512,192]{1,0:T(8,128)(2,1)S(1)} %copy.30.col_unit_ref, s32[34,1]{1,0:T(8,128)S(1)} %copy.29.row_rec_ref, s32[1,512]{1,0:T(1,128)S(1)} %fusion.21.col_rec_ref), custom_call_target="tpu_custom_call" | custom-call | flops 7012352 | bytes 275200 | tf_op jit(solution)/shard_map/pallas_call | solution.py:133
  (25 shorter events, 0.3 us)
Async XLA Ops:
  0.0 20.0 %copy-start = (f32[2048,192]{0,1:T(8,128)S(1)}, f32[2048,192]{0,1:T(8,128)}, u32[]{:S(2)}) copy-start(f32[2048,192]{0,1:T(8,128)} %param.16) | copy-start | bytes 4718596
  0.0 1.6 %copy-start.6 = (s32[64]{0:T(128)S(1)}, s32[64]{0:T(128)}, u32[]{:S(2)}) copy-start(s32[64]{0:T(128)} %param.11) | copy-start | bytes 772
  0.0 1.6 %copy-start.7 = (s32[64]{0:T(128)S(1)}, s32[64]{0:T(128)}, u32[]{:S(2)}) copy-start(s32[64]{0:T(128)} %param.12) | copy-start | bytes 772
  0.0 1.6 %copy-start.8 = (s32[64]{0:T(128)S(1)}, s32[64]{0:T(128)}, u32[]{:S(2)}) copy-start(s32[64]{0:T(128)} %param.13) | copy-start | bytes 772
  0.0 1.6 %copy-start.3 = (f32[1024]{0:T(1024)S(1)}, f32[1024]{0:T(1024)}, u32[]{:S(2)}) copy-start(f32[1024]{0:T(1024)} %param.15) | copy-start | bytes 12292
  1.6 1.2 %copy-start.2 = (f32[240,1024]{1,0:T(8,128)S(1)}, f32[240,1024]{1,0:T(8,128)}, u32[]{:S(2)}) copy-start(f32[240,1024]{1,0:T(8,128)} %w_hbm.1) | copy-start | bytes 2949124
  21.8 1.3 %collective-permute-start = (f32[72,192]{1,0:T(8,128)S(1)}, f32[72,192]{1,0:T(8,128)S(1)}, u32[]{:S(2)}, u32[]{:S(2)}) collective-permute-start(f32[72,192]{1,0:T(8,128)S(1)} %get-tuple-element.24), channel_id=1, source_target_pairs={{0,1},{1,0},{2,3},{3,2},{4,5},{5,4},{6,7},{7,6},{8,9},{9,8},{10,11... | collective-permute-start | bytes 165896 | tf_op jit(solution)/shard_map/ppermute | solution.py:156
  23.1 7.4 %collective-permute-start.1 = (f32[2,72,192]{2,1,0:T(8,128)S(1)}, f32[2,72,192]{2,1,0:T(8,128)S(1)}, u32[]{:S(2)}, u32[]{:S(2)}) collective-permute-start(f32[2,72,192]{2,1,0:T(8,128)S(1)} %pad_maximum_fusion), channel_id=1, source_target_pairs={{0,2},{1,3},{2,0},{3,1},{4,6},{5,7},{6,4},{7,5},{8,10},{9,11},{10,... | collective-permute-start | bytes 331784 | tf_op jit(solution)/shard_map/ppermute | solution.py:160
  24.7 9.7 %collective-permute-start.2 = (f32[2,72,192]{2,1,0:T(8,128)S(1)}, f32[2,72,192]{2,1,0:T(8,128)S(1)}, u32[]{:S(2)}, u32[]{:S(2)}) collective-permute-start(f32[2,72,192]{2,1,0:T(8,128)S(1)} %pad_maximum_fusion), channel_id=1, source_target_pairs={{0,4},{1,5},{2,6},{3,7},{4,0},{5,1},{6,2},{7,3},{8,12},{9,13},{10,... | collective-permute-start | bytes 331784 | tf_op jit(solution)/shard_map/ppermute | solution.py:160
  26.3 10.1 %collective-permute-start.3 = (f32[2,72,192]{2,1,0:T(8,128)S(1)}, f32[2,72,192]{2,1,0:T(8,128)S(1)}, u32[]{:S(2)}, u32[]{:S(2)}) collective-permute-start(f32[2,72,192]{2,1,0:T(8,128)S(1)} %pad_maximum_fusion), channel_id=1, source_target_pairs={{0,6},{1,7},{2,4},{3,5},{4,2},{5,3},{6,0},{7,1},{8,14},{9,15},{10,... | collective-permute-start | bytes 331784 | tf_op jit(solution)/shard_map/ppermute | solution.py:160
  26.7 11.1 %collective-permute-start.4 = (f32[2,72,192]{2,1,0:T(8,128)S(1)}, f32[2,72,192]{2,1,0:T(8,128)S(1)}, u32[]{:S(2)}, u32[]{:S(2)}) collective-permute-start(f32[2,72,192]{2,1,0:T(8,128)S(1)} %pad_maximum_fusion), channel_id=1, source_target_pairs={{0,8},{1,9},{2,10},{3,11},{4,12},{5,13},{6,14},{7,15},{8,0},{9,1},... | collective-permute-start | bytes 331784 | tf_op jit(solution)/shard_map/ppermute | solution.py:160
  26.7 20.7 %collective-permute-start.5 = (f32[2,72,192]{2,1,0:T(8,128)S(1)}, f32[2,72,192]{2,1,0:T(8,128)S(1)}, u32[]{:S(2)}, u32[]{:S(2)}) collective-permute-start(f32[2,72,192]{2,1,0:T(8,128)S(1)} %pad_maximum_fusion), channel_id=1, source_target_pairs={{0,10},{1,11},{2,8},{3,9},{4,14},{5,15},{6,12},{7,13},{8,2},{9,3},... | collective-permute-start | bytes 331784 | tf_op jit(solution)/shard_map/ppermute | solution.py:160
  30.6 22.8 %collective-permute-start.6 = (f32[2,72,192]{2,1,0:T(8,128)S(1)}, f32[2,72,192]{2,1,0:T(8,128)S(1)}, u32[]{:S(2)}, u32[]{:S(2)}) collective-permute-start(f32[2,72,192]{2,1,0:T(8,128)S(1)} %pad_maximum_fusion), channel_id=1, source_target_pairs={{0,12},{1,13},{2,14},{3,15},{4,8},{5,9},{6,10},{7,11},{8,4},{9,5},... | collective-permute-start | bytes 331784 | tf_op jit(solution)/shard_map/ppermute | solution.py:160
  34.4 21.5 %collective-permute-start.7 = (f32[2,72,192]{2,1,0:T(8,128)S(1)}, f32[2,72,192]{2,1,0:T(8,128)S(1)}, u32[]{:S(2)}, u32[]{:S(2)}) collective-permute-start(f32[2,72,192]{2,1,0:T(8,128)S(1)} %pad_maximum_fusion), channel_id=1, source_target_pairs={{0,14},{1,15},{2,12},{3,13},{4,10},{5,11},{6,8},{7,9},{8,6},{9,7},... | collective-permute-start | bytes 331784 | tf_op jit(solution)/shard_map/ppermute | solution.py:160
  57.4 2.9 %copy-start.4 = (f32[16,64,192]{2,1,0:T(8,128)S(1)}, f32[16,64,192]{2,1,0:T(8,128)}, u32[]{:S(2)}) copy-start(f32[16,64,192]{2,1,0:T(8,128)} %get-tuple-element.18) | copy-start | bytes 2359300
  59.2 1.3 %copy-start.5 = (bf16[1024,1]{1,0:T(8,128)(2,1)S(1)}, bf16[1024,1]{1,0:T(8,128)(2,1)}, u32[]{:S(2)}) copy-start(bf16[1024,1]{1,0:T(8,128)(2,1)} %get-tuple-element.20) | copy-start | bytes 6148
  61.4 0.7 %copy-start.1 = (f32[3,3]{1,0:T(4,128)S(1)}, f32[3,3]{1,0:T(4,128)}, u32[]{:S(2)}) copy-start(f32[3,3]{1,0:T(4,128)} %k_ref.1) | copy-start | bytes 112

commit v14 on v13

--- a/solution.py
+++ b/solution.py
@@ -150,16 +150,25 @@
 
 def gather_wide(x, group_size):
     my_index = lax.axis_index("wide")
-    if group_size % 2 or group_size & (group_size - 1):
+    if group_size & (group_size - 1):
         every = lax.all_gather(x, "wide", axis=0, tiled=False)
         return every, jnp.arange(group_size, dtype=jnp.int32)
-    pair = jnp.stack([x, lax.ppermute(x, "wide", [(i, i ^ 1) for i in range(group_size)])])
-    blocks = [pair]
-    for flip in range(2, group_size, 2):
-        perm = [(i, i ^ flip) for i in range(group_size)]
-        blocks.append(lax.ppermute(pair, "wide", perm))
-    buf = jnp.concatenate(blocks, axis=0)
-    source = jnp.arange(group_size, dtype=jnp.int32) ^ my_index
+    pattern = [0]
+    buf = x[None]
+    bit = group_size.bit_length() - 2
+    while bit >= 0:
+        if bit >= 2:
+            flips = [m << (bit - 1) for m in (1, 2, 3)]
+            bit -= 2
+        else:
+            flips = [1 << bit]
+            bit -= 1
+        received = [
+            lax.ppermute(buf, "wide", [(i, i ^ f) for i in range(group_size)]) for f in flips
+        ]
+        buf = jnp.concatenate([buf] + received, axis=0)
+        pattern = pattern + [p ^ f for f in flips for p in pattern]
+    source = jnp.asarray(pattern, dtype=jnp.int32) ^ my_index
     return buf, source
 
 

time: 63.9 us -> 51.8 us (0.81)
  the two profiles are of different devices: /device:TPU:16 before, /device:TPU:0 now
where the time goes in v14:
time: 51.8 us; the launch traced here: 51.6 us
  Pallas kernels  18.8 us (36%)
  waiting for transfers between devices  11.2 us (22%)
  starting transfers between devices  7.27 us (14%)
  local copies, waits for them, and re-layouts  6.76 us (13%)
  other arithmetic  4.84 us (9%)
  matrix products  2.5 us (5%)
    pallas_call x1, Pallas kernels, pool_slots(): pl.pallas_call(_pool_kernel, out_shape=jax.ShapeDtypeStruct((slots, 2 * C...  17.2 us
    ppermute x5, waiting for transfers between devices, gather_wide(): lax.ppermute(buf, 'wide', [(i, i ^ f) for i in range(group_size)])  11.2 us
    ppermute x5, starting transfers between devices, gather_wide(): lax.ppermute(buf, 'wide', [(i, i ^ f) for i in range(group_size)])  7.27 us
    unnamed x25, local copies, waits for them, and re-layouts  4.96 us
    pallas_call x1, Pallas kernels, smooth_affinity(): pl.pallas_call(_affinity_kernel, out_shape=jax.ShapeDtypeStruct((height,...  1.65 us
    dot_general x1, matrix products, per_device(): jnp.dot(pooled, proj_weight, precision=PRECISE, preferred_element_type=jn...  1.64 us
    convert_element_type x1, other arithmetic, per_device(): rec_hi = (all_rec // 16).astype(jnp.bfloat16)[:, None]  1.24 us
    reduce_sum x1, other arithmetic, per_device(): jnp.sum(centred * centred, axis=1, keepdims=True) + 1e-06  1.08 us
  transfers between devices with their start and end apart: 5, of which 4 were waited for; matrix products, arithmetic and copies ran while one was open for 5% of the time, Pallas kernels for 0%

profile of v14, /device:TPU:0, one launch (start us, length us, event | category | flops | bytes accessed | tf_op | source)
XLA Modules:
  0.0 51.6 jit_solution(4185953215199257896)
XLA Ops:
  0.0 0.0 copy-start
  0.0 0.0 copy-start.6
  0.0 0.0 copy-start.7
  0.0 0.0 copy-start.8
  0.0 0.0 copy-start.3
  0.0 1.5 %copy.24.frames_hbm = f32[2048,80]{1,0:T(8,128)S(1)} copy(f32[2048,80]{0,1:T(8,128)} %param.11) | data formatting | bytes 1310720 | tf_op args[0]
  1.6 0.0 copy-done.6
  1.6 0.0 copy-done.7
  1.6 0.0 copy-done.8
  1.6 0.0 copy-done.3
  1.6 0.0 copy-start.2
  1.6 1.2 %copy-done.2 = f32[240,1024]{1,0:T(8,128)S(1)} copy-done((f32[240,1024]{1,0:T(8,128)S(1)}, f32[240,1024]{1,0:T(8,128)}, u32[]{:S(2)}) %copy-start.2) | copy-done | bytes 983064
  2.8 17.2 %shard_map.91 = f32[64,2048]{1,0:T(8,128)S(1)} custom-call(s32[64]{0:T(128)S(1)} %broadcast_clamp_fusion.starts_ref, f32[2048,80]{1,0:T(8,128)S(1)} %copy.24.frames_hbm, f32[240,1024]{1,0:T(8,128)S(1)} %copy-done.2, f32[1,1024]{1,0:T(1,128)S(1)} %bitcast.22), custom_call_target="tpu_custom_call" | custom-call | flops 6077546496 | bytes 2162688 | tf_op jit(solution)/shard_map/pallas_call | solution.py:83
  20.0 0.0 copy-done
  20.0 1.6 %fusion.18 = f32[64,192]{1,0:T(8,128)S(1)} fusion(f32[64,2048]{1,0:T(8,128)S(1)} %shard_map.91, f32[2048,192]{0,1:T(8,128)S(1)} %copy-done), kind=kOutput, calls=%fused_computation.61 | convolution fusion | flops 301989888 | bytes 2146304 | tf_op jit(solution)/shard_map/dot_general | solution.py:181
  21.7 0.1 maximum_bitcast_fusion
  21.8 0.0 copy-start.9
  21.8 3.1 %collective-permute-start = (f32[1,72,192]{2,1,0:T(8,128)S(1)}, f32[1,72,192]{2,1,0:T(8,128)S(1)}, u32[]{:S(2)}, u32[]{:S(2)}) collective-permute-start(f32[1,72,192]{2,1,0:T(8,128)S(1)} %fusion.13), channel_id=1, source_target_pairs={{0,4},{1,5},{2,6},{3,7},{4,0},{5,1},{6,2},{7,3},{8,12},{9,13},{10,... | collective-permute-start | bytes 165896 | tf_op jit(solution)/shard_map/ppermute | solution.py:167
  24.9 2.6 %collective-permute-start.1 = (f32[1,72,192]{2,1,0:T(8,128)S(1)}, f32[1,72,192]{2,1,0:T(8,128)S(1)}, u32[]{:S(2)}, u32[]{:S(2)}) collective-permute-start(f32[1,72,192]{2,1,0:T(8,128)S(1)} %fusion.13), channel_id=1, source_target_pairs={{0,8},{1,9},{2,10},{3,11},{4,12},{5,13},{6,14},{7,15},{8,0},{9,1},... | collective-permute-start | bytes 165896 | tf_op jit(solution)/shard_map/ppermute | solution.py:167
  27.5 0.0 collective-permute-start.2
  27.5 0.6 %constant_dynamic-update-slice_fusion.4 = (f32[8,72,192]{2,1,0:T(8,128)}, f32[16,72,192]{2,1,0:T(8,128)S(1)}) fusion(f32[1,128]{1,0:T(1,128)S(1)} %maximum_bitcast_fusion, f32[64,192]{1,0:T(8,128)S(1)} %fusion.18), kind=kLoop, calls=%fused_computation.36 | loop fusion | flops 41470 | bytes 197120
  28.1 0.0 collective-permute-done
  28.1 4.6 %collective-permute-done.1 = f32[1,72,192]{2,1,0:T(8,128)S(1)} collective-permute-done((f32[1,72,192]{2,1,0:T(8,128)S(1)}, f32[1,72,192]{2,1,0:T(8,128)S(1)}, u32[]{:S(2)}, u32[]{:S(2)}) %collective-permute-start.1) | collective-permute-done | bytes 55328 | tf_op jit(solution)/shard_map/ppermute | solution.py:167
  32.6 1.1 %collective-permute-done.2 = f32[1,72,192]{2,1,0:T(8,128)S(1)} collective-permute-done((f32[1,72,192]{2,1,0:T(8,128)S(1)}, f32[1,72,192]{2,1,0:T(8,128)S(1)}, u32[]{:S(2)}, u32[]{:S(2)}) %collective-permute-start.2) | collective-permute-done | bytes 55328 | tf_op jit(solution)/shard_map/ppermute | solution.py:167
  33.7 1.6 %collective-permute-start.3 = (f32[4,72,192]{2,1,0:T(8,128)S(1)}, f32[4,72,192]{2,1,0:T(8,128)S(1)}, u32[]{:S(2)}, u32[]{:S(2)}) collective-permute-start(f32[4,72,192]{2,1,0:T(8,128)S(1)} %pad_maximum_fusion), channel_id=1, source_target_pairs={{0,2},{1,3},{2,0},{3,1},{4,6},{5,7},{6,4},{7,5},{8,10},{9,11},{10,... | collective-permute-start | bytes 663560 | tf_op jit(solution)/shard_map/ppermute | solution.py:167
  35.3 0.6 %constant_dynamic-update-slice_fusion.3 = (f32[8,72,192]{2,1,0:T(8,128)}, f32[16,72,192]{2,1,0:T(8,128)S(1)}) fusion(f32[8,72,192]{2,1,0:T(8,128)} %get-tuple-element.31, f32[1,72,192]{2,1,0:T(8,128)S(1)} %collective-permute-done, f32[16,72,192]{2,1,0:T(8,128)S(1)} %get-tuple-element.32), kind=kLoop, calls=%fused_computation.35 | loop fusion | bytes 221184
  36.0 0.6 %constant_dynamic-update-slice_fusion.2 = (f32[8,72,192]{2,1,0:T(8,128)}, f32[16,72,192]{2,1,0:T(8,128)S(1)}) fusion(f32[8,72,192]{2,1,0:T(8,128)} %get-tuple-element.29, f32[1,72,192]{2,1,0:T(8,128)S(1)} %collective-permute-done.1, f32[16,72,192]{2,1,0:T(8,128)S(1)} %get-tuple-element.30), kind=kLoop, calls=%fused_computation.34 | loop fusion | bytes 221184
  36.6 0.6 %constant_dynamic-update-slice_fusion.1 = (f32[8,72,192]{2,1,0:T(8,128)}, f32[16,72,192]{2,1,0:T(8,128)S(1)}) fusion(f32[8,72,192]{2,1,0:T(8,128)} %get-tuple-element.27, f32[1,72,192]{2,1,0:T(8,128)S(1)} %collective-permute-done.2, f32[16,72,192]{2,1,0:T(8,128)S(1)} %get-tuple-element.28), kind=kLoop, calls=%fused_computation.33 | loop fusion | bytes 221184
  37.2 3.5 %collective-permute-done.3 = f32[4,72,192]{2,1,0:T(8,128)S(1)} collective-permute-done((f32[4,72,192]{2,1,0:T(8,128)S(1)}, f32[4,72,192]{2,1,0:T(8,128)S(1)}, u32[]{:S(2)}, u32[]{:S(2)}) %collective-permute-start.3) | collective-permute-done | bytes 221216 | tf_op jit(solution)/shard_map/ppermute | solution.py:167
  40.7 0.8 %constant_dynamic-update-slice_fusion = (f32[8,72,192]{2,1,0:T(8,128)}, f32[16,72,192]{2,1,0:T(8,128)S(1)}) fusion(f32[8,72,192]{2,1,0:T(8,128)} %get-tuple-element.25, f32[4,72,192]{2,1,0:T(8,128)S(1)} %collective-permute-done.3, f32[16,72,192]{2,1,0:T(8,128)S(1)} %get-tuple-element.26), kind=kLoop, calls=%fused_computation.32 | loop fusion | bytes 884736 | tf_op jit(solution)/shard_map/concatenate | solution.py:169
  41.5 0.0 collective-permute-start.4
  41.5 0.0 copy-done.9
  41.5 0.1 iota_add_fusion
  41.6 0.1 add.87
  41.7 2.1 %collective-permute-done.4 = f32[8,72,192]{2,1,0:T(8,128)S(1)} collective-permute-done((f32[8,72,192]{2,1,0:T(8,128)}, f32[8,72,192]{2,1,0:T(8,128)S(1)}, u32[]{:S(2)}, u32[]{:S(2)}) %collective-permute-start.4) | collective-permute-done | bytes 442400 | tf_op jit(solution)/shard_map/ppermute | solution.py:167
  43.8 0.1 reshape.241
  43.9 0.1 slice_convert_fusion.1
  44.0 0.2 select_reduce_fusion
  44.2 1.1 %multiply_reduce_fusion = (f32[16,64]{1,0:T(8,128)S(1)}, f32[16,64,192]{2,1,0:T(8,128)}) fusion(f32[192]{0:T(256)S(1)} %broadcast_multiply_fusion, f32[16,72,192]{2,1,0:T(8,128)S(1)} %constant_dynamic-update-slice_fusion.5), kind=kLoop, calls=%fused_computation.6 | loop fusion | flops 588800 | bytes 1577728 | tf_op jit(solution)/shard_map/reduce_sum | solution.py:206
  45.3 0.0 copy-start.4
  45.3 0.1 sqrt.12
  45.4 0.5 convert_element_type.100
  45.8 1.2 %fusion.4 = (bf16[1024,1]{1,0:T(8,128)(2,1)S(1)}, bf16[1024,1]{1,0:T(8,128)(2,1)}) fusion(s32[1024,1]{1,0:T(8,128)S(1)} %convert_element_type.100), kind=kLoop, calls=%fused_computation.14 | loop fusion | flops 21504 | bytes 8192 | tf_op jit(solution)/shard_map/convert_element_type | solution.py:218
  47.1 0.0 copy-start.5
  47.1 0.1 convert_element_type.90
  47.1 1.0 %convert_reduce_fusion = s32[1024]{0:T(1024)S(1)} fusion(s32[1024]{0:T(1024)S(1)} %convert_element_type.90, s32[1024]{0:T(1024)S(1)} %add.87), kind=kLoop, calls=%fused_computation | loop fusion | flops 5241856 | bytes 12288 | tf_op jit(solution)/shard_map/reduce_sum | solution.py:211
  48.2 0.0 copy-done.4
  48.2 0.2 fusion.2
  48.4 0.0 copy-done.5
  48.4 0.9 %fusion = f32[512,194]{0,1:T(8,128)S(1)} fusion(s32[1024]{0:T(1024)S(1)} %add_select_fusion.2, bf16[1024,1]{1,0:T(8,128)(2,1)S(1)} %copy-done.5, bf16[1024,1]{1,0:T(8,128)(2,1)S(1)} %get-tuple-element.19, bf16[1024,192]{1,0:T(8,128)(2,1)S(1)} %fusion.2), kind=kOutput, calls=%fused_computation.2 | convolution fusion | flops 205139968 | bytes 798720 | tf_op jit(solution)/shard_map/dot_general | solution.py:222
  49.3 0.0 copy-start.1
  49.4 0.1 copy.31.col_unit_ref
  49.5 0.1 pad_add_fusion
  49.6 0.1 dynamic-slice_bitcast_fusion
  49.7 0.1 copy.30.row_rec_ref
  49.8 0.2 copy-done.1
  50.0 1.6 %shard_map.92 = f32[32,512]{1,0:T(8,128)} custom-call(f32[3,3]{1,0:T(4,128)S(1)} %copy-done.1, bf16[34,192]{1,0:T(8,128)(2,1)S(1)} %fusion.15.row_unit_ref, bf16[512,192]{1,0:T(8,128)(2,1)S(1)} %copy.31.col_unit_ref, s32[34,1]{1,0:T(8,128)S(1)} %copy.30.row_rec_ref, s32[1,512]{1,0:T(1,128)S(1)} %fusion.21.col_rec_ref), custom_call_target="tpu_custom_call" | custom-call | flops 7012352 | bytes 275200 | tf_op jit(solution)/shard_map/pallas_call | solution.py:133
  (17 shorter events, 0.2 us)
Async XLA Ops:
  0.0 20.0 %copy-start = (f32[2048,192]{0,1:T(8,128)S(1)}, f32[2048,192]{0,1:T(8,128)}, u32[]{:S(2)}) copy-start(f32[2048,192]{0,1:T(8,128)} %param.17) | copy-start | bytes 4718596
  0.0 1.6 %copy-start.6 = (s32[64]{0:T(128)S(1)}, s32[64]{0:T(128)}, u32[]{:S(2)}) copy-start(s32[64]{0:T(128)} %param.12) | copy-start | bytes 772
  0.0 1.6 %copy-start.7 = (s32[64]{0:T(128)S(1)}, s32[64]{0:T(128)}, u32[]{:S(2)}) copy-start(s32[64]{0:T(128)} %param.13) | copy-start | bytes 772
  0.0 1.6 %copy-start.8 = (s32[64]{0:T(128)S(1)}, s32[64]{0:T(128)}, u32[]{:S(2)}) copy-start(s32[64]{0:T(128)} %param.14) | copy-start | bytes 772
  0.0 1.6 %copy-start.3 = (f32[1024]{0:T(1024)S(1)}, f32[1024]{0:T(1024)}, u32[]{:S(2)}) copy-start(f32[1024]{0:T(1024)} %param.16) | copy-start | bytes 12292
  1.6 1.2 %copy-start.2 = (f32[240,1024]{1,0:T(8,128)S(1)}, f32[240,1024]{1,0:T(8,128)}, u32[]{:S(2)}) copy-start(f32[240,1024]{1,0:T(8,128)} %w_hbm.1) | copy-start | bytes 2949124
  21.8 19.7 %copy-start.9 = (s32[16]{0:T(128)S(1)}, s32[16]{0:T(128)}, u32[]{:S(2)}) copy-start(s32[16]{0:T(128)} %constant.85.clone) | copy-start | bytes 196
  21.8 6.3 %collective-permute-start = (f32[1,72,192]{2,1,0:T(8,128)S(1)}, f32[1,72,192]{2,1,0:T(8,128)S(1)}, u32[]{:S(2)}, u32[]{:S(2)}) collective-permute-start(f32[1,72,192]{2,1,0:T(8,128)S(1)} %fusion.13), channel_id=1, source_target_pairs={{0,4},{1,5},{2,6},{3,7},{4,0},{5,1},{6,2},{7,3},{8,12},{9,13},{10,... | collective-permute-start | bytes 165896 | tf_op jit(solution)/shard_map/ppermute | solution.py:167
  24.9 7.8 %collective-permute-start.1 = (f32[1,72,192]{2,1,0:T(8,128)S(1)}, f32[1,72,192]{2,1,0:T(8,128)S(1)}, u32[]{:S(2)}, u32[]{:S(2)}) collective-permute-start(f32[1,72,192]{2,1,0:T(8,128)S(1)} %fusion.13), channel_id=1, source_target_pairs={{0,8},{1,9},{2,10},{3,11},{4,12},{5,13},{6,14},{7,15},{8,0},{9,1},... | collective-permute-start | bytes 165896 | tf_op jit(solution)/shard_map/ppermute | solution.py:167
  27.5 6.3 %collective-permute-start.2 = (f32[1,72,192]{2,1,0:T(8,128)S(1)}, f32[1,72,192]{2,1,0:T(8,128)S(1)}, u32[]{:S(2)}, u32[]{:S(2)}) collective-permute-start(f32[1,72,192]{2,1,0:T(8,128)S(1)} %fusion.13), channel_id=1, source_target_pairs={{0,12},{1,13},{2,14},{3,15},{4,8},{5,9},{6,10},{7,11},{8,4},{9,5},... | collective-permute-start | bytes 165896 | tf_op jit(solution)/shard_map/ppermute | solution.py:167
  33.7 7.0 %collective-permute-start.3 = (f32[4,72,192]{2,1,0:T(8,128)S(1)}, f32[4,72,192]{2,1,0:T(8,128)S(1)}, u32[]{:S(2)}, u32[]{:S(2)}) collective-permute-start(f32[4,72,192]{2,1,0:T(8,128)S(1)} %pad_maximum_fusion), channel_id=1, source_target_pairs={{0,2},{1,3},{2,0},{3,1},{4,6},{5,7},{6,4},{7,5},{8,10},{9,11},{10,... | collective-permute-start | bytes 663560 | tf_op jit(solution)/shard_map/ppermute | solution.py:167
  41.5 2.2 %collective-permute-start.4 = (f32[8,72,192]{2,1,0:T(8,128)}, f32[8,72,192]{2,1,0:T(8,128)S(1)}, u32[]{:S(2)}, u32[]{:S(2)}) collective-permute-start(f32[8,72,192]{2,1,0:T(8,128)} %get-tuple-element.21), channel_id=1, source_target_pairs={{0,1},{1,0},{2,3},{3,2},{4,5},{5,4},{6,7},{7,6},{8,9},{9,8},{10,11... | collective-permute-start | bytes 1327112 | tf_op jit(solution)/shard_map/ppermute | solution.py:167
  45.3 2.9 %copy-start.4 = (f32[16,64,192]{2,1,0:T(8,128)S(1)}, f32[16,64,192]{2,1,0:T(8,128)}, u32[]{:S(2)}) copy-start(f32[16,64,192]{2,1,0:T(8,128)} %get-tuple-element.18) | copy-start | bytes 2359300
  47.1 1.3 %copy-start.5 = (bf16[1024,1]{1,0:T(8,128)(2,1)S(1)}, bf16[1024,1]{1,0:T(8,128)(2,1)}, u32[]{:S(2)}) copy-start(bf16[1024,1]{1,0:T(8,128)(2,1)} %get-tuple-element.20) | copy-start | bytes 6148
  49.3 0.7 %copy-start.1 = (f32[3,3]{1,0:T(4,128)S(1)}, f32[3,3]{1,0:T(4,128)}, u32[]{:S(2)}) copy-start(f32[3,3]{1,0:T(4,128)} %k_ref.1) | copy-start | bytes 112

commit v15 on v14

--- a/solution.py
+++ b/solution.py
@@ -157,7 +157,7 @@
     buf = x[None]
     bit = group_size.bit_length() - 2
     while bit >= 0:
-        if bit >= 2:
+        if bit % 2:
             flips = [m << (bit - 1) for m in (1, 2, 3)]
             bit -= 2
         else:

time: 51.8 us -> 60.4 us (1.17)
  waiting for transfers between devices: 11.2 us -> 19.4 us
  local copies, waits for them, and re-layouts: 6.76 us -> 4.01 us
  other arithmetic: 4.84 us -> 7.51 us
    ppermute x5 -> x6, waiting for transfers between devices: 11.2 us -> 19.4 us  [gather_wide(): lax.ppermute(buf, 'wide', [(i, i ^ f) for i in range(group_size)])]
    unnamed x25 -> x19, local copies, waits for them, and re-layouts: 4.96 us -> 3 us
    convert_element_type x1, other arithmetic: 0.21 us -> 1.43 us  [per_device(): (centred / jnp.sqrt(jnp.sum(centred * centred, axis=1, keepdims=True) + 1...]
    convert_element_type x1, other arithmetic: 0.01 us -> 0.79 us  [per_device(): rec_id.astype(jnp.float32)]
    concatenate x2 -> x1, local copies, waits for them, and re-layouts: 0.8 us -> 0.02 us  [gather_wide(): buf = jnp.concatenate([buf] + received, axis=0)]
    convert_element_type x1, other arithmetic: 0.01 us -> 0.66 us  [per_device(): seg_dest.astype(jnp.float32)]
    min x1, other arithmetic: 0.01 us -> 0.66 us  [pool_slots(): starts = jnp.clip(seg_start, 0, rows - SEGLEN).astype(jnp.int32)]
    unnamed x1, other arithmetic: 0.63 us -> 0.01 us
  transfers between devices with their start and end apart: 5 -> 6, of which waited for: 4 -> 4; matrix products, arithmetic and copies ran while one was open for 5% -> 0% of each run, Pallas kernels for 0% -> 0%
where the time goes in v15:
time: 60.4 us; the launch traced here: 60.1 us
  waiting for transfers between devices  19.4 us (32%)
  Pallas kernels  18.8 us (31%)
  starting transfers between devices  7.61 us (13%)
  other arithmetic  7.51 us (12%)
  local copies, waits for them, and re-layouts  4.01 us (7%)
  matrix products  2.49 us (4%)
    ppermute x6, waiting for transfers between devices, gather_wide(): lax.ppermute(buf, 'wide', [(i, i ^ f) for i in range(group_size)])  19.4 us
    pallas_call x1, Pallas kernels, pool_slots(): pl.pallas_call(_pool_kernel, out_shape=jax.ShapeDtypeStruct((slots, 2 * C...  17.2 us
    ppermute x6, starting transfers between devices, gather_wide(): lax.ppermute(buf, 'wide', [(i, i ^ f) for i in range(group_size)])  7.61 us
    unnamed x19, local copies, waits for them, and re-layouts  3 us
    pallas_call x1, Pallas kernels, smooth_affinity(): pl.pallas_call(_affinity_kernel, out_shape=jax.ShapeDtypeStruct((height,...  1.65 us
    dot_general x1, matrix products, per_device(): jnp.dot(pooled, proj_weight, precision=PRECISE, preferred_element_type=jn...  1.63 us
    convert_element_type x1, other arithmetic, per_device(): (centred / jnp.sqrt(jnp.sum(centred * centred, axis=1, keepdims=True) + 1...  1.43 us
    convert_element_type x1, other arithmetic, per_device(): rec_hi = (all_rec // 16).astype(jnp.bfloat16)[:, None]  1.23 us
  transfers between devices with their start and end apart: 6, of which 4 were waited for; matrix products, arithmetic and copies ran while one was open for 0% of the time, Pallas kernels for 0%

profile of v15, /device:TPU:0, one launch (start us, length us, event | category | flops | bytes accessed | tf_op | source)
XLA Modules:
  0.0 60.1 jit_solution(965724669100546023)
XLA Ops:
  0.0 0.0 copy-start
  0.0 0.0 copy-start.3
  0.0 0.8 %convert_element_type.88 = f32[64]{0:T(128)S(1)} convert(s32[64]{0:T(128)} %param.14) | non-fusion elementwise | flops 64 | bytes 512 | tf_op jit(solution)/shard_map/convert_element_type | solution.py:184
  0.8 0.7 %convert_element_type.87 = f32[64]{0:T(128)S(1)} convert(s32[64]{0:T(128)} %param.13) | non-fusion elementwise | flops 64 | bytes 512 | tf_op jit(solution)/shard_map/convert_element_type | solution.py:184
  1.5 0.7 %broadcast_clamp_fusion.starts_ref = s32[64]{0:T(128)S(1)} fusion(s32[64]{0:T(128)} %param.12), kind=kLoop, calls=%fused_computation.55 | loop fusion | flops 64 | bytes 512 | tf_op jit(solution)/shard_map/jit(clip)/min | solution.py:81
  2.1 1.4 %copy.24.frames_hbm = f32[2048,80]{1,0:T(8,128)S(1)} copy(f32[2048,80]{0,1:T(8,128)} %param.11) | data formatting | bytes 1310720 | tf_op args[0]
  3.5 0.1 maximum_bitcast_fusion
  3.6 0.0 copy-done.3
  3.6 0.0 copy-start.2
  3.6 1.2 %copy-done.2 = f32[240,1024]{1,0:T(8,128)S(1)} copy-done((f32[240,1024]{1,0:T(8,128)S(1)}, f32[240,1024]{1,0:T(8,128)}, u32[]{:S(2)}) %copy-start.2) | copy-done | bytes 983064
  4.8 17.2 %shard_map.91 = f32[64,2048]{1,0:T(8,128)S(1)} custom-call(s32[64]{0:T(128)S(1)} %broadcast_clamp_fusion.starts_ref, f32[2048,80]{1,0:T(8,128)S(1)} %copy.24.frames_hbm, f32[240,1024]{1,0:T(8,128)S(1)} %copy-done.2, f32[1,1024]{1,0:T(1,128)S(1)} %bitcast.20), custom_call_target="tpu_custom_call" | custom-call | flops 6077546496 | bytes 2162688 | tf_op jit(solution)/shard_map/pallas_call | solution.py:83
  22.0 0.0 copy-done
  22.0 0.0 copy-start.5
  22.0 1.6 %fusion.18 = f32[64,192]{1,0:T(8,128)S(1)} fusion(f32[64,2048]{1,0:T(8,128)S(1)} %shard_map.91, f32[2048,192]{0,1:T(8,128)S(1)} %copy-done), kind=kOutput, calls=%fused_computation.57 | convolution fusion | flops 301989888 | bytes 2146304 | tf_op jit(solution)/shard_map/dot_general | solution.py:181
  23.7 3.1 %collective-permute-start = (f32[1,72,192]{2,1,0:T(8,128)S(1)}, f32[1,72,192]{2,1,0:T(8,128)S(1)}, u32[]{:S(2)}, u32[]{:S(2)}) collective-permute-start(f32[1,72,192]{2,1,0:T(8,128)S(1)} %fusion.13), channel_id=1, source_target_pairs={{0,4},{1,5},{2,6},{3,7},{4,0},{5,1},{6,2},{7,3},{8,12},{9,13},{10,... | collective-permute-start | bytes 165896 | tf_op jit(solution)/shard_map/ppermute | solution.py:167
  26.8 2.6 %collective-permute-start.1 = (f32[1,72,192]{2,1,0:T(8,128)S(1)}, f32[1,72,192]{2,1,0:T(8,128)S(1)}, u32[]{:S(2)}, u32[]{:S(2)}) collective-permute-start(f32[1,72,192]{2,1,0:T(8,128)S(1)} %fusion.13), channel_id=1, source_target_pairs={{0,8},{1,9},{2,10},{3,11},{4,12},{5,13},{6,14},{7,15},{8,0},{9,1},... | collective-permute-start | bytes 165896 | tf_op jit(solution)/shard_map/ppermute | solution.py:167
  29.3 0.0 collective-permute-start.2
  29.4 0.0 copy-done.5
  29.4 0.1 iota_add_fusion
  29.4 0.1 add.87
  29.5 0.0 collective-permute-done
  29.5 5.0 %collective-permute-done.1 = f32[1,72,192]{2,1,0:T(8,128)S(1)} collective-permute-done((f32[1,72,192]{2,1,0:T(8,128)S(1)}, f32[1,72,192]{2,1,0:T(8,128)S(1)}, u32[]{:S(2)}, u32[]{:S(2)}) %collective-permute-start.1) | collective-permute-done | bytes 55328 | tf_op jit(solution)/shard_map/ppermute | solution.py:167
  34.5 1.1 %collective-permute-done.2 = f32[1,72,192]{2,1,0:T(8,128)S(1)} collective-permute-done((f32[1,72,192]{2,1,0:T(8,128)S(1)}, f32[1,72,192]{2,1,0:T(8,128)S(1)}, u32[]{:S(2)}, u32[]{:S(2)}) %collective-permute-start.2) | collective-permute-done | bytes 55328 | tf_op jit(solution)/shard_map/ppermute | solution.py:167
  35.6 0.1 collective-permute-start.3
  35.7 1.6 %collective-permute-start.4 = (f32[4,72,192]{2,1,0:T(8,128)S(1)}, f32[4,72,192]{2,1,0:T(8,128)S(1)}, u32[]{:S(2)}, u32[]{:S(2)}) collective-permute-start(f32[4,72,192]{2,1,0:T(8,128)S(1)} %pad_maximum_fusion), channel_id=1, source_target_pairs={{0,2},{1,3},{2,0},{3,1},{4,6},{5,7},{6,4},{7,5},{8,10},{9,11},{10,... | collective-permute-start | bytes 663560 | tf_op jit(solution)/shard_map/ppermute | solution.py:167
  37.3 0.3 collective-permute-start.5
  37.6 0.0 collective-permute-done.3
  37.6 7.9 %collective-permute-done.4 = f32[4,72,192]{2,1,0:T(8,128)S(1)} collective-permute-done((f32[4,72,192]{2,1,0:T(8,128)S(1)}, f32[4,72,192]{2,1,0:T(8,128)S(1)}, u32[]{:S(2)}, u32[]{:S(2)}) %collective-permute-start.4) | collective-permute-done | bytes 221216 | tf_op jit(solution)/shard_map/ppermute | solution.py:167
  45.6 5.4 %collective-permute-done.5 = f32[4,72,192]{2,1,0:T(8,128)S(1)} collective-permute-done((f32[4,72,192]{2,1,0:T(8,128)S(1)}, f32[4,72,192]{2,1,0:T(8,128)S(1)}, u32[]{:S(2)}, u32[]{:S(2)}) %collective-permute-start.5) | collective-permute-done | bytes 221216 | tf_op jit(solution)/shard_map/ppermute | solution.py:167
  51.0 0.1 reshape.241
  51.1 0.1 slice_convert_fusion.1
  51.2 0.1 convert_element_type.90
  51.3 1.0 %convert_reduce_fusion = s32[1024]{0:T(1024)S(1)} fusion(s32[1024]{0:T(1024)S(1)} %convert_element_type.90, s32[1024]{0:T(1024)S(1)} %add.87), kind=kLoop, calls=%fused_computation | loop fusion | flops 5241856 | bytes 12288 | tf_op jit(solution)/shard_map/reduce_sum | solution.py:211
  52.3 0.5 convert_element_type.100
  52.8 1.2 %fusion.4 = (bf16[1024,1]{1,0:T(8,128)(2,1)S(1)}, bf16[1024,1]{1,0:T(8,128)(2,1)}) fusion(s32[1024,1]{1,0:T(8,128)S(1)} %convert_element_type.100), kind=kLoop, calls=%fused_computation.14 | loop fusion | flops 21504 | bytes 8192 | tf_op jit(solution)/shard_map/convert_element_type | solution.py:218
  54.0 0.2 select_reduce_fusion
  54.3 1.1 %multiply_reduce_fusion = (f32[16,64]{1,0:T(8,128)S(1)}, f32[16,64,192]{2,1,0:T(8,128)}) fusion(f32[192]{0:T(256)S(1)} %broadcast_multiply_fusion, f32[16,72,192]{2,1,0:T(8,128)S(1)} %constant_dynamic-update-slice_fusion), kind=kLoop, calls=%fused_computation.6 | loop fusion | flops 588800 | bytes 1577728 | tf_op jit(solution)/shard_map/reduce_sum | solution.py:206
  55.3 0.0 copy-start.4
  55.4 0.1 sqrt.12
  55.4 1.4 %fusion.2 = bf16[1024,192]{1,0:T(8,128)(2,1)S(1)} fusion(f32[16,64,192]{2,1,0:T(8,128)} %get-tuple-element.18, f32[1024]{0:T(1024)S(1)} %sqrt.12, f32[192]{0:T(256)S(1)} %broadcast_multiply_fusion), kind=kLoop, calls=%fused_computation.5 | loop fusion | flops 589824 | bytes 1184512 | tf_op jit(solution)/shard_map/convert_element_type | solution.py:206
  56.9 0.0 copy-done.4
  56.9 0.9 %fusion = f32[512,194]{0,1:T(8,128)S(1)} fusion(s32[1024]{0:T(1024)S(1)} %add_select_fusion.2, bf16[1024,1]{1,0:T(8,128)(2,1)S(1)} %copy-done.4, bf16[1024,1]{1,0:T(8,128)(2,1)S(1)} %get-tuple-element.19, bf16[1024,192]{1,0:T(8,128)(2,1)S(1)} %fusion.2), kind=kOutput, calls=%fused_computation.2 | convolution fusion | flops 205139968 | bytes 798720 | tf_op jit(solution)/shard_map/dot_general | solution.py:222
  57.7 0.0 copy-start.1
  57.8 0.1 copy.31.col_unit_ref
  58.0 0.1 pad_add_fusion
  58.0 0.1 dynamic-slice_bitcast_fusion
  58.1 0.1 copy.30.row_rec_ref
  58.3 0.2 copy-done.1
  58.4 1.6 %shard_map.92 = f32[32,512]{1,0:T(8,128)} custom-call(f32[3,3]{1,0:T(4,128)S(1)} %copy-done.1, bf16[34,192]{1,0:T(8,128)(2,1)S(1)} %fusion.15.row_unit_ref, bf16[512,192]{1,0:T(8,128)(2,1)S(1)} %copy.31.col_unit_ref, s32[34,1]{1,0:T(8,128)S(1)} %copy.30.row_rec_ref, s32[1,512]{1,0:T(1,128)S(1)} %fusion.21.col_rec_ref), custom_call_target="tpu_custom_call" | custom-call | flops 7012352 | bytes 275200 | tf_op jit(solution)/shard_map/pallas_call | solution.py:133
  (20 shorter events, 0.3 us)
Async XLA Ops:
  0.0 22.0 %copy-start = (f32[2048,192]{0,1:T(8,128)S(1)}, f32[2048,192]{0,1:T(8,128)}, u32[]{:S(2)}) copy-start(f32[2048,192]{0,1:T(8,128)} %param.17) | copy-start | bytes 4718596
  0.0 3.6 %copy-start.3 = (f32[1024]{0:T(1024)S(1)}, f32[1024]{0:T(1024)}, u32[]{:S(2)}) copy-start(f32[1024]{0:T(1024)} %param.16) | copy-start | bytes 12292
  3.6 1.2 %copy-start.2 = (f32[240,1024]{1,0:T(8,128)S(1)}, f32[240,1024]{1,0:T(8,128)}, u32[]{:S(2)}) copy-start(f32[240,1024]{1,0:T(8,128)} %w_hbm.1) | copy-start | bytes 2949124
  22.0 7.3 %copy-start.5 = (s32[16]{0:T(128)S(1)}, s32[16]{0:T(128)}, u32[]{:S(2)}) copy-start(s32[16]{0:T(128)} %constant.85.clone) | copy-start | bytes 196
  23.7 5.9 %collective-permute-start = (f32[1,72,192]{2,1,0:T(8,128)S(1)}, f32[1,72,192]{2,1,0:T(8,128)S(1)}, u32[]{:S(2)}, u32[]{:S(2)}) collective-permute-start(f32[1,72,192]{2,1,0:T(8,128)S(1)} %fusion.13), channel_id=1, source_target_pairs={{0,4},{1,5},{2,6},{3,7},{4,0},{5,1},{6,2},{7,3},{8,12},{9,13},{10,... | collective-permute-start | bytes 165896 | tf_op jit(solution)/shard_map/ppermute | solution.py:167
  26.8 7.8 %collective-permute-start.1 = (f32[1,72,192]{2,1,0:T(8,128)S(1)}, f32[1,72,192]{2,1,0:T(8,128)S(1)}, u32[]{:S(2)}, u32[]{:S(2)}) collective-permute-start(f32[1,72,192]{2,1,0:T(8,128)S(1)} %fusion.13), channel_id=1, source_target_pairs={{0,8},{1,9},{2,10},{3,11},{4,12},{5,13},{6,14},{7,15},{8,0},{9,1},... | collective-permute-start | bytes 165896 | tf_op jit(solution)/shard_map/ppermute | solution.py:167
  29.3 6.3 %collective-permute-start.2 = (f32[1,72,192]{2,1,0:T(8,128)S(1)}, f32[1,72,192]{2,1,0:T(8,128)S(1)}, u32[]{:S(2)}, u32[]{:S(2)}) collective-permute-start(f32[1,72,192]{2,1,0:T(8,128)S(1)} %fusion.13), channel_id=1, source_target_pairs={{0,12},{1,13},{2,14},{3,15},{4,8},{5,9},{6,10},{7,11},{8,4},{9,5},... | collective-permute-start | bytes 165896 | tf_op jit(solution)/shard_map/ppermute | solution.py:167
  35.6 2.0 %collective-permute-start.3 = (f32[4,72,192]{2,1,0:T(8,128)S(1)}, f32[4,72,192]{2,1,0:T(8,128)S(1)}, u32[]{:S(2)}, u32[]{:S(2)}) collective-permute-start(f32[4,72,192]{2,1,0:T(8,128)S(1)} %pad_maximum_fusion), channel_id=1, source_target_pairs={{0,1},{1,0},{2,3},{3,2},{4,5},{5,4},{6,7},{7,6},{8,9},{9,8},{10,11... | collective-permute-start | bytes 663560 | tf_op jit(solution)/shard_map/ppermute | solution.py:167
  35.7 9.9 %collective-permute-start.4 = (f32[4,72,192]{2,1,0:T(8,128)S(1)}, f32[4,72,192]{2,1,0:T(8,128)S(1)}, u32[]{:S(2)}, u32[]{:S(2)}) collective-permute-start(f32[4,72,192]{2,1,0:T(8,128)S(1)} %pad_maximum_fusion), channel_id=1, source_target_pairs={{0,2},{1,3},{2,0},{3,1},{4,6},{5,7},{6,4},{7,5},{8,10},{9,11},{10,... | collective-permute-start | bytes 663560 | tf_op jit(solution)/shard_map/ppermute | solution.py:167
  37.3 13.7 %collective-permute-start.5 = (f32[4,72,192]{2,1,0:T(8,128)S(1)}, f32[4,72,192]{2,1,0:T(8,128)S(1)}, u32[]{:S(2)}, u32[]{:S(2)}) collective-permute-start(f32[4,72,192]{2,1,0:T(8,128)S(1)} %pad_maximum_fusion), channel_id=1, source_target_pairs={{0,3},{1,2},{2,1},{3,0},{4,7},{5,6},{6,5},{7,4},{8,11},{9,10},{10,... | collective-permute-start | bytes 663560 | tf_op jit(solution)/shard_map/ppermute | solution.py:167
  55.3 1.5 %copy-start.4 = (bf16[1024,1]{1,0:T(8,128)(2,1)S(1)}, bf16[1024,1]{1,0:T(8,128)(2,1)}, u32[]{:S(2)}) copy-start(bf16[1024,1]{1,0:T(8,128)(2,1)} %get-tuple-element.20) | copy-start | bytes 6148
  57.7 0.7 %copy-start.1 = (f32[3,3]{1,0:T(4,128)S(1)}, f32[3,3]{1,0:T(4,128)}, u32[]{:S(2)}) copy-start(f32[3,3]{1,0:T(4,128)} %k_ref.1) | copy-start | bytes 112

commit v16 on v14

--- a/solution.py
+++ b/solution.py
@@ -215,13 +215,9 @@
     slot_of_pos = jnp.sum(jnp.where(picks, row_ids[None, :], 0), axis=1)
 
     if total_rows * slot_total <= ONE_HOT_LIMIT:
-        rec_hi = (all_rec // 16).astype(jnp.bfloat16)[:, None]
-        rec_lo = (all_rec % 16).astype(jnp.bfloat16)[:, None]
-        unit_ext = jnp.concatenate([unit, rec_hi, rec_lo], axis=1)
         selector = picks.astype(jnp.bfloat16)
-        col_ext = jnp.dot(selector, unit_ext, preferred_element_type=jnp.float32)
-        col_unit = col_ext[:, :EMB].astype(jnp.bfloat16)
-        col_rec = (col_ext[:, EMB] * 16 + col_ext[:, EMB + 1]).astype(jnp.int32)
+        col_unit = jnp.dot(selector, unit, preferred_element_type=jnp.float32).astype(jnp.bfloat16)
+        col_rec = jnp.sum(jnp.where(picks, all_rec[None, :], 0), axis=1)
     else:
         col_unit = jnp.take(unit, slot_of_pos, axis=0)
         col_rec = jnp.take(all_rec, slot_of_pos, axis=0)

time: 51.8 us -> 51.1 us (0.986)
  local copies, waits for them, and re-layouts: 6.76 us -> 6.2 us
    convert_element_type x3 -> x0, other arithmetic: 1.26 us -> none  [the longest x1 1.24 us: per_device(): rec_hi = (all_rec // 16).astype(jnp.bfloat16)[:, None]]
    convert_element_type x1, other arithmetic: 0.21 us -> 1.43 us  [per_device(): (centred / jnp.sqrt(jnp.sum(centred * centred, axis=1, keepdims=True) + 1...]
    unnamed x25 -> x20, local copies, waits for them, and re-layouts: 4.96 us -> 4.82 us
where the time goes in v16:
time: 51.1 us; the launch traced here: 50.9 us
  Pallas kernels  18.8 us (37%)
  waiting for transfers between devices  11.2 us (22%)
  starting transfers between devices  7.27 us (14%)
  local copies, waits for them, and re-layouts  6.2 us (12%)
  other arithmetic  5.11 us (10%)
  matrix products  2.1 us (4%)
    pallas_call x1, Pallas kernels, pool_slots(): pl.pallas_call(_pool_kernel, out_shape=jax.ShapeDtypeStruct((slots, 2 * C...  17.2 us
    ppermute x5, waiting for transfers between devices, gather_wide(): lax.ppermute(buf, 'wide', [(i, i ^ f) for i in range(group_size)])  11.2 us
    ppermute x5, starting transfers between devices, gather_wide(): lax.ppermute(buf, 'wide', [(i, i ^ f) for i in range(group_size)])  7.27 us
    unnamed x20, local copies, waits for them, and re-layouts  4.82 us
    pallas_call x1, Pallas kernels, smooth_affinity(): pl.pallas_call(_affinity_kernel, out_shape=jax.ShapeDtypeStruct((height,...  1.65 us
    dot_general x1, matrix products, per_device(): jnp.dot(pooled, proj_weight, precision=PRECISE, preferred_element_type=jn...  1.64 us
    convert_element_type x1, other arithmetic, per_device(): (centred / jnp.sqrt(jnp.sum(centred * centred, axis=1, keepdims=True) + 1...  1.43 us
    reduce_sum x1, other arithmetic, per_device(): jnp.sum(centred * centred, axis=1, keepdims=True) + 1e-06  1.07 us
  transfers between devices with their start and end apart: 5, of which 4 were waited for; matrix products, arithmetic and copies ran while one was open for 5% of the time, Pallas kernels for 0%

profile of v16, /device:TPU:0, one launch (start us, length us, event | category | flops | bytes accessed | tf_op | source)
XLA Modules:
  0.0 50.9 jit_solution(1405527995624583621)
XLA Ops:
  0.0 0.0 copy-start
  0.0 0.0 copy-start.4
  0.0 0.0 copy-start.5
  0.0 0.0 copy-start.6
  0.0 0.0 copy-start.3
  0.0 1.5 %copy.13.frames_hbm = f32[2048,80]{1,0:T(8,128)S(1)} copy(f32[2048,80]{0,1:T(8,128)} %param.11) | data formatting | bytes 1310720 | tf_op args[0]
  1.6 0.0 copy-done.4
  1.6 0.0 copy-done.5
  1.6 0.0 copy-done.6
  1.6 0.0 copy-done.3
  1.6 0.0 copy-start.2
  1.6 1.2 %copy-done.2 = f32[240,1024]{1,0:T(8,128)S(1)} copy-done((f32[240,1024]{1,0:T(8,128)S(1)}, f32[240,1024]{1,0:T(8,128)}, u32[]{:S(2)}) %copy-start.2) | copy-done | bytes 983064
  2.8 17.2 %shard_map.91 = f32[64,2048]{1,0:T(8,128)S(1)} custom-call(s32[64]{0:T(128)S(1)} %broadcast_clamp_fusion.starts_ref, f32[2048,80]{1,0:T(8,128)S(1)} %copy.13.frames_hbm, f32[240,1024]{1,0:T(8,128)S(1)} %copy-done.2, f32[1,1024]{1,0:T(1,128)S(1)} %bitcast.22), custom_call_target="tpu_custom_call" | custom-call | flops 6077546496 | bytes 2162688 | tf_op jit(solution)/shard_map/pallas_call | solution.py:83
  20.0 0.0 copy-done
  20.0 1.6 %fusion.8 = f32[64,192]{1,0:T(8,128)S(1)} fusion(f32[64,2048]{1,0:T(8,128)S(1)} %shard_map.91, f32[2048,192]{0,1:T(8,128)S(1)} %copy-done), kind=kOutput, calls=%fused_computation.43 | convolution fusion | flops 301989888 | bytes 2146304 | tf_op jit(solution)/shard_map/dot_general | solution.py:181
  21.7 0.1 maximum_bitcast_fusion
  21.7 0.0 copy-start.7
  21.8 3.1 %collective-permute-start = (f32[1,72,192]{2,1,0:T(8,128)S(1)}, f32[1,72,192]{2,1,0:T(8,128)S(1)}, u32[]{:S(2)}, u32[]{:S(2)}) collective-permute-start(f32[1,72,192]{2,1,0:T(8,128)S(1)} %fusion.5), channel_id=1, source_target_pairs={{0,4},{1,5},{2,6},{3,7},{4,0},{5,1},{6,2},{7,3},{8,12},{9,13},{10,... | collective-permute-start | bytes 165896 | tf_op jit(solution)/shard_map/ppermute | solution.py:167
  24.9 2.6 %collective-permute-start.1 = (f32[1,72,192]{2,1,0:T(8,128)S(1)}, f32[1,72,192]{2,1,0:T(8,128)S(1)}, u32[]{:S(2)}, u32[]{:S(2)}) collective-permute-start(f32[1,72,192]{2,1,0:T(8,128)S(1)} %fusion.5), channel_id=1, source_target_pairs={{0,8},{1,9},{2,10},{3,11},{4,12},{5,13},{6,14},{7,15},{8,0},{9,1},... | collective-permute-start | bytes 165896 | tf_op jit(solution)/shard_map/ppermute | solution.py:167
  27.4 0.0 collective-permute-start.2
  27.4 0.6 %constant_dynamic-update-slice_fusion.4 = (f32[8,72,192]{2,1,0:T(8,128)}, f32[16,72,192]{2,1,0:T(8,128)S(1)}) fusion(f32[1,128]{1,0:T(1,128)S(1)} %maximum_bitcast_fusion, f32[64,192]{1,0:T(8,128)S(1)} %fusion.8), kind=kLoop, calls=%fused_computation.22 | loop fusion | flops 41470 | bytes 197120
  28.1 0.0 collective-permute-done
  28.1 4.5 %collective-permute-done.1 = f32[1,72,192]{2,1,0:T(8,128)S(1)} collective-permute-done((f32[1,72,192]{2,1,0:T(8,128)S(1)}, f32[1,72,192]{2,1,0:T(8,128)S(1)}, u32[]{:S(2)}, u32[]{:S(2)}) %collective-permute-start.1) | collective-permute-done | bytes 55328 | tf_op jit(solution)/shard_map/ppermute | solution.py:167
  32.6 1.1 %collective-permute-done.2 = f32[1,72,192]{2,1,0:T(8,128)S(1)} collective-permute-done((f32[1,72,192]{2,1,0:T(8,128)S(1)}, f32[1,72,192]{2,1,0:T(8,128)S(1)}, u32[]{:S(2)}, u32[]{:S(2)}) %collective-permute-start.2) | collective-permute-done | bytes 55328 | tf_op jit(solution)/shard_map/ppermute | solution.py:167
  33.7 1.6 %collective-permute-start.3 = (f32[4,72,192]{2,1,0:T(8,128)S(1)}, f32[4,72,192]{2,1,0:T(8,128)S(1)}, u32[]{:S(2)}, u32[]{:S(2)}) collective-permute-start(f32[4,72,192]{2,1,0:T(8,128)S(1)} %pad_maximum_fusion), channel_id=1, source_target_pairs={{0,2},{1,3},{2,0},{3,1},{4,6},{5,7},{6,4},{7,5},{8,10},{9,11},{10,... | collective-permute-start | bytes 663560 | tf_op jit(solution)/shard_map/ppermute | solution.py:167
  35.3 0.6 %constant_dynamic-update-slice_fusion.3 = (f32[8,72,192]{2,1,0:T(8,128)}, f32[16,72,192]{2,1,0:T(8,128)S(1)}) fusion(f32[8,72,192]{2,1,0:T(8,128)} %get-tuple-element.29, f32[1,72,192]{2,1,0:T(8,128)S(1)} %collective-permute-done, f32[16,72,192]{2,1,0:T(8,128)S(1)} %get-tuple-element.30), kind=kLoop, calls=%fused_computation.21 | loop fusion | bytes 221184
  35.9 0.6 %constant_dynamic-update-slice_fusion.2 = (f32[8,72,192]{2,1,0:T(8,128)}, f32[16,72,192]{2,1,0:T(8,128)S(1)}) fusion(f32[8,72,192]{2,1,0:T(8,128)} %get-tuple-element.27, f32[1,72,192]{2,1,0:T(8,128)S(1)} %collective-permute-done.1, f32[16,72,192]{2,1,0:T(8,128)S(1)} %get-tuple-element.28), kind=kLoop, calls=%fused_computation.20 | loop fusion | bytes 221184
  36.6 0.6 %constant_dynamic-update-slice_fusion.1 = (f32[8,72,192]{2,1,0:T(8,128)}, f32[16,72,192]{2,1,0:T(8,128)S(1)}) fusion(f32[8,72,192]{2,1,0:T(8,128)} %get-tuple-element.25, f32[1,72,192]{2,1,0:T(8,128)S(1)} %collective-permute-done.2, f32[16,72,192]{2,1,0:T(8,128)S(1)} %get-tuple-element.26), kind=kLoop, calls=%fused_computation.19 | loop fusion | bytes 221184
  37.2 3.5 %collective-permute-done.3 = f32[4,72,192]{2,1,0:T(8,128)S(1)} collective-permute-done((f32[4,72,192]{2,1,0:T(8,128)S(1)}, f32[4,72,192]{2,1,0:T(8,128)S(1)}, u32[]{:S(2)}, u32[]{:S(2)}) %collective-permute-start.3) | collective-permute-done | bytes 221216 | tf_op jit(solution)/shard_map/ppermute | solution.py:167
  40.7 0.8 %constant_dynamic-update-slice_fusion = (f32[8,72,192]{2,1,0:T(8,128)}, f32[16,72,192]{2,1,0:T(8,128)S(1)}) fusion(f32[8,72,192]{2,1,0:T(8,128)} %get-tuple-element.23, f32[4,72,192]{2,1,0:T(8,128)S(1)} %collective-permute-done.3, f32[16,72,192]{2,1,0:T(8,128)S(1)} %get-tuple-element.24), kind=kLoop, calls=%fused_computation.18 | loop fusion | bytes 884736 | tf_op jit(solution)/shard_map/concatenate | solution.py:169
  41.5 0.0 collective-permute-start.4
  41.5 0.0 copy-done.7
  41.5 0.1 iota_add_fusion
  41.6 0.1 add.54
  41.6 2.1 %collective-permute-done.4 = f32[8,72,192]{2,1,0:T(8,128)S(1)} collective-permute-done((f32[8,72,192]{2,1,0:T(8,128)}, f32[8,72,192]{2,1,0:T(8,128)S(1)}, u32[]{:S(2)}, u32[]{:S(2)}) %collective-permute-start.4) | collective-permute-done | bytes 442400 | tf_op jit(solution)/shard_map/ppermute | solution.py:167
  43.8 0.1 reshape.133
  43.9 0.1 slice_convert_fusion
  44.0 0.1 convert_element_type.49
  44.0 1.0 %convert_reduce_fusion = s32[1024]{0:T(1024)S(1)} fusion(s32[1024]{0:T(1024)S(1)} %convert_element_type.49, s32[1024]{0:T(1024)S(1)} %add.54), kind=kLoop, calls=%fused_computation | loop fusion | flops 5241856 | bytes 12288 | tf_op jit(solution)/shard_map/reduce_sum | solution.py:211
  45.1 0.1 convert_element_type.54
  45.1 0.3 select_reduce_fusion
  45.4 0.1 pad_add_fusion
  45.5 0.1 dynamic-slice_bitcast_fusion
  45.6 0.1 copy.15.row_rec_ref
  45.7 0.2 select_reduce_fusion.1
  45.9 1.1 %multiply_reduce_fusion = (f32[16,64]{1,0:T(8,128)S(1)}, f32[16,64,192]{2,1,0:T(8,128)}) fusion(f32[192]{0:T(256)S(1)} %broadcast_multiply_fusion, f32[16,72,192]{2,1,0:T(8,128)S(1)} %constant_dynamic-update-slice_fusion.5), kind=kLoop, calls=%fused_computation.8 | loop fusion | flops 588800 | bytes 1577728 | tf_op jit(solution)/shard_map/reduce_sum | solution.py:206
  47.0 0.1 sqrt.12
  47.1 1.4 %fusion.3 = bf16[1024,192]{1,0:T(8,128)(2,1)S(1)} fusion(f32[16,64,192]{2,1,0:T(8,128)} %get-tuple-element.18, f32[1024]{0:T(1024)S(1)} %sqrt.12, f32[192]{0:T(256)S(1)} %broadcast_multiply_fusion), kind=kLoop, calls=%fused_computation.7 | loop fusion | flops 589824 | bytes 1184512 | tf_op jit(solution)/shard_map/convert_element_type | solution.py:206
  48.5 0.0 copy-start.1
  48.5 0.5 fusion.1.col_unit_ref
  49.1 0.1 copy-done.1
  49.2 1.6 %shard_map.92 = f32[32,512]{1,0:T(8,128)} custom-call(f32[3,3]{1,0:T(4,128)S(1)} %copy-done.1, bf16[34,192]{1,0:T(8,128)(2,1)S(1)} %fusion.7.row_unit_ref, bf16[512,192]{1,0:T(8,128)(2,1)S(1)} %fusion.1.col_unit_ref, s32[34,1]{1,0:T(8,128)S(1)} %copy.15.row_rec_ref, s32[1,512]{1,0:T(1,128)S(1)} %bitcast.21), custom_call_target="tpu_custom_call" | custom-call | flops 7012352 | bytes 275200 | tf_op jit(solution)/shard_map/pallas_call | solution.py:133
  (14 shorter events, 0.2 us)
Async XLA Ops:
  0.0 20.0 %copy-start = (f32[2048,192]{0,1:T(8,128)S(1)}, f32[2048,192]{0,1:T(8,128)}, u32[]{:S(2)}) copy-start(f32[2048,192]{0,1:T(8,128)} %param.17) | copy-start | bytes 4718596
  0.0 1.6 %copy-start.4 = (s32[64]{0:T(128)S(1)}, s32[64]{0:T(128)}, u32[]{:S(2)}) copy-start(s32[64]{0:T(128)} %param.12) | copy-start | bytes 772
  0.0 1.6 %copy-start.5 = (s32[64]{0:T(128)S(1)}, s32[64]{0:T(128)}, u32[]{:S(2)}) copy-start(s32[64]{0:T(128)} %param.13) | copy-start | bytes 772
  0.0 1.6 %copy-start.6 = (s32[64]{0:T(128)S(1)}, s32[64]{0:T(128)}, u32[]{:S(2)}) copy-start(s32[64]{0:T(128)} %param.14) | copy-start | bytes 772
  0.0 1.6 %copy-start.3 = (f32[1024]{0:T(1024)S(1)}, f32[1024]{0:T(1024)}, u32[]{:S(2)}) copy-start(f32[1024]{0:T(1024)} %param.16) | copy-start | bytes 12292
  1.6 1.2 %copy-start.2 = (f32[240,1024]{1,0:T(8,128)S(1)}, f32[240,1024]{1,0:T(8,128)}, u32[]{:S(2)}) copy-start(f32[240,1024]{1,0:T(8,128)} %w_hbm.1) | copy-start | bytes 2949124
  21.7 19.7 %copy-start.7 = (s32[16]{0:T(128)S(1)}, s32[16]{0:T(128)}, u32[]{:S(2)}) copy-start(s32[16]{0:T(128)} %constant.57.clone) | copy-start | bytes 196
  21.8 6.3 %collective-permute-start = (f32[1,72,192]{2,1,0:T(8,128)S(1)}, f32[1,72,192]{2,1,0:T(8,128)S(1)}, u32[]{:S(2)}, u32[]{:S(2)}) collective-permute-start(f32[1,72,192]{2,1,0:T(8,128)S(1)} %fusion.5), channel_id=1, source_target_pairs={{0,4},{1,5},{2,6},{3,7},{4,0},{5,1},{6,2},{7,3},{8,12},{9,13},{10,... | collective-permute-start | bytes 165896 | tf_op jit(solution)/shard_map/ppermute | solution.py:167
  24.9 7.8 %collective-permute-start.1 = (f32[1,72,192]{2,1,0:T(8,128)S(1)}, f32[1,72,192]{2,1,0:T(8,128)S(1)}, u32[]{:S(2)}, u32[]{:S(2)}) collective-permute-start(f32[1,72,192]{2,1,0:T(8,128)S(1)} %fusion.5), channel_id=1, source_target_pairs={{0,8},{1,9},{2,10},{3,11},{4,12},{5,13},{6,14},{7,15},{8,0},{9,1},... | collective-permute-start | bytes 165896 | tf_op jit(solution)/shard_map/ppermute | solution.py:167
  27.4 6.3 %collective-permute-start.2 = (f32[1,72,192]{2,1,0:T(8,128)S(1)}, f32[1,72,192]{2,1,0:T(8,128)S(1)}, u32[]{:S(2)}, u32[]{:S(2)}) collective-permute-start(f32[1,72,192]{2,1,0:T(8,128)S(1)} %fusion.5), channel_id=1, source_target_pairs={{0,12},{1,13},{2,14},{3,15},{4,8},{5,9},{6,10},{7,11},{8,4},{9,5},... | collective-permute-start | bytes 165896 | tf_op jit(solution)/shard_map/ppermute | solution.py:167
  33.7 7.0 %collective-permute-start.3 = (f32[4,72,192]{2,1,0:T(8,128)S(1)}, f32[4,72,192]{2,1,0:T(8,128)S(1)}, u32[]{:S(2)}, u32[]{:S(2)}) collective-permute-start(f32[4,72,192]{2,1,0:T(8,128)S(1)} %pad_maximum_fusion), channel_id=1, source_target_pairs={{0,2},{1,3},{2,0},{3,1},{4,6},{5,7},{6,4},{7,5},{8,10},{9,11},{10,... | collective-permute-start | bytes 663560 | tf_op jit(solution)/shard_map/ppermute | solution.py:167
  41.5 2.2 %collective-permute-start.4 = (f32[8,72,192]{2,1,0:T(8,128)}, f32[8,72,192]{2,1,0:T(8,128)S(1)}, u32[]{:S(2)}, u32[]{:S(2)}) collective-permute-start(f32[8,72,192]{2,1,0:T(8,128)} %get-tuple-element.19), channel_id=1, source_target_pairs={{0,1},{1,0},{2,3},{3,2},{4,5},{5,4},{6,7},{7,6},{8,9},{9,8},{10,11... | collective-permute-start | bytes 1327112 | tf_op jit(solution)/shard_map/ppermute | solution.py:167
  48.5 0.7 %copy-start.1 = (f32[3,3]{1,0:T(4,128)S(1)}, f32[3,3]{1,0:T(4,128)}, u32[]{:S(2)}) copy-start(f32[3,3]{1,0:T(4,128)} %k_ref.1) | copy-start | bytes 112

commit v17 on v16

--- a/solution.py
+++ b/solution.py
@@ -103,7 +103,12 @@
             transcendentals=slots * CH,
             bytes_accessed=rows * FEAT * 4 + 3 * FEAT * CH * 4 + slots * 2 * CH * 4,
         ),
-    )(starts, frames, conv_weight, conv_bias.reshape(1, CH))
+    )(
+        starts,
+        frames,
+        pltpu.with_memory_space_constraint(conv_weight, pltpu.MemorySpace.HBM),
+        conv_bias.reshape(1, CH),
+    )
 
 
 def _affinity_kernel(k_ref, row_unit_ref, col_unit_ref, row_rec_ref, col_rec_ref, out_ref, pad_ref):

time: 51.1 us -> 50.2 us (0.982)
  local copies, waits for them, and re-layouts: 6.2 us -> 4.99 us
    unnamed x20 -> x18, local copies, waits for them, and re-layouts: 4.82 us -> 3.62 us
where the time goes in v17:
time: 50.2 us; the launch traced here: 49.9 us
  Pallas kernels  19.1 us (38%)
  waiting for transfers between devices  11.2 us (22%)
  starting transfers between devices  7.27 us (14%)
  other arithmetic  5.09 us (10%)
  local copies, waits for them, and re-layouts  4.99 us (10%)
  matrix products  2.1 us (4%)
    pallas_call x1, Pallas kernels, pool_slots(): pl.pallas_call(_pool_kernel, out_shape=jax.ShapeDtypeStruct((slots, 2 * C...  17.5 us
    ppermute x5, waiting for transfers between devices, gather_wide(): lax.ppermute(buf, 'wide', [(i, i ^ f) for i in range(group_size)])  11.2 us
    ppermute x5, starting transfers between devices, gather_wide(): lax.ppermute(buf, 'wide', [(i, i ^ f) for i in range(group_size)])  7.27 us
    unnamed x18, local copies, waits for them, and re-layouts  3.62 us
    pallas_call x1, Pallas kernels, smooth_affinity(): pl.pallas_call(_affinity_kernel, out_shape=jax.ShapeDtypeStruct((height,...  1.65 us
    dot_general x1, matrix products, per_device(): jnp.dot(pooled, proj_weight, precision=PRECISE, preferred_element_type=jn...  1.63 us
    convert_element_type x1, other arithmetic, per_device(): (centred / jnp.sqrt(jnp.sum(centred * centred, axis=1, keepdims=True) + 1...  1.43 us
    reduce_sum x1, other arithmetic, per_device(): jnp.sum(centred * centred, axis=1, keepdims=True) + 1e-06  1.06 us
  transfers between devices with their start and end apart: 5, of which 4 were waited for; matrix products, arithmetic and copies ran while one was open for 5% of the time, Pallas kernels for 0%

profile of v17, /device:TPU:0, one launch (start us, length us, event | category | flops | bytes accessed | tf_op | source)
XLA Modules:
  0.0 49.9 jit_solution(4972528381027072991)
XLA Ops:
  0.0 0.0 copy-start
  0.0 0.0 copy-start.3
  0.0 0.0 copy-start.4
  0.0 0.0 copy-start.5
  0.0 0.0 copy-start.2
  0.0 1.5 %copy.13.frames_hbm = f32[2048,80]{1,0:T(8,128)S(1)} copy(f32[2048,80]{0,1:T(8,128)} %param.11) | data formatting | bytes 1310720 | tf_op args[0]
  1.6 0.0 copy-done.3
  1.6 0.0 copy-done.4
  1.6 0.0 copy-done.5
  1.6 0.0 copy-done.2
  1.6 17.5 %shard_map.91 = f32[64,2048]{1,0:T(8,128)S(1)} custom-call(s32[64]{0:T(128)S(1)} %broadcast_clamp_fusion.starts_ref, f32[2048,80]{1,0:T(8,128)S(1)} %copy.13.frames_hbm, f32[240,1024]{1,0:T(8,128)} %w_hbm.1, f32[1,1024]{1,0:T(1,128)S(1)} %bitcast.22), custom_call_target="tpu_custom_call" | custom-call | flops 6077546496 | bytes 2162688 | tf_op jit(solution)/shard_map/pallas_call | solution.py:83
  19.1 0.0 copy-done
  19.1 1.6 %fusion.8 = f32[64,192]{1,0:T(8,128)S(1)} fusion(f32[64,2048]{1,0:T(8,128)S(1)} %shard_map.91, f32[2048,192]{0,1:T(8,128)S(1)} %copy-done), kind=kOutput, calls=%fused_computation.43 | convolution fusion | flops 301989888 | bytes 2146304 | tf_op jit(solution)/shard_map/dot_general | solution.py:186
  20.7 0.1 maximum_bitcast_fusion
  20.8 0.0 copy-start.6
  20.8 3.1 %collective-permute-start = (f32[1,72,192]{2,1,0:T(8,128)S(1)}, f32[1,72,192]{2,1,0:T(8,128)S(1)}, u32[]{:S(2)}, u32[]{:S(2)}) collective-permute-start(f32[1,72,192]{2,1,0:T(8,128)S(1)} %fusion.5), channel_id=1, source_target_pairs={{0,4},{1,5},{2,6},{3,7},{4,0},{5,1},{6,2},{7,3},{8,12},{9,13},{10,... | collective-permute-start | bytes 165896 | tf_op jit(solution)/shard_map/ppermute | solution.py:172
  23.9 2.6 %collective-permute-start.1 = (f32[1,72,192]{2,1,0:T(8,128)S(1)}, f32[1,72,192]{2,1,0:T(8,128)S(1)}, u32[]{:S(2)}, u32[]{:S(2)}) collective-permute-start(f32[1,72,192]{2,1,0:T(8,128)S(1)} %fusion.5), channel_id=1, source_target_pairs={{0,8},{1,9},{2,10},{3,11},{4,12},{5,13},{6,14},{7,15},{8,0},{9,1},... | collective-permute-start | bytes 165896 | tf_op jit(solution)/shard_map/ppermute | solution.py:172
  26.5 0.0 collective-permute-start.2
  26.5 0.6 %constant_dynamic-update-slice_fusion.4 = (f32[8,72,192]{2,1,0:T(8,128)}, f32[16,72,192]{2,1,0:T(8,128)S(1)}) fusion(f32[1,128]{1,0:T(1,128)S(1)} %maximum_bitcast_fusion, f32[64,192]{1,0:T(8,128)S(1)} %fusion.8), kind=kLoop, calls=%fused_computation.22 | loop fusion | flops 41470 | bytes 197120
  27.2 0.0 collective-permute-done
  27.2 4.6 %collective-permute-done.1 = f32[1,72,192]{2,1,0:T(8,128)S(1)} collective-permute-done((f32[1,72,192]{2,1,0:T(8,128)S(1)}, f32[1,72,192]{2,1,0:T(8,128)S(1)}, u32[]{:S(2)}, u32[]{:S(2)}) %collective-permute-start.1) | collective-permute-done | bytes 55328 | tf_op jit(solution)/shard_map/ppermute | solution.py:172
  31.7 1.1 %collective-permute-done.2 = f32[1,72,192]{2,1,0:T(8,128)S(1)} collective-permute-done((f32[1,72,192]{2,1,0:T(8,128)S(1)}, f32[1,72,192]{2,1,0:T(8,128)S(1)}, u32[]{:S(2)}, u32[]{:S(2)}) %collective-permute-start.2) | collective-permute-done | bytes 55328 | tf_op jit(solution)/shard_map/ppermute | solution.py:172
  32.8 1.6 %collective-permute-start.3 = (f32[4,72,192]{2,1,0:T(8,128)S(1)}, f32[4,72,192]{2,1,0:T(8,128)S(1)}, u32[]{:S(2)}, u32[]{:S(2)}) collective-permute-start(f32[4,72,192]{2,1,0:T(8,128)S(1)} %pad_maximum_fusion), channel_id=1, source_target_pairs={{0,2},{1,3},{2,0},{3,1},{4,6},{5,7},{6,4},{7,5},{8,10},{9,11},{10,... | collective-permute-start | bytes 663560 | tf_op jit(solution)/shard_map/ppermute | solution.py:172
  34.4 0.6 %constant_dynamic-update-slice_fusion.3 = (f32[8,72,192]{2,1,0:T(8,128)}, f32[16,72,192]{2,1,0:T(8,128)S(1)}) fusion(f32[8,72,192]{2,1,0:T(8,128)} %get-tuple-element.29, f32[1,72,192]{2,1,0:T(8,128)S(1)} %collective-permute-done, f32[16,72,192]{2,1,0:T(8,128)S(1)} %get-tuple-element.30), kind=kLoop, calls=%fused_computation.21 | loop fusion | bytes 221184
  35.0 0.6 %constant_dynamic-update-slice_fusion.2 = (f32[8,72,192]{2,1,0:T(8,128)}, f32[16,72,192]{2,1,0:T(8,128)S(1)}) fusion(f32[8,72,192]{2,1,0:T(8,128)} %get-tuple-element.27, f32[1,72,192]{2,1,0:T(8,128)S(1)} %collective-permute-done.1, f32[16,72,192]{2,1,0:T(8,128)S(1)} %get-tuple-element.28), kind=kLoop, calls=%fused_computation.20 | loop fusion | bytes 221184
  35.7 0.6 %constant_dynamic-update-slice_fusion.1 = (f32[8,72,192]{2,1,0:T(8,128)}, f32[16,72,192]{2,1,0:T(8,128)S(1)}) fusion(f32[8,72,192]{2,1,0:T(8,128)} %get-tuple-element.25, f32[1,72,192]{2,1,0:T(8,128)S(1)} %collective-permute-done.2, f32[16,72,192]{2,1,0:T(8,128)S(1)} %get-tuple-element.26), kind=kLoop, calls=%fused_computation.19 | loop fusion | bytes 221184
  36.3 3.5 %collective-permute-done.3 = f32[4,72,192]{2,1,0:T(8,128)S(1)} collective-permute-done((f32[4,72,192]{2,1,0:T(8,128)S(1)}, f32[4,72,192]{2,1,0:T(8,128)S(1)}, u32[]{:S(2)}, u32[]{:S(2)}) %collective-permute-start.3) | collective-permute-done | bytes 221216 | tf_op jit(solution)/shard_map/ppermute | solution.py:172
  39.8 0.8 %constant_dynamic-update-slice_fusion = (f32[8,72,192]{2,1,0:T(8,128)}, f32[16,72,192]{2,1,0:T(8,128)S(1)}) fusion(f32[8,72,192]{2,1,0:T(8,128)} %get-tuple-element.23, f32[4,72,192]{2,1,0:T(8,128)S(1)} %collective-permute-done.3, f32[16,72,192]{2,1,0:T(8,128)S(1)} %get-tuple-element.24), kind=kLoop, calls=%fused_computation.18 | loop fusion | bytes 884736 | tf_op jit(solution)/shard_map/concatenate | solution.py:174
  40.6 0.0 collective-permute-start.4
  40.6 0.0 copy-done.6
  40.6 0.1 iota_add_fusion
  40.6 0.1 add.54
  40.7 2.1 %collective-permute-done.4 = f32[8,72,192]{2,1,0:T(8,128)S(1)} collective-permute-done((f32[8,72,192]{2,1,0:T(8,128)}, f32[8,72,192]{2,1,0:T(8,128)S(1)}, u32[]{:S(2)}, u32[]{:S(2)}) %collective-permute-start.4) | collective-permute-done | bytes 442400 | tf_op jit(solution)/shard_map/ppermute | solution.py:172
  42.8 0.1 reshape.133
  42.9 0.1 slice_convert_fusion
  43.0 0.1 convert_element_type.49
  43.1 1.0 %convert_reduce_fusion = s32[1024]{0:T(1024)S(1)} fusion(s32[1024]{0:T(1024)S(1)} %convert_element_type.49, s32[1024]{0:T(1024)S(1)} %add.54), kind=kLoop, calls=%fused_computation | loop fusion | flops 5241856 | bytes 12288 | tf_op jit(solution)/shard_map/reduce_sum | solution.py:216
  44.1 0.1 convert_element_type.54
  44.2 0.3 select_reduce_fusion
  44.5 0.1 pad_add_fusion
  44.6 0.1 dynamic-slice_bitcast_fusion
  44.7 0.1 copy.15.row_rec_ref
  44.8 0.2 select_reduce_fusion.1
  45.0 1.1 %multiply_reduce_fusion = (f32[16,64]{1,0:T(8,128)S(1)}, f32[16,64,192]{2,1,0:T(8,128)}) fusion(f32[192]{0:T(256)S(1)} %broadcast_multiply_fusion, f32[16,72,192]{2,1,0:T(8,128)S(1)} %constant_dynamic-update-slice_fusion.5), kind=kLoop, calls=%fused_computation.8 | loop fusion | flops 588800 | bytes 1577728 | tf_op jit(solution)/shard_map/reduce_sum | solution.py:211
  46.1 0.1 sqrt.12
  46.1 1.4 %fusion.3 = bf16[1024,192]{1,0:T(8,128)(2,1)S(1)} fusion(f32[16,64,192]{2,1,0:T(8,128)} %get-tuple-element.18, f32[1024]{0:T(1024)S(1)} %sqrt.12, f32[192]{0:T(256)S(1)} %broadcast_multiply_fusion), kind=kLoop, calls=%fused_computation.7 | loop fusion | flops 589824 | bytes 1184512 | tf_op jit(solution)/shard_map/convert_element_type | solution.py:211
  47.6 0.0 copy-start.1
  47.6 0.5 fusion.1.col_unit_ref
  48.1 0.1 copy-done.1
  48.3 1.6 %shard_map.92 = f32[32,512]{1,0:T(8,128)} custom-call(f32[3,3]{1,0:T(4,128)S(1)} %copy-done.1, bf16[34,192]{1,0:T(8,128)(2,1)S(1)} %fusion.7.row_unit_ref, bf16[512,192]{1,0:T(8,128)(2,1)S(1)} %fusion.1.col_unit_ref, s32[34,1]{1,0:T(8,128)S(1)} %copy.15.row_rec_ref, s32[1,512]{1,0:T(1,128)S(1)} %bitcast.21), custom_call_target="tpu_custom_call" | custom-call | flops 7012352 | bytes 275200 | tf_op jit(solution)/shard_map/pallas_call | solution.py:138
  (14 shorter events, 0.2 us)
Async XLA Ops:
  0.0 19.1 %copy-start = (f32[2048,192]{0,1:T(8,128)S(1)}, f32[2048,192]{0,1:T(8,128)}, u32[]{:S(2)}) copy-start(f32[2048,192]{0,1:T(8,128)} %param.17) | copy-start | bytes 4718596
  0.0 1.6 %copy-start.3 = (s32[64]{0:T(128)S(1)}, s32[64]{0:T(128)}, u32[]{:S(2)}) copy-start(s32[64]{0:T(128)} %param.12) | copy-start | bytes 772
  0.0 1.6 %copy-start.4 = (s32[64]{0:T(128)S(1)}, s32[64]{0:T(128)}, u32[]{:S(2)}) copy-start(s32[64]{0:T(128)} %param.13) | copy-start | bytes 772
  0.0 1.6 %copy-start.5 = (s32[64]{0:T(128)S(1)}, s32[64]{0:T(128)}, u32[]{:S(2)}) copy-start(s32[64]{0:T(128)} %param.14) | copy-start | bytes 772
  0.0 1.6 %copy-start.2 = (f32[1024]{0:T(1024)S(1)}, f32[1024]{0:T(1024)}, u32[]{:S(2)}) copy-start(f32[1024]{0:T(1024)} %param.16) | copy-start | bytes 12292
  20.8 19.7 %copy-start.6 = (s32[16]{0:T(128)S(1)}, s32[16]{0:T(128)}, u32[]{:S(2)}) copy-start(s32[16]{0:T(128)} %constant.57.clone) | copy-start | bytes 196
  20.8 6.3 %collective-permute-start = (f32[1,72,192]{2,1,0:T(8,128)S(1)}, f32[1,72,192]{2,1,0:T(8,128)S(1)}, u32[]{:S(2)}, u32[]{:S(2)}) collective-permute-start(f32[1,72,192]{2,1,0:T(8,128)S(1)} %fusion.5), channel_id=1, source_target_pairs={{0,4},{1,5},{2,6},{3,7},{4,0},{5,1},{6,2},{7,3},{8,12},{9,13},{10,... | collective-permute-start | bytes 165896 | tf_op jit(solution)/shard_map/ppermute | solution.py:172
  23.9 7.8 %collective-permute-start.1 = (f32[1,72,192]{2,1,0:T(8,128)S(1)}, f32[1,72,192]{2,1,0:T(8,128)S(1)}, u32[]{:S(2)}, u32[]{:S(2)}) collective-permute-start(f32[1,72,192]{2,1,0:T(8,128)S(1)} %fusion.5), channel_id=1, source_target_pairs={{0,8},{1,9},{2,10},{3,11},{4,12},{5,13},{6,14},{7,15},{8,0},{9,1},... | collective-permute-start | bytes 165896 | tf_op jit(solution)/shard_map/ppermute | solution.py:172
  26.5 6.3 %collective-permute-start.2 = (f32[1,72,192]{2,1,0:T(8,128)S(1)}, f32[1,72,192]{2,1,0:T(8,128)S(1)}, u32[]{:S(2)}, u32[]{:S(2)}) collective-permute-start(f32[1,72,192]{2,1,0:T(8,128)S(1)} %fusion.5), channel_id=1, source_target_pairs={{0,12},{1,13},{2,14},{3,15},{4,8},{5,9},{6,10},{7,11},{8,4},{9,5},... | collective-permute-start | bytes 165896 | tf_op jit(solution)/shard_map/ppermute | solution.py:172
  32.8 7.0 %collective-permute-start.3 = (f32[4,72,192]{2,1,0:T(8,128)S(1)}, f32[4,72,192]{2,1,0:T(8,128)S(1)}, u32[]{:S(2)}, u32[]{:S(2)}) collective-permute-start(f32[4,72,192]{2,1,0:T(8,128)S(1)} %pad_maximum_fusion), channel_id=1, source_target_pairs={{0,2},{1,3},{2,0},{3,1},{4,6},{5,7},{6,4},{7,5},{8,10},{9,11},{10,... | collective-permute-start | bytes 663560 | tf_op jit(solution)/shard_map/ppermute | solution.py:172
  40.6 2.2 %collective-permute-start.4 = (f32[8,72,192]{2,1,0:T(8,128)}, f32[8,72,192]{2,1,0:T(8,128)S(1)}, u32[]{:S(2)}, u32[]{:S(2)}) collective-permute-start(f32[8,72,192]{2,1,0:T(8,128)} %get-tuple-element.19), channel_id=1, source_target_pairs={{0,1},{1,0},{2,3},{3,2},{4,5},{5,4},{6,7},{7,6},{8,9},{9,8},{10,11... | collective-permute-start | bytes 1327112 | tf_op jit(solution)/shard_map/ppermute | solution.py:172
  47.6 0.7 %copy-start.1 = (f32[3,3]{1,0:T(4,128)S(1)}, f32[3,3]{1,0:T(4,128)}, u32[]{:S(2)}) copy-start(f32[3,3]{1,0:T(4,128)} %k_ref.1) | copy-start | bytes 112

commit v18 on v17

--- a/solution.py
+++ b/solution.py
@@ -25,14 +25,14 @@
 def _pool_kernel(
     starts_ref, frames_hbm, w_hbm, b_ref, out_ref, frames_ref, w_ref, x3_ref, act_ref, sem
 ):
-    rows = frames_ref.shape[0]
+    rows = frames_ref.shape[1]
     slots = out_ref.shape[0]
     frames_copy = pltpu.make_async_copy(frames_hbm, frames_ref, sem.at[0])
     w_copy = pltpu.make_async_copy(w_hbm, w_ref, sem.at[1])
     frames_copy.start()
     w_copy.start()
     frames_copy.wait()
-    frames = frames_ref[...]
+    frames = jnp.transpose(frames_ref[...])
     x3_ref[...] = jnp.concatenate(
         [pltpu.roll(frames, 1, 0), frames, pltpu.roll(frames, rows - 1, 0)], axis=1
     )
@@ -91,7 +91,7 @@
         ],
         out_specs=pl.BlockSpec(memory_space=vmem),
         scratch_shapes=[
-            pltpu.VMEM((rows, FEAT), jnp.float32),
+            pltpu.VMEM((FEAT, rows), jnp.float32),
             pltpu.VMEM((3 * FEAT, CH), jnp.float32),
             pltpu.VMEM((rows, 3 * FEAT), jnp.float32),
             pltpu.VMEM((rows, CH), jnp.float32),
@@ -105,7 +105,7 @@
         ),
     )(
         starts,
-        frames,
+        pltpu.with_memory_space_constraint(frames.T, pltpu.MemorySpace.HBM),
         pltpu.with_memory_space_constraint(conv_weight, pltpu.MemorySpace.HBM),
         conv_bias.reshape(1, CH),
     )

time: 50.2 us -> 52.1 us (1.038)
  other arithmetic: 5.09 us -> 7.17 us
  local copies, waits for them, and re-layouts: 4.99 us -> 4.13 us
  Pallas kernels: 19.1 us -> 19.8 us
    unnamed x18 -> x11, local copies, waits for them, and re-layouts: 3.62 us -> 2.74 us
    min x1, other arithmetic: 0.01 us -> 0.78 us  [pool_slots(): starts = jnp.clip(seg_start, 0, rows - SEGLEN).astype(jnp.int32)]
    pallas_call x1, Pallas kernels: 17.5 us -> 18.2 us  [pool_slots(): pl.pallas_call(_pool_kernel, out_shape=jax.ShapeDtypeStruct((slots, 2 * C...]
    convert_element_type x1, other arithmetic: 0.01 us -> 0.66 us  [per_device(): seg_dest.astype(jnp.float32)]
    convert_element_type x1, other arithmetic: 0.01 us -> 0.66 us  [per_device(): rec_id.astype(jnp.float32)]
where the time goes in v18:
time: 52.1 us; the launch traced here: 51.8 us
  Pallas kernels  19.8 us (38%)
  waiting for transfers between devices  11.2 us (21%)
  starting transfers between devices  7.27 us (14%)
  other arithmetic  7.17 us (14%)
  local copies, waits for them, and re-layouts  4.13 us (8%)
  matrix products  2.11 us (4%)
    pallas_call x1, Pallas kernels, pool_slots(): pl.pallas_call(_pool_kernel, out_shape=jax.ShapeDtypeStruct((slots, 2 * C...  18.2 us
    ppermute x5, waiting for transfers between devices, gather_wide(): lax.ppermute(buf, 'wide', [(i, i ^ f) for i in range(group_size)])  11.2 us
    ppermute x5, starting transfers between devices, gather_wide(): lax.ppermute(buf, 'wide', [(i, i ^ f) for i in range(group_size)])  7.27 us
    unnamed x11, local copies, waits for them, and re-layouts  2.74 us
    pallas_call x1, Pallas kernels, smooth_affinity(): pl.pallas_call(_affinity_kernel, out_shape=jax.ShapeDtypeStruct((height,...  1.65 us
    dot_general x1, matrix products, per_device(): jnp.dot(pooled, proj_weight, precision=PRECISE, preferred_element_type=jn...  1.64 us
    convert_element_type x1, other arithmetic, per_device(): (centred / jnp.sqrt(jnp.sum(centred * centred, axis=1, keepdims=True) + 1...  1.43 us
    reduce_sum x1, other arithmetic, per_device(): jnp.sum(centred * centred, axis=1, keepdims=True) + 1e-06  1.06 us
  transfers between devices with their start and end apart: 5, of which 4 were waited for; matrix products, arithmetic and copies ran while one was open for 5% of the time, Pallas kernels for 0%

profile of v18, /device:TPU:0, one launch (start us, length us, event | category | flops | bytes accessed | tf_op | source)
XLA Modules:
  0.0 51.8 jit_solution(100841387648960043)
XLA Ops:
  0.0 0.0 copy-start
  0.0 0.8 %broadcast_clamp_fusion.starts_ref = s32[64]{0:T(128)S(1)} fusion(s32[64]{0:T(128)} %param.12), kind=kLoop, calls=%fused_computation.42 | loop fusion | flops 64 | bytes 512 | tf_op jit(solution)/shard_map/jit(clip)/min | solution.py:81
  0.8 0.7 %convert_element_type.46 = f32[64]{0:T(128)S(1)} convert(s32[64]{0:T(128)} %param.13) | non-fusion elementwise | flops 64 | bytes 512 | tf_op jit(solution)/shard_map/convert_element_type | solution.py:189
  1.4 0.7 %convert_element_type.47 = f32[64]{0:T(128)S(1)} convert(s32[64]{0:T(128)} %param.14) | non-fusion elementwise | flops 64 | bytes 512 | tf_op jit(solution)/shard_map/convert_element_type | solution.py:189
  2.1 0.0 copy-start.2
  2.1 0.7 %copy-done.2 = f32[1024]{0:T(1024)S(1)} copy-done((f32[1024]{0:T(1024)S(1)}, f32[1024]{0:T(1024)}, u32[]{:S(2)}) %copy-start.2) | copy-done | bytes 4120
  2.8 18.2 %shard_map.91 = f32[64,2048]{1,0:T(8,128)S(1)} custom-call(s32[64]{0:T(128)S(1)} %broadcast_clamp_fusion.starts_ref, f32[80,2048]{1,0:T(8,128)} %bitcast.24, f32[240,1024]{1,0:T(8,128)} %w_hbm.1, f32[1,1024]{1,0:T(1,128)S(1)} %bitcast.23), custom_call_target="tpu_custom_call" | custom-call | flops 6077546496 | bytes 2162688 | tf_op jit(solution)/shard_map/pallas_call | solution.py:83
  21.0 0.0 copy-done
  21.0 1.6 %fusion.8 = f32[64,192]{1,0:T(8,128)S(1)} fusion(f32[64,2048]{1,0:T(8,128)S(1)} %shard_map.91, f32[2048,192]{0,1:T(8,128)S(1)} %copy-done), kind=kOutput, calls=%fused_computation.43 | convolution fusion | flops 301989888 | bytes 2146304 | tf_op jit(solution)/shard_map/dot_general | solution.py:186
  22.6 0.1 maximum_bitcast_fusion
  22.7 0.0 copy-start.3
  22.7 3.1 %collective-permute-start = (f32[1,72,192]{2,1,0:T(8,128)S(1)}, f32[1,72,192]{2,1,0:T(8,128)S(1)}, u32[]{:S(2)}, u32[]{:S(2)}) collective-permute-start(f32[1,72,192]{2,1,0:T(8,128)S(1)} %fusion.5), channel_id=1, source_target_pairs={{0,4},{1,5},{2,6},{3,7},{4,0},{5,1},{6,2},{7,3},{8,12},{9,13},{10,... | collective-permute-start | bytes 165896 | tf_op jit(solution)/shard_map/ppermute | solution.py:172
  25.8 2.6 %collective-permute-start.1 = (f32[1,72,192]{2,1,0:T(8,128)S(1)}, f32[1,72,192]{2,1,0:T(8,128)S(1)}, u32[]{:S(2)}, u32[]{:S(2)}) collective-permute-start(f32[1,72,192]{2,1,0:T(8,128)S(1)} %fusion.5), channel_id=1, source_target_pairs={{0,8},{1,9},{2,10},{3,11},{4,12},{5,13},{6,14},{7,15},{8,0},{9,1},... | collective-permute-start | bytes 165896 | tf_op jit(solution)/shard_map/ppermute | solution.py:172
  28.4 0.0 collective-permute-start.2
  28.4 0.6 %constant_dynamic-update-slice_fusion.4 = (f32[8,72,192]{2,1,0:T(8,128)}, f32[16,72,192]{2,1,0:T(8,128)S(1)}) fusion(f32[1,128]{1,0:T(1,128)S(1)} %maximum_bitcast_fusion, f32[64,192]{1,0:T(8,128)S(1)} %fusion.8), kind=kLoop, calls=%fused_computation.22 | loop fusion | flops 41470 | bytes 197120
  29.0 0.0 collective-permute-done
  29.0 4.6 %collective-permute-done.1 = f32[1,72,192]{2,1,0:T(8,128)S(1)} collective-permute-done((f32[1,72,192]{2,1,0:T(8,128)S(1)}, f32[1,72,192]{2,1,0:T(8,128)S(1)}, u32[]{:S(2)}, u32[]{:S(2)}) %collective-permute-start.1) | collective-permute-done | bytes 55328 | tf_op jit(solution)/shard_map/ppermute | solution.py:172
  33.6 1.1 %collective-permute-done.2 = f32[1,72,192]{2,1,0:T(8,128)S(1)} collective-permute-done((f32[1,72,192]{2,1,0:T(8,128)S(1)}, f32[1,72,192]{2,1,0:T(8,128)S(1)}, u32[]{:S(2)}, u32[]{:S(2)}) %collective-permute-start.2) | collective-permute-done | bytes 55328 | tf_op jit(solution)/shard_map/ppermute | solution.py:172
  34.7 1.6 %collective-permute-start.3 = (f32[4,72,192]{2,1,0:T(8,128)S(1)}, f32[4,72,192]{2,1,0:T(8,128)S(1)}, u32[]{:S(2)}, u32[]{:S(2)}) collective-permute-start(f32[4,72,192]{2,1,0:T(8,128)S(1)} %pad_maximum_fusion), channel_id=1, source_target_pairs={{0,2},{1,3},{2,0},{3,1},{4,6},{5,7},{6,4},{7,5},{8,10},{9,11},{10,... | collective-permute-start | bytes 663560 | tf_op jit(solution)/shard_map/ppermute | solution.py:172
  36.3 0.6 %constant_dynamic-update-slice_fusion.3 = (f32[8,72,192]{2,1,0:T(8,128)}, f32[16,72,192]{2,1,0:T(8,128)S(1)}) fusion(f32[8,72,192]{2,1,0:T(8,128)} %get-tuple-element.29, f32[1,72,192]{2,1,0:T(8,128)S(1)} %collective-permute-done, f32[16,72,192]{2,1,0:T(8,128)S(1)} %get-tuple-element.30), kind=kLoop, calls=%fused_computation.21 | loop fusion | bytes 221184
  36.9 0.6 %constant_dynamic-update-slice_fusion.2 = (f32[8,72,192]{2,1,0:T(8,128)}, f32[16,72,192]{2,1,0:T(8,128)S(1)}) fusion(f32[8,72,192]{2,1,0:T(8,128)} %get-tuple-element.27, f32[1,72,192]{2,1,0:T(8,128)S(1)} %collective-permute-done.1, f32[16,72,192]{2,1,0:T(8,128)S(1)} %get-tuple-element.28), kind=kLoop, calls=%fused_computation.20 | loop fusion | bytes 221184
  37.5 0.6 %constant_dynamic-update-slice_fusion.1 = (f32[8,72,192]{2,1,0:T(8,128)}, f32[16,72,192]{2,1,0:T(8,128)S(1)}) fusion(f32[8,72,192]{2,1,0:T(8,128)} %get-tuple-element.25, f32[1,72,192]{2,1,0:T(8,128)S(1)} %collective-permute-done.2, f32[16,72,192]{2,1,0:T(8,128)S(1)} %get-tuple-element.26), kind=kLoop, calls=%fused_computation.19 | loop fusion | bytes 221184
  38.2 3.5 %collective-permute-done.3 = f32[4,72,192]{2,1,0:T(8,128)S(1)} collective-permute-done((f32[4,72,192]{2,1,0:T(8,128)S(1)}, f32[4,72,192]{2,1,0:T(8,128)S(1)}, u32[]{:S(2)}, u32[]{:S(2)}) %collective-permute-start.3) | collective-permute-done | bytes 221216 | tf_op jit(solution)/shard_map/ppermute | solution.py:172
  41.7 0.8 %constant_dynamic-update-slice_fusion = (f32[8,72,192]{2,1,0:T(8,128)}, f32[16,72,192]{2,1,0:T(8,128)S(1)}) fusion(f32[8,72,192]{2,1,0:T(8,128)} %get-tuple-element.23, f32[4,72,192]{2,1,0:T(8,128)S(1)} %collective-permute-done.3, f32[16,72,192]{2,1,0:T(8,128)S(1)} %get-tuple-element.24), kind=kLoop, calls=%fused_computation.18 | loop fusion | bytes 884736 | tf_op jit(solution)/shard_map/concatenate | solution.py:174
  42.5 0.0 collective-permute-start.4
  42.5 0.0 copy-done.3
  42.5 0.1 iota_add_fusion
  42.5 0.1 add.54
  42.6 2.1 %collective-permute-done.4 = f32[8,72,192]{2,1,0:T(8,128)S(1)} collective-permute-done((f32[8,72,192]{2,1,0:T(8,128)}, f32[8,72,192]{2,1,0:T(8,128)S(1)}, u32[]{:S(2)}, u32[]{:S(2)}) %collective-permute-start.4) | collective-permute-done | bytes 442400 | tf_op jit(solution)/shard_map/ppermute | solution.py:172
  44.7 0.1 reshape.133
  44.8 0.1 slice_convert_fusion
  44.9 0.1 convert_element_type.49
  45.0 1.0 %convert_reduce_fusion = s32[1024]{0:T(1024)S(1)} fusion(s32[1024]{0:T(1024)S(1)} %convert_element_type.49, s32[1024]{0:T(1024)S(1)} %add.54), kind=kLoop, calls=%fused_computation | loop fusion | flops 5241856 | bytes 12288 | tf_op jit(solution)/shard_map/reduce_sum | solution.py:216
  46.0 0.1 convert_element_type.54
  46.1 0.3 select_reduce_fusion
  46.4 0.1 pad_add_fusion
  46.5 0.1 dynamic-slice_bitcast_fusion
  46.6 0.1 copy.13.row_rec_ref
  46.7 0.2 select_reduce_fusion.1
  46.9 1.1 %multiply_reduce_fusion = (f32[16,64]{1,0:T(8,128)S(1)}, f32[16,64,192]{2,1,0:T(8,128)}) fusion(f32[192]{0:T(256)S(1)} %broadcast_multiply_fusion, f32[16,72,192]{2,1,0:T(8,128)S(1)} %constant_dynamic-update-slice_fusion.5), kind=kLoop, calls=%fused_computation.8 | loop fusion | flops 588800 | bytes 1577728 | tf_op jit(solution)/shard_map/reduce_sum | solution.py:211
  48.0 0.1 sqrt.12
  48.0 1.4 %fusion.3 = bf16[1024,192]{1,0:T(8,128)(2,1)S(1)} fusion(f32[16,64,192]{2,1,0:T(8,128)} %get-tuple-element.18, f32[1024]{0:T(1024)S(1)} %sqrt.12, f32[192]{0:T(256)S(1)} %broadcast_multiply_fusion), kind=kLoop, calls=%fused_computation.7 | loop fusion | flops 589824 | bytes 1184512 | tf_op jit(solution)/shard_map/convert_element_type | solution.py:211
  49.5 0.0 copy-start.1
  49.5 0.5 fusion.1.col_unit_ref
  50.0 0.1 copy-done.1
  50.2 1.6 %shard_map.92 = f32[32,512]{1,0:T(8,128)} custom-call(f32[3,3]{1,0:T(4,128)S(1)} %copy-done.1, bf16[34,192]{1,0:T(8,128)(2,1)S(1)} %fusion.7.row_unit_ref, bf16[512,192]{1,0:T(8,128)(2,1)S(1)} %fusion.1.col_unit_ref, s32[34,1]{1,0:T(8,128)S(1)} %copy.13.row_rec_ref, s32[1,512]{1,0:T(1,128)S(1)} %bitcast.22), custom_call_target="tpu_custom_call" | custom-call | flops 7012352 | bytes 275200 | tf_op jit(solution)/shard_map/pallas_call | solution.py:138
  (11 shorter events, 0.2 us)
Async XLA Ops:
  0.0 21.0 %copy-start = (f32[2048,192]{0,1:T(8,128)S(1)}, f32[2048,192]{0,1:T(8,128)}, u32[]{:S(2)}) copy-start(f32[2048,192]{0,1:T(8,128)} %param.17) | copy-start | bytes 4718596
  2.1 0.7 %copy-start.2 = (f32[1024]{0:T(1024)S(1)}, f32[1024]{0:T(1024)}, u32[]{:S(2)}) copy-start(f32[1024]{0:T(1024)} %param.16) | copy-start | bytes 12292
  22.7 19.8 %copy-start.3 = (s32[16]{0:T(128)S(1)}, s32[16]{0:T(128)}, u32[]{:S(2)}) copy-start(s32[16]{0:T(128)} %constant.57.clone) | copy-start | bytes 196
  22.7 6.3 %collective-permute-start = (f32[1,72,192]{2,1,0:T(8,128)S(1)}, f32[1,72,192]{2,1,0:T(8,128)S(1)}, u32[]{:S(2)}, u32[]{:S(2)}) collective-permute-start(f32[1,72,192]{2,1,0:T(8,128)S(1)} %fusion.5), channel_id=1, source_target_pairs={{0,4},{1,5},{2,6},{3,7},{4,0},{5,1},{6,2},{7,3},{8,12},{9,13},{10,... | collective-permute-start | bytes 165896 | tf_op jit(solution)/shard_map/ppermute | solution.py:172
  25.8 7.8 %collective-permute-start.1 = (f32[1,72,192]{2,1,0:T(8,128)S(1)}, f32[1,72,192]{2,1,0:T(8,128)S(1)}, u32[]{:S(2)}, u32[]{:S(2)}) collective-permute-start(f32[1,72,192]{2,1,0:T(8,128)S(1)} %fusion.5), channel_id=1, source_target_pairs={{0,8},{1,9},{2,10},{3,11},{4,12},{5,13},{6,14},{7,15},{8,0},{9,1},... | collective-permute-start | bytes 165896 | tf_op jit(solution)/shard_map/ppermute | solution.py:172
  28.4 6.3 %collective-permute-start.2 = (f32[1,72,192]{2,1,0:T(8,128)S(1)}, f32[1,72,192]{2,1,0:T(8,128)S(1)}, u32[]{:S(2)}, u32[]{:S(2)}) collective-permute-start(f32[1,72,192]{2,1,0:T(8,128)S(1)} %fusion.5), channel_id=1, source_target_pairs={{0,12},{1,13},{2,14},{3,15},{4,8},{5,9},{6,10},{7,11},{8,4},{9,5},... | collective-permute-start | bytes 165896 | tf_op jit(solution)/shard_map/ppermute | solution.py:172
  34.7 7.0 %collective-permute-start.3 = (f32[4,72,192]{2,1,0:T(8,128)S(1)}, f32[4,72,192]{2,1,0:T(8,128)S(1)}, u32[]{:S(2)}, u32[]{:S(2)}) collective-permute-start(f32[4,72,192]{2,1,0:T(8,128)S(1)} %pad_maximum_fusion), channel_id=1, source_target_pairs={{0,2},{1,3},{2,0},{3,1},{4,6},{5,7},{6,4},{7,5},{8,10},{9,11},{10,... | collective-permute-start | bytes 663560 | tf_op jit(solution)/shard_map/ppermute | solution.py:172
  42.5 2.2 %collective-permute-start.4 = (f32[8,72,192]{2,1,0:T(8,128)}, f32[8,72,192]{2,1,0:T(8,128)S(1)}, u32[]{:S(2)}, u32[]{:S(2)}) collective-permute-start(f32[8,72,192]{2,1,0:T(8,128)} %get-tuple-element.19), channel_id=1, source_target_pairs={{0,1},{1,0},{2,3},{3,2},{4,5},{5,4},{6,7},{7,6},{8,9},{9,8},{10,11... | collective-permute-start | bytes 1327112 | tf_op jit(solution)/shard_map/ppermute | solution.py:172
  49.5 0.7 %copy-start.1 = (f32[3,3]{1,0:T(4,128)S(1)}, f32[3,3]{1,0:T(4,128)}, u32[]{:S(2)}) copy-start(f32[3,3]{1,0:T(4,128)} %k_ref.1) | copy-start | bytes 112

commit v19 on v17

--- a/solution.py
+++ b/solution.py
@@ -23,14 +23,17 @@
 
 
 def _pool_kernel(
-    starts_ref, frames_hbm, w_hbm, b_ref, out_ref, frames_ref, w_ref, x3_ref, act_ref, sem
+    starts_ref, frames_hbm, w_hbm, b_ref, proj_hbm, meta_ref, out_ref,
+    frames_ref, w_ref, proj_ref, pooled_ref, x3_ref, act_ref, sem
 ):
     rows = frames_ref.shape[0]
-    slots = out_ref.shape[0]
+    slots = pooled_ref.shape[0]
     frames_copy = pltpu.make_async_copy(frames_hbm, frames_ref, sem.at[0])
     w_copy = pltpu.make_async_copy(w_hbm, w_ref, sem.at[1])
+    proj_copy = pltpu.make_async_copy(proj_hbm, proj_ref, sem.at[2])
     frames_copy.start()
     w_copy.start()
+    proj_copy.start()
     frames_copy.wait()
     frames = frames_ref[...]
     x3_ref[...] = jnp.concatenate(
@@ -68,24 +71,36 @@
             means.append(frame_mean)
             stds.append(jnp.sqrt(frame_var + 1e-05))
         row0 = pl.multiple_of(blk * SEG_BLOCK, SEG_BLOCK)
-        out_ref[pl.ds(row0, SEG_BLOCK), :CH] = jnp.concatenate(means, axis=0)
-        out_ref[pl.ds(row0, SEG_BLOCK), CH:] = jnp.concatenate(stds, axis=0)
+        pooled_ref[pl.ds(row0, SEG_BLOCK), :CH] = jnp.concatenate(means, axis=0)
+        pooled_ref[pl.ds(row0, SEG_BLOCK), CH:] = jnp.concatenate(stds, axis=0)
         return carry
 
     lax.fori_loop(0, slots // SEG_BLOCK, stats_block, 0)
-
-
-def pool_slots(frames, seg_start, conv_weight, conv_bias):
+    proj_copy.wait()
+    out_ref[:slots, :] = jnp.dot(
+        pooled_ref[...], proj_ref[...], precision=PRECISE, preferred_element_type=jnp.float32
+    )
+    out_ref[slots:, :] = meta_ref[...]
+
+
+def embed_slots(frames, seg_start, seg_dest, rec_id, conv_weight, conv_bias, proj_weight):
     rows = frames.shape[0]
     slots = seg_start.shape[0]
     starts = jnp.clip(seg_start, 0, rows - SEGLEN).astype(jnp.int32)
+    meta = jnp.concatenate([seg_dest.astype(jnp.float32), rec_id.astype(jnp.float32)])
+    meta_len = -(-meta.shape[0] // EMB) * EMB
+    meta_rows = jnp.pad(meta, (0, meta_len - meta.shape[0])).reshape(-1, EMB)
+    meta_rows = jnp.pad(meta_rows, ((0, -(-meta_rows.shape[0] // 8) * 8 - meta_rows.shape[0]), (0, 0)))
     vmem = pltpu.MemorySpace.VMEM
+    hbm = pltpu.MemorySpace.HBM
     return pl.pallas_call(
         _pool_kernel,
-        out_shape=jax.ShapeDtypeStruct((slots, 2 * CH), jnp.float32),
+        out_shape=jax.ShapeDtypeStruct((slots + meta_rows.shape[0], EMB), jnp.float32),
         in_specs=[
             pl.BlockSpec(memory_space=pltpu.MemorySpace.SMEM),
             pl.BlockSpec(memory_space=pl.ANY),
+            pl.BlockSpec(memory_space=pl.ANY),
+            pl.BlockSpec(memory_space=vmem),
             pl.BlockSpec(memory_space=pl.ANY),
             pl.BlockSpec(memory_space=vmem),
         ],
@@ -93,21 +108,25 @@
         scratch_shapes=[
             pltpu.VMEM((rows, FEAT), jnp.float32),
             pltpu.VMEM((3 * FEAT, CH), jnp.float32),
+            pltpu.VMEM((2 * CH, EMB), jnp.float32),
+            pltpu.VMEM((slots, 2 * CH), jnp.float32),
             pltpu.VMEM((rows, 3 * FEAT), jnp.float32),
             pltpu.VMEM((rows, CH), jnp.float32),
-            pltpu.SemaphoreType.DMA((2,)),
+            pltpu.SemaphoreType.DMA((3,)),
         ],
         compiler_params=pltpu.CompilerParams(vmem_limit_bytes=48 * 1024 * 1024),
         cost_estimate=pl.CostEstimate(
-            flops=2 * rows * 3 * FEAT * CH * 6 + 8 * slots * WIN * CH,
+            flops=2 * rows * 3 * FEAT * CH * 6 + 8 * slots * WIN * CH + 2 * slots * 2 * CH * EMB * 6,
             transcendentals=slots * CH,
-            bytes_accessed=rows * FEAT * 4 + 3 * FEAT * CH * 4 + slots * 2 * CH * 4,
+            bytes_accessed=rows * FEAT * 4 + 3 * FEAT * CH * 4 + 2 * CH * EMB * 4 + slots * EMB * 4,
         ),
     )(
         starts,
         frames,
-        pltpu.with_memory_space_constraint(conv_weight, pltpu.MemorySpace.HBM),
+        pltpu.with_memory_space_constraint(conv_weight, hbm),
         conv_bias.reshape(1, CH),
+        pltpu.with_memory_space_constraint(proj_weight, hbm),
+        meta_rows,
     )
 
 
@@ -182,18 +201,8 @@
 ):
     group_size = lax.axis_size("wide")
     total_rows = SEG_DEV * group_size
-    pooled = pool_slots(frames, seg_start, conv_weight, conv_bias)
-    embedded = jnp.dot(pooled, proj_weight, precision=PRECISE, preferred_element_type=jnp.float32)
-    slots = embedded.shape[0]
-    meta = jnp.concatenate(
-        [seg_dest.astype(jnp.float32), rec_id.astype(jnp.float32)]
-    )
-    if meta.shape[0] <= EMB:
-        meta_rows = jnp.zeros((8, EMB), jnp.float32).at[0, : meta.shape[0]].set(meta)
-    else:
-        meta_rows = jnp.zeros((-(-meta.shape[0] // EMB) // 8 * 8 + 8, EMB), jnp.float32)
-        meta_rows = meta_rows.reshape(-1).at[: meta.shape[0]].set(meta).reshape(-1, EMB)
-    packed = jnp.concatenate([embedded, meta_rows], axis=0)
+    packed = embed_slots(frames, seg_start, seg_dest, rec_id, conv_weight, conv_bias, proj_weight)
+    slots = seg_start.shape[0]
     blocks, source = gather_wide(packed, group_size)
     per_block = slots
     all_emb = blocks[:, :slots, :].reshape(group_size * slots, EMB)

time: 50.2 us -> 48.9 us (0.974)
  other arithmetic: 5.09 us -> 2.4 us
  waiting for transfers between devices: 11.2 us -> 13.4 us
  matrix products: 2.1 us -> 0.47 us
  Pallas kernels: 19.1 us -> 20.4 us
  local copies, waits for them, and re-layouts: 4.99 us -> 4.43 us
    ppermute x5, waiting for transfers between devices: 11.2 us -> 13.4 us  [gather_wide(): lax.ppermute(buf, 'wide', [(i, i ^ f) for i in range(group_size)])]
    dot_general x1 -> x0, matrix products: 1.63 us -> none  [per_device(): jnp.dot(pooled, proj_weight, precision=PRECISE, preferred_element_type=jn...]
    pallas_call x1, Pallas kernels: 17.5 us -> 18.8 us  [embed_slots(): pl.pallas_call(_pool_kernel, out_shape=jax.ShapeDtypeStruct((slots + meta...]
    convert_element_type x1, other arithmetic: 1.43 us -> 0.21 us  [per_device(): (centred / jnp.sqrt(jnp.sum(centred * centred, axis=1, keepdims=True) + 1...]
    reduce_sum x1, other arithmetic: 1.06 us -> 0.24 us  [per_device(): jnp.sum(centred * centred, axis=1, keepdims=True) + 1e-06]
    concatenate x2, local copies, waits for them, and re-layouts: 0.79 us -> 0.08 us  [gather_wide(): buf = jnp.concatenate([buf] + received, axis=0)]
    unnamed x1 -> x0, other arithmetic: 0.63 us -> none
    unnamed x18 -> x20, local copies, waits for them, and re-layouts: 3.62 us -> 3.77 us
  transfers between devices with their start and end apart: 5 -> 5, of which waited for: 4 -> 4; matrix products, arithmetic and copies ran while one was open for 5% -> 0% of each run, Pallas kernels for 0% -> 0%
where the time goes in v19:
time: 48.9 us; the launch traced here: 48.7 us
  Pallas kernels  20.4 us (42%)
  waiting for transfers between devices  13.4 us (27%)
  starting transfers between devices  7.34 us (15%)
  local copies, waits for them, and re-layouts  4.43 us (9%)
  other arithmetic  2.4 us (5%)
    pallas_call x1, Pallas kernels, embed_slots(): pl.pallas_call(_pool_kernel, out_shape=jax.ShapeDtypeStruct((slots + meta...  18.8 us
    ppermute x5, waiting for transfers between devices, gather_wide(): lax.ppermute(buf, 'wide', [(i, i ^ f) for i in range(group_size)])  13.4 us
    ppermute x5, starting transfers between devices, gather_wide(): lax.ppermute(buf, 'wide', [(i, i ^ f) for i in range(group_size)])  7.34 us
    unnamed x20, local copies, waits for them, and re-layouts  3.77 us
    pallas_call x1, Pallas kernels, smooth_affinity(): pl.pallas_call(_affinity_kernel, out_shape=jax.ShapeDtypeStruct((height,...  1.65 us
    reduce_sum x1, other arithmetic, per_device(): rank = jnp.sum(earlier.astype(jnp.int32), axis=1)  1.03 us
  transfers between devices with their start and end apart: 5, of which 4 were waited for; matrix products, arithmetic and copies ran while one was open for 0% of the time, Pallas kernels for 0%

profile of v19, /device:TPU:0, one launch (start us, length us, event | category | flops | bytes accessed | tf_op | source)
XLA Modules:
  0.0 48.7 jit_solution(2947402702503751660)
XLA Ops:
  0.0 0.0 copy-start.2
  0.0 2.9 %copy.15.proj_hbm = f32[2048,192]{1,0:T(8,128)} copy(f32[2048,192]{0,1:T(8,128)} %param.15) | data formatting | bytes 3145728 | tf_op args[6]
  2.9 0.0 copy-done.2
  2.9 0.0 copy-start.3
  2.9 0.0 copy-start.4
  2.9 0.0 copy-start.5
  2.9 0.0 copy-start.1
  3.0 0.3 copy.14.frames_hbm
  3.3 0.3 copy-done.3
  3.6 0.0 copy-done.4
  3.6 0.0 copy-done.5
  3.6 0.1 select_maximum_fusion
  3.7 0.0 copy-done.1
  3.7 18.8 %shard_map.91 = f32[72,192]{1,0:T(8,128)S(1)} custom-call(s32[64]{0:T(128)S(1)} %broadcast_clamp_fusion.starts_ref, f32[2048,80]{1,0:T(8,128)S(1)} %copy.14.frames_hbm, f32[240,1024]{1,0:T(8,128)} %w_hbm.1, f32[1,1024]{1,0:T(1,128)S(1)} %bitcast.20, f32[2048,192]{1,0:T(8,128)} %copy.15.proj_hbm, f32[8,192]{1,0:T(8,128)S(1)} %pad.9.meta_ref), custom_call_target="tpu_custom_call" | custom-call | flops 6379536384 | bytes 3260416 | tf_op jit(solution)/shard_map/pallas_call | solution.py:96
  22.5 0.0 copy-start.6
  22.5 3.1 %collective-permute-start = (f32[1,72,192]{2,1,0:T(8,128)S(1)}, f32[1,72,192]{2,1,0:T(8,128)S(1)}, u32[]{:S(2)}, u32[]{:S(2)}) collective-permute-start(f32[1,72,192]{2,1,0:T(8,128)S(1)} %bitcast.15), channel_id=1, source_target_pairs={{0,4},{1,5},{2,6},{3,7},{4,0},{5,1},{6,2},{7,3},{8,12},{9,13},{10,... | collective-permute-start | bytes 165896 | tf_op jit(solution)/shard_map/ppermute | solution.py:191
  25.6 2.6 %collective-permute-start.1 = (f32[1,72,192]{2,1,0:T(8,128)S(1)}, f32[1,72,192]{2,1,0:T(8,128)S(1)}, u32[]{:S(2)}, u32[]{:S(2)}) collective-permute-start(f32[1,72,192]{2,1,0:T(8,128)S(1)} %bitcast.16), channel_id=1, source_target_pairs={{0,8},{1,9},{2,10},{3,11},{4,12},{5,13},{6,14},{7,15},{8,0},{9,1},... | collective-permute-start | bytes 165896 | tf_op jit(solution)/shard_map/ppermute | solution.py:191
  28.2 0.0 collective-permute-start.2
  28.2 0.0 collective-permute-done
  28.2 5.2 %collective-permute-done.1 = f32[1,72,192]{2,1,0:T(8,128)S(1)} collective-permute-done((f32[1,72,192]{2,1,0:T(8,128)S(1)}, f32[1,72,192]{2,1,0:T(8,128)S(1)}, u32[]{:S(2)}, u32[]{:S(2)}) %collective-permute-start.1) | collective-permute-done | bytes 55328 | tf_op jit(solution)/shard_map/ppermute | solution.py:191
  33.4 1.1 %collective-permute-done.2 = f32[1,72,192]{2,1,0:T(8,128)S(1)} collective-permute-done((f32[1,72,192]{2,1,0:T(8,128)S(1)}, f32[1,72,192]{2,1,0:T(8,128)S(1)}, u32[]{:S(2)}, u32[]{:S(2)}) %collective-permute-start.2) | collective-permute-done | bytes 55328 | tf_op jit(solution)/shard_map/ppermute | solution.py:191
  34.5 1.6 %collective-permute-start.3 = (f32[4,72,192]{2,1,0:T(8,128)S(1)}, f32[4,72,192]{2,1,0:T(8,128)S(1)}, u32[]{:S(2)}, u32[]{:S(2)}) collective-permute-start(f32[4,72,192]{2,1,0:T(8,128)S(1)} %pad_maximum_fusion), channel_id=1, source_target_pairs={{0,2},{1,3},{2,0},{3,1},{4,6},{5,7},{6,4},{7,5},{8,10},{9,11},{10,... | collective-permute-start | bytes 663560 | tf_op jit(solution)/shard_map/ppermute | solution.py:191
  36.1 5.4 %collective-permute-done.3 = f32[4,72,192]{2,1,0:T(8,128)S(1)} collective-permute-done((f32[4,72,192]{2,1,0:T(8,128)S(1)}, f32[4,72,192]{2,1,0:T(8,128)S(1)}, u32[]{:S(2)}, u32[]{:S(2)}) %collective-permute-start.3) | collective-permute-done | bytes 221216 | tf_op jit(solution)/shard_map/ppermute | solution.py:191
  41.5 0.1 collective-permute-start.4
  41.6 0.0 copy-done.6
  41.6 0.1 iota_add_fusion
  41.7 0.1 add.54
  41.8 1.8 %collective-permute-done.4 = f32[8,72,192]{2,1,0:T(8,128)S(1)} collective-permute-done((f32[8,72,192]{2,1,0:T(8,128)S(1)}, f32[8,72,192]{2,1,0:T(8,128)S(1)}, u32[]{:S(2)}, u32[]{:S(2)}) %collective-permute-start.4) | collective-permute-done | bytes 442400 | tf_op jit(solution)/shard_map/ppermute | solution.py:191
  43.6 0.1 reshape.106
  43.7 0.1 slice_convert_fusion
  43.8 0.1 convert_element_type.53
  43.9 1.0 %convert_reduce_fusion = s32[1024]{0:T(1024)S(1)} fusion(s32[1024]{0:T(1024)S(1)} %convert_element_type.53, s32[1024]{0:T(1024)S(1)} %add.54), kind=kLoop, calls=%fused_computation | loop fusion | flops 5241856 | bytes 12288 | tf_op jit(solution)/shard_map/reduce_sum | solution.py:225
  44.9 0.1 convert_element_type.58
  45.0 0.3 select_reduce_fusion
  45.3 0.1 pad_add_fusion
  45.4 0.1 dynamic-slice_bitcast_fusion
  45.5 0.1 copy.17.row_rec_ref
  45.6 0.2 select_reduce_fusion.1
  45.8 0.2 multiply_reduce_fusion
  46.1 0.1 sqrt.12
  46.1 0.2 fusion.3
  46.4 0.0 copy-start
  46.4 0.5 fusion.1.col_unit_ref
  46.9 0.1 copy-done
  47.0 1.6 %shard_map.92 = f32[32,512]{1,0:T(8,128)} custom-call(f32[3,3]{1,0:T(4,128)S(1)} %copy-done, bf16[34,192]{1,0:T(8,128)(2,1)S(1)} %fusion.6.row_unit_ref, bf16[512,192]{1,0:T(8,128)(2,1)S(1)} %fusion.1.col_unit_ref, s32[34,1]{1,0:T(8,128)S(1)} %copy.17.row_rec_ref, s32[1,512]{1,0:T(1,128)S(1)} %bitcast.19), custom_call_target="tpu_custom_call" | custom-call | flops 7012352 | bytes 275200 | tf_op jit(solution)/shard_map/pallas_call | solution.py:157
  (19 shorter events, 0.3 us)
Async XLA Ops:
  0.0 2.9 %copy-start.2 = (f32[2048,80]{0,1:T(8,128)S(1)}, f32[2048,80]{0,1:T(8,128)}, u32[]{:S(2)}) copy-start(f32[2048,80]{0,1:T(8,128)} %param.9) | copy-start | bytes 1966084
  2.9 0.7 %copy-start.3 = (s32[64]{0:T(128)S(1)}, s32[64]{0:T(128)}, u32[]{:S(2)}) copy-start(s32[64]{0:T(128)} %param.11) | copy-start | bytes 772
  2.9 0.7 %copy-start.4 = (s32[64]{0:T(128)S(1)}, s32[64]{0:T(128)}, u32[]{:S(2)}) copy-start(s32[64]{0:T(128)} %param.12) | copy-start | bytes 772
  2.9 0.7 %copy-start.5 = (s32[64]{0:T(128)S(1)}, s32[64]{0:T(128)}, u32[]{:S(2)}) copy-start(s32[64]{0:T(128)} %param.10) | copy-start | bytes 772
  2.9 0.8 %copy-start.1 = (f32[1024]{0:T(1024)S(1)}, f32[1024]{0:T(1024)}, u32[]{:S(2)}) copy-start(f32[1024]{0:T(1024)} %param.14) | copy-start | bytes 12292
  22.5 19.1 %copy-start.6 = (s32[16]{0:T(128)S(1)}, s32[16]{0:T(128)}, u32[]{:S(2)}) copy-start(s32[16]{0:T(128)} %constant.32.clone) | copy-start | bytes 196
  22.5 5.7 %collective-permute-start = (f32[1,72,192]{2,1,0:T(8,128)S(1)}, f32[1,72,192]{2,1,0:T(8,128)S(1)}, u32[]{:S(2)}, u32[]{:S(2)}) collective-permute-start(f32[1,72,192]{2,1,0:T(8,128)S(1)} %bitcast.15), channel_id=1, source_target_pairs={{0,4},{1,5},{2,6},{3,7},{4,0},{5,1},{6,2},{7,3},{8,12},{9,13},{10,... | collective-permute-start | bytes 165896 | tf_op jit(solution)/shard_map/ppermute | solution.py:191
  25.6 7.8 %collective-permute-start.1 = (f32[1,72,192]{2,1,0:T(8,128)S(1)}, f32[1,72,192]{2,1,0:T(8,128)S(1)}, u32[]{:S(2)}, u32[]{:S(2)}) collective-permute-start(f32[1,72,192]{2,1,0:T(8,128)S(1)} %bitcast.16), channel_id=1, source_target_pairs={{0,8},{1,9},{2,10},{3,11},{4,12},{5,13},{6,14},{7,15},{8,0},{9,1},... | collective-permute-start | bytes 165896 | tf_op jit(solution)/shard_map/ppermute | solution.py:191
  28.2 6.3 %collective-permute-start.2 = (f32[1,72,192]{2,1,0:T(8,128)S(1)}, f32[1,72,192]{2,1,0:T(8,128)S(1)}, u32[]{:S(2)}, u32[]{:S(2)}) collective-permute-start(f32[1,72,192]{2,1,0:T(8,128)S(1)} %bitcast.17), channel_id=1, source_target_pairs={{0,12},{1,13},{2,14},{3,15},{4,8},{5,9},{6,10},{7,11},{8,4},{9,5},... | collective-permute-start | bytes 165896 | tf_op jit(solution)/shard_map/ppermute | solution.py:191
  34.5 7.0 %collective-permute-start.3 = (f32[4,72,192]{2,1,0:T(8,128)S(1)}, f32[4,72,192]{2,1,0:T(8,128)S(1)}, u32[]{:S(2)}, u32[]{:S(2)}) collective-permute-start(f32[4,72,192]{2,1,0:T(8,128)S(1)} %pad_maximum_fusion), channel_id=1, source_target_pairs={{0,2},{1,3},{2,0},{3,1},{4,6},{5,7},{6,4},{7,5},{8,10},{9,11},{10,... | collective-permute-start | bytes 663560 | tf_op jit(solution)/shard_map/ppermute | solution.py:191
  41.5 2.1 %collective-permute-start.4 = (f32[8,72,192]{2,1,0:T(8,128)S(1)}, f32[8,72,192]{2,1,0:T(8,128)S(1)}, u32[]{:S(2)}, u32[]{:S(2)}) collective-permute-start(f32[8,72,192]{2,1,0:T(8,128)S(1)} %get-tuple-element.7), channel_id=1, source_target_pairs={{0,1},{1,0},{2,3},{3,2},{4,5},{5,4},{6,7},{7,6},{8,9},{9,8},{10,11... | collective-permute-start | bytes 1327112 | tf_op jit(solution)/shard_map/ppermute | solution.py:191
  46.4 0.7 %copy-start = (f32[3,3]{1,0:T(4,128)S(1)}, f32[3,3]{1,0:T(4,128)}, u32[]{:S(2)}) copy-start(f32[3,3]{1,0:T(4,128)} %k_ref.1) | copy-start | bytes 112

commit v20 on v19

--- a/solution.py
+++ b/solution.py
@@ -77,8 +77,12 @@
 
     lax.fori_loop(0, slots // SEG_BLOCK, stats_block, 0)
     proj_copy.wait()
-    out_ref[:slots, :] = jnp.dot(
-        pooled_ref[...], proj_ref[...], precision=PRECISE, preferred_element_type=jnp.float32
+    out_ref[:slots, :] = lax.dot_general(
+        pooled_ref[...],
+        proj_ref[...],
+        (((1,), (1,)), ((), ())),
+        precision=PRECISE,
+        preferred_element_type=jnp.float32,
     )
     out_ref[slots:, :] = meta_ref[...]
 
@@ -108,7 +112,7 @@
         scratch_shapes=[
             pltpu.VMEM((rows, FEAT), jnp.float32),
             pltpu.VMEM((3 * FEAT, CH), jnp.float32),
-            pltpu.VMEM((2 * CH, EMB), jnp.float32),
+            pltpu.VMEM((EMB, 2 * CH), jnp.float32),
             pltpu.VMEM((slots, 2 * CH), jnp.float32),
             pltpu.VMEM((rows, 3 * FEAT), jnp.float32),
             pltpu.VMEM((rows, CH), jnp.float32),
@@ -125,7 +129,7 @@
         frames,
         pltpu.with_memory_space_constraint(conv_weight, hbm),
         conv_bias.reshape(1, CH),
-        pltpu.with_memory_space_constraint(proj_weight, hbm),
+        pltpu.with_memory_space_constraint(proj_weight.T, hbm),
         meta_rows,
     )
 

time: 48.9 us -> 47.1 us (0.963)
  local copies, waits for them, and re-layouts: 4.43 us -> 2.34 us
    unnamed x20 -> x17, local copies, waits for them, and re-layouts: 3.77 us -> 1.68 us
where the time goes in v20:
time: 47.1 us; the launch traced here: 46.9 us
  Pallas kernels  20.7 us (44%)
  waiting for transfers between devices  13.4 us (28%)
  starting transfers between devices  7.34 us (16%)
  other arithmetic  2.4 us (5%)
  local copies, waits for them, and re-layouts  2.34 us (5%)
    pallas_call x1, Pallas kernels, embed_slots(): pl.pallas_call(_pool_kernel, out_shape=jax.ShapeDtypeStruct((slots + meta...  19.1 us
    ppermute x5, waiting for transfers between devices, gather_wide(): lax.ppermute(buf, 'wide', [(i, i ^ f) for i in range(group_size)])  13.4 us
    ppermute x5, starting transfers between devices, gather_wide(): lax.ppermute(buf, 'wide', [(i, i ^ f) for i in range(group_size)])  7.34 us
    unnamed x17, local copies, waits for them, and re-layouts  1.68 us
    pallas_call x1, Pallas kernels, smooth_affinity(): pl.pallas_call(_affinity_kernel, out_shape=jax.ShapeDtypeStruct((height,...  1.65 us
    reduce_sum x1, other arithmetic, per_device(): rank = jnp.sum(earlier.astype(jnp.int32), axis=1)  1.03 us
  transfers between devices with their start and end apart: 5, of which 4 were waited for; matrix products, arithmetic and copies ran while one was open for 0% of the time, Pallas kernels for 0%

profile of v20, /device:TPU:0, one launch (start us, length us, event | category | flops | bytes accessed | tf_op | source)
XLA Modules:
  0.0 46.9 jit_solution(3965241580029053324)
XLA Ops:
  0.0 0.0 copy-start.2
  0.0 0.0 copy-start.3
  0.0 0.0 copy-start.4
  0.0 0.0 copy-start.1
  0.0 1.5 %copy.13.frames_hbm = f32[2048,80]{1,0:T(8,128)S(1)} copy(f32[2048,80]{0,1:T(8,128)} %param.9) | data formatting | bytes 1310720 | tf_op args[0]
  1.5 0.0 copy-done.2
  1.5 0.0 copy-done.3
  1.5 0.0 copy-done.4
  1.6 0.1 select_maximum_fusion
  1.6 0.0 copy-done.1
  1.6 19.1 %shard_map.91 = f32[72,192]{1,0:T(8,128)S(1)} custom-call(s32[64]{0:T(128)S(1)} %broadcast_clamp_fusion.starts_ref, f32[2048,80]{1,0:T(8,128)S(1)} %copy.13.frames_hbm, f32[240,1024]{1,0:T(8,128)} %w_hbm.1, f32[1,1024]{1,0:T(1,128)S(1)} %bitcast.21, f32[192,2048]{1,0:T(8,128)} %bitcast.23, f32[8,192]{1,0:T(8,128)S(1)} %pad.9.meta_ref), custom_call_target="tpu_custom_call" | custom-call | flops 6379536384 | bytes 3260416 | tf_op jit(solution)/shard_map/pallas_call | solution.py:100
  20.7 0.0 copy-start.5
  20.7 3.1 %collective-permute-start = (f32[1,72,192]{2,1,0:T(8,128)S(1)}, f32[1,72,192]{2,1,0:T(8,128)S(1)}, u32[]{:S(2)}, u32[]{:S(2)}) collective-permute-start(f32[1,72,192]{2,1,0:T(8,128)S(1)} %bitcast.16), channel_id=1, source_target_pairs={{0,4},{1,5},{2,6},{3,7},{4,0},{5,1},{6,2},{7,3},{8,12},{9,13},{10,... | collective-permute-start | bytes 165896 | tf_op jit(solution)/shard_map/ppermute | solution.py:195
  23.8 2.6 %collective-permute-start.1 = (f32[1,72,192]{2,1,0:T(8,128)S(1)}, f32[1,72,192]{2,1,0:T(8,128)S(1)}, u32[]{:S(2)}, u32[]{:S(2)}) collective-permute-start(f32[1,72,192]{2,1,0:T(8,128)S(1)} %bitcast.17), channel_id=1, source_target_pairs={{0,8},{1,9},{2,10},{3,11},{4,12},{5,13},{6,14},{7,15},{8,0},{9,1},... | collective-permute-start | bytes 165896 | tf_op jit(solution)/shard_map/ppermute | solution.py:195
  26.4 0.0 collective-permute-start.2
  26.4 0.0 collective-permute-done
  26.4 5.2 %collective-permute-done.1 = f32[1,72,192]{2,1,0:T(8,128)S(1)} collective-permute-done((f32[1,72,192]{2,1,0:T(8,128)S(1)}, f32[1,72,192]{2,1,0:T(8,128)S(1)}, u32[]{:S(2)}, u32[]{:S(2)}) %collective-permute-start.1) | collective-permute-done | bytes 55328 | tf_op jit(solution)/shard_map/ppermute | solution.py:195
  31.6 1.1 %collective-permute-done.2 = f32[1,72,192]{2,1,0:T(8,128)S(1)} collective-permute-done((f32[1,72,192]{2,1,0:T(8,128)S(1)}, f32[1,72,192]{2,1,0:T(8,128)S(1)}, u32[]{:S(2)}, u32[]{:S(2)}) %collective-permute-start.2) | collective-permute-done | bytes 55328 | tf_op jit(solution)/shard_map/ppermute | solution.py:195
  32.7 1.6 %collective-permute-start.3 = (f32[4,72,192]{2,1,0:T(8,128)S(1)}, f32[4,72,192]{2,1,0:T(8,128)S(1)}, u32[]{:S(2)}, u32[]{:S(2)}) collective-permute-start(f32[4,72,192]{2,1,0:T(8,128)S(1)} %pad_maximum_fusion), channel_id=1, source_target_pairs={{0,2},{1,3},{2,0},{3,1},{4,6},{5,7},{6,4},{7,5},{8,10},{9,11},{10,... | collective-permute-start | bytes 663560 | tf_op jit(solution)/shard_map/ppermute | solution.py:195
  34.3 5.4 %collective-permute-done.3 = f32[4,72,192]{2,1,0:T(8,128)S(1)} collective-permute-done((f32[4,72,192]{2,1,0:T(8,128)S(1)}, f32[4,72,192]{2,1,0:T(8,128)S(1)}, u32[]{:S(2)}, u32[]{:S(2)}) %collective-permute-start.3) | collective-permute-done | bytes 221216 | tf_op jit(solution)/shard_map/ppermute | solution.py:195
  39.7 0.1 collective-permute-start.4
  39.8 0.0 copy-done.5
  39.8 0.1 iota_add_fusion
  39.9 0.1 add.54
  40.0 1.8 %collective-permute-done.4 = f32[8,72,192]{2,1,0:T(8,128)S(1)} collective-permute-done((f32[8,72,192]{2,1,0:T(8,128)S(1)}, f32[8,72,192]{2,1,0:T(8,128)S(1)}, u32[]{:S(2)}, u32[]{:S(2)}) %collective-permute-start.4) | collective-permute-done | bytes 442400 | tf_op jit(solution)/shard_map/ppermute | solution.py:195
  41.9 0.1 reshape.106
  42.0 0.1 slice_convert_fusion
  42.1 0.1 convert_element_type.53
  42.1 1.0 %convert_reduce_fusion = s32[1024]{0:T(1024)S(1)} fusion(s32[1024]{0:T(1024)S(1)} %convert_element_type.53, s32[1024]{0:T(1024)S(1)} %add.54), kind=kLoop, calls=%fused_computation | loop fusion | flops 5241856 | bytes 12288 | tf_op jit(solution)/shard_map/reduce_sum | solution.py:229
  43.2 0.1 convert_element_type.58
  43.3 0.3 select_reduce_fusion
  43.5 0.1 pad_add_fusion
  43.6 0.1 dynamic-slice_bitcast_fusion
  43.7 0.1 copy.15.row_rec_ref
  43.8 0.2 select_reduce_fusion.1
  44.0 0.2 multiply_reduce_fusion
  44.3 0.1 sqrt.12
  44.4 0.2 fusion.3
  44.6 0.0 copy-start
  44.6 0.5 fusion.1.col_unit_ref
  45.1 0.1 copy-done
  45.3 1.6 %shard_map.92 = f32[32,512]{1,0:T(8,128)} custom-call(f32[3,3]{1,0:T(4,128)S(1)} %copy-done, bf16[34,192]{1,0:T(8,128)(2,1)S(1)} %fusion.6.row_unit_ref, bf16[512,192]{1,0:T(8,128)(2,1)S(1)} %fusion.1.col_unit_ref, s32[34,1]{1,0:T(8,128)S(1)} %copy.15.row_rec_ref, s32[1,512]{1,0:T(1,128)S(1)} %bitcast.20), custom_call_target="tpu_custom_call" | custom-call | flops 7012352 | bytes 275200 | tf_op jit(solution)/shard_map/pallas_call | solution.py:161
  (19 shorter events, 0.3 us)
Async XLA Ops:
  0.0 1.5 %copy-start.2 = (s32[64]{0:T(128)S(1)}, s32[64]{0:T(128)}, u32[]{:S(2)}) copy-start(s32[64]{0:T(128)} %param.11) | copy-start | bytes 772
  0.0 1.5 %copy-start.3 = (s32[64]{0:T(128)S(1)}, s32[64]{0:T(128)}, u32[]{:S(2)}) copy-start(s32[64]{0:T(128)} %param.12) | copy-start | bytes 772
  0.0 1.5 %copy-start.4 = (s32[64]{0:T(128)S(1)}, s32[64]{0:T(128)}, u32[]{:S(2)}) copy-start(s32[64]{0:T(128)} %param.10) | copy-start | bytes 772
  0.0 1.6 %copy-start.1 = (f32[1024]{0:T(1024)S(1)}, f32[1024]{0:T(1024)}, u32[]{:S(2)}) copy-start(f32[1024]{0:T(1024)} %param.14) | copy-start | bytes 12292
  20.7 19.1 %copy-start.5 = (s32[16]{0:T(128)S(1)}, s32[16]{0:T(128)}, u32[]{:S(2)}) copy-start(s32[16]{0:T(128)} %constant.32.clone) | copy-start | bytes 196
  20.7 5.7 %collective-permute-start = (f32[1,72,192]{2,1,0:T(8,128)S(1)}, f32[1,72,192]{2,1,0:T(8,128)S(1)}, u32[]{:S(2)}, u32[]{:S(2)}) collective-permute-start(f32[1,72,192]{2,1,0:T(8,128)S(1)} %bitcast.16), channel_id=1, source_target_pairs={{0,4},{1,5},{2,6},{3,7},{4,0},{5,1},{6,2},{7,3},{8,12},{9,13},{10,... | collective-permute-start | bytes 165896 | tf_op jit(solution)/shard_map/ppermute | solution.py:195
  23.8 7.8 %collective-permute-start.1 = (f32[1,72,192]{2,1,0:T(8,128)S(1)}, f32[1,72,192]{2,1,0:T(8,128)S(1)}, u32[]{:S(2)}, u32[]{:S(2)}) collective-permute-start(f32[1,72,192]{2,1,0:T(8,128)S(1)} %bitcast.17), channel_id=1, source_target_pairs={{0,8},{1,9},{2,10},{3,11},{4,12},{5,13},{6,14},{7,15},{8,0},{9,1},... | collective-permute-start | bytes 165896 | tf_op jit(solution)/shard_map/ppermute | solution.py:195
  26.4 6.3 %collective-permute-start.2 = (f32[1,72,192]{2,1,0:T(8,128)S(1)}, f32[1,72,192]{2,1,0:T(8,128)S(1)}, u32[]{:S(2)}, u32[]{:S(2)}) collective-permute-start(f32[1,72,192]{2,1,0:T(8,128)S(1)} %bitcast.18), channel_id=1, source_target_pairs={{0,12},{1,13},{2,14},{3,15},{4,8},{5,9},{6,10},{7,11},{8,4},{9,5},... | collective-permute-start | bytes 165896 | tf_op jit(solution)/shard_map/ppermute | solution.py:195
  32.7 7.0 %collective-permute-start.3 = (f32[4,72,192]{2,1,0:T(8,128)S(1)}, f32[4,72,192]{2,1,0:T(8,128)S(1)}, u32[]{:S(2)}, u32[]{:S(2)}) collective-permute-start(f32[4,72,192]{2,1,0:T(8,128)S(1)} %pad_maximum_fusion), channel_id=1, source_target_pairs={{0,2},{1,3},{2,0},{3,1},{4,6},{5,7},{6,4},{7,5},{8,10},{9,11},{10,... | collective-permute-start | bytes 663560 | tf_op jit(solution)/shard_map/ppermute | solution.py:195
  39.7 2.1 %collective-permute-start.4 = (f32[8,72,192]{2,1,0:T(8,128)S(1)}, f32[8,72,192]{2,1,0:T(8,128)S(1)}, u32[]{:S(2)}, u32[]{:S(2)}) collective-permute-start(f32[8,72,192]{2,1,0:T(8,128)S(1)} %get-tuple-element.7), channel_id=1, source_target_pairs={{0,1},{1,0},{2,3},{3,2},{4,5},{5,4},{6,7},{7,6},{8,9},{9,8},{10,11... | collective-permute-start | bytes 1327112 | tf_op jit(solution)/shard_map/ppermute | solution.py:195
  44.6 0.7 %copy-start = (f32[3,3]{1,0:T(4,128)S(1)}, f32[3,3]{1,0:T(4,128)}, u32[]{:S(2)}) copy-start(f32[3,3]{1,0:T(4,128)} %k_ref.1) | copy-start | bytes 112

commit v21 on v20

--- a/solution.py
+++ b/solution.py
@@ -18,7 +18,7 @@
 AFF_SCALE = 8.0
 SEG_BLOCK = 8
 WIN = SEGLEN + 8
-CONV_ROWS = 256
+CONV_ROWS = 512
 ONE_HOT_LIMIT = 1 << 20
 
 

time: 47.1 us -> 46.2 us (0.981)
  Pallas kernels: 20.7 us -> 19.8 us
    pallas_call x1, Pallas kernels: 19.1 us -> 18.2 us  [embed_slots(): pl.pallas_call(_pool_kernel, out_shape=jax.ShapeDtypeStruct((slots + meta...]
where the time goes in v21:
time: 46.2 us; the launch traced here: 46 us
  Pallas kernels  19.8 us (43%)
  waiting for transfers between devices  13.4 us (29%)
  starting transfers between devices  7.33 us (16%)
  other arithmetic  2.4 us (5%)
  local copies, waits for them, and re-layouts  2.34 us (5%)
  matrix products  0.47 us (1%)
    pallas_call x1, Pallas kernels, embed_slots(): pl.pallas_call(_pool_kernel, out_shape=jax.ShapeDtypeStruct((slots + meta...  18.2 us
    ppermute x5, waiting for transfers between devices, gather_wide(): lax.ppermute(buf, 'wide', [(i, i ^ f) for i in range(group_size)])  13.4 us
    ppermute x5, starting transfers between devices, gather_wide(): lax.ppermute(buf, 'wide', [(i, i ^ f) for i in range(group_size)])  7.33 us
    unnamed x17, local copies, waits for them, and re-layouts  1.68 us
    pallas_call x1, Pallas kernels, smooth_affinity(): pl.pallas_call(_affinity_kernel, out_shape=jax.ShapeDtypeStruct((height,...  1.65 us
    reduce_sum x1, other arithmetic, per_device(): rank = jnp.sum(earlier.astype(jnp.int32), axis=1)  1.03 us
  transfers between devices with their start and end apart: 5, of which 4 were waited for; matrix products, arithmetic and copies ran while one was open for 0% of the time, Pallas kernels for 0%

profile of v21, /device:TPU:0, one launch (start us, length us, event | category | flops | bytes accessed | tf_op | source)
XLA Modules:
  0.0 46.0 jit_solution(17615914790415317713)
XLA Ops:
  0.0 0.0 copy-start.2
  0.0 0.0 copy-start.3
  0.0 0.0 copy-start.4
  0.0 0.0 copy-start.1
  0.0 1.5 %copy.13.frames_hbm = f32[2048,80]{1,0:T(8,128)S(1)} copy(f32[2048,80]{0,1:T(8,128)} %param.9) | data formatting | bytes 1310720 | tf_op args[0]
  1.5 0.0 copy-done.2
  1.5 0.0 copy-done.3
  1.5 0.0 copy-done.4
  1.6 0.1 select_maximum_fusion
  1.6 0.0 copy-done.1
  1.6 18.2 %shard_map.91 = f32[72,192]{1,0:T(8,128)S(1)} custom-call(s32[64]{0:T(128)S(1)} %broadcast_clamp_fusion.starts_ref, f32[2048,80]{1,0:T(8,128)S(1)} %copy.13.frames_hbm, f32[240,1024]{1,0:T(8,128)} %w_hbm.1, f32[1,1024]{1,0:T(1,128)S(1)} %bitcast.21, f32[192,2048]{1,0:T(8,128)} %bitcast.23, f32[8,192]{1,0:T(8,128)S(1)} %pad.9.meta_ref), custom_call_target="tpu_custom_call" | custom-call | flops 6379536384 | bytes 3260416 | tf_op jit(solution)/shard_map/pallas_call | solution.py:100
  19.8 0.0 copy-start.5
  19.8 3.1 %collective-permute-start = (f32[1,72,192]{2,1,0:T(8,128)S(1)}, f32[1,72,192]{2,1,0:T(8,128)S(1)}, u32[]{:S(2)}, u32[]{:S(2)}) collective-permute-start(f32[1,72,192]{2,1,0:T(8,128)S(1)} %bitcast.16), channel_id=1, source_target_pairs={{0,4},{1,5},{2,6},{3,7},{4,0},{5,1},{6,2},{7,3},{8,12},{9,13},{10,... | collective-permute-start | bytes 165896 | tf_op jit(solution)/shard_map/ppermute | solution.py:195
  22.9 2.6 %collective-permute-start.1 = (f32[1,72,192]{2,1,0:T(8,128)S(1)}, f32[1,72,192]{2,1,0:T(8,128)S(1)}, u32[]{:S(2)}, u32[]{:S(2)}) collective-permute-start(f32[1,72,192]{2,1,0:T(8,128)S(1)} %bitcast.17), channel_id=1, source_target_pairs={{0,8},{1,9},{2,10},{3,11},{4,12},{5,13},{6,14},{7,15},{8,0},{9,1},... | collective-permute-start | bytes 165896 | tf_op jit(solution)/shard_map/ppermute | solution.py:195
  25.5 0.0 collective-permute-start.2
  25.5 0.0 collective-permute-done
  25.5 5.2 %collective-permute-done.1 = f32[1,72,192]{2,1,0:T(8,128)S(1)} collective-permute-done((f32[1,72,192]{2,1,0:T(8,128)S(1)}, f32[1,72,192]{2,1,0:T(8,128)S(1)}, u32[]{:S(2)}, u32[]{:S(2)}) %collective-permute-start.1) | collective-permute-done | bytes 55328 | tf_op jit(solution)/shard_map/ppermute | solution.py:195
  30.7 1.1 %collective-permute-done.2 = f32[1,72,192]{2,1,0:T(8,128)S(1)} collective-permute-done((f32[1,72,192]{2,1,0:T(8,128)S(1)}, f32[1,72,192]{2,1,0:T(8,128)S(1)}, u32[]{:S(2)}, u32[]{:S(2)}) %collective-permute-start.2) | collective-permute-done | bytes 55328 | tf_op jit(solution)/shard_map/ppermute | solution.py:195
  31.8 1.6 %collective-permute-start.3 = (f32[4,72,192]{2,1,0:T(8,128)S(1)}, f32[4,72,192]{2,1,0:T(8,128)S(1)}, u32[]{:S(2)}, u32[]{:S(2)}) collective-permute-start(f32[4,72,192]{2,1,0:T(8,128)S(1)} %pad_maximum_fusion), channel_id=1, source_target_pairs={{0,2},{1,3},{2,0},{3,1},{4,6},{5,7},{6,4},{7,5},{8,10},{9,11},{10,... | collective-permute-start | bytes 663560 | tf_op jit(solution)/shard_map/ppermute | solution.py:195
  33.4 5.4 %collective-permute-done.3 = f32[4,72,192]{2,1,0:T(8,128)S(1)} collective-permute-done((f32[4,72,192]{2,1,0:T(8,128)S(1)}, f32[4,72,192]{2,1,0:T(8,128)S(1)}, u32[]{:S(2)}, u32[]{:S(2)}) %collective-permute-start.3) | collective-permute-done | bytes 221216 | tf_op jit(solution)/shard_map/ppermute | solution.py:195
  38.8 0.1 collective-permute-start.4
  38.9 0.0 copy-done.5
  38.9 0.1 iota_add_fusion
  39.0 0.1 add.54
  39.1 1.8 %collective-permute-done.4 = f32[8,72,192]{2,1,0:T(8,128)S(1)} collective-permute-done((f32[8,72,192]{2,1,0:T(8,128)S(1)}, f32[8,72,192]{2,1,0:T(8,128)S(1)}, u32[]{:S(2)}, u32[]{:S(2)}) %collective-permute-start.4) | collective-permute-done | bytes 442400 | tf_op jit(solution)/shard_map/ppermute | solution.py:195
  41.0 0.1 reshape.106
  41.1 0.1 slice_convert_fusion
  41.2 0.1 convert_element_type.53
  41.2 1.0 %convert_reduce_fusion = s32[1024]{0:T(1024)S(1)} fusion(s32[1024]{0:T(1024)S(1)} %convert_element_type.53, s32[1024]{0:T(1024)S(1)} %add.54), kind=kLoop, calls=%fused_computation | loop fusion | flops 5241856 | bytes 12288 | tf_op jit(solution)/shard_map/reduce_sum | solution.py:229
  42.3 0.1 convert_element_type.58
  42.3 0.3 select_reduce_fusion
  42.6 0.1 pad_add_fusion
  42.7 0.1 dynamic-slice_bitcast_fusion
  42.8 0.1 copy.15.row_rec_ref
  42.9 0.2 select_reduce_fusion.1
  43.1 0.2 multiply_reduce_fusion
  43.4 0.1 sqrt.12
  43.5 0.2 fusion.3
  43.7 0.0 copy-start
  43.7 0.5 %fusion.1.col_unit_ref = bf16[512,192]{1,0:T(8,128)(2,1)S(1)} fusion(bf16[1024,192]{1,0:T(8,128)(2,1)S(1)} %fusion.3, s32[1024]{0:T(1024)S(1)} %add_select_fusion), kind=kOutput, calls=%fused_computation.4 | convolution fusion | flops 201949184 | bytes 593920 | tf_op jit(solution)/shard_map/dot_general | solution.py:237
  44.2 0.1 copy-done
  44.4 1.6 %shard_map.92 = f32[32,512]{1,0:T(8,128)} custom-call(f32[3,3]{1,0:T(4,128)S(1)} %copy-done, bf16[34,192]{1,0:T(8,128)(2,1)S(1)} %fusion.6.row_unit_ref, bf16[512,192]{1,0:T(8,128)(2,1)S(1)} %fusion.1.col_unit_ref, s32[34,1]{1,0:T(8,128)S(1)} %copy.15.row_rec_ref, s32[1,512]{1,0:T(1,128)S(1)} %bitcast.20), custom_call_target="tpu_custom_call" | custom-call | flops 7012352 | bytes 275200 | tf_op jit(solution)/shard_map/pallas_call | solution.py:161
  (19 shorter events, 0.3 us)
Async XLA Ops:
  0.0 1.5 %copy-start.2 = (s32[64]{0:T(128)S(1)}, s32[64]{0:T(128)}, u32[]{:S(2)}) copy-start(s32[64]{0:T(128)} %param.11) | copy-start | bytes 772
  0.0 1.5 %copy-start.3 = (s32[64]{0:T(128)S(1)}, s32[64]{0:T(128)}, u32[]{:S(2)}) copy-start(s32[64]{0:T(128)} %param.12) | copy-start | bytes 772
  0.0 1.5 %copy-start.4 = (s32[64]{0:T(128)S(1)}, s32[64]{0:T(128)}, u32[]{:S(2)}) copy-start(s32[64]{0:T(128)} %param.10) | copy-start | bytes 772
  0.0 1.6 %copy-start.1 = (f32[1024]{0:T(1024)S(1)}, f32[1024]{0:T(1024)}, u32[]{:S(2)}) copy-start(f32[1024]{0:T(1024)} %param.14) | copy-start | bytes 12292
  19.8 19.1 %copy-start.5 = (s32[16]{0:T(128)S(1)}, s32[16]{0:T(128)}, u32[]{:S(2)}) copy-start(s32[16]{0:T(128)} %constant.32.clone) | copy-start | bytes 196
  19.8 5.7 %collective-permute-start = (f32[1,72,192]{2,1,0:T(8,128)S(1)}, f32[1,72,192]{2,1,0:T(8,128)S(1)}, u32[]{:S(2)}, u32[]{:S(2)}) collective-permute-start(f32[1,72,192]{2,1,0:T(8,128)S(1)} %bitcast.16), channel_id=1, source_target_pairs={{0,4},{1,5},{2,6},{3,7},{4,0},{5,1},{6,2},{7,3},{8,12},{9,13},{10,... | collective-permute-start | bytes 165896 | tf_op jit(solution)/shard_map/ppermute | solution.py:195
  22.9 7.8 %collective-permute-start.1 = (f32[1,72,192]{2,1,0:T(8,128)S(1)}, f32[1,72,192]{2,1,0:T(8,128)S(1)}, u32[]{:S(2)}, u32[]{:S(2)}) collective-permute-start(f32[1,72,192]{2,1,0:T(8,128)S(1)} %bitcast.17), channel_id=1, source_target_pairs={{0,8},{1,9},{2,10},{3,11},{4,12},{5,13},{6,14},{7,15},{8,0},{9,1},... | collective-permute-start | bytes 165896 | tf_op jit(solution)/shard_map/ppermute | solution.py:195
  25.5 6.3 %collective-permute-start.2 = (f32[1,72,192]{2,1,0:T(8,128)S(1)}, f32[1,72,192]{2,1,0:T(8,128)S(1)}, u32[]{:S(2)}, u32[]{:S(2)}) collective-permute-start(f32[1,72,192]{2,1,0:T(8,128)S(1)} %bitcast.18), channel_id=1, source_target_pairs={{0,12},{1,13},{2,14},{3,15},{4,8},{5,9},{6,10},{7,11},{8,4},{9,5},... | collective-permute-start | bytes 165896 | tf_op jit(solution)/shard_map/ppermute | solution.py:195
  31.8 7.0 %collective-permute-start.3 = (f32[4,72,192]{2,1,0:T(8,128)S(1)}, f32[4,72,192]{2,1,0:T(8,128)S(1)}, u32[]{:S(2)}, u32[]{:S(2)}) collective-permute-start(f32[4,72,192]{2,1,0:T(8,128)S(1)} %pad_maximum_fusion), channel_id=1, source_target_pairs={{0,2},{1,3},{2,0},{3,1},{4,6},{5,7},{6,4},{7,5},{8,10},{9,11},{10,... | collective-permute-start | bytes 663560 | tf_op jit(solution)/shard_map/ppermute | solution.py:195
  38.8 2.1 %collective-permute-start.4 = (f32[8,72,192]{2,1,0:T(8,128)S(1)}, f32[8,72,192]{2,1,0:T(8,128)S(1)}, u32[]{:S(2)}, u32[]{:S(2)}) collective-permute-start(f32[8,72,192]{2,1,0:T(8,128)S(1)} %get-tuple-element.7), channel_id=1, source_target_pairs={{0,1},{1,0},{2,3},{3,2},{4,5},{5,4},{6,7},{7,6},{8,9},{9,8},{10,11... | collective-permute-start | bytes 1327112 | tf_op jit(solution)/shard_map/ppermute | solution.py:195
  43.7 0.7 %copy-start = (f32[3,3]{1,0:T(4,128)S(1)}, f32[3,3]{1,0:T(4,128)}, u32[]{:S(2)}) copy-start(f32[3,3]{1,0:T(4,128)} %k_ref.1) | copy-start | bytes 112

commit v22 on v21

--- a/solution.py
+++ b/solution.py
@@ -18,7 +18,7 @@
 AFF_SCALE = 8.0
 SEG_BLOCK = 8
 WIN = SEGLEN + 8
-CONV_ROWS = 512
+CONV_ROWS = 1024
 ONE_HOT_LIMIT = 1 << 20
 
 

time: 46.2 us -> 45.8 us (level)
  no operation moved by 1% of the time
where the time goes in v22:
time: 45.8 us; the launch traced here: 45.6 us
  Pallas kernels  19.4 us (42%)
  waiting for transfers between devices  13.4 us (29%)
  starting transfers between devices  7.34 us (16%)
  other arithmetic  2.4 us (5%)
  local copies, waits for them, and re-layouts  2.34 us (5%)
  matrix products  0.47 us (1%)
    pallas_call x1, Pallas kernels, embed_slots(): pl.pallas_call(_pool_kernel, out_shape=jax.ShapeDtypeStruct((slots + meta...  17.7 us
    ppermute x5, waiting for transfers between devices, gather_wide(): lax.ppermute(buf, 'wide', [(i, i ^ f) for i in range(group_size)])  13.4 us
    ppermute x5, starting transfers between devices, gather_wide(): lax.ppermute(buf, 'wide', [(i, i ^ f) for i in range(group_size)])  7.34 us
    unnamed x17, local copies, waits for them, and re-layouts  1.68 us
    pallas_call x1, Pallas kernels, smooth_affinity(): pl.pallas_call(_affinity_kernel, out_shape=jax.ShapeDtypeStruct((height,...  1.65 us
    reduce_sum x1, other arithmetic, per_device(): rank = jnp.sum(earlier.astype(jnp.int32), axis=1)  1.03 us
  transfers between devices with their start and end apart: 5, of which 4 were waited for; matrix products, arithmetic and copies ran while one was open for 0% of the time, Pallas kernels for 0%

profile of v22, /device:TPU:0, one launch (start us, length us, event | category | flops | bytes accessed | tf_op | source)
XLA Modules:
  0.0 45.6 jit_solution(15540609273568057256)
XLA Ops:
  0.0 0.0 copy-start.2
  0.0 0.0 copy-start.3
  0.0 0.0 copy-start.4
  0.0 0.0 copy-start.1
  0.0 1.5 %copy.13.frames_hbm = f32[2048,80]{1,0:T(8,128)S(1)} copy(f32[2048,80]{0,1:T(8,128)} %param.9) | data formatting | bytes 1310720 | tf_op args[0]
  1.5 0.0 copy-done.2
  1.5 0.0 copy-done.3
  1.5 0.0 copy-done.4
  1.6 0.1 select_maximum_fusion
  1.6 0.0 copy-done.1
  1.6 17.7 %shard_map.91 = f32[72,192]{1,0:T(8,128)S(1)} custom-call(s32[64]{0:T(128)S(1)} %broadcast_clamp_fusion.starts_ref, f32[2048,80]{1,0:T(8,128)S(1)} %copy.13.frames_hbm, f32[240,1024]{1,0:T(8,128)} %w_hbm.1, f32[1,1024]{1,0:T(1,128)S(1)} %bitcast.21, f32[192,2048]{1,0:T(8,128)} %bitcast.23, f32[8,192]{1,0:T(8,128)S(1)} %pad.9.meta_ref), custom_call_target="tpu_custom_call" | custom-call | flops 6379536384 | bytes 3260416 | tf_op jit(solution)/shard_map/pallas_call | solution.py:100
  19.4 0.0 copy-start.5
  19.4 3.1 %collective-permute-start = (f32[1,72,192]{2,1,0:T(8,128)S(1)}, f32[1,72,192]{2,1,0:T(8,128)S(1)}, u32[]{:S(2)}, u32[]{:S(2)}) collective-permute-start(f32[1,72,192]{2,1,0:T(8,128)S(1)} %bitcast.16), channel_id=1, source_target_pairs={{0,4},{1,5},{2,6},{3,7},{4,0},{5,1},{6,2},{7,3},{8,12},{9,13},{10,... | collective-permute-start | bytes 165896 | tf_op jit(solution)/shard_map/ppermute | solution.py:195
  22.5 2.6 %collective-permute-start.1 = (f32[1,72,192]{2,1,0:T(8,128)S(1)}, f32[1,72,192]{2,1,0:T(8,128)S(1)}, u32[]{:S(2)}, u32[]{:S(2)}) collective-permute-start(f32[1,72,192]{2,1,0:T(8,128)S(1)} %bitcast.17), channel_id=1, source_target_pairs={{0,8},{1,9},{2,10},{3,11},{4,12},{5,13},{6,14},{7,15},{8,0},{9,1},... | collective-permute-start | bytes 165896 | tf_op jit(solution)/shard_map/ppermute | solution.py:195
  25.1 0.0 collective-permute-start.2
  25.1 0.0 collective-permute-done
  25.1 5.2 %collective-permute-done.1 = f32[1,72,192]{2,1,0:T(8,128)S(1)} collective-permute-done((f32[1,72,192]{2,1,0:T(8,128)S(1)}, f32[1,72,192]{2,1,0:T(8,128)S(1)}, u32[]{:S(2)}, u32[]{:S(2)}) %collective-permute-start.1) | collective-permute-done | bytes 55328 | tf_op jit(solution)/shard_map/ppermute | solution.py:195
  30.3 1.1 %collective-permute-done.2 = f32[1,72,192]{2,1,0:T(8,128)S(1)} collective-permute-done((f32[1,72,192]{2,1,0:T(8,128)S(1)}, f32[1,72,192]{2,1,0:T(8,128)S(1)}, u32[]{:S(2)}, u32[]{:S(2)}) %collective-permute-start.2) | collective-permute-done | bytes 55328 | tf_op jit(solution)/shard_map/ppermute | solution.py:195
  31.4 1.6 %collective-permute-start.3 = (f32[4,72,192]{2,1,0:T(8,128)S(1)}, f32[4,72,192]{2,1,0:T(8,128)S(1)}, u32[]{:S(2)}, u32[]{:S(2)}) collective-permute-start(f32[4,72,192]{2,1,0:T(8,128)S(1)} %pad_maximum_fusion), channel_id=1, source_target_pairs={{0,2},{1,3},{2,0},{3,1},{4,6},{5,7},{6,4},{7,5},{8,10},{9,11},{10,... | collective-permute-start | bytes 663560 | tf_op jit(solution)/shard_map/ppermute | solution.py:195
  33.0 5.4 %collective-permute-done.3 = f32[4,72,192]{2,1,0:T(8,128)S(1)} collective-permute-done((f32[4,72,192]{2,1,0:T(8,128)S(1)}, f32[4,72,192]{2,1,0:T(8,128)S(1)}, u32[]{:S(2)}, u32[]{:S(2)}) %collective-permute-start.3) | collective-permute-done | bytes 221216 | tf_op jit(solution)/shard_map/ppermute | solution.py:195
  38.4 0.1 collective-permute-start.4
  38.5 0.0 copy-done.5
  38.5 0.1 iota_add_fusion
  38.6 0.1 add.54
  38.7 1.8 %collective-permute-done.4 = f32[8,72,192]{2,1,0:T(8,128)S(1)} collective-permute-done((f32[8,72,192]{2,1,0:T(8,128)S(1)}, f32[8,72,192]{2,1,0:T(8,128)S(1)}, u32[]{:S(2)}, u32[]{:S(2)}) %collective-permute-start.4) | collective-permute-done | bytes 442400 | tf_op jit(solution)/shard_map/ppermute | solution.py:195
  40.6 0.1 reshape.106
  40.6 0.1 slice_convert_fusion
  40.7 0.1 convert_element_type.53
  40.8 1.0 %convert_reduce_fusion = s32[1024]{0:T(1024)S(1)} fusion(s32[1024]{0:T(1024)S(1)} %convert_element_type.53, s32[1024]{0:T(1024)S(1)} %add.54), kind=kLoop, calls=%fused_computation | loop fusion | flops 5241856 | bytes 12288 | tf_op jit(solution)/shard_map/reduce_sum | solution.py:229
  41.9 0.1 convert_element_type.58
  41.9 0.3 select_reduce_fusion
  42.2 0.1 pad_add_fusion
  42.3 0.1 dynamic-slice_bitcast_fusion
  42.4 0.1 copy.15.row_rec_ref
  42.5 0.2 select_reduce_fusion.1
  42.7 0.2 multiply_reduce_fusion
  43.0 0.1 sqrt.12
  43.0 0.2 fusion.3
  43.3 0.0 copy-start
  43.3 0.5 %fusion.1.col_unit_ref = bf16[512,192]{1,0:T(8,128)(2,1)S(1)} fusion(bf16[1024,192]{1,0:T(8,128)(2,1)S(1)} %fusion.3, s32[1024]{0:T(1024)S(1)} %add_select_fusion), kind=kOutput, calls=%fused_computation.4 | convolution fusion | flops 201949184 | bytes 593920 | tf_op jit(solution)/shard_map/dot_general | solution.py:237
  43.8 0.1 copy-done
  43.9 1.6 %shard_map.92 = f32[32,512]{1,0:T(8,128)} custom-call(f32[3,3]{1,0:T(4,128)S(1)} %copy-done, bf16[34,192]{1,0:T(8,128)(2,1)S(1)} %fusion.6.row_unit_ref, bf16[512,192]{1,0:T(8,128)(2,1)S(1)} %fusion.1.col_unit_ref, s32[34,1]{1,0:T(8,128)S(1)} %copy.15.row_rec_ref, s32[1,512]{1,0:T(1,128)S(1)} %bitcast.20), custom_call_target="tpu_custom_call" | custom-call | flops 7012352 | bytes 275200 | tf_op jit(solution)/shard_map/pallas_call | solution.py:161
  (19 shorter events, 0.3 us)
Async XLA Ops:
  0.0 1.5 %copy-start.2 = (s32[64]{0:T(128)S(1)}, s32[64]{0:T(128)}, u32[]{:S(2)}) copy-start(s32[64]{0:T(128)} %param.11) | copy-start | bytes 772
  0.0 1.5 %copy-start.3 = (s32[64]{0:T(128)S(1)}, s32[64]{0:T(128)}, u32[]{:S(2)}) copy-start(s32[64]{0:T(128)} %param.12) | copy-start | bytes 772
  0.0 1.5 %copy-start.4 = (s32[64]{0:T(128)S(1)}, s32[64]{0:T(128)}, u32[]{:S(2)}) copy-start(s32[64]{0:T(128)} %param.10) | copy-start | bytes 772
  0.0 1.6 %copy-start.1 = (f32[1024]{0:T(1024)S(1)}, f32[1024]{0:T(1024)}, u32[]{:S(2)}) copy-start(f32[1024]{0:T(1024)} %param.14) | copy-start | bytes 12292
  19.4 19.1 %copy-start.5 = (s32[16]{0:T(128)S(1)}, s32[16]{0:T(128)}, u32[]{:S(2)}) copy-start(s32[16]{0:T(128)} %constant.32.clone) | copy-start | bytes 196
  19.4 5.7 %collective-permute-start = (f32[1,72,192]{2,1,0:T(8,128)S(1)}, f32[1,72,192]{2,1,0:T(8,128)S(1)}, u32[]{:S(2)}, u32[]{:S(2)}) collective-permute-start(f32[1,72,192]{2,1,0:T(8,128)S(1)} %bitcast.16), channel_id=1, source_target_pairs={{0,4},{1,5},{2,6},{3,7},{4,0},{5,1},{6,2},{7,3},{8,12},{9,13},{10,... | collective-permute-start | bytes 165896 | tf_op jit(solution)/shard_map/ppermute | solution.py:195
  22.5 7.8 %collective-permute-start.1 = (f32[1,72,192]{2,1,0:T(8,128)S(1)}, f32[1,72,192]{2,1,0:T(8,128)S(1)}, u32[]{:S(2)}, u32[]{:S(2)}) collective-permute-start(f32[1,72,192]{2,1,0:T(8,128)S(1)} %bitcast.17), channel_id=1, source_target_pairs={{0,8},{1,9},{2,10},{3,11},{4,12},{5,13},{6,14},{7,15},{8,0},{9,1},... | collective-permute-start | bytes 165896 | tf_op jit(solution)/shard_map/ppermute | solution.py:195
  25.1 6.3 %collective-permute-start.2 = (f32[1,72,192]{2,1,0:T(8,128)S(1)}, f32[1,72,192]{2,1,0:T(8,128)S(1)}, u32[]{:S(2)}, u32[]{:S(2)}) collective-permute-start(f32[1,72,192]{2,1,0:T(8,128)S(1)} %bitcast.18), channel_id=1, source_target_pairs={{0,12},{1,13},{2,14},{3,15},{4,8},{5,9},{6,10},{7,11},{8,4},{9,5},... | collective-permute-start | bytes 165896 | tf_op jit(solution)/shard_map/ppermute | solution.py:195
  31.4 7.0 %collective-permute-start.3 = (f32[4,72,192]{2,1,0:T(8,128)S(1)}, f32[4,72,192]{2,1,0:T(8,128)S(1)}, u32[]{:S(2)}, u32[]{:S(2)}) collective-permute-start(f32[4,72,192]{2,1,0:T(8,128)S(1)} %pad_maximum_fusion), channel_id=1, source_target_pairs={{0,2},{1,3},{2,0},{3,1},{4,6},{5,7},{6,4},{7,5},{8,10},{9,11},{10,... | collective-permute-start | bytes 663560 | tf_op jit(solution)/shard_map/ppermute | solution.py:195
  38.4 2.1 %collective-permute-start.4 = (f32[8,72,192]{2,1,0:T(8,128)S(1)}, f32[8,72,192]{2,1,0:T(8,128)S(1)}, u32[]{:S(2)}, u32[]{:S(2)}) collective-permute-start(f32[8,72,192]{2,1,0:T(8,128)S(1)} %get-tuple-element.7), channel_id=1, source_target_pairs={{0,1},{1,0},{2,3},{3,2},{4,5},{5,4},{6,7},{7,6},{8,9},{9,8},{10,11... | collective-permute-start | bytes 1327112 | tf_op jit(solution)/shard_map/ppermute | solution.py:195
  43.3 0.7 %copy-start = (f32[3,3]{1,0:T(4,128)S(1)}, f32[3,3]{1,0:T(4,128)}, u32[]{:S(2)}) copy-start(f32[3,3]{1,0:T(4,128)} %k_ref.1) | copy-start | bytes 112

commit v23 on v22

--- a/solution.py
+++ b/solution.py
@@ -18,7 +18,7 @@
 AFF_SCALE = 8.0
 SEG_BLOCK = 8
 WIN = SEGLEN + 8
-CONV_ROWS = 1024
+CONV_ROWS = 2048
 ONE_HOT_LIMIT = 1 << 20
 
 

time: 45.8 us -> 48 us (1.048)
  Pallas kernels: 19.4 us -> 21.6 us
    pallas_call x1, Pallas kernels: 17.7 us -> 19.9 us  [embed_slots(): pl.pallas_call(_pool_kernel, out_shape=jax.ShapeDtypeStruct((slots + meta...]
where the time goes in v23:
time: 48 us; the launch traced here: 47.8 us
  Pallas kernels  21.6 us (45%)
  waiting for transfers between devices  13.4 us (28%)
  starting transfers between devices  7.34 us (15%)
  other arithmetic  2.4 us (5%)
  local copies, waits for them, and re-layouts  2.34 us (5%)
    pallas_call x1, Pallas kernels, embed_slots(): pl.pallas_call(_pool_kernel, out_shape=jax.ShapeDtypeStruct((slots + meta...  19.9 us
    ppermute x5, waiting for transfers between devices, gather_wide(): lax.ppermute(buf, 'wide', [(i, i ^ f) for i in range(group_size)])  13.4 us
    ppermute x5, starting transfers between devices, gather_wide(): lax.ppermute(buf, 'wide', [(i, i ^ f) for i in range(group_size)])  7.34 us
    unnamed x17, local copies, waits for them, and re-layouts  1.68 us
    pallas_call x1, Pallas kernels, smooth_affinity(): pl.pallas_call(_affinity_kernel, out_shape=jax.ShapeDtypeStruct((height,...  1.65 us
    reduce_sum x1, other arithmetic, per_device(): rank = jnp.sum(earlier.astype(jnp.int32), axis=1)  1.03 us
  transfers between devices with their start and end apart: 5, of which 4 were waited for; matrix products, arithmetic and copies ran while one was open for 0% of the time, Pallas kernels for 0%

profile of v23, /device:TPU:0, one launch (start us, length us, event | category | flops | bytes accessed | tf_op | source)
XLA Modules:
  0.0 47.8 jit_solution(10787400222539942693)
XLA Ops:
  0.0 0.0 copy-start.2
  0.0 0.0 copy-start.3
  0.0 0.0 copy-start.4
  0.0 0.0 copy-start.1
  0.0 1.5 %copy.13.frames_hbm = f32[2048,80]{1,0:T(8,128)S(1)} copy(f32[2048,80]{0,1:T(8,128)} %param.9) | data formatting | bytes 1310720 | tf_op args[0]
  1.5 0.0 copy-done.2
  1.5 0.0 copy-done.3
  1.5 0.0 copy-done.4
  1.6 0.1 select_maximum_fusion
  1.6 0.0 copy-done.1
  1.6 19.9 %shard_map.91 = f32[72,192]{1,0:T(8,128)S(1)} custom-call(s32[64]{0:T(128)S(1)} %broadcast_clamp_fusion.starts_ref, f32[2048,80]{1,0:T(8,128)S(1)} %copy.13.frames_hbm, f32[240,1024]{1,0:T(8,128)} %w_hbm.1, f32[1,1024]{1,0:T(1,128)S(1)} %bitcast.21, f32[192,2048]{1,0:T(8,128)} %bitcast.23, f32[8,192]{1,0:T(8,128)S(1)} %pad.9.meta_ref), custom_call_target="tpu_custom_call" | custom-call | flops 6379536384 | bytes 3260416 | tf_op jit(solution)/shard_map/pallas_call | solution.py:100
  21.6 0.0 copy-start.5
  21.6 3.1 %collective-permute-start = (f32[1,72,192]{2,1,0:T(8,128)S(1)}, f32[1,72,192]{2,1,0:T(8,128)S(1)}, u32[]{:S(2)}, u32[]{:S(2)}) collective-permute-start(f32[1,72,192]{2,1,0:T(8,128)S(1)} %bitcast.16), channel_id=1, source_target_pairs={{0,4},{1,5},{2,6},{3,7},{4,0},{5,1},{6,2},{7,3},{8,12},{9,13},{10,... | collective-permute-start | bytes 165896 | tf_op jit(solution)/shard_map/ppermute | solution.py:195
  24.7 2.6 %collective-permute-start.1 = (f32[1,72,192]{2,1,0:T(8,128)S(1)}, f32[1,72,192]{2,1,0:T(8,128)S(1)}, u32[]{:S(2)}, u32[]{:S(2)}) collective-permute-start(f32[1,72,192]{2,1,0:T(8,128)S(1)} %bitcast.17), channel_id=1, source_target_pairs={{0,8},{1,9},{2,10},{3,11},{4,12},{5,13},{6,14},{7,15},{8,0},{9,1},... | collective-permute-start | bytes 165896 | tf_op jit(solution)/shard_map/ppermute | solution.py:195
  27.3 0.0 collective-permute-start.2
  27.3 0.0 collective-permute-done
  27.3 5.2 %collective-permute-done.1 = f32[1,72,192]{2,1,0:T(8,128)S(1)} collective-permute-done((f32[1,72,192]{2,1,0:T(8,128)S(1)}, f32[1,72,192]{2,1,0:T(8,128)S(1)}, u32[]{:S(2)}, u32[]{:S(2)}) %collective-permute-start.1) | collective-permute-done | bytes 55328 | tf_op jit(solution)/shard_map/ppermute | solution.py:195
  32.5 1.1 %collective-permute-done.2 = f32[1,72,192]{2,1,0:T(8,128)S(1)} collective-permute-done((f32[1,72,192]{2,1,0:T(8,128)S(1)}, f32[1,72,192]{2,1,0:T(8,128)S(1)}, u32[]{:S(2)}, u32[]{:S(2)}) %collective-permute-start.2) | collective-permute-done | bytes 55328 | tf_op jit(solution)/shard_map/ppermute | solution.py:195
  33.5 1.6 %collective-permute-start.3 = (f32[4,72,192]{2,1,0:T(8,128)S(1)}, f32[4,72,192]{2,1,0:T(8,128)S(1)}, u32[]{:S(2)}, u32[]{:S(2)}) collective-permute-start(f32[4,72,192]{2,1,0:T(8,128)S(1)} %pad_maximum_fusion), channel_id=1, source_target_pairs={{0,2},{1,3},{2,0},{3,1},{4,6},{5,7},{6,4},{7,5},{8,10},{9,11},{10,... | collective-permute-start | bytes 663560 | tf_op jit(solution)/shard_map/ppermute | solution.py:195
  35.2 5.4 %collective-permute-done.3 = f32[4,72,192]{2,1,0:T(8,128)S(1)} collective-permute-done((f32[4,72,192]{2,1,0:T(8,128)S(1)}, f32[4,72,192]{2,1,0:T(8,128)S(1)}, u32[]{:S(2)}, u32[]{:S(2)}) %collective-permute-start.3) | collective-permute-done | bytes 221216 | tf_op jit(solution)/shard_map/ppermute | solution.py:195
  40.6 0.1 collective-permute-start.4
  40.7 0.0 copy-done.5
  40.7 0.1 iota_add_fusion
  40.8 0.1 add.54
  40.8 1.8 %collective-permute-done.4 = f32[8,72,192]{2,1,0:T(8,128)S(1)} collective-permute-done((f32[8,72,192]{2,1,0:T(8,128)S(1)}, f32[8,72,192]{2,1,0:T(8,128)S(1)}, u32[]{:S(2)}, u32[]{:S(2)}) %collective-permute-start.4) | collective-permute-done | bytes 442400 | tf_op jit(solution)/shard_map/ppermute | solution.py:195
  42.7 0.1 reshape.106
  42.8 0.1 slice_convert_fusion
  42.9 0.1 convert_element_type.53
  43.0 1.0 %convert_reduce_fusion = s32[1024]{0:T(1024)S(1)} fusion(s32[1024]{0:T(1024)S(1)} %convert_element_type.53, s32[1024]{0:T(1024)S(1)} %add.54), kind=kLoop, calls=%fused_computation | loop fusion | flops 5241856 | bytes 12288 | tf_op jit(solution)/shard_map/reduce_sum | solution.py:229
  44.0 0.1 convert_element_type.58
  44.1 0.3 select_reduce_fusion
  44.4 0.1 pad_add_fusion
  44.5 0.1 dynamic-slice_bitcast_fusion
  44.6 0.1 copy.15.row_rec_ref
  44.7 0.2 select_reduce_fusion.1
  44.9 0.2 multiply_reduce_fusion
  45.2 0.1 sqrt.12
  45.2 0.2 fusion.3
  45.4 0.0 copy-start
  45.5 0.5 fusion.1.col_unit_ref
  46.0 0.1 copy-done
  46.1 1.6 %shard_map.92 = f32[32,512]{1,0:T(8,128)} custom-call(f32[3,3]{1,0:T(4,128)S(1)} %copy-done, bf16[34,192]{1,0:T(8,128)(2,1)S(1)} %fusion.6.row_unit_ref, bf16[512,192]{1,0:T(8,128)(2,1)S(1)} %fusion.1.col_unit_ref, s32[34,1]{1,0:T(8,128)S(1)} %copy.15.row_rec_ref, s32[1,512]{1,0:T(1,128)S(1)} %bitcast.20), custom_call_target="tpu_custom_call" | custom-call | flops 7012352 | bytes 275200 | tf_op jit(solution)/shard_map/pallas_call | solution.py:161
  (19 shorter events, 0.3 us)
Async XLA Ops:
  0.0 1.5 %copy-start.2 = (s32[64]{0:T(128)S(1)}, s32[64]{0:T(128)}, u32[]{:S(2)}) copy-start(s32[64]{0:T(128)} %param.11) | copy-start | bytes 772
  0.0 1.5 %copy-start.3 = (s32[64]{0:T(128)S(1)}, s32[64]{0:T(128)}, u32[]{:S(2)}) copy-start(s32[64]{0:T(128)} %param.12) | copy-start | bytes 772
  0.0 1.5 %copy-start.4 = (s32[64]{0:T(128)S(1)}, s32[64]{0:T(128)}, u32[]{:S(2)}) copy-start(s32[64]{0:T(128)} %param.10) | copy-start | bytes 772
  0.0 1.6 %copy-start.1 = (f32[1024]{0:T(1024)S(1)}, f32[1024]{0:T(1024)}, u32[]{:S(2)}) copy-start(f32[1024]{0:T(1024)} %param.14) | copy-start | bytes 12292
  21.6 19.1 %copy-start.5 = (s32[16]{0:T(128)S(1)}, s32[16]{0:T(128)}, u32[]{:S(2)}) copy-start(s32[16]{0:T(128)} %constant.32.clone) | copy-start | bytes 196
  21.6 5.7 %collective-permute-start = (f32[1,72,192]{2,1,0:T(8,128)S(1)}, f32[1,72,192]{2,1,0:T(8,128)S(1)}, u32[]{:S(2)}, u32[]{:S(2)}) collective-permute-start(f32[1,72,192]{2,1,0:T(8,128)S(1)} %bitcast.16), channel_id=1, source_target_pairs={{0,4},{1,5},{2,6},{3,7},{4,0},{5,1},{6,2},{7,3},{8,12},{9,13},{10,... | collective-permute-start | bytes 165896 | tf_op jit(solution)/shard_map/ppermute | solution.py:195
  24.7 7.8 %collective-permute-start.1 = (f32[1,72,192]{2,1,0:T(8,128)S(1)}, f32[1,72,192]{2,1,0:T(8,128)S(1)}, u32[]{:S(2)}, u32[]{:S(2)}) collective-permute-start(f32[1,72,192]{2,1,0:T(8,128)S(1)} %bitcast.17), channel_id=1, source_target_pairs={{0,8},{1,9},{2,10},{3,11},{4,12},{5,13},{6,14},{7,15},{8,0},{9,1},... | collective-permute-start | bytes 165896 | tf_op jit(solution)/shard_map/ppermute | solution.py:195
  27.3 6.3 %collective-permute-start.2 = (f32[1,72,192]{2,1,0:T(8,128)S(1)}, f32[1,72,192]{2,1,0:T(8,128)S(1)}, u32[]{:S(2)}, u32[]{:S(2)}) collective-permute-start(f32[1,72,192]{2,1,0:T(8,128)S(1)} %bitcast.18), channel_id=1, source_target_pairs={{0,12},{1,13},{2,14},{3,15},{4,8},{5,9},{6,10},{7,11},{8,4},{9,5},... | collective-permute-start | bytes 165896 | tf_op jit(solution)/shard_map/ppermute | solution.py:195
  33.5 7.0 %collective-permute-start.3 = (f32[4,72,192]{2,1,0:T(8,128)S(1)}, f32[4,72,192]{2,1,0:T(8,128)S(1)}, u32[]{:S(2)}, u32[]{:S(2)}) collective-permute-start(f32[4,72,192]{2,1,0:T(8,128)S(1)} %pad_maximum_fusion), channel_id=1, source_target_pairs={{0,2},{1,3},{2,0},{3,1},{4,6},{5,7},{6,4},{7,5},{8,10},{9,11},{10,... | collective-permute-start | bytes 663560 | tf_op jit(solution)/shard_map/ppermute | solution.py:195
  40.6 2.1 %collective-permute-start.4 = (f32[8,72,192]{2,1,0:T(8,128)S(1)}, f32[8,72,192]{2,1,0:T(8,128)S(1)}, u32[]{:S(2)}, u32[]{:S(2)}) collective-permute-start(f32[8,72,192]{2,1,0:T(8,128)S(1)} %get-tuple-element.7), channel_id=1, source_target_pairs={{0,1},{1,0},{2,3},{3,2},{4,5},{5,4},{6,7},{7,6},{8,9},{9,8},{10,11... | collective-permute-start | bytes 1327112 | tf_op jit(solution)/shard_map/ppermute | solution.py:195
  45.4 0.7 %copy-start = (f32[3,3]{1,0:T(4,128)S(1)}, f32[3,3]{1,0:T(4,128)}, u32[]{:S(2)}) copy-start(f32[3,3]{1,0:T(4,128)} %k_ref.1) | copy-start | bytes 112

commit v24 on v22

--- a/solution.py
+++ b/solution.py
@@ -16,7 +16,7 @@
 
 PRECISE = lax.Precision.HIGHEST
 AFF_SCALE = 8.0
-SEG_BLOCK = 8
+SEG_BLOCK = 16
 WIN = SEGLEN + 8
 CONV_ROWS = 1024
 ONE_HOT_LIMIT = 1 << 20

time: 45.8 us -> 45.8 us (level)
  no operation moved by 1% of the time
where the time goes in v24:
time: 45.8 us; the launch traced here: 45.6 us
  Pallas kernels  19.4 us (42%)
  waiting for transfers between devices  13.4 us (29%)
  starting transfers between devices  7.34 us (16%)
  other arithmetic  2.4 us (5%)
  local copies, waits for them, and re-layouts  2.34 us (5%)
  matrix products  0.47 us (1%)
    pallas_call x1, Pallas kernels, embed_slots(): pl.pallas_call(_pool_kernel, out_shape=jax.ShapeDtypeStruct((slots + meta...  17.8 us
    ppermute x5, waiting for transfers between devices, gather_wide(): lax.ppermute(buf, 'wide', [(i, i ^ f) for i in range(group_size)])  13.4 us
    ppermute x5, starting transfers between devices, gather_wide(): lax.ppermute(buf, 'wide', [(i, i ^ f) for i in range(group_size)])  7.34 us
    unnamed x17, local copies, waits for them, and re-layouts  1.68 us
    pallas_call x1, Pallas kernels, smooth_affinity(): pl.pallas_call(_affinity_kernel, out_shape=jax.ShapeDtypeStruct((height,...  1.65 us
    reduce_sum x1, other arithmetic, per_device(): rank = jnp.sum(earlier.astype(jnp.int32), axis=1)  1.03 us
  transfers between devices with their start and end apart: 5, of which 4 were waited for; matrix products, arithmetic and copies ran while one was open for 0% of the time, Pallas kernels for 0%

profile of v24, /device:TPU:0, one launch (start us, length us, event | category | flops | bytes accessed | tf_op | source)
XLA Modules:
  0.0 45.6 jit_solution(15442537417035154809)
XLA Ops:
  0.0 0.0 copy-start.2
  0.0 0.0 copy-start.3
  0.0 0.0 copy-start.4
  0.0 0.0 copy-start.1
  0.0 1.5 %copy.13.frames_hbm = f32[2048,80]{1,0:T(8,128)S(1)} copy(f32[2048,80]{0,1:T(8,128)} %param.9) | data formatting | bytes 1310720 | tf_op args[0]
  1.5 0.0 copy-done.2
  1.5 0.0 copy-done.3
  1.5 0.0 copy-done.4
  1.6 0.1 select_maximum_fusion
  1.6 0.0 copy-done.1
  1.6 17.8 %shard_map.91 = f32[72,192]{1,0:T(8,128)S(1)} custom-call(s32[64]{0:T(128)S(1)} %broadcast_clamp_fusion.starts_ref, f32[2048,80]{1,0:T(8,128)S(1)} %copy.13.frames_hbm, f32[240,1024]{1,0:T(8,128)} %w_hbm.1, f32[1,1024]{1,0:T(1,128)S(1)} %bitcast.21, f32[192,2048]{1,0:T(8,128)} %bitcast.23, f32[8,192]{1,0:T(8,128)S(1)} %pad.9.meta_ref), custom_call_target="tpu_custom_call" | custom-call | flops 6379536384 | bytes 3260416 | tf_op jit(solution)/shard_map/pallas_call | solution.py:100
  19.4 0.0 copy-start.5
  19.4 3.1 %collective-permute-start = (f32[1,72,192]{2,1,0:T(8,128)S(1)}, f32[1,72,192]{2,1,0:T(8,128)S(1)}, u32[]{:S(2)}, u32[]{:S(2)}) collective-permute-start(f32[1,72,192]{2,1,0:T(8,128)S(1)} %bitcast.16), channel_id=1, source_target_pairs={{0,4},{1,5},{2,6},{3,7},{4,0},{5,1},{6,2},{7,3},{8,12},{9,13},{10,... | collective-permute-start | bytes 165896 | tf_op jit(solution)/shard_map/ppermute | solution.py:195
  22.5 2.6 %collective-permute-start.1 = (f32[1,72,192]{2,1,0:T(8,128)S(1)}, f32[1,72,192]{2,1,0:T(8,128)S(1)}, u32[]{:S(2)}, u32[]{:S(2)}) collective-permute-start(f32[1,72,192]{2,1,0:T(8,128)S(1)} %bitcast.17), channel_id=1, source_target_pairs={{0,8},{1,9},{2,10},{3,11},{4,12},{5,13},{6,14},{7,15},{8,0},{9,1},... | collective-permute-start | bytes 165896 | tf_op jit(solution)/shard_map/ppermute | solution.py:195
  25.1 0.0 collective-permute-start.2
  25.1 0.0 collective-permute-done
  25.1 5.2 %collective-permute-done.1 = f32[1,72,192]{2,1,0:T(8,128)S(1)} collective-permute-done((f32[1,72,192]{2,1,0:T(8,128)S(1)}, f32[1,72,192]{2,1,0:T(8,128)S(1)}, u32[]{:S(2)}, u32[]{:S(2)}) %collective-permute-start.1) | collective-permute-done | bytes 55328 | tf_op jit(solution)/shard_map/ppermute | solution.py:195
  30.3 1.1 %collective-permute-done.2 = f32[1,72,192]{2,1,0:T(8,128)S(1)} collective-permute-done((f32[1,72,192]{2,1,0:T(8,128)S(1)}, f32[1,72,192]{2,1,0:T(8,128)S(1)}, u32[]{:S(2)}, u32[]{:S(2)}) %collective-permute-start.2) | collective-permute-done | bytes 55328 | tf_op jit(solution)/shard_map/ppermute | solution.py:195
  31.4 1.6 %collective-permute-start.3 = (f32[4,72,192]{2,1,0:T(8,128)S(1)}, f32[4,72,192]{2,1,0:T(8,128)S(1)}, u32[]{:S(2)}, u32[]{:S(2)}) collective-permute-start(f32[4,72,192]{2,1,0:T(8,128)S(1)} %pad_maximum_fusion), channel_id=1, source_target_pairs={{0,2},{1,3},{2,0},{3,1},{4,6},{5,7},{6,4},{7,5},{8,10},{9,11},{10,... | collective-permute-start | bytes 663560 | tf_op jit(solution)/shard_map/ppermute | solution.py:195
  33.0 5.4 %collective-permute-done.3 = f32[4,72,192]{2,1,0:T(8,128)S(1)} collective-permute-done((f32[4,72,192]{2,1,0:T(8,128)S(1)}, f32[4,72,192]{2,1,0:T(8,128)S(1)}, u32[]{:S(2)}, u32[]{:S(2)}) %collective-permute-start.3) | collective-permute-done | bytes 221216 | tf_op jit(solution)/shard_map/ppermute | solution.py:195
  38.4 0.1 collective-permute-start.4
  38.5 0.0 copy-done.5
  38.5 0.1 iota_add_fusion
  38.6 0.1 add.54
  38.7 1.8 %collective-permute-done.4 = f32[8,72,192]{2,1,0:T(8,128)S(1)} collective-permute-done((f32[8,72,192]{2,1,0:T(8,128)S(1)}, f32[8,72,192]{2,1,0:T(8,128)S(1)}, u32[]{:S(2)}, u32[]{:S(2)}) %collective-permute-start.4) | collective-permute-done | bytes 442400 | tf_op jit(solution)/shard_map/ppermute | solution.py:195
  40.6 0.1 reshape.106
  40.7 0.1 slice_convert_fusion
  40.7 0.1 convert_element_type.53
  40.8 1.0 %convert_reduce_fusion = s32[1024]{0:T(1024)S(1)} fusion(s32[1024]{0:T(1024)S(1)} %convert_element_type.53, s32[1024]{0:T(1024)S(1)} %add.54), kind=kLoop, calls=%fused_computation | loop fusion | flops 5241856 | bytes 12288 | tf_op jit(solution)/shard_map/reduce_sum | solution.py:229
  41.9 0.1 convert_element_type.58
  41.9 0.3 select_reduce_fusion
  42.2 0.1 pad_add_fusion
  42.3 0.1 dynamic-slice_bitcast_fusion
  42.4 0.1 copy.15.row_rec_ref
  42.5 0.2 select_reduce_fusion.1
  42.7 0.2 multiply_reduce_fusion
  43.0 0.1 sqrt.12
  43.1 0.2 fusion.3
  43.3 0.0 copy-start
  43.3 0.5 %fusion.1.col_unit_ref = bf16[512,192]{1,0:T(8,128)(2,1)S(1)} fusion(bf16[1024,192]{1,0:T(8,128)(2,1)S(1)} %fusion.3, s32[1024]{0:T(1024)S(1)} %add_select_fusion), kind=kOutput, calls=%fused_computation.4 | convolution fusion | flops 201949184 | bytes 593920 | tf_op jit(solution)/shard_map/dot_general | solution.py:237
  43.8 0.1 copy-done
  44.0 1.6 %shard_map.92 = f32[32,512]{1,0:T(8,128)} custom-call(f32[3,3]{1,0:T(4,128)S(1)} %copy-done, bf16[34,192]{1,0:T(8,128)(2,1)S(1)} %fusion.6.row_unit_ref, bf16[512,192]{1,0:T(8,128)(2,1)S(1)} %fusion.1.col_unit_ref, s32[34,1]{1,0:T(8,128)S(1)} %copy.15.row_rec_ref, s32[1,512]{1,0:T(1,128)S(1)} %bitcast.20), custom_call_target="tpu_custom_call" | custom-call | flops 7012352 | bytes 275200 | tf_op jit(solution)/shard_map/pallas_call | solution.py:161
  (19 shorter events, 0.3 us)
Async XLA Ops:
  0.0 1.5 %copy-start.2 = (s32[64]{0:T(128)S(1)}, s32[64]{0:T(128)}, u32[]{:S(2)}) copy-start(s32[64]{0:T(128)} %param.11) | copy-start | bytes 772
  0.0 1.5 %copy-start.3 = (s32[64]{0:T(128)S(1)}, s32[64]{0:T(128)}, u32[]{:S(2)}) copy-start(s32[64]{0:T(128)} %param.12) | copy-start | bytes 772
  0.0 1.5 %copy-start.4 = (s32[64]{0:T(128)S(1)}, s32[64]{0:T(128)}, u32[]{:S(2)}) copy-start(s32[64]{0:T(128)} %param.10) | copy-start | bytes 772
  0.0 1.6 %copy-start.1 = (f32[1024]{0:T(1024)S(1)}, f32[1024]{0:T(1024)}, u32[]{:S(2)}) copy-start(f32[1024]{0:T(1024)} %param.14) | copy-start | bytes 12292
  19.4 19.1 %copy-start.5 = (s32[16]{0:T(128)S(1)}, s32[16]{0:T(128)}, u32[]{:S(2)}) copy-start(s32[16]{0:T(128)} %constant.32.clone) | copy-start | bytes 196
  19.4 5.7 %collective-permute-start = (f32[1,72,192]{2,1,0:T(8,128)S(1)}, f32[1,72,192]{2,1,0:T(8,128)S(1)}, u32[]{:S(2)}, u32[]{:S(2)}) collective-permute-start(f32[1,72,192]{2,1,0:T(8,128)S(1)} %bitcast.16), channel_id=1, source_target_pairs={{0,4},{1,5},{2,6},{3,7},{4,0},{5,1},{6,2},{7,3},{8,12},{9,13},{10,... | collective-permute-start | bytes 165896 | tf_op jit(solution)/shard_map/ppermute | solution.py:195
  22.5 7.8 %collective-permute-start.1 = (f32[1,72,192]{2,1,0:T(8,128)S(1)}, f32[1,72,192]{2,1,0:T(8,128)S(1)}, u32[]{:S(2)}, u32[]{:S(2)}) collective-permute-start(f32[1,72,192]{2,1,0:T(8,128)S(1)} %bitcast.17), channel_id=1, source_target_pairs={{0,8},{1,9},{2,10},{3,11},{4,12},{5,13},{6,14},{7,15},{8,0},{9,1},... | collective-permute-start | bytes 165896 | tf_op jit(solution)/shard_map/ppermute | solution.py:195
  25.1 6.3 %collective-permute-start.2 = (f32[1,72,192]{2,1,0:T(8,128)S(1)}, f32[1,72,192]{2,1,0:T(8,128)S(1)}, u32[]{:S(2)}, u32[]{:S(2)}) collective-permute-start(f32[1,72,192]{2,1,0:T(8,128)S(1)} %bitcast.18), channel_id=1, source_target_pairs={{0,12},{1,13},{2,14},{3,15},{4,8},{5,9},{6,10},{7,11},{8,4},{9,5},... | collective-permute-start | bytes 165896 | tf_op jit(solution)/shard_map/ppermute | solution.py:195
  31.4 7.0 %collective-permute-start.3 = (f32[4,72,192]{2,1,0:T(8,128)S(1)}, f32[4,72,192]{2,1,0:T(8,128)S(1)}, u32[]{:S(2)}, u32[]{:S(2)}) collective-permute-start(f32[4,72,192]{2,1,0:T(8,128)S(1)} %pad_maximum_fusion), channel_id=1, source_target_pairs={{0,2},{1,3},{2,0},{3,1},{4,6},{5,7},{6,4},{7,5},{8,10},{9,11},{10,... | collective-permute-start | bytes 663560 | tf_op jit(solution)/shard_map/ppermute | solution.py:195
  38.4 2.1 %collective-permute-start.4 = (f32[8,72,192]{2,1,0:T(8,128)S(1)}, f32[8,72,192]{2,1,0:T(8,128)S(1)}, u32[]{:S(2)}, u32[]{:S(2)}) collective-permute-start(f32[8,72,192]{2,1,0:T(8,128)S(1)} %get-tuple-element.7), channel_id=1, source_target_pairs={{0,1},{1,0},{2,3},{3,2},{4,5},{5,4},{6,7},{7,6},{8,9},{9,8},{10,11... | collective-permute-start | bytes 1327112 | tf_op jit(solution)/shard_map/ppermute | solution.py:195
  43.3 0.7 %copy-start = (f32[3,3]{1,0:T(4,128)S(1)}, f32[3,3]{1,0:T(4,128)}, u32[]{:S(2)}) copy-start(f32[3,3]{1,0:T(4,128)} %k_ref.1) | copy-start | bytes 112

commit v25 on v22

--- a/solution.py
+++ b/solution.py
@@ -60,7 +60,7 @@
         means = []
         stds = []
         for j in range(SEG_BLOCK):
-            start = starts_ref[blk * SEG_BLOCK + j]
+            start = jnp.clip(starts_ref[blk * SEG_BLOCK + j], 0, rows - SEGLEN)
             base = jnp.minimum((start // 8) * 8, rows - WIN)
             shift = start - base
             inside = (frame_idx >= shift) & (frame_idx < shift + SEGLEN)
@@ -90,7 +90,7 @@
 def embed_slots(frames, seg_start, seg_dest, rec_id, conv_weight, conv_bias, proj_weight):
     rows = frames.shape[0]
     slots = seg_start.shape[0]
-    starts = jnp.clip(seg_start, 0, rows - SEGLEN).astype(jnp.int32)
+    starts = seg_start.astype(jnp.int32)
     meta = jnp.concatenate([seg_dest.astype(jnp.float32), rec_id.astype(jnp.float32)])
     meta_len = -(-meta.shape[0] // EMB) * EMB
     meta_rows = jnp.pad(meta, (0, meta_len - meta.shape[0])).reshape(-1, EMB)

time: 45.8 us -> 45.7 us (level)
  no operation moved by 1% of the time
where the time goes in v25:
time: 45.7 us; the launch traced here: 45.6 us
  Pallas kernels  19.4 us (42%)
  waiting for transfers between devices  13.4 us (29%)
  starting transfers between devices  7.33 us (16%)
  other arithmetic  2.4 us (5%)
  local copies, waits for them, and re-layouts  2.34 us (5%)
  matrix products  0.46 us (1%)
    pallas_call x1, Pallas kernels, embed_slots(): pl.pallas_call(_pool_kernel, out_shape=jax.ShapeDtypeStruct((slots + meta...  17.7 us
    ppermute x5, waiting for transfers between devices, gather_wide(): lax.ppermute(buf, 'wide', [(i, i ^ f) for i in range(group_size)])  13.4 us
    ppermute x5, starting transfers between devices, gather_wide(): lax.ppermute(buf, 'wide', [(i, i ^ f) for i in range(group_size)])  7.33 us
    unnamed x17, local copies, waits for them, and re-layouts  1.68 us
    pallas_call x1, Pallas kernels, smooth_affinity(): pl.pallas_call(_affinity_kernel, out_shape=jax.ShapeDtypeStruct((height,...  1.65 us
    reduce_sum x1, other arithmetic, per_device(): rank = jnp.sum(earlier.astype(jnp.int32), axis=1)  1.03 us
  transfers between devices with their start and end apart: 5, of which 4 were waited for; matrix products, arithmetic and copies ran while one was open for 0% of the time, Pallas kernels for 0%

profile of v25, /device:TPU:0, one launch (start us, length us, event | category | flops | bytes accessed | tf_op | source)
XLA Modules:
  0.0 45.6 jit_solution(11627748200353282785)
XLA Ops:
  0.0 0.0 copy-start.3
  0.0 0.0 copy-start.4
  0.0 0.0 copy-start.1
  0.0 0.0 copy-start.2
  0.0 1.5 %copy.13.frames_hbm = f32[2048,80]{1,0:T(8,128)S(1)} copy(f32[2048,80]{0,1:T(8,128)} %param.9) | data formatting | bytes 1310720 | tf_op args[0]
  1.5 0.0 copy-done.3
  1.5 0.0 copy-done.4
  1.5 0.1 select_maximum_fusion
  1.6 0.0 copy-done.1
  1.6 0.0 copy-done.2
  1.6 17.7 %shard_map.91 = f32[72,192]{1,0:T(8,128)S(1)} custom-call(s32[64]{0:T(128)S(1)} %copy-done.2, f32[2048,80]{1,0:T(8,128)S(1)} %copy.13.frames_hbm, f32[240,1024]{1,0:T(8,128)} %w_hbm.1, f32[1,1024]{1,0:T(1,128)S(1)} %bitcast.21, f32[192,2048]{1,0:T(8,128)} %bitcast.23, f32[8,192]{1,0:T(8,128)S(1)} %pad.9.meta_ref), custom_call_target="tpu_custom_call" | custom-call | flops 6379536384 | bytes 3260416 | tf_op jit(solution)/shard_map/pallas_call | solution.py:100
  19.4 0.0 copy-start.5
  19.4 3.1 %collective-permute-start = (f32[1,72,192]{2,1,0:T(8,128)S(1)}, f32[1,72,192]{2,1,0:T(8,128)S(1)}, u32[]{:S(2)}, u32[]{:S(2)}) collective-permute-start(f32[1,72,192]{2,1,0:T(8,128)S(1)} %bitcast.16), channel_id=1, source_target_pairs={{0,4},{1,5},{2,6},{3,7},{4,0},{5,1},{6,2},{7,3},{8,12},{9,13},{10,... | collective-permute-start | bytes 165896 | tf_op jit(solution)/shard_map/ppermute | solution.py:195
  22.5 2.6 %collective-permute-start.1 = (f32[1,72,192]{2,1,0:T(8,128)S(1)}, f32[1,72,192]{2,1,0:T(8,128)S(1)}, u32[]{:S(2)}, u32[]{:S(2)}) collective-permute-start(f32[1,72,192]{2,1,0:T(8,128)S(1)} %bitcast.17), channel_id=1, source_target_pairs={{0,8},{1,9},{2,10},{3,11},{4,12},{5,13},{6,14},{7,15},{8,0},{9,1},... | collective-permute-start | bytes 165896 | tf_op jit(solution)/shard_map/ppermute | solution.py:195
  25.1 0.0 collective-permute-start.2
  25.1 0.0 collective-permute-done
  25.1 5.2 %collective-permute-done.1 = f32[1,72,192]{2,1,0:T(8,128)S(1)} collective-permute-done((f32[1,72,192]{2,1,0:T(8,128)S(1)}, f32[1,72,192]{2,1,0:T(8,128)S(1)}, u32[]{:S(2)}, u32[]{:S(2)}) %collective-permute-start.1) | collective-permute-done | bytes 55328 | tf_op jit(solution)/shard_map/ppermute | solution.py:195
  30.3 1.1 %collective-permute-done.2 = f32[1,72,192]{2,1,0:T(8,128)S(1)} collective-permute-done((f32[1,72,192]{2,1,0:T(8,128)S(1)}, f32[1,72,192]{2,1,0:T(8,128)S(1)}, u32[]{:S(2)}, u32[]{:S(2)}) %collective-permute-start.2) | collective-permute-done | bytes 55328 | tf_op jit(solution)/shard_map/ppermute | solution.py:195
  31.3 1.6 %collective-permute-start.3 = (f32[4,72,192]{2,1,0:T(8,128)S(1)}, f32[4,72,192]{2,1,0:T(8,128)S(1)}, u32[]{:S(2)}, u32[]{:S(2)}) collective-permute-start(f32[4,72,192]{2,1,0:T(8,128)S(1)} %pad_maximum_fusion), channel_id=1, source_target_pairs={{0,2},{1,3},{2,0},{3,1},{4,6},{5,7},{6,4},{7,5},{8,10},{9,11},{10,... | collective-permute-start | bytes 663560 | tf_op jit(solution)/shard_map/ppermute | solution.py:195
  33.0 5.4 %collective-permute-done.3 = f32[4,72,192]{2,1,0:T(8,128)S(1)} collective-permute-done((f32[4,72,192]{2,1,0:T(8,128)S(1)}, f32[4,72,192]{2,1,0:T(8,128)S(1)}, u32[]{:S(2)}, u32[]{:S(2)}) %collective-permute-start.3) | collective-permute-done | bytes 221216 | tf_op jit(solution)/shard_map/ppermute | solution.py:195
  38.4 0.1 collective-permute-start.4
  38.5 0.0 copy-done.5
  38.5 0.1 iota_add_fusion
  38.6 0.1 add.54
  38.6 1.8 %collective-permute-done.4 = f32[8,72,192]{2,1,0:T(8,128)S(1)} collective-permute-done((f32[8,72,192]{2,1,0:T(8,128)S(1)}, f32[8,72,192]{2,1,0:T(8,128)S(1)}, u32[]{:S(2)}, u32[]{:S(2)}) %collective-permute-start.4) | collective-permute-done | bytes 442400 | tf_op jit(solution)/shard_map/ppermute | solution.py:195
  40.5 0.1 reshape.106
  40.6 0.1 slice_convert_fusion
  40.7 0.1 convert_element_type.53
  40.8 1.0 %convert_reduce_fusion = s32[1024]{0:T(1024)S(1)} fusion(s32[1024]{0:T(1024)S(1)} %convert_element_type.53, s32[1024]{0:T(1024)S(1)} %add.54), kind=kLoop, calls=%fused_computation | loop fusion | flops 5241856 | bytes 12288 | tf_op jit(solution)/shard_map/reduce_sum | solution.py:229
  41.8 0.1 convert_element_type.58
  41.9 0.3 select_reduce_fusion
  42.2 0.1 pad_add_fusion
  42.3 0.1 dynamic-slice_bitcast_fusion
  42.3 0.1 copy.15.row_rec_ref
  42.5 0.2 select_reduce_fusion.1
  42.7 0.2 multiply_reduce_fusion
  42.9 0.1 sqrt.12
  43.0 0.2 fusion.3
  43.2 0.0 copy-start
  43.2 0.5 %fusion.1.col_unit_ref = bf16[512,192]{1,0:T(8,128)(2,1)S(1)} fusion(bf16[1024,192]{1,0:T(8,128)(2,1)S(1)} %fusion.3, s32[1024]{0:T(1024)S(1)} %add_select_fusion), kind=kOutput, calls=%fused_computation.4 | convolution fusion | flops 201949184 | bytes 593920 | tf_op jit(solution)/shard_map/dot_general | solution.py:237
  43.8 0.1 copy-done
  43.9 1.6 %shard_map.92 = f32[32,512]{1,0:T(8,128)} custom-call(f32[3,3]{1,0:T(4,128)S(1)} %copy-done, bf16[34,192]{1,0:T(8,128)(2,1)S(1)} %fusion.6.row_unit_ref, bf16[512,192]{1,0:T(8,128)(2,1)S(1)} %fusion.1.col_unit_ref, s32[34,1]{1,0:T(8,128)S(1)} %copy.15.row_rec_ref, s32[1,512]{1,0:T(1,128)S(1)} %bitcast.20), custom_call_target="tpu_custom_call" | custom-call | flops 7012352 | bytes 275200 | tf_op jit(solution)/shard_map/pallas_call | solution.py:161
  (18 shorter events, 0.3 us)
Async XLA Ops:
  0.0 1.5 %copy-start.3 = (s32[64]{0:T(128)S(1)}, s32[64]{0:T(128)}, u32[]{:S(2)}) copy-start(s32[64]{0:T(128)} %param.11) | copy-start | bytes 772
  0.0 1.5 %copy-start.4 = (s32[64]{0:T(128)S(1)}, s32[64]{0:T(128)}, u32[]{:S(2)}) copy-start(s32[64]{0:T(128)} %param.12) | copy-start | bytes 772
  0.0 1.6 %copy-start.1 = (f32[1024]{0:T(1024)S(1)}, f32[1024]{0:T(1024)}, u32[]{:S(2)}) copy-start(f32[1024]{0:T(1024)} %param.14) | copy-start | bytes 12292
  0.0 1.6 %copy-start.2 = (s32[64]{0:T(128)S(1)}, s32[64]{0:T(128)}, u32[]{:S(2)}) copy-start(s32[64]{0:T(128)} %starts_ref.1) | copy-start | bytes 772
  19.4 19.1 %copy-start.5 = (s32[16]{0:T(128)S(1)}, s32[16]{0:T(128)}, u32[]{:S(2)}) copy-start(s32[16]{0:T(128)} %constant.30.clone) | copy-start | bytes 196
  19.4 5.7 %collective-permute-start = (f32[1,72,192]{2,1,0:T(8,128)S(1)}, f32[1,72,192]{2,1,0:T(8,128)S(1)}, u32[]{:S(2)}, u32[]{:S(2)}) collective-permute-start(f32[1,72,192]{2,1,0:T(8,128)S(1)} %bitcast.16), channel_id=1, source_target_pairs={{0,4},{1,5},{2,6},{3,7},{4,0},{5,1},{6,2},{7,3},{8,12},{9,13},{10,... | collective-permute-start | bytes 165896 | tf_op jit(solution)/shard_map/ppermute | solution.py:195
  22.5 7.8 %collective-permute-start.1 = (f32[1,72,192]{2,1,0:T(8,128)S(1)}, f32[1,72,192]{2,1,0:T(8,128)S(1)}, u32[]{:S(2)}, u32[]{:S(2)}) collective-permute-start(f32[1,72,192]{2,1,0:T(8,128)S(1)} %bitcast.17), channel_id=1, source_target_pairs={{0,8},{1,9},{2,10},{3,11},{4,12},{5,13},{6,14},{7,15},{8,0},{9,1},... | collective-permute-start | bytes 165896 | tf_op jit(solution)/shard_map/ppermute | solution.py:195
  25.1 6.3 %collective-permute-start.2 = (f32[1,72,192]{2,1,0:T(8,128)S(1)}, f32[1,72,192]{2,1,0:T(8,128)S(1)}, u32[]{:S(2)}, u32[]{:S(2)}) collective-permute-start(f32[1,72,192]{2,1,0:T(8,128)S(1)} %bitcast.18), channel_id=1, source_target_pairs={{0,12},{1,13},{2,14},{3,15},{4,8},{5,9},{6,10},{7,11},{8,4},{9,5},... | collective-permute-start | bytes 165896 | tf_op jit(solution)/shard_map/ppermute | solution.py:195
  31.3 7.0 %collective-permute-start.3 = (f32[4,72,192]{2,1,0:T(8,128)S(1)}, f32[4,72,192]{2,1,0:T(8,128)S(1)}, u32[]{:S(2)}, u32[]{:S(2)}) collective-permute-start(f32[4,72,192]{2,1,0:T(8,128)S(1)} %pad_maximum_fusion), channel_id=1, source_target_pairs={{0,2},{1,3},{2,0},{3,1},{4,6},{5,7},{6,4},{7,5},{8,10},{9,11},{10,... | collective-permute-start | bytes 663560 | tf_op jit(solution)/shard_map/ppermute | solution.py:195
  38.4 2.1 %collective-permute-start.4 = (f32[8,72,192]{2,1,0:T(8,128)S(1)}, f32[8,72,192]{2,1,0:T(8,128)S(1)}, u32[]{:S(2)}, u32[]{:S(2)}) collective-permute-start(f32[8,72,192]{2,1,0:T(8,128)S(1)} %get-tuple-element.7), channel_id=1, source_target_pairs={{0,1},{1,0},{2,3},{3,2},{4,5},{5,4},{6,7},{7,6},{8,9},{9,8},{10,11... | collective-permute-start | bytes 1327112 | tf_op jit(solution)/shard_map/ppermute | solution.py:195
  43.2 0.7 %copy-start = (f32[3,3]{1,0:T(4,128)S(1)}, f32[3,3]{1,0:T(4,128)}, u32[]{:S(2)}) copy-start(f32[3,3]{1,0:T(4,128)} %k_ref.1) | copy-start | bytes 112

commit v26 on v25

--- a/solution.py
+++ b/solution.py
@@ -186,7 +186,7 @@
     bit = group_size.bit_length() - 2
     while bit >= 0:
         if bit >= 2:
-            flips = [m << (bit - 1) for m in (1, 2, 3)]
+            flips = [m << (bit - 1) for m in (3, 2, 1)]
             bit -= 2
         else:
             flips = [1 << bit]

time: 45.7 us -> 46.6 us (1.020)
  waiting for transfers between devices: 13.4 us -> 14.2 us
    ppermute x5, waiting for transfers between devices: 13.4 us -> 14.2 us  [gather_wide(): lax.ppermute(buf, 'wide', [(i, i ^ f) for i in range(group_size)])]
where the time goes in v26:
time: 46.6 us; the launch traced here: 46.4 us
  Pallas kernels  19.4 us (42%)
  waiting for transfers between devices  14.2 us (30%)
  starting transfers between devices  7.41 us (16%)
  other arithmetic  2.4 us (5%)
  local copies, waits for them, and re-layouts  2.34 us (5%)
    pallas_call x1, Pallas kernels, embed_slots(): pl.pallas_call(_pool_kernel, out_shape=jax.ShapeDtypeStruct((slots + meta...  17.7 us
    ppermute x5, waiting for transfers between devices, gather_wide(): lax.ppermute(buf, 'wide', [(i, i ^ f) for i in range(group_size)])  14.2 us
    ppermute x5, starting transfers between devices, gather_wide(): lax.ppermute(buf, 'wide', [(i, i ^ f) for i in range(group_size)])  7.41 us
    unnamed x17, local copies, waits for them, and re-layouts  1.68 us
    pallas_call x1, Pallas kernels, smooth_affinity(): pl.pallas_call(_affinity_kernel, out_shape=jax.ShapeDtypeStruct((height,...  1.65 us
    reduce_sum x1, other arithmetic, per_device(): rank = jnp.sum(earlier.astype(jnp.int32), axis=1)  1.03 us
  transfers between devices with their start and end apart: 5, of which 4 were waited for; matrix products, arithmetic and copies ran while one was open for 0% of the time, Pallas kernels for 0%

profile of v26, /device:TPU:0, one launch (start us, length us, event | category | flops | bytes accessed | tf_op | source)
XLA Modules:
  0.0 46.4 jit_solution(11778472106077145555)
XLA Ops:
  0.0 0.0 copy-start.3
  0.0 0.0 copy-start.4
  0.0 0.0 copy-start.1
  0.0 0.0 copy-start.2
  0.0 1.5 %copy.13.frames_hbm = f32[2048,80]{1,0:T(8,128)S(1)} copy(f32[2048,80]{0,1:T(8,128)} %param.9) | data formatting | bytes 1310720 | tf_op args[0]
  1.5 0.0 copy-done.3
  1.5 0.0 copy-done.4
  1.5 0.1 select_maximum_fusion
  1.6 0.0 copy-done.1
  1.6 0.0 copy-done.2
  1.6 17.7 %shard_map.91 = f32[72,192]{1,0:T(8,128)S(1)} custom-call(s32[64]{0:T(128)S(1)} %copy-done.2, f32[2048,80]{1,0:T(8,128)S(1)} %copy.13.frames_hbm, f32[240,1024]{1,0:T(8,128)} %w_hbm.1, f32[1,1024]{1,0:T(1,128)S(1)} %bitcast.21, f32[192,2048]{1,0:T(8,128)} %bitcast.23, f32[8,192]{1,0:T(8,128)S(1)} %pad.9.meta_ref), custom_call_target="tpu_custom_call" | custom-call | flops 6379536384 | bytes 3260416 | tf_op jit(solution)/shard_map/pallas_call | solution.py:100
  19.4 0.0 copy-start.5
  19.4 5.1 %collective-permute-start = (f32[1,72,192]{2,1,0:T(8,128)S(1)}, f32[1,72,192]{2,1,0:T(8,128)S(1)}, u32[]{:S(2)}, u32[]{:S(2)}) collective-permute-start(f32[1,72,192]{2,1,0:T(8,128)S(1)} %bitcast.16), channel_id=1, source_target_pairs={{0,12},{1,13},{2,14},{3,15},{4,8},{5,9},{6,10},{7,11},{8,4},{9,5},... | collective-permute-start | bytes 165896 | tf_op jit(solution)/shard_map/ppermute | solution.py:195
  24.5 0.0 collective-permute-start.1
  24.5 0.6 %collective-permute-start.2 = (f32[1,72,192]{2,1,0:T(8,128)S(1)}, f32[1,72,192]{2,1,0:T(8,128)S(1)}, u32[]{:S(2)}, u32[]{:S(2)}) collective-permute-start(f32[1,72,192]{2,1,0:T(8,128)S(1)} %bitcast.18), channel_id=1, source_target_pairs={{0,4},{1,5},{2,6},{3,7},{4,0},{5,1},{6,2},{7,3},{8,12},{9,13},{10,... | collective-permute-start | bytes 165896 | tf_op jit(solution)/shard_map/ppermute | solution.py:195
  25.2 2.1 %collective-permute-done = f32[1,72,192]{2,1,0:T(8,128)S(1)} collective-permute-done((f32[1,72,192]{2,1,0:T(8,128)S(1)}, f32[1,72,192]{2,1,0:T(8,128)S(1)}, u32[]{:S(2)}, u32[]{:S(2)}) %collective-permute-start) | collective-permute-done | bytes 55328 | tf_op jit(solution)/shard_map/ppermute | solution.py:195
  27.3 3.5 %collective-permute-done.1 = f32[1,72,192]{2,1,0:T(8,128)S(1)} collective-permute-done((f32[1,72,192]{2,1,0:T(8,128)S(1)}, f32[1,72,192]{2,1,0:T(8,128)S(1)}, u32[]{:S(2)}, u32[]{:S(2)}) %collective-permute-start.1) | collective-permute-done | bytes 55328 | tf_op jit(solution)/shard_map/ppermute | solution.py:195
  30.7 0.0 collective-permute-done.2
  30.7 1.6 %collective-permute-start.3 = (f32[4,72,192]{2,1,0:T(8,128)S(1)}, f32[4,72,192]{2,1,0:T(8,128)S(1)}, u32[]{:S(2)}, u32[]{:S(2)}) collective-permute-start(f32[4,72,192]{2,1,0:T(8,128)S(1)} %pad_maximum_fusion), channel_id=1, source_target_pairs={{0,2},{1,3},{2,0},{3,1},{4,6},{5,7},{6,4},{7,5},{8,10},{9,11},{10,... | collective-permute-start | bytes 663560 | tf_op jit(solution)/shard_map/ppermute | solution.py:195
  32.4 6.8 %collective-permute-done.3 = f32[4,72,192]{2,1,0:T(8,128)S(1)} collective-permute-done((f32[4,72,192]{2,1,0:T(8,128)S(1)}, f32[4,72,192]{2,1,0:T(8,128)S(1)}, u32[]{:S(2)}, u32[]{:S(2)}) %collective-permute-start.3) | collective-permute-done | bytes 221216 | tf_op jit(solution)/shard_map/ppermute | solution.py:195
  39.2 0.1 collective-permute-start.4
  39.3 0.0 copy-done.5
  39.3 0.1 iota_add_fusion
  39.4 0.1 add.54
  39.5 1.8 %collective-permute-done.4 = f32[8,72,192]{2,1,0:T(8,128)S(1)} collective-permute-done((f32[8,72,192]{2,1,0:T(8,128)S(1)}, f32[8,72,192]{2,1,0:T(8,128)S(1)}, u32[]{:S(2)}, u32[]{:S(2)}) %collective-permute-start.4) | collective-permute-done | bytes 442400 | tf_op jit(solution)/shard_map/ppermute | solution.py:195
  41.3 0.1 reshape.106
  41.4 0.1 slice_convert_fusion
  41.5 0.1 convert_element_type.53
  41.6 1.0 %convert_reduce_fusion = s32[1024]{0:T(1024)S(1)} fusion(s32[1024]{0:T(1024)S(1)} %convert_element_type.53, s32[1024]{0:T(1024)S(1)} %add.54), kind=kLoop, calls=%fused_computation | loop fusion | flops 5241856 | bytes 12288 | tf_op jit(solution)/shard_map/reduce_sum | solution.py:229
  42.6 0.1 convert_element_type.58
  42.7 0.3 select_reduce_fusion
  43.0 0.1 pad_add_fusion
  43.1 0.1 dynamic-slice_bitcast_fusion
  43.2 0.1 copy.15.row_rec_ref
  43.3 0.2 select_reduce_fusion.1
  43.5 0.2 multiply_reduce_fusion
  43.8 0.1 sqrt.12
  43.8 0.2 fusion.3
  44.1 0.0 copy-start
  44.1 0.5 %fusion.1.col_unit_ref = bf16[512,192]{1,0:T(8,128)(2,1)S(1)} fusion(bf16[1024,192]{1,0:T(8,128)(2,1)S(1)} %fusion.3, s32[1024]{0:T(1024)S(1)} %add_select_fusion), kind=kOutput, calls=%fused_computation.4 | convolution fusion | flops 201949184 | bytes 593920 | tf_op jit(solution)/shard_map/dot_general | solution.py:237
  44.6 0.1 copy-done
  44.7 1.6 %shard_map.92 = f32[32,512]{1,0:T(8,128)} custom-call(f32[3,3]{1,0:T(4,128)S(1)} %copy-done, bf16[34,192]{1,0:T(8,128)(2,1)S(1)} %fusion.6.row_unit_ref, bf16[512,192]{1,0:T(8,128)(2,1)S(1)} %fusion.1.col_unit_ref, s32[34,1]{1,0:T(8,128)S(1)} %copy.15.row_rec_ref, s32[1,512]{1,0:T(1,128)S(1)} %bitcast.20), custom_call_target="tpu_custom_call" | custom-call | flops 7012352 | bytes 275200 | tf_op jit(solution)/shard_map/pallas_call | solution.py:161
  (18 shorter events, 0.3 us)
Async XLA Ops:
  0.0 1.5 %copy-start.3 = (s32[64]{0:T(128)S(1)}, s32[64]{0:T(128)}, u32[]{:S(2)}) copy-start(s32[64]{0:T(128)} %param.11) | copy-start | bytes 772
  0.0 1.5 %copy-start.4 = (s32[64]{0:T(128)S(1)}, s32[64]{0:T(128)}, u32[]{:S(2)}) copy-start(s32[64]{0:T(128)} %param.12) | copy-start | bytes 772
  0.0 1.6 %copy-start.1 = (f32[1024]{0:T(1024)S(1)}, f32[1024]{0:T(1024)}, u32[]{:S(2)}) copy-start(f32[1024]{0:T(1024)} %param.14) | copy-start | bytes 12292
  0.0 1.6 %copy-start.2 = (s32[64]{0:T(128)S(1)}, s32[64]{0:T(128)}, u32[]{:S(2)}) copy-start(s32[64]{0:T(128)} %starts_ref.1) | copy-start | bytes 772
  19.4 19.9 %copy-start.5 = (s32[16]{0:T(128)S(1)}, s32[16]{0:T(128)}, u32[]{:S(2)}) copy-start(s32[16]{0:T(128)} %constant.30.clone) | copy-start | bytes 196
  19.4 7.9 %collective-permute-start = (f32[1,72,192]{2,1,0:T(8,128)S(1)}, f32[1,72,192]{2,1,0:T(8,128)S(1)}, u32[]{:S(2)}, u32[]{:S(2)}) collective-permute-start(f32[1,72,192]{2,1,0:T(8,128)S(1)} %bitcast.16), channel_id=1, source_target_pairs={{0,12},{1,13},{2,14},{3,15},{4,8},{5,9},{6,10},{7,11},{8,4},{9,5},... | collective-permute-start | bytes 165896 | tf_op jit(solution)/shard_map/ppermute | solution.py:195
  24.5 6.2 %collective-permute-start.1 = (f32[1,72,192]{2,1,0:T(8,128)S(1)}, f32[1,72,192]{2,1,0:T(8,128)S(1)}, u32[]{:S(2)}, u32[]{:S(2)}) collective-permute-start(f32[1,72,192]{2,1,0:T(8,128)S(1)} %bitcast.17), channel_id=1, source_target_pairs={{0,8},{1,9},{2,10},{3,11},{4,12},{5,13},{6,14},{7,15},{8,0},{9,1},... | collective-permute-start | bytes 165896 | tf_op jit(solution)/shard_map/ppermute | solution.py:195
  24.5 6.2 %collective-permute-start.2 = (f32[1,72,192]{2,1,0:T(8,128)S(1)}, f32[1,72,192]{2,1,0:T(8,128)S(1)}, u32[]{:S(2)}, u32[]{:S(2)}) collective-permute-start(f32[1,72,192]{2,1,0:T(8,128)S(1)} %bitcast.18), channel_id=1, source_target_pairs={{0,4},{1,5},{2,6},{3,7},{4,0},{5,1},{6,2},{7,3},{8,12},{9,13},{10,... | collective-permute-start | bytes 165896 | tf_op jit(solution)/shard_map/ppermute | solution.py:195
  30.7 8.4 %collective-permute-start.3 = (f32[4,72,192]{2,1,0:T(8,128)S(1)}, f32[4,72,192]{2,1,0:T(8,128)S(1)}, u32[]{:S(2)}, u32[]{:S(2)}) collective-permute-start(f32[4,72,192]{2,1,0:T(8,128)S(1)} %pad_maximum_fusion), channel_id=1, source_target_pairs={{0,2},{1,3},{2,0},{3,1},{4,6},{5,7},{6,4},{7,5},{8,10},{9,11},{10,... | collective-permute-start | bytes 663560 | tf_op jit(solution)/shard_map/ppermute | solution.py:195
  39.2 2.1 %collective-permute-start.4 = (f32[8,72,192]{2,1,0:T(8,128)S(1)}, f32[8,72,192]{2,1,0:T(8,128)S(1)}, u32[]{:S(2)}, u32[]{:S(2)}) collective-permute-start(f32[8,72,192]{2,1,0:T(8,128)S(1)} %get-tuple-element.7), channel_id=1, source_target_pairs={{0,1},{1,0},{2,3},{3,2},{4,5},{5,4},{6,7},{7,6},{8,9},{9,8},{10,11... | collective-permute-start | bytes 1327112 | tf_op jit(solution)/shard_map/ppermute | solution.py:195
  44.1 0.7 %copy-start = (f32[3,3]{1,0:T(4,128)S(1)}, f32[3,3]{1,0:T(4,128)}, u32[]{:S(2)}) copy-start(f32[3,3]{1,0:T(4,128)} %k_ref.1) | copy-start | bytes 112
